TPU v7x, 32 devices: a whole 2x2x4 slice. The times are simulated.
32 devices in a mesh: gx: 8 (over z, x), gy: 4 (over y, core).
Axes of the slice: x: 2, y: 2, z: 4, core: 2. Of those that a mesh axis runs over, the one named last changes fastest.
Arguments:
- layer_slowness: float32 [8], replicated, may hold values from 0.5 to 2
- layer_rigidity: float32 [8], replicated, may hold values from 0.5 to 4
- layer_damping: float32 [8], replicated, may hold values from 0.02 to 0.2
- layer_of_level: int32 [32], replicated, may hold values from 0 to 7
- slot_offset: int32 [8192], replicated, may hold values from 0 to 2047
- slot_level: int32 [8192], replicated, may hold values from 0 to 31
- slot_target: int32 [8192], P(('gx', 'gy')), may hold values from 0 to 786431
- live_count: int32 [32], P(('gx', 'gy')), may hold values from 1 to 256, 4096 in all
- moduli: float32 [2, 256, 128, 256], P(None, 'gx', 'gy'), may hold values from 0.02 to 0.06
- field_old: float32 [3, 256, 128, 256], P(None, 'gx', 'gy'), may hold values from -0.3 to 0.3
- field_now: float32 [3, 256, 128, 256], P(None, 'gx', 'gy'), may hold values from -0.3 to 0.3
Outputs:
- final_field: float32 [3, 256, 128, 256], P(None, 'gx', 'gy')
- prior_field: float32 [3, 256, 128, 256], P(None, 'gx', 'gy')
Inputs may be any that keep to these rules, and one draw needn't show every extreme that they name: live_count sums to 8192 // 2 over all owners, and some owner uses all 256 slots.
All inputs are finite; a program needn't handle non-finite values. No bound on the sum of `live_count` on one device may be relied on, other than what follows from the above.
Results may differ from a plain program's by a relative error of at most 0.0036.
Values may be sent and summed in bfloat16 or wider, within the bound.
No kernel may reach another device: no remote copies, remote signals or barrier semaphores. Data moves between devices by JAX's collectives and lax.ppermute only.
A program may use at most 128 MiB of HBM per device.

v0:
```python
import math

import jax
import jax.numpy as jnp
from jax import lax
from jax.sharding import PartitionSpec as P
from jax.experimental import pallas as pl
from jax.experimental.pallas import tpu as pltpu
import functools

F = 128
NK = 1024
NR = 2048
ND = 32
STEPS = 4
TSTART = 32


step_depth = 0.25


def padded_2(block, sides, width):
    for axis, dim in sides:
        count = lax.axis_size(axis)
        forward = [(i, i + 1) for i in range(count - 1)]
        backward = [(target, source) for source, target in forward]
        low = lax.ppermute(
            lax.slice_in_dim(block, block.shape[dim] - width, None, axis=dim), axis, forward
        )
        high = lax.ppermute(lax.slice_in_dim(block, 0, width, axis=dim), axis, backward)
        block = jnp.concatenate([low, block, high], axis=dim)
    return block


TAPS = ((-2, -1.0), (-1, 16.0), (1, 16.0), (2, -1.0))


def step_kernel(up_ref, prev_ref, mod_ref, src_ref, out_ref, *, bx):
    i = pl.program_id(0)
    depth = out_ref.shape[3]
    lane = lax.broadcasted_iota(jnp.int32, (8, depth), 1)
    masks = {dz: (lane + dz >= 0) & (lane + dz < depth) for dz in (-2, -1, 1, 2)}

    def zs(v, dz):
        if dz == 0:
            return v
        return jnp.where(masks[dz], pltpu.roll(v, (-dz) % depth, 1), 0.0)

    def plane(p, carry):
        xp = i * bx + p + 2
        for g in range(out_ref.shape[2] // 8):
            def load(c, dx, dy):
                return up_ref[c, xp + dx, pl.ds(8 * g + 2 + dy, 8), :]

            lam = mod_ref[0, p, pl.ds(8 * g, 8), :]
            mu = mod_ref[1, p, pl.ds(8 * g, 8), :]
            stiff = lam + 2.0 * mu
            coup = lam + mu
            centers = [load(c, 0, 0) for c in range(3)]

            def curv(c, axis):
                center = centers[c]
                acc = -30.0 * center
                for off, w in TAPS:
                    if axis == 0:
                        t = load(c, off, 0)
                    elif axis == 1:
                        t = load(c, 0, off)
                    else:
                        t = zs(center, off)
                    acc = acc + w * t
                return acc / 12.0

            def mixed(p_c, a, b):
                acc = None
                for sa in (1, -1):
                    for sb in (1, -1):
                        d = [0, 0, 0]
                        d[a] = sa
                        d[b] = sb
                        t = zs(load(p_c, d[0], d[1]), d[2])
                        t = t if sa * sb > 0 else -t
                        acc = t if acc is None else acc + t
                return acc / 4.0

            for c in range(3):
                upd = stiff * curv(c, c)
                for e in range(3):
                    if e != c:
                        upd = upd + mu * curv(c, e)
                        upd = upd + coup * mixed(e, c, e)
                prev = prev_ref[c, p, pl.ds(8 * g, 8), :]
                src = src_ref[c, p, pl.ds(8 * g, 8), :]
                out_ref[c, p, pl.ds(8 * g, 8), :] = (2.0 * centers[c] - prev + upd) + src
        return carry

    lax.fori_loop(0, bx, plane, 0)


def elastic_step(upad, prev, moduli, sources, instant, bx=8):
    _, px, py, depth = upad.shape
    nx, ny = px - 4, py - 4
    kernel = functools.partial(step_kernel, bx=bx)
    block = lambda i: (0, i, 0, 0)
    return pl.pallas_call(
        kernel,
        grid=(nx // bx,),
        in_specs=[
            pl.BlockSpec((3, px, py, depth), lambda i: (0, 0, 0, 0)),
            pl.BlockSpec((3, bx, ny, depth), block),
            pl.BlockSpec((2, bx, ny, depth), block),
            pl.BlockSpec((None, 3, bx, ny, depth), lambda i: (instant, 0, i, 0, 0)),
        ],
        out_specs=pl.BlockSpec((3, bx, ny, depth), block),
        out_shape=jax.ShapeDtypeStruct((3, nx, ny, depth), jnp.float32),
    )(upad, prev, moduli, sources)


def halo_padded(block, width):
    size_x = lax.axis_size("gx")
    size_y = lax.axis_size("gy")
    nx, ny = block.shape[1], block.shape[2]

    def shift(piece, step_x, step_y):
        pairs = []
        for ix in range(size_x):
            for iy in range(size_y):
                jx, jy = ix + step_x, iy + step_y
                if 0 <= jx < size_x and 0 <= jy < size_y:
                    pairs.append((ix * size_y + iy, jx * size_y + jy))
        return lax.ppermute(piece, ("gx", "gy"), pairs)

    lo_x = slice(0, width)
    hi_x = slice(nx - width, nx)
    lo_y = slice(0, width)
    hi_y = slice(ny - width, ny)
    whole = slice(None)
    part = lambda sx, sy: block[:, sx, sy, :]
    left = shift(part(hi_x, whole), 1, 0)
    right = shift(part(lo_x, whole), -1, 0)
    down = shift(part(whole, hi_y), 0, 1)
    up = shift(part(whole, lo_y), 0, -1)
    ll = shift(part(hi_x, hi_y), 1, 1)
    lh = shift(part(hi_x, lo_y), 1, -1)
    hl = shift(part(lo_x, hi_y), -1, 1)
    hh = shift(part(lo_x, lo_y), -1, -1)
    low_row = jnp.concatenate([ll, left, lh], axis=2)
    mid_row = jnp.concatenate([down, block, up], axis=2)
    high_row = jnp.concatenate([hl, right, hh], axis=2)
    return jnp.concatenate([low_row, mid_row, high_row], axis=1)


def level_table(values, layer_of_level):
    one_hot = (
        layer_of_level[:, None] == jnp.arange(values.shape[0], dtype=jnp.int32)[None, :]
    ).astype(jnp.float32)
    return jnp.sum(one_hot * values[None, :], axis=1)


def wave_kernel(angular, slowness, rigidity, damping, count_k):
    wavenum = (jnp.arange(count_k, dtype=jnp.float32) + 0.5) * (4.0 / count_k)
    spread = angular[None, :, None] * slowness[:, None, None]
    vertical = jnp.sqrt(wavenum[None, None, :] * wavenum[None, None, :] + spread * spread)
    impedance = rigidity[:, None, None] * vertical
    beneath = jnp.concatenate([impedance[1:], impedance[-1:]], axis=0)
    reflect = (impedance - beneath) / (impedance + beneath)
    fading = jnp.exp(-2.0 * step_depth * vertical * damping[:, None, None])
    two_way = 2.0 * step_depth * vertical
    trip_re = fading * jnp.cos(two_way)
    trip_im = -fading * jnp.sin(two_way)

    def upward(state_in, layer_data):
        refl_re, refl_im = state_in
        coefficient, along_re, along_im = layer_data
        upper_re = coefficient + refl_re
        lower_re = 1.0 + coefficient * refl_re
        lower_im = coefficient * refl_im
        magnitude = lower_re * lower_re + lower_im * lower_im
        ratio_re = (upper_re * lower_re + refl_im * lower_im) / magnitude
        ratio_im = (refl_im * lower_re - upper_re * lower_im) / magnitude
        fresh_re = along_re * ratio_re - along_im * ratio_im
        fresh_im = along_re * ratio_im + along_im * ratio_re
        return ((fresh_re, fresh_im), (fresh_re, fresh_im))

    bottom = jnp.zeros(vertical.shape[1:], jnp.float32)
    _, (refl_re, refl_im) = lax.scan(
        upward, (bottom, bottom), (reflect, trip_re, trip_im), reverse=True
    )
    travel = step_depth * vertical
    phases = jnp.cumsum(travel, axis=0) - travel
    absorbed = travel * damping[:, None, None]
    losses = jnp.cumsum(absorbed, axis=0) - absorbed
    down_size = jnp.exp(-losses)
    down_re = down_size * jnp.cos(phases)
    down_im = -down_size * jnp.sin(phases)
    weight = 1.0 / math.sqrt(count_k)
    kernel_re = weight * (down_re * (1.0 + refl_re) - down_im * refl_im)
    kernel_im = weight * (down_re * refl_im + down_im * (1.0 + refl_re))
    return jnp.transpose(jnp.stack([kernel_re, kernel_im]), (0, 2, 1, 3))


def offset_basis(count_k, count_r):
    modulus = count_k * count_r // 2
    low_count = 64
    odd_index = 2 * jnp.arange(count_k, dtype=jnp.int32) + 1
    high = jnp.arange(count_r // low_count, dtype=jnp.int32) * low_count
    low = jnp.arange(low_count, dtype=jnp.int32)
    scale = 2.0 * math.pi / modulus
    high_angle = (odd_index[:, None] * high[None, :] % modulus).astype(jnp.float32) * scale
    low_angle = (odd_index[:, None] * low[None, :] % modulus).astype(jnp.float32) * scale
    cos_h, sin_h = jnp.cos(high_angle), jnp.sin(high_angle)
    cos_l, sin_l = jnp.cos(low_angle), jnp.sin(low_angle)
    basis = cos_h[:, :, None] * cos_l[:, None, :] - sin_h[:, :, None] * sin_l[:, None, :]
    basis = basis.reshape(count_k, count_r).astype(jnp.bfloat16)
    return lax.optimization_barrier(basis)


def time_basis(freq_ids, count_f, count_steps, first_time):
    period = 2 * count_f
    times = first_time + jnp.arange(count_steps, dtype=jnp.int32)
    turns = (freq_ids[None, :] + 1) * times[:, None] % period
    angles = turns.astype(jnp.float32) * (2.0 * math.pi / period)
    weight = 1.0 / math.sqrt(count_f)
    return jnp.stack([weight * jnp.cos(angles), -weight * jnp.sin(angles)], axis=1)


def shifted(grid_block, step_x, step_y, step_z):
    width_x = grid_block.shape[0] - 4
    width_y = grid_block.shape[1] - 4
    width_z = grid_block.shape[2] - 4
    return grid_block[
        2 + step_x : 2 + step_x + width_x,
        2 + step_y : 2 + step_y + width_y,
        2 + step_z : 2 + step_z + width_z,
    ]


def curvature(grid_block, first_axis):
    summed = None
    for offset, factor in [(-2, -1.0), (-1, 16.0), (0, -30.0), (1, 16.0), (2, -1.0)]:
        moves = tuple((offset if index == first_axis else 0 for index in range(3)))
        contrib = factor * shifted(grid_block, moves[0], moves[1], moves[2])
        summed = contrib if summed is None else summed + contrib
    return summed / 12.0


def mixed(grid_block, first_axis, second_axis):
    summed = None
    for sign_a, sign_b, factor in [(1, 1, 1.0), (1, -1, -1.0), (-1, 1, -1.0), (-1, -1, 1.0)]:
        moves = tuple(
            (
                sign_a if index == first_axis else sign_b if index == second_axis else 0
                for index in range(3)
            )
        )
        contrib = factor * shifted(grid_block, moves[0], moves[1], moves[2])
        summed = contrib if summed is None else summed + contrib
    return summed / 4.0


def elastic(padded, moduli):
    first_lame = moduli[0]
    shear_mod = moduli[1]
    stiffness = first_lame + 2.0 * shear_mod
    coupling = first_lame + shear_mod
    result = []
    for component in range(3):
        update = stiffness * curvature(padded[component], component)
        for partner in range(3):
            if partner != component:
                update = update + shear_mod * curvature(padded[component], partner)
                update = update + coupling * mixed(padded[partner], component, partner)
        result.append(update)
    return jnp.stack(result)


def shards(
    layer_slowness,
    layer_rigidity,
    layer_damping,
    layer_of_level,
    slot_offset,
    slot_level,
    slot_target,
    live_count,
    moduli,
    field_old,
    field_now,
):
    size_gx = lax.axis_size("gx")
    size_gy = lax.axis_size("gy")
    groups = size_gx * size_gy
    per_device = F // groups
    device = lax.axis_index("gx") * size_gy + lax.axis_index("gy")
    freq_ids = device * per_device + jnp.arange(per_device, dtype=jnp.int32)
    angular = (freq_ids + 1).astype(jnp.float32) * (4.0 / F)
    slowness = level_table(layer_slowness, layer_of_level)
    rigidity = level_table(layer_rigidity, layer_of_level)
    damping = level_table(layer_damping, layer_of_level)
    kernel = wave_kernel(angular, slowness, rigidity, damping, NK).astype(jnp.bfloat16)
    cosines = offset_basis(NK, NR)
    spectrum_table = jnp.dot(
        kernel.reshape(2 * per_device * ND, NK), cosines, preferred_element_type=jnp.float32
    )
    table_rounded = spectrum_table.astype(jnp.bfloat16)
    all_slots = slot_offset.shape[0]
    width = math.gcd(all_slots, 4096)
    count_blocks = all_slots // width
    offset_blocks = slot_offset.reshape(count_blocks, width)
    level_blocks = slot_level.reshape(count_blocks, width)

    def select_block(pair):
        offsets, levels = pair
        offset_hot = (jnp.arange(NR, dtype=jnp.int32)[:, None] == offsets[None, :]).astype(
            jnp.bfloat16
        )
        rows = jnp.dot(table_rounded, offset_hot, preferred_element_type=jnp.float32).reshape(
            2, per_device, ND, width
        )
        level_hot = (jnp.arange(ND, dtype=jnp.int32)[:, None] == levels[None, :]).astype(
            jnp.float32
        )
        return jnp.sum(rows * level_hot[None, None, :, :], axis=2)

    selected = lax.map(select_block, (offset_blocks, level_blocks))
    spectra = (
        jnp.transpose(selected, (1, 2, 0, 3)).reshape(2, per_device, all_slots).astype(jnp.bfloat16)
    )
    slots_dev = slot_target.shape[0]
    occupied = (jnp.arange(slots_dev, dtype=jnp.int32) < live_count[0]).astype(jnp.float32)
    parcel = spectra.reshape(2, per_device, groups, slots_dev)
    arrived = lax.all_to_all(parcel, ("gx", "gy"), split_axis=2, concat_axis=1, tiled=True)
    freq_order = jnp.arange(F, dtype=jnp.int32)
    waveforms = time_basis(freq_order, F, STEPS, TSTART).reshape(STEPS, 2 * F)
    traces = jnp.dot(
        waveforms,
        arrived.reshape(2 * F, slots_dev).astype(jnp.float32),
        precision=lax.Precision.HIGHEST,
    )
    block_x = field_now.shape[1]
    block_y = field_now.shape[2]
    depth = field_now.shape[3]
    columns = slot_target // depth
    layer_z = slot_target % depth
    weighted = traces * occupied[None, :]
    column_hot = (
        jnp.arange(3 * block_x * block_y, dtype=jnp.int32)[:, None] == columns[None, :]
    ).astype(jnp.float32)
    depth_hot = (layer_z[:, None] == jnp.arange(depth, dtype=jnp.int32)[None, :]).astype(
        jnp.float32
    )
    spread_traces = weighted[:, :, None] * depth_hot[None, :, :]
    sources = jnp.einsum("ag,ngz->naz", column_hot, spread_traces, precision=lax.Precision.HIGHEST)
    sources = sources.reshape(STEPS, 3, block_x, block_y, depth)
    previous, current = (field_old, field_now)
    for instant in range(STEPS):
        padded = halo_padded(current, 2)
        advanced = elastic_step(padded, previous, moduli, sources, instant)
        previous, current = (current, advanced)
    return (current, previous)


def solution(mesh):
    in_specs = (
        P(),
        P(),
        P(),
        P(),
        P(),
        P(),
        P(("gx", "gy")),
        P(("gx", "gy")),
        P(None, "gx", "gy", None),
        P(None, "gx", "gy", None),
        P(None, "gx", "gy", None),
    )
    out_specs = (P(None, "gx", "gy", None), P(None, "gx", "gy", None))
    return jax.shard_map(shards, mesh=mesh, in_specs=in_specs, out_specs=out_specs, check_vma=False)
```

profile of v0, /device:TPU:12, one launch (start us, length us, event | category | flops | bytes accessed | tf_op | source)
XLA Modules:
  0.0 308.2 jit_solution(7774343623349148989)
XLA Ops:
  2.9 4.9 %sine_multiply_fusion.1 = (f32[32,4,1024]{2,1,0:T(4,128)S(1)}, f32[32,4,1024]{2,1,0:T(4,128)S(1)}, f32[32,4,1024]{2,1,0:T(4,128)S(1)}) fusion(f32[32]{0:T(128)S(1)} %get-tuple-element.303, f32[32,4]{1,0:T(8,128)S(1)} %copy.28, f32[1024]{0:T(1024)S(1)} %multiply_multiply_fusion, f32[1,4,1024]{2,1,0:T(4,128)S(1)} %slice.137, f32[31,4,1024]{2,1,0:T(4,128)S(1)} %slice.136, ...), kind=kLoop, calls=%fused_computation.43 | loop fusion | flops 1441792 | bytes 2102016 | tf_op jit(solution)/shard_map/mul | solution.py:170
  8.1 2.2 while.32
  11.2 4.3 %fusion.37 = (bf16[1,32,4,1024]{3,2,1,0:T(4,128)(2,1)S(1)}, bf16[1,32,4,1024]{3,2,1,0:T(4,128)(2,1)S(1)}) fusion(f32[32,4,1024]{2,1,0:T(4,128)S(1)} %get-tuple-element.191, f32[32,4,1024]{2,1,0:T(4,128)S(1)} %get-tuple-element.190, f32[32,4,1024]{2,1,0:T(4,128)S(1)} %negate_exponential_fusion, f32[32,4,1024]{2,1,0:T(4,128)S(1)} %fusion.21), kind=kLoop, calls=%fused_computation.72 | loop fusion | flops 1835008 | bytes 2621440 | tf_op jit(solution)/shard_map/stack | solution.py:199
  17.7 3.6 %subtract_convert_fusion = bf16[1024,32,64]{0,2,1:T(8,128)(2,1)} fusion(f32[1024,64]{0,1:T(8,128)S(1)} %get-tuple-element.297, f32[1024,32]{0,1:T(8,128)S(1)} %get-tuple-element.295, f32[1024,64]{0,1:T(8,128)S(1)} %get-tuple-element.296, f32[1024,32]{0,1:T(8,128)S(1)} %get-tuple-element.294), kind=kLoop, calls=%fused_computation.24 | loop fusion | flops 8388608 | bytes 4980736 | tf_op jit(solution)/shard_map/convert_element_type | solution.py:214
  21.4 4.4 %convolution_convert_fusion = bf16[256,2048]{1,0:T(8,128)(2,1)} fusion(bf16[256,1024]{1,0:T(8,128)(2,1)S(1)} %bitcast.107, bf16[1024,2048]{0,1:T(8,128)(2,1)} %bitcast.105), kind=kOutput, calls=%fused_computation.32 | convolution fusion | flops 1074266112 | bytes 5767168 | tf_op jit(solution)/shard_map/dot_general | solution.py:302
  25.8 16.1 %while.31 = (s32[]{:T(128)}, bf16[2,2,4,4096]{3,2,1,0:T(4,128)(2,1)S(1)}, s32[2,4096]{1,0:T(2,128)S(1)}, bf16[256,2048]{1,0:T(8,128)(2,1)}, s32[2,4096]{1,0:T(2,128)S(1)}, /*index=5*/s32[]{:T(128)}) while((s32[]{:T(128)}, bf16[2,2,4,4096]{3,2,1,0:T(4,128)(2,1)S(1)}, s32[2,4096]{1,0:T(2,128)S(1)}, bf16[256,2048]{1,0:T(8,128)(2,1)}, ...), condition=%wide.region_9.10_spmd, body=%wide.region_7.9_spmd.sunk | while | flops 4305682432 | bytes 2392141 | solution.py:325
  25.9 8.0 %multiply_reduce_fusion.2 = bf16[2,4,4096]{2,1,0:T(4,128)(2,1)S(1)} fusion(f32[32,4096]{1,0:T(8,128)S(1)} %fusion.76, bf16[256,2048]{1,0:T(8,128)(2,1)} %get-tuple-element.444, s32[4096]{0:T(1024)S(1)} %bitcast.109), kind=kOutput, calls=%fused_computation.3.clone.1 | convolution fusion | flops 4305420288 | bytes 1654784 | tf_op jit(solution)/shard_map/while/body/eval_jaxpr/dot_general | solution.py:317
  34.0 7.8 %multiply_reduce_fusion.2 = bf16[2,4,4096]{2,1,0:T(4,128)(2,1)S(1)} fusion(f32[32,4096]{1,0:T(8,128)S(1)} %fusion.76, bf16[256,2048]{1,0:T(8,128)(2,1)} %get-tuple-element.444, s32[4096]{0:T(1024)S(1)} %bitcast.109), kind=kOutput, calls=%fused_computation.3.clone.1 | convolution fusion | flops 4305420288 | bytes 1654784 | tf_op jit(solution)/shard_map/while/body/eval_jaxpr/dot_general | solution.py:317
  42.9 6.0 %all-to-all-start = ((bf16[2,4,32,256]{3,1,0,2:T(4,128)(2,1)}), bf16[2,4,32,256]{3,1,0,2:T(4,128)(2,1)S(1)}, u32[]{:S(2)}, u32[]{:S(2)}) async-start(bf16[2,4,32,256]{3,1,0,2:T(4,128)(2,1)} %copy.31), calls=%async_computation | async-start | bytes 262144 | tf_op jit(solution)/shard_map/all_to_all | solution.py:332
  48.9 3.1 %collective-permute-start = (f32[3,2,2,256]{3,2,1,0:T(2,128)S(1)}, f32[3,2,2,256]{3,2,1,0:T(2,128)S(1)}, u32[]{:S(2)}, u32[]{:S(2)}) collective-permute-start(f32[3,2,2,256]{3,2,1,0:T(2,128)S(1)} %get-tuple-element.281), channel_id=1, source_target_pairs={{0,5},{1,6},{2,7},{4,9},{5,10},{6,11},{8,13},{9,14},{10,15},{12,17... | collective-permute-start | bytes 36872 | tf_op jit(solution)/shard_map/ppermute | solution.py:131
  52.0 4.3 %collective-permute-start.2 = (f32[3,2,2,256]{3,2,1,0:T(2,128)S(1)}, f32[3,2,2,256]{3,2,1,0:T(2,128)S(1)}, u32[]{:S(2)}, u32[]{:S(2)}) collective-permute-start(f32[3,2,2,256]{3,2,1,0:T(2,128)S(1)} %get-tuple-element.283), channel_id=1, source_target_pairs={{1,4},{2,5},{3,6},{5,8},{6,9},{7,10},{9,12},{10,13},{11,14},{13,16... | collective-permute-start | bytes 36872 | tf_op jit(solution)/shard_map/ppermute | solution.py:131
  56.3 2.2 collective-permute-start.5
  58.5 3.1 %collective-permute-start.1 = (f32[3,2,32,256]{3,2,1,0:T(8,128)S(1)}, f32[3,2,32,256]{3,2,1,0:T(8,128)S(1)}, u32[]{:S(2)}, u32[]{:S(2)}) collective-permute-start(f32[3,2,32,256]{3,2,1,0:T(8,128)S(1)} %get-tuple-element.285), channel_id=1, source_target_pairs={{0,4},{1,5},{2,6},{3,7},{4,8},{5,9},{6,10},{7,11},{8,12},{9,13},{1... | collective-permute-start | bytes 589832 | tf_op jit(solution)/shard_map/ppermute | solution.py:131
  63.8 3.6 %collective-permute-start.4 = (f32[3,32,2,256]{3,2,1,0:T(2,128)S(1)}, f32[3,32,2,256]{3,2,1,0:T(2,128)S(1)}, u32[]{:S(2)}, u32[]{:S(2)}) collective-permute-start(f32[3,32,2,256]{3,2,1,0:T(2,128)S(1)} %get-tuple-element.288), channel_id=1, source_target_pairs={{1,0},{2,1},{3,2},{5,4},{6,5},{7,6},{9,8},{10,9},{11,10},{13,12},{... | collective-permute-start | bytes 589832 | tf_op jit(solution)/shard_map/ppermute | solution.py:131
  67.5 4.0 %collective-permute-start.6 = (f32[3,2,32,256]{3,2,1,0:T(8,128)S(1)}, f32[3,2,32,256]{3,2,1,0:T(8,128)S(1)}, u32[]{:S(2)}, u32[]{:S(2)}) collective-permute-start(f32[3,2,32,256]{3,2,1,0:T(8,128)S(1)} %get-tuple-element.286), channel_id=1, source_target_pairs={{4,0},{5,1},{6,2},{7,3},{8,4},{9,5},{10,6},{11,7},{12,8},{13,9},{1... | collective-permute-start | bytes 589832 | tf_op jit(solution)/shard_map/ppermute | solution.py:131
  74.2 3.1 collective-permute-done.7
  77.3 2.6 maximum_maximum_fusion.up_ref
  80.1 8.2 %convolution_bitcast_fusion = f32[4,3072,256]{1,2,0:T(8,128)} fusion(s32[256]{0:T(256)S(1)} %get-tuple-element.301, f32[256,256]{0,1:T(8,128)S(1)} %fusion.40, f32[4,256]{1,0:T(4,128)S(1)} %convolution_multiply_fusion), kind=kOutput, calls=%fused_computation.25 | convolution fusion | flops 9664724992 | bytes 12850176 | tf_op jit(solution)/shard_map/ag,ngz->naz/dot_general | solution.py:353
  88.4 12.6 %copy.33 = f32[4,3072,256]{2,1,0:T(8,128)} copy(f32[4,3072,256]{1,2,0:T(8,128)} %convolution_bitcast_fusion) | data formatting | bytes 25165824 | tf_op jit(solution)/shard_map/ag,ngz->naz/transpose | solution.py:353
  101.0 19.6 %shard_map.122.prev_ref = f32[3,32,32,256]{3,2,1,0:T(8,128)} custom-call(f32[3,36,36,256]{3,2,1,0:T(8,128)} %maximum_maximum_fusion.up_ref, f32[3,32,32,256]{3,2,1,0:T(8,128)} %prev_ref.2, f32[2,32,32,256]{3,2,1,0:T(8,128)} %mod_ref.7, f32[4,3,32,32,256]{4,3,2,1,0:T(8,128)} %bitcast.101), custom_call_target="tpu_custom_call" | custom-call | tf_op jit(solution)/shard_map/pallas_call | solution.py:105
  125.1 3.6 %collective-permute-start.12 = (f32[3,32,2,256]{3,2,1,0:T(2,128)S(1)}, f32[3,32,2,256]{3,2,1,0:T(2,128)S(1)}, u32[]{:S(2)}, u32[]{:S(2)}) collective-permute-start(f32[3,32,2,256]{3,2,1,0:T(2,128)S(1)} %get-tuple-element.280), channel_id=1, source_target_pairs={{1,0},{2,1},{3,2},{5,4},{6,5},{7,6},{9,8},{10,9},{11,10},{13,12},{... | collective-permute-start | bytes 589832 | tf_op jit(solution)/shard_map/ppermute | solution.py:131
  128.7 2.8 collective-permute-start.14
  131.5 3.0 collective-permute-start.9
  135.5 2.9 collective-permute-start.10
  138.3 3.0 collective-permute-done.10
  143.3 4.0 %collective-permute-done.13 = f32[3,2,2,256]{3,2,1,0:T(2,128)S(1)} collective-permute-done((f32[3,2,2,256]{3,2,1,0:T(2,128)S(1)}, f32[3,2,2,256]{3,2,1,0:T(2,128)S(1)}, u32[]{:S(2)}, u32[]{:S(2)}) %collective-permute-start.13) | collective-permute-done | bytes 12320 | tf_op jit(solution)/shard_map/ppermute | solution.py:131
  147.3 3.4 %collective-permute-start.15 = (f32[3,2,2,256]{3,2,1,0:T(2,128)S(1)}, f32[3,2,2,256]{3,2,1,0:T(2,128)S(1)}, u32[]{:S(2)}, u32[]{:S(2)}) collective-permute-start(f32[3,2,2,256]{3,2,1,0:T(2,128)S(1)} %get-tuple-element.274), channel_id=1, source_target_pairs={{5,0},{6,1},{7,2},{9,4},{10,5},{11,6},{13,8},{14,9},{15,10},{17,12... | collective-permute-start | bytes 36872 | tf_op jit(solution)/shard_map/ppermute | solution.py:131
  154.2 4.9 %collective-permute-done.8 = f32[3,2,2,256]{3,2,1,0:T(2,128)S(1)} collective-permute-done((f32[3,2,2,256]{3,2,1,0:T(2,128)S(1)}, f32[3,2,2,256]{3,2,1,0:T(2,128)S(1)}, u32[]{:S(2)}, u32[]{:S(2)}) %collective-permute-start.8) | collective-permute-done | bytes 12320 | tf_op jit(solution)/shard_map/ppermute | solution.py:131
  159.1 3.8 %maximum_maximum_fusion.1.up_ref = f32[3,36,36,256]{3,2,1,0:T(8,128)} fusion(f32[3,2,2,256]{3,2,1,0:T(2,128)S(1)} %collective-permute-done.15, f32[3,2,32,256]{3,2,1,0:T(8,128)S(1)} %collective-permute-done.14, f32[3,2,2,256]{3,2,1,0:T(2,128)S(1)} %collective-permute-done.13, f32[3,32,2,256]{3,2,1,0:T(2,128)S(1)} %collective-permute-done.12, ...), kind=kLoop, calls=%fused_computation.27 | loop fusion | flops 7962624 | bytes 7962624 | tf_op jit(solution)/shard_map/concatenate | solution.py:150
  163.0 19.6 %shard_map.123.prev_ref = f32[3,32,32,256]{3,2,1,0:T(8,128)} custom-call(f32[3,36,36,256]{3,2,1,0:T(8,128)} %maximum_maximum_fusion.1.up_ref, f32[3,32,32,256]{3,2,1,0:T(8,128)} %prev_ref.3, f32[2,32,32,256]{3,2,1,0:T(8,128)} %mod_ref.7, f32[4,3,32,32,256]{4,3,2,1,0:T(8,128)} %bitcast.102), custom_call_target="tpu_custom_call" | custom-call | tf_op jit(solution)/shard_map/pallas_call | solution.py:105
  185.1 4.1 %collective-permute-start.17 = (f32[3,2,32,256]{3,2,1,0:T(8,128)S(1)}, f32[3,2,32,256]{3,2,1,0:T(8,128)S(1)}, u32[]{:S(2)}, u32[]{:S(2)}) collective-permute-start(f32[3,2,32,256]{3,2,1,0:T(8,128)S(1)} %get-tuple-element.269), channel_id=1, source_target_pairs={{0,4},{1,5},{2,6},{3,7},{4,8},{5,9},{6,10},{7,11},{8,12},{9,13},{1... | collective-permute-start | bytes 589832 | tf_op jit(solution)/shard_map/ppermute | solution.py:131
  191.1 3.6 %collective-permute-start.20 = (f32[3,32,2,256]{3,2,1,0:T(2,128)S(1)}, f32[3,32,2,256]{3,2,1,0:T(2,128)S(1)}, u32[]{:S(2)}, u32[]{:S(2)}) collective-permute-start(f32[3,32,2,256]{3,2,1,0:T(2,128)S(1)} %get-tuple-element.272), channel_id=1, source_target_pairs={{1,0},{2,1},{3,2},{5,4},{6,5},{7,6},{9,8},{10,9},{11,10},{13,12},{... | collective-permute-start | bytes 589832 | tf_op jit(solution)/shard_map/ppermute | solution.py:131
  194.7 2.7 collective-permute-start.22
  200.2 4.9 %collective-permute-done.16 = f32[3,2,2,256]{3,2,1,0:T(2,128)S(1)} collective-permute-done((f32[3,2,2,256]{3,2,1,0:T(2,128)S(1)}, f32[3,2,2,256]{3,2,1,0:T(2,128)S(1)}, u32[]{:S(2)}, u32[]{:S(2)}) %collective-permute-start.16) | collective-permute-done | bytes 12320 | tf_op jit(solution)/shard_map/ppermute | solution.py:131
  207.0 4.0 %collective-permute-done.18 = f32[3,2,2,256]{3,2,1,0:T(2,128)S(1)} collective-permute-done((f32[3,2,2,256]{3,2,1,0:T(2,128)S(1)}, f32[3,2,2,256]{3,2,1,0:T(2,128)S(1)}, u32[]{:S(2)}, u32[]{:S(2)}) %collective-permute-start.18) | collective-permute-done | bytes 12320 | tf_op jit(solution)/shard_map/ppermute | solution.py:131
  213.0 4.0 %collective-permute-done.21 = f32[3,2,2,256]{3,2,1,0:T(2,128)S(1)} collective-permute-done((f32[3,2,2,256]{3,2,1,0:T(2,128)S(1)}, f32[3,2,2,256]{3,2,1,0:T(2,128)S(1)}, u32[]{:S(2)}, u32[]{:S(2)}) %collective-permute-start.21) | collective-permute-done | bytes 12320 | tf_op jit(solution)/shard_map/ppermute | solution.py:131
  218.9 3.1 %collective-permute-done.23 = f32[3,2,2,256]{3,2,1,0:T(2,128)S(1)} collective-permute-done((f32[3,2,2,256]{3,2,1,0:T(2,128)S(1)}, f32[3,2,2,256]{3,2,1,0:T(2,128)S(1)}, u32[]{:S(2)}, u32[]{:S(2)}) %collective-permute-start.23) | collective-permute-done | bytes 12320 | tf_op jit(solution)/shard_map/ppermute | solution.py:131
  222.0 3.8 %maximum_maximum_fusion.2.up_ref = f32[3,36,36,256]{3,2,1,0:T(8,128)} fusion(f32[3,2,2,256]{3,2,1,0:T(2,128)S(1)} %collective-permute-done.23, f32[3,2,32,256]{3,2,1,0:T(8,128)S(1)} %collective-permute-done.22, f32[3,2,2,256]{3,2,1,0:T(2,128)S(1)} %collective-permute-done.21, f32[3,32,2,256]{3,2,1,0:T(2,128)S(1)} %collective-permute-done.20, ...), kind=kLoop, calls=%fused_computation.28 | loop fusion | flops 7962624 | bytes 7962624 | tf_op jit(solution)/shard_map/concatenate | solution.py:150
  225.8 19.6 %shard_map.124 = f32[3,32,32,256]{3,2,1,0:T(8,128)} custom-call(f32[3,36,36,256]{3,2,1,0:T(8,128)} %maximum_maximum_fusion.2.up_ref, f32[3,32,32,256]{3,2,1,0:T(8,128)} %shard_map.122.prev_ref, f32[2,32,32,256]{3,2,1,0:T(8,128)} %mod_ref.7, f32[4,3,32,32,256]{4,3,2,1,0:T(8,128)} %bitcast.103), custom_call_target="tpu_custom_call" | custom-call | tf_op jit(solution)/shard_map/pallas_call | solution.py:105
  247.9 3.2 %collective-permute-start.25 = (f32[3,2,32,256]{3,2,1,0:T(8,128)S(1)}, f32[3,2,32,256]{3,2,1,0:T(8,128)S(1)}, u32[]{:S(2)}, u32[]{:S(2)}) collective-permute-start(f32[3,2,32,256]{3,2,1,0:T(8,128)S(1)} %get-tuple-element.261), channel_id=1, source_target_pairs={{0,4},{1,5},{2,6},{3,7},{4,8},{5,9},{6,10},{7,11},{8,12},{9,13},{1... | collective-permute-start | bytes 589832 | tf_op jit(solution)/shard_map/ppermute | solution.py:131
  253.1 3.6 %collective-permute-start.28 = (f32[3,32,2,256]{3,2,1,0:T(2,128)S(1)}, f32[3,32,2,256]{3,2,1,0:T(2,128)S(1)}, u32[]{:S(2)}, u32[]{:S(2)}) collective-permute-start(f32[3,32,2,256]{3,2,1,0:T(2,128)S(1)} %get-tuple-element.264), channel_id=1, source_target_pairs={{1,0},{2,1},{3,2},{5,4},{6,5},{7,6},{9,8},{10,9},{11,10},{13,12},{... | collective-permute-start | bytes 589832 | tf_op jit(solution)/shard_map/ppermute | solution.py:131
  256.7 3.6 %collective-permute-start.30 = (f32[3,2,32,256]{3,2,1,0:T(8,128)S(1)}, f32[3,2,32,256]{3,2,1,0:T(8,128)S(1)}, u32[]{:S(2)}, u32[]{:S(2)}) collective-permute-start(f32[3,2,32,256]{3,2,1,0:T(8,128)S(1)} %get-tuple-element.262), channel_id=1, source_target_pairs={{4,0},{5,1},{6,2},{7,3},{8,4},{9,5},{10,6},{11,7},{12,8},{13,9},{1... | collective-permute-start | bytes 589832 | tf_op jit(solution)/shard_map/ppermute | solution.py:131
  263.1 4.9 %collective-permute-done.24 = f32[3,2,2,256]{3,2,1,0:T(2,128)S(1)} collective-permute-done((f32[3,2,2,256]{3,2,1,0:T(2,128)S(1)}, f32[3,2,2,256]{3,2,1,0:T(2,128)S(1)}, u32[]{:S(2)}, u32[]{:S(2)}) %collective-permute-start.24) | collective-permute-done | bytes 12320 | tf_op jit(solution)/shard_map/ppermute | solution.py:131
  269.9 4.0 %collective-permute-done.26 = f32[3,2,2,256]{3,2,1,0:T(2,128)S(1)} collective-permute-done((f32[3,2,2,256]{3,2,1,0:T(2,128)S(1)}, f32[3,2,2,256]{3,2,1,0:T(2,128)S(1)}, u32[]{:S(2)}, u32[]{:S(2)}) %collective-permute-start.26) | collective-permute-done | bytes 12320 | tf_op jit(solution)/shard_map/ppermute | solution.py:131
  275.8 4.0 %collective-permute-done.29 = f32[3,2,2,256]{3,2,1,0:T(2,128)S(1)} collective-permute-done((f32[3,2,2,256]{3,2,1,0:T(2,128)S(1)}, f32[3,2,2,256]{3,2,1,0:T(2,128)S(1)}, u32[]{:S(2)}, u32[]{:S(2)}) %collective-permute-start.29) | collective-permute-done | bytes 12320 | tf_op jit(solution)/shard_map/ppermute | solution.py:131
  281.7 3.1 %collective-permute-done.31 = f32[3,2,2,256]{3,2,1,0:T(2,128)S(1)} collective-permute-done((f32[3,2,2,256]{3,2,1,0:T(2,128)S(1)}, f32[3,2,2,256]{3,2,1,0:T(2,128)S(1)}, u32[]{:S(2)}, u32[]{:S(2)}) %collective-permute-start.31) | collective-permute-done | bytes 12320 | tf_op jit(solution)/shard_map/ppermute | solution.py:131
  284.8 3.8 %maximum_maximum_fusion.3.up_ref = f32[3,36,36,256]{3,2,1,0:T(8,128)} fusion(f32[3,2,2,256]{3,2,1,0:T(2,128)S(1)} %collective-permute-done.31, f32[3,2,32,256]{3,2,1,0:T(8,128)S(1)} %collective-permute-done.30, f32[3,2,2,256]{3,2,1,0:T(2,128)S(1)} %collective-permute-done.29, f32[3,32,2,256]{3,2,1,0:T(2,128)S(1)} %collective-permute-done.28, ...), kind=kLoop, calls=%fused_computation.29 | loop fusion | flops 7962624 | bytes 7962624 | tf_op jit(solution)/shard_map/concatenate | solution.py:150
  288.7 19.6 %shard_map.125 = f32[3,32,32,256]{3,2,1,0:T(8,128)} custom-call(f32[3,36,36,256]{3,2,1,0:T(8,128)} %maximum_maximum_fusion.3.up_ref, f32[3,32,32,256]{3,2,1,0:T(8,128)} %shard_map.123.prev_ref, f32[2,32,32,256]{3,2,1,0:T(8,128)} %mod_ref.7, f32[4,3,32,32,256]{4,3,2,1,0:T(8,128)} %bitcast.104), custom_call_target="tpu_custom_call" | custom-call | tf_op jit(solution)/shard_map/pallas_call | solution.py:105
  (130 shorter events, 49.8 us)
Async XLA Ops:
  15.5 5.8 %copy-start.1 = (s32[8192]{0:T(1024)S(1)}, s32[8192]{0:T(1024)}, u32[]{:S(2)}) copy-start(s32[8192]{0:T(1024)} %param.19) | copy-start | bytes 98308
  15.5 5.8 %copy-start.2 = (s32[8192]{0:T(1024)S(1)}, s32[8192]{0:T(1024)}, u32[]{:S(2)}) copy-start(s32[8192]{0:T(1024)} %param.20) | copy-start | bytes 98308
  25.8 23.1 %copy-start = (f32[3,32,32,256]{3,2,1,0:T(8,128)S(1)}, f32[3,32,32,256]{3,2,1,0:T(8,128)}, u32[]{:S(2)}) copy-start(f32[3,32,32,256]{3,2,1,0:T(8,128)} %prev_ref.3) | copy-start | bytes 9437188
  25.8 37.9 %copy-start.3 = (s32[256]{0:T(256)S(1)}, s32[256]{0:T(256)}, u32[]{:S(2)}) copy-start(s32[256]{0:T(256)} %param.21) | copy-start | bytes 3076
  42.9 37.0 %all-to-all-start = ((bf16[2,4,32,256]{3,1,0,2:T(4,128)(2,1)}), bf16[2,4,32,256]{3,1,0,2:T(4,128)(2,1)S(1)}, u32[]{:S(2)}, u32[]{:S(2)}) async-start(bf16[2,4,32,256]{3,1,0,2:T(4,128)(2,1)} %copy.31), calls=%async_computation | async-start | bytes 262144 | tf_op jit(solution)/shard_map/all_to_all | solution.py:332
  48.9 14.9 %collective-permute-start = (f32[3,2,2,256]{3,2,1,0:T(2,128)S(1)}, f32[3,2,2,256]{3,2,1,0:T(2,128)S(1)}, u32[]{:S(2)}, u32[]{:S(2)}) collective-permute-start(f32[3,2,2,256]{3,2,1,0:T(2,128)S(1)} %get-tuple-element.281), channel_id=1, source_target_pairs={{0,5},{1,6},{2,7},{4,9},{5,10},{6,11},{8,13},{9,14},{10,15},{12,17... | collective-permute-start | bytes 36872 | tf_op jit(solution)/shard_map/ppermute | solution.py:131
  52.0 15.5 %collective-permute-start.2 = (f32[3,2,2,256]{3,2,1,0:T(2,128)S(1)}, f32[3,2,2,256]{3,2,1,0:T(2,128)S(1)}, u32[]{:S(2)}, u32[]{:S(2)}) collective-permute-start(f32[3,2,2,256]{3,2,1,0:T(2,128)S(1)} %get-tuple-element.283), channel_id=1, source_target_pairs={{1,4},{2,5},{3,6},{5,8},{6,9},{7,10},{9,12},{10,13},{11,14},{13,16... | collective-permute-start | bytes 36872 | tf_op jit(solution)/shard_map/ppermute | solution.py:131
  56.3 15.9 %collective-permute-start.5 = (f32[3,2,2,256]{3,2,1,0:T(2,128)S(1)}, f32[3,2,2,256]{3,2,1,0:T(2,128)S(1)}, u32[]{:S(2)}, u32[]{:S(2)}) collective-permute-start(f32[3,2,2,256]{3,2,1,0:T(2,128)S(1)} %get-tuple-element.282), channel_id=1, source_target_pairs={{4,1},{5,2},{6,3},{8,5},{9,6},{10,7},{12,9},{13,10},{14,11},{16,13... | collective-permute-start | bytes 36872 | tf_op jit(solution)/shard_map/ppermute | solution.py:131
  58.5 18.7 %collective-permute-start.1 = (f32[3,2,32,256]{3,2,1,0:T(8,128)S(1)}, f32[3,2,32,256]{3,2,1,0:T(8,128)S(1)}, u32[]{:S(2)}, u32[]{:S(2)}) collective-permute-start(f32[3,2,32,256]{3,2,1,0:T(8,128)S(1)} %get-tuple-element.285), channel_id=1, source_target_pairs={{0,4},{1,5},{2,6},{3,7},{4,8},{5,9},{6,10},{7,11},{8,12},{9,13},{1... | collective-permute-start | bytes 589832 | tf_op jit(solution)/shard_map/ppermute | solution.py:131
  61.8 15.5 %collective-permute-start.3 = (f32[3,32,2,256]{3,2,1,0:T(2,128)S(1)}, f32[3,32,2,256]{3,2,1,0:T(2,128)S(1)}, u32[]{:S(2)}, u32[]{:S(2)}) collective-permute-start(f32[3,32,2,256]{3,2,1,0:T(2,128)S(1)} %get-tuple-element.287), channel_id=1, source_target_pairs={{0,1},{1,2},{2,3},{4,5},{5,6},{6,7},{8,9},{9,10},{10,11},{12,13},{... | collective-permute-start | bytes 589832 | tf_op jit(solution)/shard_map/ppermute | solution.py:131
  63.8 13.4 %collective-permute-start.4 = (f32[3,32,2,256]{3,2,1,0:T(2,128)S(1)}, f32[3,32,2,256]{3,2,1,0:T(2,128)S(1)}, u32[]{:S(2)}, u32[]{:S(2)}) collective-permute-start(f32[3,32,2,256]{3,2,1,0:T(2,128)S(1)} %get-tuple-element.288), channel_id=1, source_target_pairs={{1,0},{2,1},{3,2},{5,4},{6,5},{7,6},{9,8},{10,9},{11,10},{13,12},{... | collective-permute-start | bytes 589832 | tf_op jit(solution)/shard_map/ppermute | solution.py:131
  67.5 9.8 %collective-permute-start.6 = (f32[3,2,32,256]{3,2,1,0:T(8,128)S(1)}, f32[3,2,32,256]{3,2,1,0:T(8,128)S(1)}, u32[]{:S(2)}, u32[]{:S(2)}) collective-permute-start(f32[3,2,32,256]{3,2,1,0:T(8,128)S(1)} %get-tuple-element.286), channel_id=1, source_target_pairs={{4,0},{5,1},{6,2},{7,3},{8,4},{9,5},{10,6},{11,7},{12,8},{13,9},{1... | collective-permute-start | bytes 589832 | tf_op jit(solution)/shard_map/ppermute | solution.py:131
  72.2 5.0 %collective-permute-start.7 = (f32[3,2,2,256]{3,2,1,0:T(2,128)S(1)}, f32[3,2,2,256]{3,2,1,0:T(2,128)S(1)}, u32[]{:S(2)}, u32[]{:S(2)}) collective-permute-start(f32[3,2,2,256]{3,2,1,0:T(2,128)S(1)} %get-tuple-element.284), channel_id=1, source_target_pairs={{5,0},{6,1},{7,2},{9,4},{10,5},{11,6},{13,8},{14,9},{15,10},{17,12... | collective-permute-start | bytes 36872 | tf_op jit(solution)/shard_map/ppermute | solution.py:131
  123.1 36.0 %collective-permute-start.11 = (f32[3,32,2,256]{3,2,1,0:T(2,128)S(1)}, f32[3,32,2,256]{3,2,1,0:T(2,128)S(1)}, u32[]{:S(2)}, u32[]{:S(2)}) collective-permute-start(f32[3,32,2,256]{3,2,1,0:T(2,128)S(1)} %get-tuple-element.279), channel_id=1, source_target_pairs={{0,1},{1,2},{2,3},{4,5},{5,6},{6,7},{8,9},{9,10},{10,11},{12,13},{... | collective-permute-start | bytes 589832 | tf_op jit(solution)/shard_map/ppermute | solution.py:131
  125.1 34.0 %collective-permute-start.12 = (f32[3,32,2,256]{3,2,1,0:T(2,128)S(1)}, f32[3,32,2,256]{3,2,1,0:T(2,128)S(1)}, u32[]{:S(2)}, u32[]{:S(2)}) collective-permute-start(f32[3,32,2,256]{3,2,1,0:T(2,128)S(1)} %get-tuple-element.280), channel_id=1, source_target_pairs={{1,0},{2,1},{3,2},{5,4},{6,5},{7,6},{9,8},{10,9},{11,10},{13,12},{... | collective-permute-start | bytes 589832 | tf_op jit(solution)/shard_map/ppermute | solution.py:131
  128.7 30.4 %collective-permute-start.14 = (f32[3,2,32,256]{3,2,1,0:T(8,128)S(1)}, f32[3,2,32,256]{3,2,1,0:T(8,128)S(1)}, u32[]{:S(2)}, u32[]{:S(2)}) collective-permute-start(f32[3,2,32,256]{3,2,1,0:T(8,128)S(1)} %get-tuple-element.278), channel_id=1, source_target_pairs={{4,0},{5,1},{6,2},{7,3},{8,4},{9,5},{10,6},{11,7},{12,8},{13,9},{1... | collective-permute-start | bytes 589832 | tf_op jit(solution)/shard_map/ppermute | solution.py:131
  131.5 27.6 %collective-permute-start.9 = (f32[3,2,32,256]{3,2,1,0:T(8,128)S(1)}, f32[3,2,32,256]{3,2,1,0:T(8,128)S(1)}, u32[]{:S(2)}, u32[]{:S(2)}) collective-permute-start(f32[3,2,32,256]{3,2,1,0:T(8,128)S(1)} %get-tuple-element.277), channel_id=1, source_target_pairs={{0,4},{1,5},{2,6},{3,7},{4,8},{5,9},{6,10},{7,11},{8,12},{9,13},{1... | collective-permute-start | bytes 589832 | tf_op jit(solution)/shard_map/ppermute | solution.py:131
  135.5 5.9 %collective-permute-start.10 = (f32[3,2,2,256]{3,2,1,0:T(2,128)S(1)}, f32[3,2,2,256]{3,2,1,0:T(2,128)S(1)}, u32[]{:S(2)}, u32[]{:S(2)}) collective-permute-start(f32[3,2,2,256]{3,2,1,0:T(2,128)S(1)} %get-tuple-element.276), channel_id=1, source_target_pairs={{1,4},{2,5},{3,6},{5,8},{6,9},{7,10},{9,12},{10,13},{11,14},{13,16... | collective-permute-start | bytes 36872 | tf_op jit(solution)/shard_map/ppermute | solution.py:131
  141.4 5.9 %collective-permute-start.13 = (f32[3,2,2,256]{3,2,1,0:T(2,128)S(1)}, f32[3,2,2,256]{3,2,1,0:T(2,128)S(1)}, u32[]{:S(2)}, u32[]{:S(2)}) collective-permute-start(f32[3,2,2,256]{3,2,1,0:T(2,128)S(1)} %get-tuple-element.275), channel_id=1, source_target_pairs={{4,1},{5,2},{6,3},{8,5},{9,6},{10,7},{12,9},{13,10},{14,11},{16,13... | collective-permute-start | bytes 36872 | tf_op jit(solution)/shard_map/ppermute | solution.py:131
  147.3 5.0 %collective-permute-start.15 = (f32[3,2,2,256]{3,2,1,0:T(2,128)S(1)}, f32[3,2,2,256]{3,2,1,0:T(2,128)S(1)}, u32[]{:S(2)}, u32[]{:S(2)}) collective-permute-start(f32[3,2,2,256]{3,2,1,0:T(2,128)S(1)} %get-tuple-element.274), channel_id=1, source_target_pairs={{5,0},{6,1},{7,2},{9,4},{10,5},{11,6},{13,8},{14,9},{15,10},{17,12... | collective-permute-start | bytes 36872 | tf_op jit(solution)/shard_map/ppermute | solution.py:131
  152.3 6.8 %collective-permute-start.8 = (f32[3,2,2,256]{3,2,1,0:T(2,128)S(1)}, f32[3,2,2,256]{3,2,1,0:T(2,128)S(1)}, u32[]{:S(2)}, u32[]{:S(2)}) collective-permute-start(f32[3,2,2,256]{3,2,1,0:T(2,128)S(1)} %get-tuple-element.273), channel_id=1, source_target_pairs={{0,5},{1,6},{2,7},{4,9},{5,10},{6,11},{8,13},{9,14},{10,15},{12,17... | collective-permute-start | bytes 36872 | tf_op jit(solution)/shard_map/ppermute | solution.py:131
  185.1 36.9 %collective-permute-start.17 = (f32[3,2,32,256]{3,2,1,0:T(8,128)S(1)}, f32[3,2,32,256]{3,2,1,0:T(8,128)S(1)}, u32[]{:S(2)}, u32[]{:S(2)}) collective-permute-start(f32[3,2,32,256]{3,2,1,0:T(8,128)S(1)} %get-tuple-element.269), channel_id=1, source_target_pairs={{0,4},{1,5},{2,6},{3,7},{4,8},{5,9},{6,10},{7,11},{8,12},{9,13},{1... | collective-permute-start | bytes 589832 | tf_op jit(solution)/shard_map/ppermute | solution.py:131
  189.2 32.8 %collective-permute-start.19 = (f32[3,32,2,256]{3,2,1,0:T(2,128)S(1)}, f32[3,32,2,256]{3,2,1,0:T(2,128)S(1)}, u32[]{:S(2)}, u32[]{:S(2)}) collective-permute-start(f32[3,32,2,256]{3,2,1,0:T(2,128)S(1)} %get-tuple-element.271), channel_id=1, source_target_pairs={{0,1},{1,2},{2,3},{4,5},{5,6},{6,7},{8,9},{9,10},{10,11},{12,13},{... | collective-permute-start | bytes 589832 | tf_op jit(solution)/shard_map/ppermute | solution.py:131
  191.1 30.8 %collective-permute-start.20 = (f32[3,32,2,256]{3,2,1,0:T(2,128)S(1)}, f32[3,32,2,256]{3,2,1,0:T(2,128)S(1)}, u32[]{:S(2)}, u32[]{:S(2)}) collective-permute-start(f32[3,32,2,256]{3,2,1,0:T(2,128)S(1)} %get-tuple-element.272), channel_id=1, source_target_pairs={{1,0},{2,1},{3,2},{5,4},{6,5},{7,6},{9,8},{10,9},{11,10},{13,12},{... | collective-permute-start | bytes 589832 | tf_op jit(solution)/shard_map/ppermute | solution.py:131
  194.7 27.2 %collective-permute-start.22 = (f32[3,2,32,256]{3,2,1,0:T(8,128)S(1)}, f32[3,2,32,256]{3,2,1,0:T(8,128)S(1)}, u32[]{:S(2)}, u32[]{:S(2)}) collective-permute-start(f32[3,2,32,256]{3,2,1,0:T(8,128)S(1)} %get-tuple-element.270), channel_id=1, source_target_pairs={{4,0},{5,1},{6,2},{7,3},{8,4},{9,5},{10,6},{11,7},{12,8},{13,9},{1... | collective-permute-start | bytes 589832 | tf_op jit(solution)/shard_map/ppermute | solution.py:131
  198.3 6.8 %collective-permute-start.16 = (f32[3,2,2,256]{3,2,1,0:T(2,128)S(1)}, f32[3,2,2,256]{3,2,1,0:T(2,128)S(1)}, u32[]{:S(2)}, u32[]{:S(2)}) collective-permute-start(f32[3,2,2,256]{3,2,1,0:T(2,128)S(1)} %get-tuple-element.265), channel_id=1, source_target_pairs={{0,5},{1,6},{2,7},{4,9},{5,10},{6,11},{8,13},{9,14},{10,15},{12,17... | collective-permute-start | bytes 36872 | tf_op jit(solution)/shard_map/ppermute | solution.py:131
  205.1 5.9 %collective-permute-start.18 = (f32[3,2,2,256]{3,2,1,0:T(2,128)S(1)}, f32[3,2,2,256]{3,2,1,0:T(2,128)S(1)}, u32[]{:S(2)}, u32[]{:S(2)}) collective-permute-start(f32[3,2,2,256]{3,2,1,0:T(2,128)S(1)} %get-tuple-element.268), channel_id=1, source_target_pairs={{1,4},{2,5},{3,6},{5,8},{6,9},{7,10},{9,12},{10,13},{11,14},{13,16... | collective-permute-start | bytes 36872 | tf_op jit(solution)/shard_map/ppermute | solution.py:131
  211.0 5.9 %collective-permute-start.21 = (f32[3,2,2,256]{3,2,1,0:T(2,128)S(1)}, f32[3,2,2,256]{3,2,1,0:T(2,128)S(1)}, u32[]{:S(2)}, u32[]{:S(2)}) collective-permute-start(f32[3,2,2,256]{3,2,1,0:T(2,128)S(1)} %get-tuple-element.267), channel_id=1, source_target_pairs={{4,1},{5,2},{6,3},{8,5},{9,6},{10,7},{12,9},{13,10},{14,11},{16,13... | collective-permute-start | bytes 36872 | tf_op jit(solution)/shard_map/ppermute | solution.py:131
  216.9 5.0 %collective-permute-start.23 = (f32[3,2,2,256]{3,2,1,0:T(2,128)S(1)}, f32[3,2,2,256]{3,2,1,0:T(2,128)S(1)}, u32[]{:S(2)}, u32[]{:S(2)}) collective-permute-start(f32[3,2,2,256]{3,2,1,0:T(2,128)S(1)} %get-tuple-element.266), channel_id=1, source_target_pairs={{5,0},{6,1},{7,2},{9,4},{10,5},{11,6},{13,8},{14,9},{15,10},{17,12... | collective-permute-start | bytes 36872 | tf_op jit(solution)/shard_map/ppermute | solution.py:131
  247.9 36.9 %collective-permute-start.25 = (f32[3,2,32,256]{3,2,1,0:T(8,128)S(1)}, f32[3,2,32,256]{3,2,1,0:T(8,128)S(1)}, u32[]{:S(2)}, u32[]{:S(2)}) collective-permute-start(f32[3,2,32,256]{3,2,1,0:T(8,128)S(1)} %get-tuple-element.261), channel_id=1, source_target_pairs={{0,4},{1,5},{2,6},{3,7},{4,8},{5,9},{6,10},{7,11},{8,12},{9,13},{1... | collective-permute-start | bytes 589832 | tf_op jit(solution)/shard_map/ppermute | solution.py:131
  251.1 33.7 %collective-permute-start.27 = (f32[3,32,2,256]{3,2,1,0:T(2,128)S(1)}, f32[3,32,2,256]{3,2,1,0:T(2,128)S(1)}, u32[]{:S(2)}, u32[]{:S(2)}) collective-permute-start(f32[3,32,2,256]{3,2,1,0:T(2,128)S(1)} %get-tuple-element.263), channel_id=1, source_target_pairs={{0,1},{1,2},{2,3},{4,5},{5,6},{6,7},{8,9},{9,10},{10,11},{12,13},{... | collective-permute-start | bytes 589832 | tf_op jit(solution)/shard_map/ppermute | solution.py:131
  253.1 31.8 %collective-permute-start.28 = (f32[3,32,2,256]{3,2,1,0:T(2,128)S(1)}, f32[3,32,2,256]{3,2,1,0:T(2,128)S(1)}, u32[]{:S(2)}, u32[]{:S(2)}) collective-permute-start(f32[3,32,2,256]{3,2,1,0:T(2,128)S(1)} %get-tuple-element.264), channel_id=1, source_target_pairs={{1,0},{2,1},{3,2},{5,4},{6,5},{7,6},{9,8},{10,9},{11,10},{13,12},{... | collective-permute-start | bytes 589832 | tf_op jit(solution)/shard_map/ppermute | solution.py:131
  256.7 28.1 %collective-permute-start.30 = (f32[3,2,32,256]{3,2,1,0:T(8,128)S(1)}, f32[3,2,32,256]{3,2,1,0:T(8,128)S(1)}, u32[]{:S(2)}, u32[]{:S(2)}) collective-permute-start(f32[3,2,32,256]{3,2,1,0:T(8,128)S(1)} %get-tuple-element.262), channel_id=1, source_target_pairs={{4,0},{5,1},{6,2},{7,3},{8,4},{9,5},{10,6},{11,7},{12,8},{13,9},{1... | collective-permute-start | bytes 589832 | tf_op jit(solution)/shard_map/ppermute | solution.py:131
  261.2 6.8 %collective-permute-start.24 = (f32[3,2,2,256]{3,2,1,0:T(2,128)S(1)}, f32[3,2,2,256]{3,2,1,0:T(2,128)S(1)}, u32[]{:S(2)}, u32[]{:S(2)}) collective-permute-start(f32[3,2,2,256]{3,2,1,0:T(2,128)S(1)} %get-tuple-element.257), channel_id=1, source_target_pairs={{0,5},{1,6},{2,7},{4,9},{5,10},{6,11},{8,13},{9,14},{10,15},{12,17... | collective-permute-start | bytes 36872 | tf_op jit(solution)/shard_map/ppermute | solution.py:131
  268.0 5.9 %collective-permute-start.26 = (f32[3,2,2,256]{3,2,1,0:T(2,128)S(1)}, f32[3,2,2,256]{3,2,1,0:T(2,128)S(1)}, u32[]{:S(2)}, u32[]{:S(2)}) collective-permute-start(f32[3,2,2,256]{3,2,1,0:T(2,128)S(1)} %get-tuple-element.260), channel_id=1, source_target_pairs={{1,4},{2,5},{3,6},{5,8},{6,9},{7,10},{9,12},{10,13},{11,14},{13,16... | collective-permute-start | bytes 36872 | tf_op jit(solution)/shard_map/ppermute | solution.py:131
  273.9 5.9 %collective-permute-start.29 = (f32[3,2,2,256]{3,2,1,0:T(2,128)S(1)}, f32[3,2,2,256]{3,2,1,0:T(2,128)S(1)}, u32[]{:S(2)}, u32[]{:S(2)}) collective-permute-start(f32[3,2,2,256]{3,2,1,0:T(2,128)S(1)} %get-tuple-element.259), channel_id=1, source_target_pairs={{4,1},{5,2},{6,3},{8,5},{9,6},{10,7},{12,9},{13,10},{14,11},{16,13... | collective-permute-start | bytes 36872 | tf_op jit(solution)/shard_map/ppermute | solution.py:131
  279.8 5.0 %collective-permute-start.31 = (f32[3,2,2,256]{3,2,1,0:T(2,128)S(1)}, f32[3,2,2,256]{3,2,1,0:T(2,128)S(1)}, u32[]{:S(2)}, u32[]{:S(2)}) collective-permute-start(f32[3,2,2,256]{3,2,1,0:T(2,128)S(1)} %get-tuple-element.258), channel_id=1, source_target_pairs={{5,0},{6,1},{7,2},{9,4},{10,5},{11,6},{13,8},{14,9},{15,10},{17,12... | collective-permute-start | bytes 36872 | tf_op jit(solution)/shard_map/ppermute | solution.py:131
where the time goes:
time: 311 us; the launch traced here: 308 us
  starting transfers between devices  91.5 us (29%)
  Pallas kernels  78.2 us (25%)
  waiting for transfers between devices  48.5 us (16%)
  other arithmetic  33.9 us (11%)
  matrix products  28.6 us (9%)
  local copies, waits for them, and re-layouts  25 us (8%)
    ppermute x32, starting transfers between devices, shift(): return lax.ppermute(piece, ('gx', 'gy'), pairs)  85.5 us
    pallas_call x4, Pallas kernels, elastic_step(): pl.pallas_call(kernel, grid=(nx // bx,), in_specs=[pl.BlockSpec((3, px, p...  78.2 us
    ppermute x32, waiting for transfers between devices, shift(): return lax.ppermute(piece, ('gx', 'gy'), pairs)  48.5 us
    dot_general x2, matrix products, select_block(): jnp.dot(table_rounded, offset_hot, preferred_element_type=jnp.float32)  15.8 us
    concatenate x4, other arithmetic, halo_padded(): return jnp.concatenate([low_row, mid_row, high_row], axis=1)  14.1 us
    transpose x1, local copies, waits for them, and re-layouts, shards(): jnp.einsum('ag,ngz->naz', column_hot, spread_traces, precision=lax.Precis...  12.6 us
    slice x12, local copies, waits for them, and re-layouts, halo_padded(): part = lambda sx, sy: block[:, sx, sy, :]  10.6 us
    dot_general x1, matrix products, shards(): jnp.einsum('ag,ngz->naz', column_hot, spread_traces, precision=lax.Precis...  8.24 us
  transfers between devices with their start and end apart: 33, of which 13 were waited for; matrix products, arithmetic and copies ran while one was open for 2% of the time, Pallas kernels for 0%

commit v1 on v0

--- a/solution.py
+++ b/solution.py
@@ -97,7 +97,7 @@
     lax.fori_loop(0, bx, plane, 0)
 
 
-def elastic_step(upad, prev, moduli, sources, instant, bx=8):
+def elastic_step(upad, prev, moduli, sources, bx=8):
     _, px, py, depth = upad.shape
     nx, ny = px - 4, py - 4
     kernel = functools.partial(step_kernel, bx=bx)
@@ -109,7 +109,7 @@
             pl.BlockSpec((3, px, py, depth), lambda i: (0, 0, 0, 0)),
             pl.BlockSpec((3, bx, ny, depth), block),
             pl.BlockSpec((2, bx, ny, depth), block),
-            pl.BlockSpec((None, 3, bx, ny, depth), lambda i: (instant, 0, i, 0, 0)),
+            pl.BlockSpec((3, bx, ny, depth), block),
         ],
         out_specs=pl.BlockSpec((3, bx, ny, depth), block),
         out_shape=jax.ShapeDtypeStruct((3, nx, ny, depth), jnp.float32),
@@ -349,13 +349,13 @@
     depth_hot = (layer_z[:, None] == jnp.arange(depth, dtype=jnp.int32)[None, :]).astype(
         jnp.float32
     )
-    spread_traces = weighted[:, :, None] * depth_hot[None, :, :]
-    sources = jnp.einsum("ag,ngz->naz", column_hot, spread_traces, precision=lax.Precision.HIGHEST)
-    sources = sources.reshape(STEPS, 3, block_x, block_y, depth)
     previous, current = (field_old, field_now)
     for instant in range(STEPS):
-        padded = halo_padded(current, 2)
-        advanced = elastic_step(padded, previous, moduli, sources, instant)
+        spread = weighted[instant][:, None] * depth_hot
+        source = jnp.dot(column_hot, spread, precision=lax.Precision.HIGHEST)
+        source = source.reshape(3, block_x, block_y, depth)
+        padded = padded_2(current, (("gx", 1), ("gy", 2)), 2)
+        advanced = elastic_step(padded, previous, moduli, source)
         previous, current = (current, advanced)
     return (current, previous)
 

time: 311 us -> 245 us (0.79)
  starting transfers between devices: 91.5 us -> 55.7 us
  waiting for transfers between devices: 48.5 us -> 23.9 us
  local copies, waits for them, and re-layouts: 25 us -> 12.2 us
  matrix products: 28.6 us -> 34.1 us
    ppermute x32 -> x16, starting transfers between devices: 85.5 us -> 49.7 us  [the longest x8 30.8 us: padded_2(): lax.ppermute(lax.slice_in_dim(block, 0, width, axis=dim), axis, backward)]
    ppermute x32 -> x16, waiting for transfers between devices: 48.5 us -> 23.9 us  [the longest x8 14 us: padded_2(): lax.ppermute(lax.slice_in_dim(block, 0, width, axis=dim), axis, backward)]
    transpose x1 -> x0, local copies, waits for them, and re-layouts: 12.6 us -> none  [shards(): jnp.einsum('ag,ngz->naz', column_hot, spread_traces, precision=lax.Precis...]
    slice x12 -> x6, local copies, waits for them, and re-layouts: 10.6 us -> 5.13 us  [the longest x4 4.5 us: padded_2(): lax.slice_in_dim(block, block.shape[dim] - width, None, axis=dim)]
    slice x0 -> x3, other arithmetic: none -> 4.63 us  [padded_2(): lax.slice_in_dim(block, block.shape[dim] - width, None, axis=dim)]
    dot_general x1 -> x4, matrix products: 8.24 us -> 12.8 us  [shards(): source = jnp.dot(column_hot, spread, precision=lax.Precision.HIGHEST)]
  transfers between devices with their start and end apart: 33 -> 17, of which waited for: 13 -> 10; matrix products, arithmetic and copies ran while one was open for 2% -> 8% of each run, Pallas kernels for 0% -> 0%
where the time goes in v1:
time: 245 us; the launch traced here: 243 us
  Pallas kernels  78.2 us (32%)
  starting transfers between devices  55.7 us (23%)
  other arithmetic  36.2 us (15%)
  matrix products  34.1 us (14%)
  waiting for transfers between devices  23.9 us (10%)
  local copies, waits for them, and re-layouts  12.2 us (5%)
    pallas_call x4, Pallas kernels, elastic_step(): pl.pallas_call(kernel, grid=(nx // bx,), in_specs=[pl.BlockSpec((3, px, p...  78.2 us
    ppermute x8, starting transfers between devices, padded_2(): lax.ppermute(lax.slice_in_dim(block, 0, width, axis=dim), axis, backward)  30.8 us
    ppermute x8, starting transfers between devices, padded_2(): lax.ppermute(lax.slice_in_dim(block, block.shape[dim] - width, None, axis...  18.9 us
    dot_general x2, matrix products, select_block(): jnp.dot(table_rounded, offset_hot, preferred_element_type=jnp.float32)  15.8 us
    ppermute x8, waiting for transfers between devices, padded_2(): lax.ppermute(lax.slice_in_dim(block, 0, width, axis=dim), axis, backward)  14 us
    dot_general x4, matrix products, shards(): source = jnp.dot(column_hot, spread, precision=lax.Precision.HIGHEST)  12.8 us
    concatenate x4, other arithmetic, padded_2(): block = jnp.concatenate([low, block, high], axis=dim)  11.3 us
    ppermute x8, waiting for transfers between devices, padded_2(): lax.ppermute(lax.slice_in_dim(block, block.shape[dim] - width, None, axis...  9.96 us
  transfers between devices with their start and end apart: 17, of which 10 were waited for; matrix products, arithmetic and copies ran while one was open for 8% of the time, Pallas kernels for 0%

profile of v1, /device:TPU:12, one launch (start us, length us, event | category | flops | bytes accessed | tf_op | source)
XLA Modules:
  0.0 242.6 jit_solution(16170736512600683372)
XLA Ops:
  2.9 4.9 %sine_multiply_fusion.1 = (f32[32,4,1024]{2,1,0:T(4,128)S(1)}, f32[32,4,1024]{2,1,0:T(4,128)S(1)}, f32[32,4,1024]{2,1,0:T(4,128)S(1)}) fusion(f32[32]{0:T(128)S(1)} %get-tuple-element.291, f32[32,4]{1,0:T(8,128)S(1)} %copy.24, f32[1024]{0:T(1024)S(1)} %multiply_multiply_fusion, f32[1,4,1024]{2,1,0:T(4,128)S(1)} %slice.91, f32[31,4,1024]{2,1,0:T(4,128)S(1)} %slice.90, ...), kind=kLoop, calls=%fused_computation.45 | loop fusion | flops 1441792 | bytes 2102016 | tf_op jit(solution)/shard_map/mul | solution.py:170
  8.1 2.2 while.32
  11.2 4.3 %fusion.43 = (bf16[1,32,4,1024]{3,2,1,0:T(4,128)(2,1)S(1)}, bf16[1,32,4,1024]{3,2,1,0:T(4,128)(2,1)S(1)}) fusion(f32[32,4,1024]{2,1,0:T(4,128)S(1)} %get-tuple-element.191, f32[32,4,1024]{2,1,0:T(4,128)S(1)} %get-tuple-element.190, f32[32,4,1024]{2,1,0:T(4,128)S(1)} %negate_exponential_fusion, f32[32,4,1024]{2,1,0:T(4,128)S(1)} %fusion.23), kind=kLoop, calls=%fused_computation.78 | loop fusion | flops 1835008 | bytes 2621440 | tf_op jit(solution)/shard_map/stack | solution.py:199
  17.7 3.6 %subtract_convert_fusion = bf16[1024,32,64]{0,2,1:T(8,128)(2,1)} fusion(f32[1024,64]{0,1:T(8,128)S(1)} %get-tuple-element.285, f32[1024,32]{0,1:T(8,128)S(1)} %get-tuple-element.279, f32[1024,64]{0,1:T(8,128)S(1)} %get-tuple-element.284, f32[1024,32]{0,1:T(8,128)S(1)} %get-tuple-element.278), kind=kLoop, calls=%fused_computation.24 | loop fusion | flops 8388608 | bytes 4980736 | tf_op jit(solution)/shard_map/convert_element_type | solution.py:214
  21.4 4.4 %convolution_convert_fusion = bf16[256,2048]{1,0:T(8,128)(2,1)} fusion(bf16[256,1024]{1,0:T(8,128)(2,1)S(1)} %bitcast.109, bf16[1024,2048]{0,1:T(8,128)(2,1)} %bitcast.107), kind=kOutput, calls=%fused_computation.34 | convolution fusion | flops 1074266112 | bytes 5767168 | tf_op jit(solution)/shard_map/dot_general | solution.py:302
  25.8 16.1 %while.31 = (s32[]{:T(128)}, bf16[2,2,4,4096]{3,2,1,0:T(4,128)(2,1)S(1)}, s32[2,4096]{1,0:T(2,128)S(1)}, bf16[256,2048]{1,0:T(8,128)(2,1)}, s32[2,4096]{1,0:T(2,128)S(1)}, /*index=5*/s32[]{:T(128)}) while((s32[]{:T(128)}, bf16[2,2,4,4096]{3,2,1,0:T(4,128)(2,1)S(1)}, s32[2,4096]{1,0:T(2,128)S(1)}, bf16[256,2048]{1,0:T(8,128)(2,1)}, ...), condition=%wide.region_9.10_spmd, body=%wide.region_7.9_spmd.sunk | while | flops 4305682432 | bytes 2392141 | solution.py:325
  25.9 8.0 %multiply_reduce_fusion.2 = bf16[2,4,4096]{2,1,0:T(4,128)(2,1)S(1)} fusion(f32[32,4096]{1,0:T(8,128)S(1)} %fusion.91, bf16[256,2048]{1,0:T(8,128)(2,1)} %get-tuple-element.432, s32[4096]{0:T(1024)S(1)} %bitcast.110), kind=kOutput, calls=%fused_computation.3.clone.1 | convolution fusion | flops 4305420288 | bytes 1654784 | tf_op jit(solution)/shard_map/while/body/eval_jaxpr/dot_general | solution.py:317
  34.0 7.8 %multiply_reduce_fusion.2 = bf16[2,4,4096]{2,1,0:T(4,128)(2,1)S(1)} fusion(f32[32,4096]{1,0:T(8,128)S(1)} %fusion.91, bf16[256,2048]{1,0:T(8,128)(2,1)} %get-tuple-element.432, s32[4096]{0:T(1024)S(1)} %bitcast.110), kind=kOutput, calls=%fused_computation.3.clone.1 | convolution fusion | flops 4305420288 | bytes 1654784 | tf_op jit(solution)/shard_map/while/body/eval_jaxpr/dot_general | solution.py:317
  42.9 6.1 %all-to-all-start = ((bf16[2,4,32,256]{3,1,0,2:T(4,128)(2,1)}), bf16[2,4,32,256]{3,1,0,2:T(4,128)(2,1)}, u32[]{:S(2)}, u32[]{:S(2)}) async-start(bf16[2,4,32,256]{3,1,0,2:T(4,128)(2,1)} %copy.27), calls=%async_computation | async-start | bytes 262144 | tf_op jit(solution)/shard_map/all_to_all | solution.py:332
  49.0 3.4 %collective-permute-start = (f32[3,2,32,256]{3,2,1,0:T(8,128)S(1)}, f32[3,2,32,256]{3,2,1,0:T(8,128)S(1)}, u32[]{:S(2)}, u32[]{:S(2)}) collective-permute-start(f32[3,2,32,256]{3,2,1,0:T(8,128)S(1)} %get-tuple-element.272), channel_id=1, source_target_pairs={{0,4},{4,8},{8,12},{12,16},{16,20},{20,24},{24,28},{1,5},{5,9},{9,... | collective-permute-start | bytes 589832 | tf_op jit(solution)/shard_map/ppermute | solution.py:27
  52.4 3.4 %collective-permute-start.1 = (f32[3,2,32,256]{3,2,1,0:T(8,128)S(1)}, f32[3,2,32,256]{3,2,1,0:T(8,128)S(1)}, u32[]{:S(2)}, u32[]{:S(2)}) collective-permute-start(f32[3,2,32,256]{3,2,1,0:T(8,128)S(1)} %get-tuple-element.271), channel_id=1, source_target_pairs={{4,0},{8,4},{12,8},{16,12},{20,16},{24,20},{28,24},{5,1},{9,5},{13... | collective-permute-start | bytes 589832 | tf_op jit(solution)/shard_map/ppermute | solution.py:30
  57.1 4.0 %collective-permute-done = f32[3,2,32,256]{3,2,1,0:T(8,128)S(1)} collective-permute-done((f32[3,2,32,256]{3,2,1,0:T(8,128)S(1)}, f32[3,2,32,256]{3,2,1,0:T(8,128)S(1)}, u32[]{:S(2)}, u32[]{:S(2)}) %collective-permute-start) | collective-permute-done | bytes 196640 | tf_op jit(solution)/shard_map/ppermute | solution.py:27
  63.1 1.7 copy-done.4
  65.7 2.3 collective-permute-start.2
  68.0 3.5 %collective-permute-start.3 = (f32[3,36,2,256]{3,2,1,0:T(2,128)}, f32[3,36,2,256]{3,2,1,0:T(2,128)}, u32[]{:S(2)}, u32[]{:S(2)}) collective-permute-start(f32[3,36,2,256]{3,2,1,0:T(2,128)} %get-tuple-element.264), channel_id=1, source_target_pairs={{1,0},{2,1},{3,2},{5,4},{6,5},{7,6},{9,8},{10,9},{11,10},{13,12},{... | collective-permute-start | bytes 663560 | tf_op jit(solution)/shard_map/ppermute | solution.py:30
  71.6 1.6 copy.28
  73.2 1.6 reshape.400
  76.4 3.2 %fusion.10 = f32[3072,256]{1,0:T(8,128)} fusion(s32[256]{0:T(256)S(1)} %get-tuple-element.287, f32[256]{0:T(256)S(1)} %bitcast.115, s32[256]{0:T(256)S(1)} %get-tuple-element.286), kind=kOutput, calls=%fused_computation.33 | convolution fusion | flops 2416836608 | bytes 3148800 | tf_op jit(solution)/shard_map/dot_general | solution.py:355
  79.6 3.8 %pad_maximum_fusion.up_ref = f32[3,36,36,256]{3,2,1,0:T(8,128)} fusion(f32[3,36,2,256]{3,2,1,0:T(2,128)} %collective-permute-done.3, f32[3,36,32,256]{3,2,1,0:T(8,128)S(1)} %copy-done.5, f32[3,36,2,256]{3,2,1,0:T(2,128)} %collective-permute-done.2), kind=kLoop, calls=%fused_computation.25 | loop fusion | flops 1990656 | bytes 7962624 | tf_op jit(solution)/shard_map/concatenate | solution.py:31
  83.5 19.5 %shard_map.122.prev_ref = f32[3,32,32,256]{3,2,1,0:T(8,128)} custom-call(f32[3,36,36,256]{3,2,1,0:T(8,128)} %pad_maximum_fusion.up_ref, f32[3,32,32,256]{3,2,1,0:T(8,128)} %prev_ref.2, f32[2,32,32,256]{3,2,1,0:T(8,128)} %mod_ref.7, f32[3,32,32,256]{3,2,1,0:T(8,128)} %bitcast.106), custom_call_target="tpu_custom_call" | custom-call | tf_op jit(solution)/shard_map/pallas_call | solution.py:105
  104.2 2.9 %collective-permute-start.4 = (f32[3,2,32,256]{3,2,1,0:T(8,128)S(1)}, f32[3,2,32,256]{3,2,1,0:T(8,128)S(1)}, u32[]{:S(2)}, u32[]{:S(2)}) collective-permute-start(f32[3,2,32,256]{3,2,1,0:T(8,128)S(1)} %get-tuple-element.269), channel_id=1, source_target_pairs={{0,4},{4,8},{8,12},{12,16},{16,20},{20,24},{24,28},{1,5},{5,9},{9,... | collective-permute-start | bytes 589832 | tf_op jit(solution)/shard_map/ppermute | solution.py:27
  107.1 3.9 %collective-permute-start.5 = (f32[3,2,32,256]{3,2,1,0:T(8,128)S(1)}, f32[3,2,32,256]{3,2,1,0:T(8,128)S(1)}, u32[]{:S(2)}, u32[]{:S(2)}) collective-permute-start(f32[3,2,32,256]{3,2,1,0:T(8,128)S(1)} %get-tuple-element.270), channel_id=1, source_target_pairs={{4,0},{8,4},{12,8},{16,12},{20,16},{24,20},{28,24},{5,1},{9,5},{13... | collective-permute-start | bytes 589832 | tf_op jit(solution)/shard_map/ppermute | solution.py:30
  111.0 2.5 %collective-permute-done.4 = f32[3,2,32,256]{3,2,1,0:T(8,128)S(1)} collective-permute-done((f32[3,2,32,256]{3,2,1,0:T(8,128)S(1)}, f32[3,2,32,256]{3,2,1,0:T(8,128)S(1)}, u32[]{:S(2)}, u32[]{:S(2)}) %collective-permute-start.4) | collective-permute-done | bytes 196640 | tf_op jit(solution)/shard_map/ppermute | solution.py:27
  113.5 4.1 %collective-permute-done.5 = f32[3,2,32,256]{3,2,1,0:T(8,128)S(1)} collective-permute-done((f32[3,2,32,256]{3,2,1,0:T(8,128)S(1)}, f32[3,2,32,256]{3,2,1,0:T(8,128)S(1)}, u32[]{:S(2)}, u32[]{:S(2)}) %collective-permute-start.5) | collective-permute-done | bytes 196640 | tf_op jit(solution)/shard_map/ppermute | solution.py:30
  117.6 1.5 pad_maximum_fusion.13
  119.1 1.9 collective-permute-start.6
  121.0 3.6 %collective-permute-start.7 = (f32[3,36,2,256]{3,2,1,0:T(2,128)S(1)}, f32[3,36,2,256]{3,2,1,0:T(2,128)S(1)}, u32[]{:S(2)}, u32[]{:S(2)}) collective-permute-start(f32[3,36,2,256]{3,2,1,0:T(2,128)S(1)} %get-tuple-element.262), channel_id=1, source_target_pairs={{1,0},{2,1},{3,2},{5,4},{6,5},{7,6},{9,8},{10,9},{11,10},{13,12},{... | collective-permute-start | bytes 663560 | tf_op jit(solution)/shard_map/ppermute | solution.py:30
  124.7 3.2 %fusion.9 = f32[3072,256]{1,0:T(8,128)} fusion(s32[256]{0:T(256)S(1)} %get-tuple-element.287, f32[256]{0:T(256)S(1)} %bitcast.114, s32[256]{0:T(256)S(1)} %get-tuple-element.286), kind=kOutput, calls=%fused_computation.32 | convolution fusion | flops 2416836608 | bytes 3148800 | tf_op jit(solution)/shard_map/dot_general | solution.py:355
  128.1 2.5 %pad_maximum_fusion.1.up_ref = f32[3,36,36,256]{3,2,1,0:T(8,128)} fusion(f32[3,36,2,256]{3,2,1,0:T(2,128)S(1)} %collective-permute-done.7, f32[3,2,32,256]{3,2,1,0:T(8,128)S(1)} %collective-permute-done.5, f32[3,32,32,256]{3,2,1,0:T(8,128)S(1)} %copy-done.1, f32[3,2,32,256]{3,2,1,0:T(8,128)S(1)} %collective-permute-done.4, ...), kind=kLoop, calls=%fused_computation.26 | loop fusion | flops 3981312 | bytes 7962624 | tf_op jit(solution)/shard_map/concatenate | solution.py:31
  130.6 19.6 %shard_map.123.prev_ref = f32[3,32,32,256]{3,2,1,0:T(8,128)} custom-call(f32[3,36,36,256]{3,2,1,0:T(8,128)} %pad_maximum_fusion.1.up_ref, f32[3,32,32,256]{3,2,1,0:T(8,128)} %prev_ref.3, f32[2,32,32,256]{3,2,1,0:T(8,128)} %mod_ref.7, f32[3,32,32,256]{3,2,1,0:T(8,128)} %bitcast.105), custom_call_target="tpu_custom_call" | custom-call | tf_op jit(solution)/shard_map/pallas_call | solution.py:105
  151.4 2.1 collective-permute-start.8
  153.4 4.7 %collective-permute-start.9 = (f32[3,2,32,256]{3,2,1,0:T(8,128)S(1)}, f32[3,2,32,256]{3,2,1,0:T(8,128)S(1)}, u32[]{:S(2)}, u32[]{:S(2)}) collective-permute-start(f32[3,2,32,256]{3,2,1,0:T(8,128)S(1)} %get-tuple-element.268), channel_id=1, source_target_pairs={{4,0},{8,4},{12,8},{16,12},{20,16},{24,20},{28,24},{5,1},{9,5},{13... | collective-permute-start | bytes 589832 | tf_op jit(solution)/shard_map/ppermute | solution.py:30
  158.1 1.7 collective-permute-done.8
  159.8 4.0 %collective-permute-done.9 = f32[3,2,32,256]{3,2,1,0:T(8,128)S(1)} collective-permute-done((f32[3,2,32,256]{3,2,1,0:T(8,128)S(1)}, f32[3,2,32,256]{3,2,1,0:T(8,128)S(1)}, u32[]{:S(2)}, u32[]{:S(2)}) %collective-permute-start.9) | collective-permute-done | bytes 196640 | tf_op jit(solution)/shard_map/ppermute | solution.py:30
  165.3 1.9 collective-permute-start.10
  167.3 3.6 %collective-permute-start.11 = (f32[3,36,2,256]{3,2,1,0:T(2,128)S(1)}, f32[3,36,2,256]{3,2,1,0:T(2,128)S(1)}, u32[]{:S(2)}, u32[]{:S(2)}) collective-permute-start(f32[3,36,2,256]{3,2,1,0:T(2,128)S(1)} %get-tuple-element.260), channel_id=1, source_target_pairs={{1,0},{2,1},{3,2},{5,4},{6,5},{7,6},{9,8},{10,9},{11,10},{13,12},{... | collective-permute-start | bytes 663560 | tf_op jit(solution)/shard_map/ppermute | solution.py:30
  170.9 3.2 %fusion.8 = f32[3072,256]{1,0:T(8,128)} fusion(s32[256]{0:T(256)S(1)} %get-tuple-element.287, f32[256]{0:T(256)S(1)} %bitcast.113, s32[256]{0:T(256)S(1)} %get-tuple-element.286), kind=kOutput, calls=%fused_computation.31 | convolution fusion | flops 2416836608 | bytes 3148800 | tf_op jit(solution)/shard_map/dot_general | solution.py:355
  174.4 2.5 %pad_maximum_fusion.2.up_ref = f32[3,36,36,256]{3,2,1,0:T(8,128)} fusion(f32[3,36,2,256]{3,2,1,0:T(2,128)S(1)} %collective-permute-done.11, f32[3,2,32,256]{3,2,1,0:T(8,128)S(1)} %collective-permute-done.9, f32[3,32,32,256]{3,2,1,0:T(8,128)S(1)} %copy-done, f32[3,2,32,256]{3,2,1,0:T(8,128)S(1)} %collective-permute-done.8, ...), kind=kLoop, calls=%fused_computation.27 | loop fusion | flops 3981312 | bytes 7962624 | tf_op jit(solution)/shard_map/concatenate | solution.py:31
  176.8 19.6 %shard_map.124 = f32[3,32,32,256]{3,2,1,0:T(8,128)} custom-call(f32[3,36,36,256]{3,2,1,0:T(8,128)} %pad_maximum_fusion.2.up_ref, f32[3,32,32,256]{3,2,1,0:T(8,128)} %shard_map.122.prev_ref, f32[2,32,32,256]{3,2,1,0:T(8,128)} %mod_ref.7, f32[3,32,32,256]{3,2,1,0:T(8,128)} %bitcast.104), custom_call_target="tpu_custom_call" | custom-call | tf_op jit(solution)/shard_map/pallas_call | solution.py:105
  197.6 2.6 %collective-permute-start.12 = (f32[3,2,32,256]{3,2,1,0:T(8,128)S(1)}, f32[3,2,32,256]{3,2,1,0:T(8,128)S(1)}, u32[]{:S(2)}, u32[]{:S(2)}) collective-permute-start(f32[3,2,32,256]{3,2,1,0:T(8,128)S(1)} %get-tuple-element.265), channel_id=1, source_target_pairs={{0,4},{4,8},{8,12},{12,16},{16,20},{20,24},{24,28},{1,5},{5,9},{9,... | collective-permute-start | bytes 589832 | tf_op jit(solution)/shard_map/ppermute | solution.py:27
  200.2 4.2 %collective-permute-start.13 = (f32[3,2,32,256]{3,2,1,0:T(8,128)S(1)}, f32[3,2,32,256]{3,2,1,0:T(8,128)S(1)}, u32[]{:S(2)}, u32[]{:S(2)}) collective-permute-start(f32[3,2,32,256]{3,2,1,0:T(8,128)S(1)} %get-tuple-element.266), channel_id=1, source_target_pairs={{4,0},{8,4},{12,8},{16,12},{20,16},{24,20},{28,24},{5,1},{9,5},{13... | collective-permute-start | bytes 589832 | tf_op jit(solution)/shard_map/ppermute | solution.py:30
  204.4 1.7 collective-permute-done.12
  206.1 4.0 %collective-permute-done.13 = f32[3,2,32,256]{3,2,1,0:T(8,128)S(1)} collective-permute-done((f32[3,2,32,256]{3,2,1,0:T(8,128)S(1)}, f32[3,2,32,256]{3,2,1,0:T(8,128)S(1)}, u32[]{:S(2)}, u32[]{:S(2)}) %collective-permute-start.13) | collective-permute-done | bytes 196640 | tf_op jit(solution)/shard_map/ppermute | solution.py:30
  211.6 1.9 collective-permute-start.14
  213.5 3.9 %collective-permute-start.15 = (f32[3,36,2,256]{3,2,1,0:T(2,128)S(1)}, f32[3,36,2,256]{3,2,1,0:T(2,128)S(1)}, u32[]{:S(2)}, u32[]{:S(2)}) collective-permute-start(f32[3,36,2,256]{3,2,1,0:T(2,128)S(1)} %get-tuple-element.258), channel_id=1, source_target_pairs={{1,0},{2,1},{3,2},{5,4},{6,5},{7,6},{9,8},{10,9},{11,10},{13,12},{... | collective-permute-start | bytes 663560 | tf_op jit(solution)/shard_map/ppermute | solution.py:30
  217.4 3.2 %fusion.7 = f32[3072,256]{1,0:T(8,128)} fusion(s32[256]{0:T(256)S(1)} %get-tuple-element.287, f32[256]{0:T(256)S(1)} %bitcast.112, s32[256]{0:T(256)S(1)} %get-tuple-element.286), kind=kOutput, calls=%fused_computation.30 | convolution fusion | flops 2416836608 | bytes 3148800 | tf_op jit(solution)/shard_map/dot_general | solution.py:355
  220.6 2.5 %pad_maximum_fusion.3.up_ref = f32[3,36,36,256]{3,2,1,0:T(8,128)} fusion(f32[3,36,2,256]{3,2,1,0:T(2,128)S(1)} %collective-permute-done.15, f32[3,2,32,256]{3,2,1,0:T(8,128)S(1)} %collective-permute-done.13, f32[3,32,32,256]{3,2,1,0:T(8,128)S(1)} %copy-done.2, f32[3,2,32,256]{3,2,1,0:T(8,128)S(1)} %collective-permute-done.12, ...), kind=kLoop, calls=%fused_computation.28 | loop fusion | flops 3981312 | bytes 7962624 | tf_op jit(solution)/shard_map/concatenate | solution.py:31
  223.1 19.6 %shard_map.125 = f32[3,32,32,256]{3,2,1,0:T(8,128)} custom-call(f32[3,36,36,256]{3,2,1,0:T(8,128)} %pad_maximum_fusion.3.up_ref, f32[3,32,32,256]{3,2,1,0:T(8,128)} %shard_map.123.prev_ref, f32[2,32,32,256]{3,2,1,0:T(8,128)} %mod_ref.7, f32[3,32,32,256]{3,2,1,0:T(8,128)} %bitcast.103), custom_call_target="tpu_custom_call" | custom-call | tf_op jit(solution)/shard_map/pallas_call | solution.py:105
  (111 shorter events, 20.8 us)
Async XLA Ops:
  15.5 5.8 %copy-start.6 = (s32[8192]{0:T(1024)S(1)}, s32[8192]{0:T(1024)}, u32[]{:S(2)}) copy-start(s32[8192]{0:T(1024)} %param.19) | copy-start | bytes 98308
  15.5 5.8 %copy-start.7 = (s32[8192]{0:T(1024)S(1)}, s32[8192]{0:T(1024)}, u32[]{:S(2)}) copy-start(s32[8192]{0:T(1024)} %param.20) | copy-start | bytes 98308
  25.8 23.1 %copy-start.3 = (f32[3,32,32,256]{3,2,1,0:T(8,128)S(1)}, f32[3,32,32,256]{3,2,1,0:T(8,128)}, u32[]{:S(2)}) copy-start(f32[3,32,32,256]{3,2,1,0:T(8,128)} %prev_ref.3) | copy-start | bytes 9437188
  25.8 31.3 %copy-start.9 = (s32[256]{0:T(256)S(1)}, s32[256]{0:T(256)}, u32[]{:S(2)}) copy-start(s32[256]{0:T(256)} %param.21) | copy-start | bytes 3076
  42.9 28.7 %all-to-all-start = ((bf16[2,4,32,256]{3,1,0,2:T(4,128)(2,1)}), bf16[2,4,32,256]{3,1,0,2:T(4,128)(2,1)}, u32[]{:S(2)}, u32[]{:S(2)}) async-start(bf16[2,4,32,256]{3,1,0,2:T(4,128)(2,1)} %copy.27), calls=%async_computation | async-start | bytes 262144 | tf_op jit(solution)/shard_map/all_to_all | solution.py:332
  49.0 12.2 %collective-permute-start = (f32[3,2,32,256]{3,2,1,0:T(8,128)S(1)}, f32[3,2,32,256]{3,2,1,0:T(8,128)S(1)}, u32[]{:S(2)}, u32[]{:S(2)}) collective-permute-start(f32[3,2,32,256]{3,2,1,0:T(8,128)S(1)} %get-tuple-element.272), channel_id=1, source_target_pairs={{0,4},{4,8},{8,12},{12,16},{16,20},{20,24},{24,28},{1,5},{5,9},{9,... | collective-permute-start | bytes 589832 | tf_op jit(solution)/shard_map/ppermute | solution.py:27
  52.4 10.7 %collective-permute-start.1 = (f32[3,2,32,256]{3,2,1,0:T(8,128)S(1)}, f32[3,2,32,256]{3,2,1,0:T(8,128)S(1)}, u32[]{:S(2)}, u32[]{:S(2)}) collective-permute-start(f32[3,2,32,256]{3,2,1,0:T(8,128)S(1)} %get-tuple-element.271), channel_id=1, source_target_pairs={{4,0},{8,4},{12,8},{16,12},{20,16},{24,20},{28,24},{5,1},{9,5},{13... | collective-permute-start | bytes 589832 | tf_op jit(solution)/shard_map/ppermute | solution.py:30
  63.1 1.8 copy-start.4
  65.7 13.9 %copy-start.5 = (f32[3,36,32,256]{3,2,1,0:T(8,128)S(1)}, f32[3,36,32,256]{3,2,1,0:T(8,128)}, u32[]{:S(2)}) copy-start(f32[3,36,32,256]{3,2,1,0:T(8,128)} %copy-done.4) | copy-start | bytes 10616836
  65.7 13.9 %collective-permute-start.2 = (f32[3,36,2,256]{3,2,1,0:T(2,128)}, f32[3,36,2,256]{3,2,1,0:T(2,128)}, u32[]{:S(2)}, u32[]{:S(2)}) collective-permute-start(f32[3,36,2,256]{3,2,1,0:T(2,128)} %get-tuple-element.263), channel_id=1, source_target_pairs={{0,1},{1,2},{2,3},{4,5},{5,6},{6,7},{8,9},{9,10},{10,11},{12,13},{... | collective-permute-start | bytes 663560 | tf_op jit(solution)/shard_map/ppermute | solution.py:27
  68.0 11.6 %collective-permute-start.3 = (f32[3,36,2,256]{3,2,1,0:T(2,128)}, f32[3,36,2,256]{3,2,1,0:T(2,128)}, u32[]{:S(2)}, u32[]{:S(2)}) collective-permute-start(f32[3,36,2,256]{3,2,1,0:T(2,128)} %get-tuple-element.264), channel_id=1, source_target_pairs={{1,0},{2,1},{3,2},{5,4},{6,5},{7,6},{9,8},{10,9},{11,10},{13,12},{... | collective-permute-start | bytes 663560 | tf_op jit(solution)/shard_map/ppermute | solution.py:30
  103.0 21.7 %copy-start.8 = (f32[1,256]{1,0:T(1,128)S(1)}, f32[1,256]{1,0:T(1,128)}, u32[]{:S(2)}) copy-start(f32[1,256]{1,0:T(1,128)} %get-tuple-element.282) | copy-start | bytes 3076
  103.0 25.1 %copy-start.1 = (f32[3,32,32,256]{3,2,1,0:T(8,128)S(1)}, f32[3,32,32,256]{3,2,1,0:T(8,128)}, u32[]{:S(2)}) copy-start(f32[3,32,32,256]{3,2,1,0:T(8,128)} %shard_map.122.prev_ref) | copy-start | bytes 9437188
  104.2 9.3 %collective-permute-start.4 = (f32[3,2,32,256]{3,2,1,0:T(8,128)S(1)}, f32[3,2,32,256]{3,2,1,0:T(8,128)S(1)}, u32[]{:S(2)}, u32[]{:S(2)}) collective-permute-start(f32[3,2,32,256]{3,2,1,0:T(8,128)S(1)} %get-tuple-element.269), channel_id=1, source_target_pairs={{0,4},{4,8},{8,12},{12,16},{16,20},{20,24},{24,28},{1,5},{5,9},{9,... | collective-permute-start | bytes 589832 | tf_op jit(solution)/shard_map/ppermute | solution.py:27
  107.1 10.5 %collective-permute-start.5 = (f32[3,2,32,256]{3,2,1,0:T(8,128)S(1)}, f32[3,2,32,256]{3,2,1,0:T(8,128)S(1)}, u32[]{:S(2)}, u32[]{:S(2)}) collective-permute-start(f32[3,2,32,256]{3,2,1,0:T(8,128)S(1)} %get-tuple-element.270), channel_id=1, source_target_pairs={{4,0},{8,4},{12,8},{16,12},{20,16},{24,20},{28,24},{5,1},{9,5},{13... | collective-permute-start | bytes 589832 | tf_op jit(solution)/shard_map/ppermute | solution.py:30
  119.1 8.8 %collective-permute-start.6 = (f32[3,36,2,256]{3,2,1,0:T(2,128)S(1)}, f32[3,36,2,256]{3,2,1,0:T(2,128)S(1)}, u32[]{:S(2)}, u32[]{:S(2)}) collective-permute-start(f32[3,36,2,256]{3,2,1,0:T(2,128)S(1)} %get-tuple-element.261), channel_id=1, source_target_pairs={{0,1},{1,2},{2,3},{4,5},{5,6},{6,7},{8,9},{9,10},{10,11},{12,13},{... | collective-permute-start | bytes 663560 | tf_op jit(solution)/shard_map/ppermute | solution.py:27
  121.0 7.1 %collective-permute-start.7 = (f32[3,36,2,256]{3,2,1,0:T(2,128)S(1)}, f32[3,36,2,256]{3,2,1,0:T(2,128)S(1)}, u32[]{:S(2)}, u32[]{:S(2)}) collective-permute-start(f32[3,36,2,256]{3,2,1,0:T(2,128)S(1)} %get-tuple-element.262), channel_id=1, source_target_pairs={{1,0},{2,1},{3,2},{5,4},{6,5},{7,6},{9,8},{10,9},{11,10},{13,12},{... | collective-permute-start | bytes 663560 | tf_op jit(solution)/shard_map/ppermute | solution.py:30
  150.2 24.2 %copy-start = (f32[3,32,32,256]{3,2,1,0:T(8,128)S(1)}, f32[3,32,32,256]{3,2,1,0:T(8,128)}, u32[]{:S(2)}) copy-start(f32[3,32,32,256]{3,2,1,0:T(8,128)} %shard_map.123.prev_ref) | copy-start | bytes 9437188
  151.4 8.5 %collective-permute-start.8 = (f32[3,2,32,256]{3,2,1,0:T(8,128)S(1)}, f32[3,2,32,256]{3,2,1,0:T(8,128)S(1)}, u32[]{:S(2)}, u32[]{:S(2)}) collective-permute-start(f32[3,2,32,256]{3,2,1,0:T(8,128)S(1)} %get-tuple-element.267), channel_id=1, source_target_pairs={{0,4},{4,8},{8,12},{12,16},{16,20},{20,24},{24,28},{1,5},{5,9},{9,... | collective-permute-start | bytes 589832 | tf_op jit(solution)/shard_map/ppermute | solution.py:27
  153.4 10.4 %collective-permute-start.9 = (f32[3,2,32,256]{3,2,1,0:T(8,128)S(1)}, f32[3,2,32,256]{3,2,1,0:T(8,128)S(1)}, u32[]{:S(2)}, u32[]{:S(2)}) collective-permute-start(f32[3,2,32,256]{3,2,1,0:T(8,128)S(1)} %get-tuple-element.268), channel_id=1, source_target_pairs={{4,0},{8,4},{12,8},{16,12},{20,16},{24,20},{28,24},{5,1},{9,5},{13... | collective-permute-start | bytes 589832 | tf_op jit(solution)/shard_map/ppermute | solution.py:30
  165.3 8.8 %collective-permute-start.10 = (f32[3,36,2,256]{3,2,1,0:T(2,128)S(1)}, f32[3,36,2,256]{3,2,1,0:T(2,128)S(1)}, u32[]{:S(2)}, u32[]{:S(2)}) collective-permute-start(f32[3,36,2,256]{3,2,1,0:T(2,128)S(1)} %get-tuple-element.259), channel_id=1, source_target_pairs={{0,1},{1,2},{2,3},{4,5},{5,6},{6,7},{8,9},{9,10},{10,11},{12,13},{... | collective-permute-start | bytes 663560 | tf_op jit(solution)/shard_map/ppermute | solution.py:27
  167.3 7.1 %collective-permute-start.11 = (f32[3,36,2,256]{3,2,1,0:T(2,128)S(1)}, f32[3,36,2,256]{3,2,1,0:T(2,128)S(1)}, u32[]{:S(2)}, u32[]{:S(2)}) collective-permute-start(f32[3,36,2,256]{3,2,1,0:T(2,128)S(1)} %get-tuple-element.260), channel_id=1, source_target_pairs={{1,0},{2,1},{3,2},{5,4},{6,5},{7,6},{9,8},{10,9},{11,10},{13,12},{... | collective-permute-start | bytes 663560 | tf_op jit(solution)/shard_map/ppermute | solution.py:30
  196.4 24.2 %copy-start.2 = (f32[3,32,32,256]{3,2,1,0:T(8,128)S(1)}, f32[3,32,32,256]{3,2,1,0:T(8,128)}, u32[]{:S(2)}) copy-start(f32[3,32,32,256]{3,2,1,0:T(8,128)} %shard_map.124) | copy-start | bytes 9437188
  197.6 8.5 %collective-permute-start.12 = (f32[3,2,32,256]{3,2,1,0:T(8,128)S(1)}, f32[3,2,32,256]{3,2,1,0:T(8,128)S(1)}, u32[]{:S(2)}, u32[]{:S(2)}) collective-permute-start(f32[3,2,32,256]{3,2,1,0:T(8,128)S(1)} %get-tuple-element.265), channel_id=1, source_target_pairs={{0,4},{4,8},{8,12},{12,16},{16,20},{20,24},{24,28},{1,5},{5,9},{9,... | collective-permute-start | bytes 589832 | tf_op jit(solution)/shard_map/ppermute | solution.py:27
  200.2 9.8 %collective-permute-start.13 = (f32[3,2,32,256]{3,2,1,0:T(8,128)S(1)}, f32[3,2,32,256]{3,2,1,0:T(8,128)S(1)}, u32[]{:S(2)}, u32[]{:S(2)}) collective-permute-start(f32[3,2,32,256]{3,2,1,0:T(8,128)S(1)} %get-tuple-element.266), channel_id=1, source_target_pairs={{4,0},{8,4},{12,8},{16,12},{20,16},{24,20},{28,24},{5,1},{9,5},{13... | collective-permute-start | bytes 589832 | tf_op jit(solution)/shard_map/ppermute | solution.py:30
  211.6 9.0 %collective-permute-start.14 = (f32[3,36,2,256]{3,2,1,0:T(2,128)S(1)}, f32[3,36,2,256]{3,2,1,0:T(2,128)S(1)}, u32[]{:S(2)}, u32[]{:S(2)}) collective-permute-start(f32[3,36,2,256]{3,2,1,0:T(2,128)S(1)} %get-tuple-element.257), channel_id=1, source_target_pairs={{0,1},{1,2},{2,3},{4,5},{5,6},{6,7},{8,9},{9,10},{10,11},{12,13},{... | collective-permute-start | bytes 663560 | tf_op jit(solution)/shard_map/ppermute | solution.py:27
  213.5 7.1 %collective-permute-start.15 = (f32[3,36,2,256]{3,2,1,0:T(2,128)S(1)}, f32[3,36,2,256]{3,2,1,0:T(2,128)S(1)}, u32[]{:S(2)}, u32[]{:S(2)}) collective-permute-start(f32[3,36,2,256]{3,2,1,0:T(2,128)S(1)} %get-tuple-element.258), channel_id=1, source_target_pairs={{1,0},{2,1},{3,2},{5,4},{6,5},{7,6},{9,8},{10,9},{11,10},{13,12},{... | collective-permute-start | bytes 663560 | tf_op jit(solution)/shard_map/ppermute | solution.py:30

commit v2 on v1

--- a/solution.py
+++ b/solution.py
@@ -32,7 +32,7 @@
     return block
 
 
-TAPS = ((-2, -1.0), (-1, 16.0), (1, 16.0), (2, -1.0))
+YPAD = 8
 
 
 def step_kernel(up_ref, prev_ref, mod_ref, src_ref, out_ref, *, bx):
@@ -50,7 +50,7 @@
         xp = i * bx + p + 2
         for g in range(out_ref.shape[2] // 8):
             def load(c, dx, dy):
-                return up_ref[c, xp + dx, pl.ds(8 * g + 2 + dy, 8), :]
+                return up_ref[c, xp + dx, pl.ds(8 * g + YPAD + dy, 8), :]
 
             lam = mod_ref[0, p, pl.ds(8 * g, 8), :]
             mu = mod_ref[1, p, pl.ds(8 * g, 8), :]
@@ -60,16 +60,20 @@
 
             def curv(c, axis):
                 center = centers[c]
-                acc = -30.0 * center
-                for off, w in TAPS:
+                near = None
+                far = None
+                for off in (-1, 1, -2, 2):
                     if axis == 0:
                         t = load(c, off, 0)
                     elif axis == 1:
                         t = load(c, 0, off)
                     else:
                         t = zs(center, off)
-                    acc = acc + w * t
-                return acc / 12.0
+                    if abs(off) == 1:
+                        near = t if near is None else near + t
+                    else:
+                        far = t if far is None else far + t
+                return 16.0 * near - far - 30.0 * center
 
             def mixed(p_c, a, b):
                 acc = None
@@ -79,16 +83,19 @@
                         d[a] = sa
                         d[b] = sb
                         t = zs(load(p_c, d[0], d[1]), d[2])
-                        t = t if sa * sb > 0 else -t
-                        acc = t if acc is None else acc + t
-                return acc / 4.0
+                        if acc is None:
+                            acc = t
+                        elif sa * sb > 0:
+                            acc = acc + t
+                        else:
+                            acc = acc - t
+                return acc
 
             for c in range(3):
-                upd = stiff * curv(c, c)
-                for e in range(3):
-                    if e != c:
-                        upd = upd + mu * curv(c, e)
-                        upd = upd + coup * mixed(e, c, e)
+                others = [e for e in range(3) if e != c]
+                second = stiff * curv(c, c) + mu * (curv(c, others[0]) + curv(c, others[1]))
+                cross = mixed(others[0], c, others[0]) + mixed(others[1], c, others[1])
+                upd = second * (1.0 / 12.0) + coup * (cross * 0.25)
                 prev = prev_ref[c, p, pl.ds(8 * g, 8), :]
                 src = src_ref[c, p, pl.ds(8 * g, 8), :]
                 out_ref[c, p, pl.ds(8 * g, 8), :] = (2.0 * centers[c] - prev + upd) + src
@@ -99,7 +106,7 @@
 
 def elastic_step(upad, prev, moduli, sources, bx=8):
     _, px, py, depth = upad.shape
-    nx, ny = px - 4, py - 4
+    nx, ny = px - 4, py - 2 * YPAD
     kernel = functools.partial(step_kernel, bx=bx)
     block = lambda i: (0, i, 0, 0)
     return pl.pallas_call(
@@ -114,40 +121,6 @@
         out_specs=pl.BlockSpec((3, bx, ny, depth), block),
         out_shape=jax.ShapeDtypeStruct((3, nx, ny, depth), jnp.float32),
     )(upad, prev, moduli, sources)
-
-
-def halo_padded(block, width):
-    size_x = lax.axis_size("gx")
-    size_y = lax.axis_size("gy")
-    nx, ny = block.shape[1], block.shape[2]
-
-    def shift(piece, step_x, step_y):
-        pairs = []
-        for ix in range(size_x):
-            for iy in range(size_y):
-                jx, jy = ix + step_x, iy + step_y
-                if 0 <= jx < size_x and 0 <= jy < size_y:
-                    pairs.append((ix * size_y + iy, jx * size_y + jy))
-        return lax.ppermute(piece, ("gx", "gy"), pairs)
-
-    lo_x = slice(0, width)
-    hi_x = slice(nx - width, nx)
-    lo_y = slice(0, width)
-    hi_y = slice(ny - width, ny)
-    whole = slice(None)
-    part = lambda sx, sy: block[:, sx, sy, :]
-    left = shift(part(hi_x, whole), 1, 0)
-    right = shift(part(lo_x, whole), -1, 0)
-    down = shift(part(whole, hi_y), 0, 1)
-    up = shift(part(whole, lo_y), 0, -1)
-    ll = shift(part(hi_x, hi_y), 1, 1)
-    lh = shift(part(hi_x, lo_y), 1, -1)
-    hl = shift(part(lo_x, hi_y), -1, 1)
-    hh = shift(part(lo_x, lo_y), -1, -1)
-    low_row = jnp.concatenate([ll, left, lh], axis=2)
-    mid_row = jnp.concatenate([down, block, up], axis=2)
-    high_row = jnp.concatenate([hl, right, hh], axis=2)
-    return jnp.concatenate([low_row, mid_row, high_row], axis=1)
 
 
 def level_table(values, layer_of_level):
@@ -355,6 +328,7 @@
         source = jnp.dot(column_hot, spread, precision=lax.Precision.HIGHEST)
         source = source.reshape(3, block_x, block_y, depth)
         padded = padded_2(current, (("gx", 1), ("gy", 2)), 2)
+        padded = jnp.pad(padded, ((0, 0), (0, 0), (YPAD - 2, YPAD - 2), (0, 0)))
         advanced = elastic_step(padded, previous, moduli, source)
         previous, current = (current, advanced)
     return (current, previous)

time: 245 us -> 225 us (0.918)
  Pallas kernels: 78.2 us -> 57.3 us
    pallas_call x4, Pallas kernels: 78.2 us -> 57.3 us  [elastic_step(): pl.pallas_call(kernel, grid=(nx // bx,), in_specs=[pl.BlockSpec((3, px, p...]
  transfers between devices with their start and end apart: 17 -> 17, of which waited for: 10 -> 11; matrix products, arithmetic and copies ran while one was open for 8% -> 9% of each run, Pallas kernels for 0% -> 0%
where the time goes in v2:
time: 225 us; the launch traced here: 222 us
  Pallas kernels  57.3 us (25%)
  starting transfers between devices  55.5 us (25%)
  other arithmetic  36.8 us (16%)
  matrix products  34.2 us (15%)
  waiting for transfers between devices  24.1 us (11%)
  local copies, waits for them, and re-layouts  12.1 us (5%)
    pallas_call x4, Pallas kernels, elastic_step(): pl.pallas_call(kernel, grid=(nx // bx,), in_specs=[pl.BlockSpec((3, px, p...  57.3 us
    ppermute x8, starting transfers between devices, padded_2(): lax.ppermute(lax.slice_in_dim(block, 0, width, axis=dim), axis, backward)  30.5 us
    ppermute x8, starting transfers between devices, padded_2(): lax.ppermute(lax.slice_in_dim(block, block.shape[dim] - width, None, axis...  18.9 us
    dot_general x2, matrix products, select_block(): jnp.dot(table_rounded, offset_hot, preferred_element_type=jnp.float32)  15.8 us
    ppermute x8, waiting for transfers between devices, padded_2(): lax.ppermute(lax.slice_in_dim(block, 0, width, axis=dim), axis, backward)  14.1 us
    dot_general x4, matrix products, shards(): source = jnp.dot(column_hot, spread, precision=lax.Precision.HIGHEST)  12.9 us
    concatenate x4, other arithmetic, padded_2(): block = jnp.concatenate([low, block, high], axis=dim)  11.8 us
    ppermute x8, waiting for transfers between devices, padded_2(): lax.ppermute(lax.slice_in_dim(block, block.shape[dim] - width, None, axis...  9.97 us
  transfers between devices with their start and end apart: 17, of which 11 were waited for; matrix products, arithmetic and copies ran while one was open for 9% of the time, Pallas kernels for 0%

profile of v2, /device:TPU:12, one launch (start us, length us, event | category | flops | bytes accessed | tf_op | source)
XLA Modules:
  0.0 222.3 jit_solution(16020894458864354601)
XLA Ops:
  2.9 4.9 %sine_multiply_fusion.1 = (f32[32,4,1024]{2,1,0:T(4,128)S(1)}, f32[32,4,1024]{2,1,0:T(4,128)S(1)}, f32[32,4,1024]{2,1,0:T(4,128)S(1)}) fusion(f32[32]{0:T(128)S(1)} %get-tuple-element.291, f32[32,4]{1,0:T(8,128)S(1)} %copy.24, f32[1024]{0:T(1024)S(1)} %multiply_multiply_fusion, f32[1,4,1024]{2,1,0:T(4,128)S(1)} %slice.91, f32[31,4,1024]{2,1,0:T(4,128)S(1)} %slice.90, ...), kind=kLoop, calls=%fused_computation.58 | loop fusion | flops 1441792 | bytes 2102016 | tf_op jit(solution)/shard_map/mul | solution.py:143
  8.1 2.2 while.32
  11.2 4.3 %fusion.44 = (bf16[1,32,4,1024]{3,2,1,0:T(4,128)(2,1)S(1)}, bf16[1,32,4,1024]{3,2,1,0:T(4,128)(2,1)S(1)}) fusion(f32[32,4,1024]{2,1,0:T(4,128)S(1)} %get-tuple-element.191, f32[32,4,1024]{2,1,0:T(4,128)S(1)} %get-tuple-element.190, f32[32,4,1024]{2,1,0:T(4,128)S(1)} %negate_exponential_fusion, f32[32,4,1024]{2,1,0:T(4,128)S(1)} %fusion.24), kind=kLoop, calls=%fused_computation.91 | loop fusion | flops 1835008 | bytes 2621440 | tf_op jit(solution)/shard_map/stack | solution.py:172
  17.7 3.6 %subtract_convert_fusion = bf16[1024,32,64]{0,2,1:T(8,128)(2,1)} fusion(f32[1024,64]{0,1:T(8,128)S(1)} %get-tuple-element.285, f32[1024,32]{0,1:T(8,128)S(1)} %get-tuple-element.279, f32[1024,64]{0,1:T(8,128)S(1)} %get-tuple-element.284, f32[1024,32]{0,1:T(8,128)S(1)} %get-tuple-element.278), kind=kLoop, calls=%fused_computation.24 | loop fusion | flops 8388608 | bytes 4980736 | tf_op jit(solution)/shard_map/convert_element_type | solution.py:187
  21.4 4.4 %convolution_convert_fusion = bf16[256,2048]{1,0:T(8,128)(2,1)} fusion(bf16[256,1024]{1,0:T(8,128)(2,1)S(1)} %bitcast.109, bf16[1024,2048]{0,1:T(8,128)(2,1)} %bitcast.107), kind=kOutput, calls=%fused_computation.47 | convolution fusion | flops 1074266112 | bytes 5767168 | tf_op jit(solution)/shard_map/dot_general | solution.py:275
  25.8 16.1 %while.31 = (s32[]{:T(128)}, bf16[2,2,4,4096]{3,2,1,0:T(4,128)(2,1)S(1)}, s32[2,4096]{1,0:T(2,128)S(1)}, bf16[256,2048]{1,0:T(8,128)(2,1)}, s32[2,4096]{1,0:T(2,128)S(1)}, /*index=5*/s32[]{:T(128)}) while((s32[]{:T(128)}, bf16[2,2,4,4096]{3,2,1,0:T(4,128)(2,1)S(1)}, s32[2,4096]{1,0:T(2,128)S(1)}, bf16[256,2048]{1,0:T(8,128)(2,1)}, ...), condition=%wide.region_9.10_spmd, body=%wide.region_7.9_spmd.sunk | while | flops 4305682432 | bytes 2392141 | solution.py:298
  25.9 8.0 %multiply_reduce_fusion.2 = bf16[2,4,4096]{2,1,0:T(4,128)(2,1)S(1)} fusion(f32[32,4096]{1,0:T(8,128)S(1)} %fusion.92, bf16[256,2048]{1,0:T(8,128)(2,1)} %get-tuple-element.432, s32[4096]{0:T(1024)S(1)} %bitcast.110), kind=kOutput, calls=%fused_computation.3.clone.1 | convolution fusion | flops 4305420288 | bytes 1654784 | tf_op jit(solution)/shard_map/while/body/eval_jaxpr/dot_general | solution.py:290
  34.0 7.8 %multiply_reduce_fusion.2 = bf16[2,4,4096]{2,1,0:T(4,128)(2,1)S(1)} fusion(f32[32,4096]{1,0:T(8,128)S(1)} %fusion.92, bf16[256,2048]{1,0:T(8,128)(2,1)} %get-tuple-element.432, s32[4096]{0:T(1024)S(1)} %bitcast.110), kind=kOutput, calls=%fused_computation.3.clone.1 | convolution fusion | flops 4305420288 | bytes 1654784 | tf_op jit(solution)/shard_map/while/body/eval_jaxpr/dot_general | solution.py:290
  42.9 6.1 %all-to-all-start = ((bf16[2,4,32,256]{3,1,0,2:T(4,128)(2,1)}), bf16[2,4,32,256]{3,1,0,2:T(4,128)(2,1)}, u32[]{:S(2)}, u32[]{:S(2)}) async-start(bf16[2,4,32,256]{3,1,0,2:T(4,128)(2,1)} %copy.27), calls=%async_computation | async-start | bytes 262144 | tf_op jit(solution)/shard_map/all_to_all | solution.py:305
  49.0 3.4 %collective-permute-start = (f32[3,2,32,256]{3,2,1,0:T(8,128)S(1)}, f32[3,2,32,256]{3,2,1,0:T(8,128)S(1)}, u32[]{:S(2)}, u32[]{:S(2)}) collective-permute-start(f32[3,2,32,256]{3,2,1,0:T(8,128)S(1)} %get-tuple-element.272), channel_id=1, source_target_pairs={{0,4},{4,8},{8,12},{12,16},{16,20},{20,24},{24,28},{1,5},{5,9},{9,... | collective-permute-start | bytes 589832 | tf_op jit(solution)/shard_map/ppermute | solution.py:27
  52.4 3.4 %collective-permute-start.1 = (f32[3,2,32,256]{3,2,1,0:T(8,128)S(1)}, f32[3,2,32,256]{3,2,1,0:T(8,128)S(1)}, u32[]{:S(2)}, u32[]{:S(2)}) collective-permute-start(f32[3,2,32,256]{3,2,1,0:T(8,128)S(1)} %get-tuple-element.271), channel_id=1, source_target_pairs={{4,0},{8,4},{12,8},{16,12},{20,16},{24,20},{28,24},{5,1},{9,5},{13... | collective-permute-start | bytes 589832 | tf_op jit(solution)/shard_map/ppermute | solution.py:30
  57.1 4.0 %collective-permute-done = f32[3,2,32,256]{3,2,1,0:T(8,128)S(1)} collective-permute-done((f32[3,2,32,256]{3,2,1,0:T(8,128)S(1)}, f32[3,2,32,256]{3,2,1,0:T(8,128)S(1)}, u32[]{:S(2)}, u32[]{:S(2)}) %collective-permute-start) | collective-permute-done | bytes 196640 | tf_op jit(solution)/shard_map/ppermute | solution.py:27
  63.1 1.7 copy-done.4
  65.7 2.3 %collective-permute-start.2 = (f32[3,36,2,256]{3,2,1,0:T(2,128)}, f32[3,36,2,256]{3,2,1,0:T(2,128)}, u32[]{:S(2)}, u32[]{:S(2)}) collective-permute-start(f32[3,36,2,256]{3,2,1,0:T(2,128)} %get-tuple-element.263), channel_id=1, source_target_pairs={{0,1},{1,2},{2,3},{4,5},{5,6},{6,7},{8,9},{9,10},{10,11},{12,13},{... | collective-permute-start | bytes 663560 | tf_op jit(solution)/shard_map/ppermute | solution.py:27
  68.0 3.5 %collective-permute-start.3 = (f32[3,36,2,256]{3,2,1,0:T(2,128)}, f32[3,36,2,256]{3,2,1,0:T(2,128)}, u32[]{:S(2)}, u32[]{:S(2)}) collective-permute-start(f32[3,36,2,256]{3,2,1,0:T(2,128)} %get-tuple-element.264), channel_id=1, source_target_pairs={{1,0},{2,1},{3,2},{5,4},{6,5},{7,6},{9,8},{10,9},{11,10},{13,12},{... | collective-permute-start | bytes 663560 | tf_op jit(solution)/shard_map/ppermute | solution.py:30
  71.6 1.6 copy.28
  73.2 1.6 reshape.400
  76.4 3.2 %fusion.11 = f32[3072,256]{1,0:T(8,128)} fusion(s32[256]{0:T(256)S(1)} %get-tuple-element.287, f32[256]{0:T(256)S(1)} %bitcast.115, s32[256]{0:T(256)S(1)} %get-tuple-element.286), kind=kOutput, calls=%fused_computation.46 | convolution fusion | flops 2416836608 | bytes 3148800 | tf_op jit(solution)/shard_map/dot_general | solution.py:328
  79.6 3.7 %select_maximum_fusion.12.up_ref = f32[3,36,48,256]{3,2,1,0:T(8,128)} fusion(f32[3,36,2,256]{3,2,1,0:T(2,128)} %collective-permute-done.3, f32[3,36,32,256]{3,2,1,0:T(8,128)S(1)} %copy-done.5, f32[3,36,2,256]{3,2,1,0:T(2,128)} %collective-permute-done.2), kind=kLoop, calls=%fused_computation.39 | loop fusion | flops 10616832 | bytes 9289728 | tf_op jit(solution)/shard_map/concatenate | solution.py:31
  83.3 14.3 %shard_map.122.prev_ref = f32[3,32,32,256]{3,2,1,0:T(8,128)} custom-call(f32[3,36,48,256]{3,2,1,0:T(8,128)} %select_maximum_fusion.12.up_ref, f32[3,32,32,256]{3,2,1,0:T(8,128)} %prev_ref.2, f32[2,32,32,256]{3,2,1,0:T(8,128)} %mod_ref.7, f32[3,32,32,256]{3,2,1,0:T(8,128)} %bitcast.106), custom_call_target="tpu_custom_call" | custom-call | tf_op jit(solution)/shard_map/pallas_call | solution.py:112
  98.8 2.9 %collective-permute-start.4 = (f32[3,2,32,256]{3,2,1,0:T(8,128)S(1)}, f32[3,2,32,256]{3,2,1,0:T(8,128)S(1)}, u32[]{:S(2)}, u32[]{:S(2)}) collective-permute-start(f32[3,2,32,256]{3,2,1,0:T(8,128)S(1)} %get-tuple-element.269), channel_id=1, source_target_pairs={{0,4},{4,8},{8,12},{12,16},{16,20},{20,24},{24,28},{1,5},{5,9},{9,... | collective-permute-start | bytes 589832 | tf_op jit(solution)/shard_map/ppermute | solution.py:27
  101.7 3.9 %collective-permute-start.5 = (f32[3,2,32,256]{3,2,1,0:T(8,128)S(1)}, f32[3,2,32,256]{3,2,1,0:T(8,128)S(1)}, u32[]{:S(2)}, u32[]{:S(2)}) collective-permute-start(f32[3,2,32,256]{3,2,1,0:T(8,128)S(1)} %get-tuple-element.270), channel_id=1, source_target_pairs={{4,0},{8,4},{12,8},{16,12},{20,16},{24,20},{28,24},{5,1},{9,5},{13... | collective-permute-start | bytes 589832 | tf_op jit(solution)/shard_map/ppermute | solution.py:30
  105.6 2.5 %collective-permute-done.4 = f32[3,2,32,256]{3,2,1,0:T(8,128)S(1)} collective-permute-done((f32[3,2,32,256]{3,2,1,0:T(8,128)S(1)}, f32[3,2,32,256]{3,2,1,0:T(8,128)S(1)}, u32[]{:S(2)}, u32[]{:S(2)}) %collective-permute-start.4) | collective-permute-done | bytes 196640 | tf_op jit(solution)/shard_map/ppermute | solution.py:27
  108.1 4.1 %collective-permute-done.5 = f32[3,2,32,256]{3,2,1,0:T(8,128)S(1)} collective-permute-done((f32[3,2,32,256]{3,2,1,0:T(8,128)S(1)}, f32[3,2,32,256]{3,2,1,0:T(8,128)S(1)}, u32[]{:S(2)}, u32[]{:S(2)}) %collective-permute-start.5) | collective-permute-done | bytes 196640 | tf_op jit(solution)/shard_map/ppermute | solution.py:30
  112.2 1.5 pad_maximum_fusion.9
  113.8 1.9 collective-permute-start.6
  115.7 3.6 %collective-permute-start.7 = (f32[3,36,2,256]{3,2,1,0:T(2,128)S(1)}, f32[3,36,2,256]{3,2,1,0:T(2,128)S(1)}, u32[]{:S(2)}, u32[]{:S(2)}) collective-permute-start(f32[3,36,2,256]{3,2,1,0:T(2,128)S(1)} %get-tuple-element.262), channel_id=1, source_target_pairs={{1,0},{2,1},{3,2},{5,4},{6,5},{7,6},{9,8},{10,9},{11,10},{13,12},{... | collective-permute-start | bytes 663560 | tf_op jit(solution)/shard_map/ppermute | solution.py:30
  119.4 3.2 %fusion.10 = f32[3072,256]{1,0:T(8,128)} fusion(s32[256]{0:T(256)S(1)} %get-tuple-element.287, f32[256]{0:T(256)S(1)} %bitcast.114, s32[256]{0:T(256)S(1)} %get-tuple-element.286), kind=kOutput, calls=%fused_computation.45 | convolution fusion | flops 2416836608 | bytes 3148800 | tf_op jit(solution)/shard_map/dot_general | solution.py:328
  122.8 2.7 %select_maximum_fusion.8.up_ref = f32[3,36,48,256]{3,2,1,0:T(8,128)} fusion(f32[3,36,2,256]{3,2,1,0:T(2,128)S(1)} %collective-permute-done.7, f32[3,36,2,256]{3,2,1,0:T(2,128)S(1)} %collective-permute-done.6, f32[3,2,32,256]{3,2,1,0:T(8,128)S(1)} %collective-permute-done.5, f32[3,32,32,256]{3,2,1,0:T(8,128)S(1)} %copy-done.1, ...), kind=kLoop, calls=%fused_computation.35 | loop fusion | flops 15925248 | bytes 9289728 | tf_op jit(solution)/shard_map/concatenate | solution.py:31
  125.5 14.3 %shard_map.123.prev_ref = f32[3,32,32,256]{3,2,1,0:T(8,128)} custom-call(f32[3,36,48,256]{3,2,1,0:T(8,128)} %select_maximum_fusion.8.up_ref, f32[3,32,32,256]{3,2,1,0:T(8,128)} %prev_ref.3, f32[2,32,32,256]{3,2,1,0:T(8,128)} %mod_ref.7, f32[3,32,32,256]{3,2,1,0:T(8,128)} %bitcast.105), custom_call_target="tpu_custom_call" | custom-call | tf_op jit(solution)/shard_map/pallas_call | solution.py:112
  141.0 2.1 collective-permute-start.8
  143.1 4.7 %collective-permute-start.9 = (f32[3,2,32,256]{3,2,1,0:T(8,128)S(1)}, f32[3,2,32,256]{3,2,1,0:T(8,128)S(1)}, u32[]{:S(2)}, u32[]{:S(2)}) collective-permute-start(f32[3,2,32,256]{3,2,1,0:T(8,128)S(1)} %get-tuple-element.268), channel_id=1, source_target_pairs={{4,0},{8,4},{12,8},{16,12},{20,16},{24,20},{28,24},{5,1},{9,5},{13... | collective-permute-start | bytes 589832 | tf_op jit(solution)/shard_map/ppermute | solution.py:30
  147.8 1.7 collective-permute-done.8
  149.5 4.0 %collective-permute-done.9 = f32[3,2,32,256]{3,2,1,0:T(8,128)S(1)} collective-permute-done((f32[3,2,32,256]{3,2,1,0:T(8,128)S(1)}, f32[3,2,32,256]{3,2,1,0:T(8,128)S(1)}, u32[]{:S(2)}, u32[]{:S(2)}) %collective-permute-start.9) | collective-permute-done | bytes 196640 | tf_op jit(solution)/shard_map/ppermute | solution.py:30
  155.0 1.9 collective-permute-start.10
  156.9 3.6 %collective-permute-start.11 = (f32[3,36,2,256]{3,2,1,0:T(2,128)S(1)}, f32[3,36,2,256]{3,2,1,0:T(2,128)S(1)}, u32[]{:S(2)}, u32[]{:S(2)}) collective-permute-start(f32[3,36,2,256]{3,2,1,0:T(2,128)S(1)} %get-tuple-element.260), channel_id=1, source_target_pairs={{1,0},{2,1},{3,2},{5,4},{6,5},{7,6},{9,8},{10,9},{11,10},{13,12},{... | collective-permute-start | bytes 663560 | tf_op jit(solution)/shard_map/ppermute | solution.py:30
  160.6 3.2 %fusion.9 = f32[3072,256]{1,0:T(8,128)} fusion(s32[256]{0:T(256)S(1)} %get-tuple-element.287, f32[256]{0:T(256)S(1)} %bitcast.113, s32[256]{0:T(256)S(1)} %get-tuple-element.286), kind=kOutput, calls=%fused_computation.44 | convolution fusion | flops 2416836608 | bytes 3148800 | tf_op jit(solution)/shard_map/dot_general | solution.py:328
  164.0 2.7 %select_maximum_fusion.4.up_ref = f32[3,36,48,256]{3,2,1,0:T(8,128)} fusion(f32[3,36,2,256]{3,2,1,0:T(2,128)S(1)} %collective-permute-done.11, f32[3,36,2,256]{3,2,1,0:T(2,128)S(1)} %collective-permute-done.10, f32[3,2,32,256]{3,2,1,0:T(8,128)S(1)} %collective-permute-done.9, f32[3,32,32,256]{3,2,1,0:T(8,128)S(1)} %copy-done, ...), kind=kLoop, calls=%fused_computation.31 | loop fusion | flops 15925248 | bytes 9289728 | tf_op jit(solution)/shard_map/concatenate | solution.py:31
  166.7 14.3 %shard_map.124 = f32[3,32,32,256]{3,2,1,0:T(8,128)} custom-call(f32[3,36,48,256]{3,2,1,0:T(8,128)} %select_maximum_fusion.4.up_ref, f32[3,32,32,256]{3,2,1,0:T(8,128)} %shard_map.122.prev_ref, f32[2,32,32,256]{3,2,1,0:T(8,128)} %mod_ref.7, f32[3,32,32,256]{3,2,1,0:T(8,128)} %bitcast.104), custom_call_target="tpu_custom_call" | custom-call | tf_op jit(solution)/shard_map/pallas_call | solution.py:112
  182.3 2.6 %collective-permute-start.12 = (f32[3,2,32,256]{3,2,1,0:T(8,128)S(1)}, f32[3,2,32,256]{3,2,1,0:T(8,128)S(1)}, u32[]{:S(2)}, u32[]{:S(2)}) collective-permute-start(f32[3,2,32,256]{3,2,1,0:T(8,128)S(1)} %get-tuple-element.265), channel_id=1, source_target_pairs={{0,4},{4,8},{8,12},{12,16},{16,20},{20,24},{24,28},{1,5},{5,9},{9,... | collective-permute-start | bytes 589832 | tf_op jit(solution)/shard_map/ppermute | solution.py:27
  184.8 4.2 %collective-permute-start.13 = (f32[3,2,32,256]{3,2,1,0:T(8,128)S(1)}, f32[3,2,32,256]{3,2,1,0:T(8,128)S(1)}, u32[]{:S(2)}, u32[]{:S(2)}) collective-permute-start(f32[3,2,32,256]{3,2,1,0:T(8,128)S(1)} %get-tuple-element.266), channel_id=1, source_target_pairs={{4,0},{8,4},{12,8},{16,12},{20,16},{24,20},{28,24},{5,1},{9,5},{13... | collective-permute-start | bytes 589832 | tf_op jit(solution)/shard_map/ppermute | solution.py:30
  189.0 1.7 collective-permute-done.12
  190.7 4.0 %collective-permute-done.13 = f32[3,2,32,256]{3,2,1,0:T(8,128)S(1)} collective-permute-done((f32[3,2,32,256]{3,2,1,0:T(8,128)S(1)}, f32[3,2,32,256]{3,2,1,0:T(8,128)S(1)}, u32[]{:S(2)}, u32[]{:S(2)}) %collective-permute-start.13) | collective-permute-done | bytes 196640 | tf_op jit(solution)/shard_map/ppermute | solution.py:30
  196.2 1.9 collective-permute-start.14
  198.2 3.6 %collective-permute-start.15 = (f32[3,36,2,256]{3,2,1,0:T(2,128)S(1)}, f32[3,36,2,256]{3,2,1,0:T(2,128)S(1)}, u32[]{:S(2)}, u32[]{:S(2)}) collective-permute-start(f32[3,36,2,256]{3,2,1,0:T(2,128)S(1)} %get-tuple-element.258), channel_id=1, source_target_pairs={{1,0},{2,1},{3,2},{5,4},{6,5},{7,6},{9,8},{10,9},{11,10},{13,12},{... | collective-permute-start | bytes 663560 | tf_op jit(solution)/shard_map/ppermute | solution.py:30
  201.8 3.3 %fusion.8 = f32[3072,256]{1,0:T(8,128)} fusion(s32[256]{0:T(256)S(1)} %get-tuple-element.287, f32[256]{0:T(256)S(1)} %bitcast.112, s32[256]{0:T(256)S(1)} %get-tuple-element.286), kind=kOutput, calls=%fused_computation.43 | convolution fusion | flops 2416836608 | bytes 3148800 | tf_op jit(solution)/shard_map/dot_general | solution.py:328
  205.2 2.7 %select_maximum_fusion.up_ref = f32[3,36,48,256]{3,2,1,0:T(8,128)} fusion(f32[3,36,2,256]{3,2,1,0:T(2,128)S(1)} %collective-permute-done.15, f32[3,36,2,256]{3,2,1,0:T(2,128)S(1)} %collective-permute-done.14, f32[3,2,32,256]{3,2,1,0:T(8,128)S(1)} %collective-permute-done.13, f32[3,32,32,256]{3,2,1,0:T(8,128)S(1)} %copy-done.2, ...), kind=kLoop, calls=%fused_computation.27 | loop fusion | flops 15925248 | bytes 9289728 | tf_op jit(solution)/shard_map/concatenate | solution.py:31
  207.9 14.3 %shard_map.125 = f32[3,32,32,256]{3,2,1,0:T(8,128)} custom-call(f32[3,36,48,256]{3,2,1,0:T(8,128)} %select_maximum_fusion.up_ref, f32[3,32,32,256]{3,2,1,0:T(8,128)} %shard_map.123.prev_ref, f32[2,32,32,256]{3,2,1,0:T(8,128)} %mod_ref.7, f32[3,32,32,256]{3,2,1,0:T(8,128)} %bitcast.103), custom_call_target="tpu_custom_call" | custom-call | tf_op jit(solution)/shard_map/pallas_call | solution.py:112
  (111 shorter events, 20.9 us)
Async XLA Ops:
  11.2 10.1 %copy-start.6 = (s32[8192]{0:T(1024)S(1)}, s32[8192]{0:T(1024)}, u32[]{:S(2)}) copy-start(s32[8192]{0:T(1024)} %param.19) | copy-start | bytes 98308
  11.2 10.1 %copy-start.7 = (s32[8192]{0:T(1024)S(1)}, s32[8192]{0:T(1024)}, u32[]{:S(2)}) copy-start(s32[8192]{0:T(1024)} %param.20) | copy-start | bytes 98308
  25.8 23.1 %copy-start.3 = (f32[3,32,32,256]{3,2,1,0:T(8,128)S(1)}, f32[3,32,32,256]{3,2,1,0:T(8,128)}, u32[]{:S(2)}) copy-start(f32[3,32,32,256]{3,2,1,0:T(8,128)} %prev_ref.3) | copy-start | bytes 9437188
  25.8 31.3 %copy-start.9 = (s32[256]{0:T(256)S(1)}, s32[256]{0:T(256)}, u32[]{:S(2)}) copy-start(s32[256]{0:T(256)} %param.21) | copy-start | bytes 3076
  42.9 28.7 %all-to-all-start = ((bf16[2,4,32,256]{3,1,0,2:T(4,128)(2,1)}), bf16[2,4,32,256]{3,1,0,2:T(4,128)(2,1)}, u32[]{:S(2)}, u32[]{:S(2)}) async-start(bf16[2,4,32,256]{3,1,0,2:T(4,128)(2,1)} %copy.27), calls=%async_computation | async-start | bytes 262144 | tf_op jit(solution)/shard_map/all_to_all | solution.py:305
  49.0 12.2 %collective-permute-start = (f32[3,2,32,256]{3,2,1,0:T(8,128)S(1)}, f32[3,2,32,256]{3,2,1,0:T(8,128)S(1)}, u32[]{:S(2)}, u32[]{:S(2)}) collective-permute-start(f32[3,2,32,256]{3,2,1,0:T(8,128)S(1)} %get-tuple-element.272), channel_id=1, source_target_pairs={{0,4},{4,8},{8,12},{12,16},{16,20},{20,24},{24,28},{1,5},{5,9},{9,... | collective-permute-start | bytes 589832 | tf_op jit(solution)/shard_map/ppermute | solution.py:27
  52.4 10.7 %collective-permute-start.1 = (f32[3,2,32,256]{3,2,1,0:T(8,128)S(1)}, f32[3,2,32,256]{3,2,1,0:T(8,128)S(1)}, u32[]{:S(2)}, u32[]{:S(2)}) collective-permute-start(f32[3,2,32,256]{3,2,1,0:T(8,128)S(1)} %get-tuple-element.271), channel_id=1, source_target_pairs={{4,0},{8,4},{12,8},{16,12},{20,16},{24,20},{28,24},{5,1},{9,5},{13... | collective-permute-start | bytes 589832 | tf_op jit(solution)/shard_map/ppermute | solution.py:30
  63.1 1.8 copy-start.4
  65.7 13.9 %copy-start.5 = (f32[3,36,32,256]{3,2,1,0:T(8,128)S(1)}, f32[3,36,32,256]{3,2,1,0:T(8,128)}, u32[]{:S(2)}) copy-start(f32[3,36,32,256]{3,2,1,0:T(8,128)} %copy-done.4) | copy-start | bytes 10616836
  65.7 13.9 %collective-permute-start.2 = (f32[3,36,2,256]{3,2,1,0:T(2,128)}, f32[3,36,2,256]{3,2,1,0:T(2,128)}, u32[]{:S(2)}, u32[]{:S(2)}) collective-permute-start(f32[3,36,2,256]{3,2,1,0:T(2,128)} %get-tuple-element.263), channel_id=1, source_target_pairs={{0,1},{1,2},{2,3},{4,5},{5,6},{6,7},{8,9},{9,10},{10,11},{12,13},{... | collective-permute-start | bytes 663560 | tf_op jit(solution)/shard_map/ppermute | solution.py:27
  68.0 11.6 %collective-permute-start.3 = (f32[3,36,2,256]{3,2,1,0:T(2,128)}, f32[3,36,2,256]{3,2,1,0:T(2,128)}, u32[]{:S(2)}, u32[]{:S(2)}) collective-permute-start(f32[3,36,2,256]{3,2,1,0:T(2,128)} %get-tuple-element.264), channel_id=1, source_target_pairs={{1,0},{2,1},{3,2},{5,4},{6,5},{7,6},{9,8},{10,9},{11,10},{13,12},{... | collective-permute-start | bytes 663560 | tf_op jit(solution)/shard_map/ppermute | solution.py:30
  83.3 36.1 %copy-start.8 = (f32[1,256]{1,0:T(1,128)S(1)}, f32[1,256]{1,0:T(1,128)}, u32[]{:S(2)}) copy-start(f32[1,256]{1,0:T(1,128)} %get-tuple-element.282) | copy-start | bytes 3076
  97.6 25.1 %copy-start.1 = (f32[3,32,32,256]{3,2,1,0:T(8,128)S(1)}, f32[3,32,32,256]{3,2,1,0:T(8,128)}, u32[]{:S(2)}) copy-start(f32[3,32,32,256]{3,2,1,0:T(8,128)} %shard_map.122.prev_ref) | copy-start | bytes 9437188
  98.8 9.3 %collective-permute-start.4 = (f32[3,2,32,256]{3,2,1,0:T(8,128)S(1)}, f32[3,2,32,256]{3,2,1,0:T(8,128)S(1)}, u32[]{:S(2)}, u32[]{:S(2)}) collective-permute-start(f32[3,2,32,256]{3,2,1,0:T(8,128)S(1)} %get-tuple-element.269), channel_id=1, source_target_pairs={{0,4},{4,8},{8,12},{12,16},{16,20},{20,24},{24,28},{1,5},{5,9},{9,... | collective-permute-start | bytes 589832 | tf_op jit(solution)/shard_map/ppermute | solution.py:27
  101.7 10.5 %collective-permute-start.5 = (f32[3,2,32,256]{3,2,1,0:T(8,128)S(1)}, f32[3,2,32,256]{3,2,1,0:T(8,128)S(1)}, u32[]{:S(2)}, u32[]{:S(2)}) collective-permute-start(f32[3,2,32,256]{3,2,1,0:T(8,128)S(1)} %get-tuple-element.270), channel_id=1, source_target_pairs={{4,0},{8,4},{12,8},{16,12},{20,16},{24,20},{28,24},{5,1},{9,5},{13... | collective-permute-start | bytes 589832 | tf_op jit(solution)/shard_map/ppermute | solution.py:30
  113.8 8.8 %collective-permute-start.6 = (f32[3,36,2,256]{3,2,1,0:T(2,128)S(1)}, f32[3,36,2,256]{3,2,1,0:T(2,128)S(1)}, u32[]{:S(2)}, u32[]{:S(2)}) collective-permute-start(f32[3,36,2,256]{3,2,1,0:T(2,128)S(1)} %get-tuple-element.261), channel_id=1, source_target_pairs={{0,1},{1,2},{2,3},{4,5},{5,6},{6,7},{8,9},{9,10},{10,11},{12,13},{... | collective-permute-start | bytes 663560 | tf_op jit(solution)/shard_map/ppermute | solution.py:27
  115.7 7.1 %collective-permute-start.7 = (f32[3,36,2,256]{3,2,1,0:T(2,128)S(1)}, f32[3,36,2,256]{3,2,1,0:T(2,128)S(1)}, u32[]{:S(2)}, u32[]{:S(2)}) collective-permute-start(f32[3,36,2,256]{3,2,1,0:T(2,128)S(1)} %get-tuple-element.262), channel_id=1, source_target_pairs={{1,0},{2,1},{3,2},{5,4},{6,5},{7,6},{9,8},{10,9},{11,10},{13,12},{... | collective-permute-start | bytes 663560 | tf_op jit(solution)/shard_map/ppermute | solution.py:30
  139.8 24.2 %copy-start = (f32[3,32,32,256]{3,2,1,0:T(8,128)S(1)}, f32[3,32,32,256]{3,2,1,0:T(8,128)}, u32[]{:S(2)}) copy-start(f32[3,32,32,256]{3,2,1,0:T(8,128)} %shard_map.123.prev_ref) | copy-start | bytes 9437188
  141.0 8.5 %collective-permute-start.8 = (f32[3,2,32,256]{3,2,1,0:T(8,128)S(1)}, f32[3,2,32,256]{3,2,1,0:T(8,128)S(1)}, u32[]{:S(2)}, u32[]{:S(2)}) collective-permute-start(f32[3,2,32,256]{3,2,1,0:T(8,128)S(1)} %get-tuple-element.267), channel_id=1, source_target_pairs={{0,4},{4,8},{8,12},{12,16},{16,20},{20,24},{24,28},{1,5},{5,9},{9,... | collective-permute-start | bytes 589832 | tf_op jit(solution)/shard_map/ppermute | solution.py:27
  143.1 10.4 %collective-permute-start.9 = (f32[3,2,32,256]{3,2,1,0:T(8,128)S(1)}, f32[3,2,32,256]{3,2,1,0:T(8,128)S(1)}, u32[]{:S(2)}, u32[]{:S(2)}) collective-permute-start(f32[3,2,32,256]{3,2,1,0:T(8,128)S(1)} %get-tuple-element.268), channel_id=1, source_target_pairs={{4,0},{8,4},{12,8},{16,12},{20,16},{24,20},{28,24},{5,1},{9,5},{13... | collective-permute-start | bytes 589832 | tf_op jit(solution)/shard_map/ppermute | solution.py:30
  155.0 8.8 %collective-permute-start.10 = (f32[3,36,2,256]{3,2,1,0:T(2,128)S(1)}, f32[3,36,2,256]{3,2,1,0:T(2,128)S(1)}, u32[]{:S(2)}, u32[]{:S(2)}) collective-permute-start(f32[3,36,2,256]{3,2,1,0:T(2,128)S(1)} %get-tuple-element.259), channel_id=1, source_target_pairs={{0,1},{1,2},{2,3},{4,5},{5,6},{6,7},{8,9},{9,10},{10,11},{12,13},{... | collective-permute-start | bytes 663560 | tf_op jit(solution)/shard_map/ppermute | solution.py:27
  156.9 7.1 %collective-permute-start.11 = (f32[3,36,2,256]{3,2,1,0:T(2,128)S(1)}, f32[3,36,2,256]{3,2,1,0:T(2,128)S(1)}, u32[]{:S(2)}, u32[]{:S(2)}) collective-permute-start(f32[3,36,2,256]{3,2,1,0:T(2,128)S(1)} %get-tuple-element.260), channel_id=1, source_target_pairs={{1,0},{2,1},{3,2},{5,4},{6,5},{7,6},{9,8},{10,9},{11,10},{13,12},{... | collective-permute-start | bytes 663560 | tf_op jit(solution)/shard_map/ppermute | solution.py:30
  181.1 24.2 %copy-start.2 = (f32[3,32,32,256]{3,2,1,0:T(8,128)S(1)}, f32[3,32,32,256]{3,2,1,0:T(8,128)}, u32[]{:S(2)}) copy-start(f32[3,32,32,256]{3,2,1,0:T(8,128)} %shard_map.124) | copy-start | bytes 9437188
  182.3 8.5 %collective-permute-start.12 = (f32[3,2,32,256]{3,2,1,0:T(8,128)S(1)}, f32[3,2,32,256]{3,2,1,0:T(8,128)S(1)}, u32[]{:S(2)}, u32[]{:S(2)}) collective-permute-start(f32[3,2,32,256]{3,2,1,0:T(8,128)S(1)} %get-tuple-element.265), channel_id=1, source_target_pairs={{0,4},{4,8},{8,12},{12,16},{16,20},{20,24},{24,28},{1,5},{5,9},{9,... | collective-permute-start | bytes 589832 | tf_op jit(solution)/shard_map/ppermute | solution.py:27
  184.8 9.8 %collective-permute-start.13 = (f32[3,2,32,256]{3,2,1,0:T(8,128)S(1)}, f32[3,2,32,256]{3,2,1,0:T(8,128)S(1)}, u32[]{:S(2)}, u32[]{:S(2)}) collective-permute-start(f32[3,2,32,256]{3,2,1,0:T(8,128)S(1)} %get-tuple-element.266), channel_id=1, source_target_pairs={{4,0},{8,4},{12,8},{16,12},{20,16},{24,20},{28,24},{5,1},{9,5},{13... | collective-permute-start | bytes 589832 | tf_op jit(solution)/shard_map/ppermute | solution.py:30
  196.2 8.8 %collective-permute-start.14 = (f32[3,36,2,256]{3,2,1,0:T(2,128)S(1)}, f32[3,36,2,256]{3,2,1,0:T(2,128)S(1)}, u32[]{:S(2)}, u32[]{:S(2)}) collective-permute-start(f32[3,36,2,256]{3,2,1,0:T(2,128)S(1)} %get-tuple-element.257), channel_id=1, source_target_pairs={{0,1},{1,2},{2,3},{4,5},{5,6},{6,7},{8,9},{9,10},{10,11},{12,13},{... | collective-permute-start | bytes 663560 | tf_op jit(solution)/shard_map/ppermute | solution.py:27
  198.2 7.1 %collective-permute-start.15 = (f32[3,36,2,256]{3,2,1,0:T(2,128)S(1)}, f32[3,36,2,256]{3,2,1,0:T(2,128)S(1)}, u32[]{:S(2)}, u32[]{:S(2)}) collective-permute-start(f32[3,36,2,256]{3,2,1,0:T(2,128)S(1)} %get-tuple-element.258), channel_id=1, source_target_pairs={{1,0},{2,1},{3,2},{5,4},{6,5},{7,6},{9,8},{10,9},{11,10},{13,12},{... | collective-permute-start | bytes 663560 | tf_op jit(solution)/shard_map/ppermute | solution.py:30

commit v3 on v2

--- a/solution.py
+++ b/solution.py
@@ -35,8 +35,9 @@
 YPAD = 8
 
 
-def step_kernel(up_ref, prev_ref, mod_ref, src_ref, out_ref, *, bx):
-    i = pl.program_id(0)
+def step_kernel(up_ref, prev_ref, mod_ref, src_ref, *rest, bx, first, stride):
+    out_ref = rest[-1]
+    i = first + pl.program_id(0) * stride
     depth = out_ref.shape[3]
     lane = lax.broadcasted_iota(jnp.int32, (8, depth), 1)
     masks = {dz: (lane + dz >= 0) & (lane + dz < depth) for dz in (-2, -1, 1, 2)}
@@ -104,23 +105,57 @@
     lax.fori_loop(0, bx, plane, 0)
 
 
-def elastic_step(upad, prev, moduli, sources, bx=8):
+def elastic_part(upad, prev, moduli, sources, bx, first, stride, count, into=None):
     _, px, py, depth = upad.shape
     nx, ny = px - 4, py - 2 * YPAD
-    kernel = functools.partial(step_kernel, bx=bx)
-    block = lambda i: (0, i, 0, 0)
+    kernel = functools.partial(step_kernel, bx=bx, first=first, stride=stride)
+    block = lambda i: (0, first + i * stride, 0, 0)
+    in_specs = [
+        pl.BlockSpec((3, px, py, depth), lambda i: (0, 0, 0, 0)),
+        pl.BlockSpec((3, bx, ny, depth), block),
+        pl.BlockSpec((2, bx, ny, depth), block),
+        pl.BlockSpec((3, bx, ny, depth), block),
+    ]
+    operands = [upad, prev, moduli, sources]
+    aliases = {}
+    if into is not None:
+        in_specs.append(pl.BlockSpec(memory_space=pl.ANY))
+        operands.append(into)
+        aliases = {4: 0}
     return pl.pallas_call(
         kernel,
-        grid=(nx // bx,),
-        in_specs=[
-            pl.BlockSpec((3, px, py, depth), lambda i: (0, 0, 0, 0)),
-            pl.BlockSpec((3, bx, ny, depth), block),
-            pl.BlockSpec((2, bx, ny, depth), block),
-            pl.BlockSpec((3, bx, ny, depth), block),
-        ],
+        grid=(count,),
+        in_specs=in_specs,
         out_specs=pl.BlockSpec((3, bx, ny, depth), block),
         out_shape=jax.ShapeDtypeStruct((3, nx, ny, depth), jnp.float32),
-    )(upad, prev, moduli, sources)
+        input_output_aliases=aliases,
+    )(*operands)
+
+
+def elastic_step(upad, prev, moduli, sources, bx=4):
+    nx = upad.shape[1] - 4
+    blocks = nx // bx
+    edge = elastic_part(upad, prev, moduli, sources, bx, 0, blocks - 1, 2)
+    whole = elastic_part(upad, prev, moduli, sources, bx, 1, 1, blocks - 2, into=edge)
+    return edge, whole
+
+
+def exchange(edge, whole, width):
+    size_x = lax.axis_size("gx")
+    size_y = lax.axis_size("gy")
+    nx = whole.shape[1]
+    forward_x = [(i, i + 1) for i in range(size_x - 1)]
+    backward_x = [(t, s) for s, t in forward_x]
+    low = lax.ppermute(edge[:, nx - width:], "gx", forward_x)
+    high = lax.ppermute(edge[:, :width], "gx", backward_x)
+    block = jnp.concatenate([low, whole, high], axis=1)
+    ny = block.shape[2]
+    forward_y = [(i, i + 1) for i in range(size_y - 1)]
+    backward_y = [(t, s) for s, t in forward_y]
+    low = lax.ppermute(block[:, :, ny - width:], "gy", forward_y)
+    high = lax.ppermute(block[:, :, :width], "gy", backward_y)
+    pad = jnp.zeros(block.shape[:2] + (YPAD - width,) + block.shape[3:], block.dtype)
+    return jnp.concatenate([pad, low, block, high, pad], axis=2)
 
 
 def level_table(values, layer_of_level):
@@ -323,13 +358,13 @@
         jnp.float32
     )
     previous, current = (field_old, field_now)
+    edge = field_now
     for instant in range(STEPS):
         spread = weighted[instant][:, None] * depth_hot
         source = jnp.dot(column_hot, spread, precision=lax.Precision.HIGHEST)
         source = source.reshape(3, block_x, block_y, depth)
-        padded = padded_2(current, (("gx", 1), ("gy", 2)), 2)
-        padded = jnp.pad(padded, ((0, 0), (0, 0), (YPAD - 2, YPAD - 2), (0, 0)))
-        advanced = elastic_step(padded, previous, moduli, source)
+        padded = exchange(edge, current, 2)
+        edge, advanced = elastic_step(padded, previous, moduli, source)
         previous, current = (current, advanced)
     return (current, previous)
 

time: 225 us -> 264 us (1.17)
  local copies, waits for them, and re-layouts: 12.1 us -> 65.7 us
  waiting for transfers between devices: 24.1 us -> 6.57 us
  Pallas kernels: 57.3 us -> 70.6 us
  other arithmetic: 36.8 us -> 26.2 us
    concatenate x1 -> x5, local copies, waits for them, and re-layouts: 0.01 us -> 52.4 us  [the longest x4 52.4 us: exchange(): return jnp.concatenate([pad, low, block, high, pad], axis=2)]
    ppermute x16, waiting for transfers between devices: 24.1 us -> 6.57 us  [the longest x4 4.6 us: exchange(): low = lax.ppermute(edge[:, nx - width:], 'gx', forward_x)]
    pallas_call x4 -> x8, Pallas kernels: 57.3 us -> 70.6 us  [elastic_part(): pl.pallas_call(kernel, grid=(count,), in_specs=in_specs, out_specs=pl.Blo...]
    unnamed x22 -> x18, local copies, waits for them, and re-layouts: 2.15 us -> 7.58 us
    concatenate x4 -> x3, other arithmetic: 11.8 us -> 6.44 us  [exchange(): block = jnp.concatenate([low, whole, high], axis=1)]
    slice x3 -> x0, other arithmetic: 4.63 us -> none  [padded_2(): lax.slice_in_dim(block, block.shape[dim] - width, None, axis=dim)]
  transfers between devices with their start and end apart: 17 -> 17, of which waited for: 11 -> 4; matrix products, arithmetic and copies ran while one was open for 9% -> 5% of each run, Pallas kernels for 0% -> 13%
where the time goes in v3:
time: 264 us; the launch traced here: 260 us
  Pallas kernels  70.6 us (27%)
  local copies, waits for them, and re-layouts  65.7 us (25%)
  starting transfers between devices  55.4 us (21%)
  matrix products  33.2 us (13%)
  other arithmetic  26.2 us (10%)
  waiting for transfers between devices  6.57 us (2%)
    pallas_call x8, Pallas kernels, elastic_part(): pl.pallas_call(kernel, grid=(count,), in_specs=in_specs, out_specs=pl.Blo...  70.6 us
    concatenate x4, local copies, waits for them, and re-layouts, exchange(): return jnp.concatenate([pad, low, block, high, pad], axis=2)  52.4 us
    ppermute x4, starting transfers between devices, exchange(): high = lax.ppermute(edge[:, :width], 'gx', backward_x)  16.8 us
    dot_general x2, matrix products, select_block(): jnp.dot(table_rounded, offset_hot, preferred_element_type=jnp.float32)  15.8 us
    ppermute x4, starting transfers between devices, exchange(): high = lax.ppermute(block[:, :, :width], 'gy', backward_y)  14.7 us
    dot_general x4, matrix products, shards(): source = jnp.dot(column_hot, spread, precision=lax.Precision.HIGHEST)  12.8 us
    ppermute x4, starting transfers between devices, exchange(): low = lax.ppermute(edge[:, nx - width:], 'gx', forward_x)  10.1 us
    ppermute x4, starting transfers between devices, exchange(): low = lax.ppermute(block[:, :, ny - width:], 'gy', forward_y)  7.79 us
  transfers between devices with their start and end apart: 17, of which 4 were waited for; matrix products, arithmetic and copies ran while one was open for 5% of the time, Pallas kernels for 13%

profile of v3, /device:TPU:12, one launch (start us, length us, event | category | flops | bytes accessed | tf_op | source)
XLA Modules:
  0.0 260.0 jit_solution(13686975199282481745)
XLA Ops:
  2.9 4.9 %sine_multiply_fusion.1 = (f32[32,4,1024]{2,1,0:T(4,128)S(1)}, f32[32,4,1024]{2,1,0:T(4,128)S(1)}, f32[32,4,1024]{2,1,0:T(4,128)S(1)}) fusion(f32[32]{0:T(128)S(1)} %get-tuple-element.291, f32[32,4]{1,0:T(8,128)S(1)} %copy.28, f32[1024]{0:T(1024)S(1)} %multiply_multiply_fusion, f32[1,4,1024]{2,1,0:T(4,128)S(1)} %slice.91, f32[31,4,1024]{2,1,0:T(4,128)S(1)} %slice.90, ...), kind=kLoop, calls=%fused_computation.44 | loop fusion | flops 1441792 | bytes 2102016 | tf_op jit(solution)/shard_map/mul | solution.py:178
  8.1 2.2 while.32
  11.2 4.3 %fusion.43 = (bf16[1,32,4,1024]{3,2,1,0:T(4,128)(2,1)S(1)}, bf16[1,32,4,1024]{3,2,1,0:T(4,128)(2,1)S(1)}) fusion(f32[32,4,1024]{2,1,0:T(4,128)S(1)} %get-tuple-element.191, f32[32,4,1024]{2,1,0:T(4,128)S(1)} %get-tuple-element.190, f32[32,4,1024]{2,1,0:T(4,128)S(1)} %negate_exponential_fusion, f32[32,4,1024]{2,1,0:T(4,128)S(1)} %fusion.23), kind=kLoop, calls=%fused_computation.77 | loop fusion | flops 1835008 | bytes 2621440 | tf_op jit(solution)/shard_map/stack | solution.py:207
  17.7 3.6 %subtract_convert_fusion = bf16[1024,32,64]{0,2,1:T(8,128)(2,1)} fusion(f32[1024,64]{0,1:T(8,128)S(1)} %get-tuple-element.285, f32[1024,32]{0,1:T(8,128)S(1)} %get-tuple-element.279, f32[1024,64]{0,1:T(8,128)S(1)} %get-tuple-element.284, f32[1024,32]{0,1:T(8,128)S(1)} %get-tuple-element.278), kind=kLoop, calls=%fused_computation.24 | loop fusion | flops 8388608 | bytes 4980736 | tf_op jit(solution)/shard_map/convert_element_type | solution.py:222
  21.4 4.4 %convolution_convert_fusion = bf16[256,2048]{1,0:T(8,128)(2,1)} fusion(bf16[256,1024]{1,0:T(8,128)(2,1)S(1)} %bitcast.113, bf16[1024,2048]{0,1:T(8,128)(2,1)} %bitcast.111), kind=kOutput, calls=%fused_computation.33 | convolution fusion | flops 1074266112 | bytes 5767168 | tf_op jit(solution)/shard_map/dot_general | solution.py:310
  25.8 16.1 %while.31 = (s32[]{:T(128)}, bf16[2,2,4,4096]{3,2,1,0:T(4,128)(2,1)S(1)}, s32[2,4096]{1,0:T(2,128)S(1)}, bf16[256,2048]{1,0:T(8,128)(2,1)}, s32[2,4096]{1,0:T(2,128)S(1)}, /*index=5*/s32[]{:T(128)}) while((s32[]{:T(128)}, bf16[2,2,4,4096]{3,2,1,0:T(4,128)(2,1)S(1)}, s32[2,4096]{1,0:T(2,128)S(1)}, bf16[256,2048]{1,0:T(8,128)(2,1)}, ...), condition=%wide.region_9.10_spmd, body=%wide.region_7.9_spmd.sunk | while | flops 4305682432 | bytes 2392141 | solution.py:333
  25.9 8.0 %multiply_reduce_fusion.2 = bf16[2,4,4096]{2,1,0:T(4,128)(2,1)S(1)} fusion(f32[32,4096]{1,0:T(8,128)S(1)} %fusion.94, bf16[256,2048]{1,0:T(8,128)(2,1)} %get-tuple-element.432, s32[4096]{0:T(1024)S(1)} %bitcast.115), kind=kOutput, calls=%fused_computation.3.clone.1 | convolution fusion | flops 4305420288 | bytes 1654784 | tf_op jit(solution)/shard_map/while/body/eval_jaxpr/dot_general | solution.py:325
  34.0 7.8 %multiply_reduce_fusion.2 = bf16[2,4,4096]{2,1,0:T(4,128)(2,1)S(1)} fusion(f32[32,4096]{1,0:T(8,128)S(1)} %fusion.94, bf16[256,2048]{1,0:T(8,128)(2,1)} %get-tuple-element.432, s32[4096]{0:T(1024)S(1)} %bitcast.115), kind=kOutput, calls=%fused_computation.3.clone.1 | convolution fusion | flops 4305420288 | bytes 1654784 | tf_op jit(solution)/shard_map/while/body/eval_jaxpr/dot_general | solution.py:325
  42.9 6.0 %all-to-all-start = ((bf16[2,4,32,256]{3,1,0,2:T(4,128)(2,1)}), bf16[2,4,32,256]{3,1,0,2:T(4,128)(2,1)S(1)}, u32[]{:S(2)}, u32[]{:S(2)}) async-start(bf16[2,4,32,256]{3,1,0,2:T(4,128)(2,1)} %copy.31), calls=%async_computation | async-start | bytes 262144 | tf_op jit(solution)/shard_map/all_to_all | solution.py:340
  48.9 3.4 %collective-permute-start = (f32[3,2,32,256]{3,2,1,0:T(8,128)S(1)}, f32[3,2,32,256]{3,2,1,0:T(8,128)S(1)}, u32[]{:S(2)}, u32[]{:S(2)}) collective-permute-start(f32[3,2,32,256]{3,2,1,0:T(8,128)S(1)} %get-tuple-element.272), channel_id=1, source_target_pairs={{0,4},{4,8},{8,12},{12,16},{16,20},{20,24},{24,28},{1,5},{5,9},{9,... | collective-permute-start | bytes 589832 | tf_op jit(solution)/shard_map/ppermute | solution.py:149
  52.3 3.4 %collective-permute-start.1 = (f32[3,2,32,256]{3,2,1,0:T(8,128)S(1)}, f32[3,2,32,256]{3,2,1,0:T(8,128)S(1)}, u32[]{:S(2)}, u32[]{:S(2)}) collective-permute-start(f32[3,2,32,256]{3,2,1,0:T(8,128)S(1)} %get-tuple-element.271), channel_id=1, source_target_pairs={{4,0},{8,4},{12,8},{16,12},{20,16},{24,20},{28,24},{5,1},{9,5},{13... | collective-permute-start | bytes 589832 | tf_op jit(solution)/shard_map/ppermute | solution.py:150
  56.5 4.6 %collective-permute-done = f32[3,2,32,256]{3,2,1,0:T(8,128)S(1)} collective-permute-done((f32[3,2,32,256]{3,2,1,0:T(8,128)S(1)}, f32[3,2,32,256]{3,2,1,0:T(8,128)S(1)}, u32[]{:S(2)}, u32[]{:S(2)}) %collective-permute-start) | collective-permute-done | bytes 196640 | tf_op jit(solution)/shard_map/ppermute | solution.py:149
  63.0 1.8 copy-done.4
  64.9 2.0 collective-permute-start.2
  67.0 3.5 %collective-permute-start.3 = (f32[3,36,2,256]{3,2,1,0:T(2,128)S(1)}, f32[3,36,2,256]{3,2,1,0:T(2,128)S(1)}, u32[]{:S(2)}, u32[]{:S(2)}) collective-permute-start(f32[3,36,2,256]{3,2,1,0:T(2,128)S(1)} %get-tuple-element.263), channel_id=1, source_target_pairs={{1,0},{2,1},{3,2},{5,4},{6,5},{7,6},{9,8},{10,9},{11,10},{13,12},{... | collective-permute-start | bytes 663560 | tf_op jit(solution)/shard_map/ppermute | solution.py:156
  70.8 3.2 %fusion.10 = f32[3072,256]{1,0:T(8,128)} fusion(s32[256]{0:T(256)S(1)} %get-tuple-element.287, f32[256]{0:T(256)S(1)} %bitcast.120, s32[256]{0:T(256)S(1)} %get-tuple-element.286), kind=kOutput, calls=%fused_computation.32 | convolution fusion | flops 2416836608 | bytes 3148800 | tf_op jit(solution)/shard_map/dot_general | solution.py:364
  74.1 13.1 %concatenate.28.up_ref = f32[3,36,48,256]{3,2,1,0:T(8,128)} concatenate(f32[3,36,6,256]{3,2,1,0:T(8,128)S(1)} %broadcast.438, f32[3,36,2,256]{3,2,1,0:T(2,128)S(1)} %collective-permute-done.2, f32[3,36,32,256]{3,2,1,0:T(8,128)} %copy-done.4, f32[3,36,2,256]{3,2,1,0:T(2,128)S(1)} %collective-permute-done.3, f32[3,36,6,256]{3,2,1,0:T(8,128)S(1)} %broadcast.438), dimensions={2} | concatenate | bytes 10616832 | tf_op jit(solution)/shard_map/concatenate | solution.py:158
  87.2 6.2 %shard_map.122.rest_0_ = f32[3,32,32,256]{3,2,1,0:T(8,128)} custom-call(f32[3,36,48,256]{3,2,1,0:T(8,128)} %concatenate.28.up_ref, f32[3,32,32,256]{3,2,1,0:T(8,128)} %prev_ref.5, f32[2,32,32,256]{3,2,1,0:T(8,128)} %mod_ref.15, f32[3,32,32,256]{3,2,1,0:T(8,128)} %bitcast.103), custom_call_target="tpu_custom_call" | custom-call | tf_op jit(solution)/shard_map/pallas_call | solution.py:125
  94.5 2.9 %collective-permute-start.4 = (f32[3,2,32,256]{3,2,1,0:T(8,128)S(1)}, f32[3,2,32,256]{3,2,1,0:T(8,128)S(1)}, u32[]{:S(2)}, u32[]{:S(2)}) collective-permute-start(f32[3,2,32,256]{3,2,1,0:T(8,128)S(1)} %get-tuple-element.269), channel_id=1, source_target_pairs={{0,4},{4,8},{8,12},{12,16},{16,20},{20,24},{24,28},{1,5},{5,9},{9,... | collective-permute-start | bytes 589832 | tf_op jit(solution)/shard_map/ppermute | solution.py:149
  97.3 3.9 %collective-permute-start.5 = (f32[3,2,32,256]{3,2,1,0:T(8,128)S(1)}, f32[3,2,32,256]{3,2,1,0:T(8,128)S(1)}, u32[]{:S(2)}, u32[]{:S(2)}) collective-permute-start(f32[3,2,32,256]{3,2,1,0:T(8,128)S(1)} %get-tuple-element.270), channel_id=1, source_target_pairs={{4,0},{8,4},{12,8},{16,12},{20,16},{24,20},{28,24},{5,1},{9,5},{13... | collective-permute-start | bytes 589832 | tf_op jit(solution)/shard_map/ppermute | solution.py:150
  101.2 11.5 %shard_map.123.prev_ref = f32[3,32,32,256]{3,2,1,0:T(8,128)} custom-call(f32[3,36,48,256]{3,2,1,0:T(8,128)} %concatenate.28.up_ref, f32[3,32,32,256]{3,2,1,0:T(8,128)} %prev_ref.5, f32[2,32,32,256]{3,2,1,0:T(8,128)} %mod_ref.15, f32[3,32,32,256]{3,2,1,0:T(8,128)} %bitcast.104, f32[3,32,32,256]{3,2,1,0:T(8,128)} %shard_map.122.rest_0_), custom_call_target="tpu_custom_call", output_to_operand_aliasing={{}: (4, {})} | custom-call | tf_op jit(solution)/shard_map/pallas_call | solution.py:125
  112.7 2.1 pad_maximum_fusion
  114.9 1.8 copy-done.2
  116.8 1.9 collective-permute-start.6
  118.8 3.6 %collective-permute-start.7 = (f32[3,36,2,256]{3,2,1,0:T(2,128)S(1)}, f32[3,36,2,256]{3,2,1,0:T(2,128)S(1)}, u32[]{:S(2)}, u32[]{:S(2)}) collective-permute-start(f32[3,36,2,256]{3,2,1,0:T(2,128)S(1)} %get-tuple-element.261), channel_id=1, source_target_pairs={{1,0},{2,1},{3,2},{5,4},{6,5},{7,6},{9,8},{10,9},{11,10},{13,12},{... | collective-permute-start | bytes 663560 | tf_op jit(solution)/shard_map/ppermute | solution.py:156
  122.4 3.2 %fusion.9 = f32[3072,256]{1,0:T(8,128)} fusion(s32[256]{0:T(256)S(1)} %get-tuple-element.287, f32[256]{0:T(256)S(1)} %bitcast.119, s32[256]{0:T(256)S(1)} %get-tuple-element.286), kind=kOutput, calls=%fused_computation.31 | convolution fusion | flops 2416836608 | bytes 3148800 | tf_op jit(solution)/shard_map/dot_general | solution.py:364
  125.8 13.1 %concatenate.31.up_ref = f32[3,36,48,256]{3,2,1,0:T(8,128)} concatenate(f32[3,36,6,256]{3,2,1,0:T(8,128)S(1)} %broadcast.438, f32[3,36,2,256]{3,2,1,0:T(2,128)S(1)} %collective-permute-done.6, f32[3,36,32,256]{3,2,1,0:T(8,128)} %copy-done.2, f32[3,36,2,256]{3,2,1,0:T(2,128)S(1)} %collective-permute-done.7, f32[3,36,6,256]{3,2,1,0:T(8,128)S(1)} %broadcast.438), dimensions={2} | concatenate | bytes 10616832 | tf_op jit(solution)/shard_map/concatenate | solution.py:158
  138.9 6.2 %shard_map.124.rest_0_ = f32[3,32,32,256]{3,2,1,0:T(8,128)} custom-call(f32[3,36,48,256]{3,2,1,0:T(8,128)} %concatenate.31.up_ref, f32[3,32,32,256]{3,2,1,0:T(8,128)} %prev_ref.7, f32[2,32,32,256]{3,2,1,0:T(8,128)} %mod_ref.15, f32[3,32,32,256]{3,2,1,0:T(8,128)} %bitcast.107), custom_call_target="tpu_custom_call" | custom-call | tf_op jit(solution)/shard_map/pallas_call | solution.py:125
  146.2 2.0 collective-permute-start.8
  148.2 4.8 %collective-permute-start.9 = (f32[3,2,32,256]{3,2,1,0:T(8,128)S(1)}, f32[3,2,32,256]{3,2,1,0:T(8,128)S(1)}, u32[]{:S(2)}, u32[]{:S(2)}) collective-permute-start(f32[3,2,32,256]{3,2,1,0:T(8,128)S(1)} %get-tuple-element.268), channel_id=1, source_target_pairs={{4,0},{8,4},{12,8},{16,12},{20,16},{24,20},{28,24},{5,1},{9,5},{13... | collective-permute-start | bytes 589832 | tf_op jit(solution)/shard_map/ppermute | solution.py:150
  152.9 11.5 %shard_map.125.prev_ref = f32[3,32,32,256]{3,2,1,0:T(8,128)} custom-call(f32[3,36,48,256]{3,2,1,0:T(8,128)} %concatenate.31.up_ref, f32[3,32,32,256]{3,2,1,0:T(8,128)} %prev_ref.7, f32[2,32,32,256]{3,2,1,0:T(8,128)} %mod_ref.15, f32[3,32,32,256]{3,2,1,0:T(8,128)} %bitcast.108, f32[3,32,32,256]{3,2,1,0:T(8,128)} %shard_map.124.rest_0_), custom_call_target="tpu_custom_call", output_to_operand_aliasing={{}: (4, {})} | custom-call | tf_op jit(solution)/shard_map/pallas_call | solution.py:125
  164.4 2.1 pad_maximum_fusion.1
  166.6 1.8 copy-done.3
  168.5 1.9 collective-permute-start.10
  170.5 3.6 %collective-permute-start.11 = (f32[3,36,2,256]{3,2,1,0:T(2,128)S(1)}, f32[3,36,2,256]{3,2,1,0:T(2,128)S(1)}, u32[]{:S(2)}, u32[]{:S(2)}) collective-permute-start(f32[3,36,2,256]{3,2,1,0:T(2,128)S(1)} %get-tuple-element.259), channel_id=1, source_target_pairs={{1,0},{2,1},{3,2},{5,4},{6,5},{7,6},{9,8},{10,9},{11,10},{13,12},{... | collective-permute-start | bytes 663560 | tf_op jit(solution)/shard_map/ppermute | solution.py:156
  174.1 3.2 %fusion.8 = f32[3072,256]{1,0:T(8,128)} fusion(s32[256]{0:T(256)S(1)} %get-tuple-element.287, f32[256]{0:T(256)S(1)} %bitcast.118, s32[256]{0:T(256)S(1)} %get-tuple-element.286), kind=kOutput, calls=%fused_computation.30 | convolution fusion | flops 2416836608 | bytes 3148800 | tf_op jit(solution)/shard_map/dot_general | solution.py:364
  177.6 13.1 %concatenate.33.up_ref = f32[3,36,48,256]{3,2,1,0:T(8,128)} concatenate(f32[3,36,6,256]{3,2,1,0:T(8,128)S(1)} %broadcast.438, f32[3,36,2,256]{3,2,1,0:T(2,128)S(1)} %collective-permute-done.10, f32[3,36,32,256]{3,2,1,0:T(8,128)} %copy-done.3, f32[3,36,2,256]{3,2,1,0:T(2,128)S(1)} %collective-permute-done.11, f32[3,36,6,256]{3,2,1,0:T(8,128)S(1)} %broadcast.438), dimensions={2} | concatenate | bytes 10616832 | tf_op jit(solution)/shard_map/concatenate | solution.py:158
  190.7 6.2 %shard_map.126.rest_0_ = f32[3,32,32,256]{3,2,1,0:T(8,128)} custom-call(f32[3,36,48,256]{3,2,1,0:T(8,128)} %concatenate.33.up_ref, f32[3,32,32,256]{3,2,1,0:T(8,128)} %shard_map.123.prev_ref, f32[2,32,32,256]{3,2,1,0:T(8,128)} %mod_ref.15, f32[3,32,32,256]{3,2,1,0:T(8,128)} %bitcast.105), custom_call_target="tpu_custom_call" | custom-call | tf_op jit(solution)/shard_map/pallas_call | solution.py:125
  197.9 1.9 collective-permute-start.12
  199.8 4.8 %collective-permute-start.13 = (f32[3,2,32,256]{3,2,1,0:T(8,128)S(1)}, f32[3,2,32,256]{3,2,1,0:T(8,128)S(1)}, u32[]{:S(2)}, u32[]{:S(2)}) collective-permute-start(f32[3,2,32,256]{3,2,1,0:T(8,128)S(1)} %get-tuple-element.266), channel_id=1, source_target_pairs={{4,0},{8,4},{12,8},{16,12},{20,16},{24,20},{28,24},{5,1},{9,5},{13... | collective-permute-start | bytes 589832 | tf_op jit(solution)/shard_map/ppermute | solution.py:150
  204.6 11.5 %shard_map.127 = f32[3,32,32,256]{3,2,1,0:T(8,128)} custom-call(f32[3,36,48,256]{3,2,1,0:T(8,128)} %concatenate.33.up_ref, f32[3,32,32,256]{3,2,1,0:T(8,128)} %shard_map.123.prev_ref, f32[2,32,32,256]{3,2,1,0:T(8,128)} %mod_ref.15, f32[3,32,32,256]{3,2,1,0:T(8,128)} %bitcast.106, f32[3,32,32,256]{3,2,1,0:T(8,128)} %shard_map.126.rest_0_), custom_call_target="tpu_custom_call", output_to_operand_aliasing={{}: (4, {})} | custom-call | tf_op jit(solution)/shard_map/pallas_call | solution.py:125
  216.1 2.1 pad_maximum_fusion.2
  220.2 1.9 collective-permute-start.14
  222.2 3.9 %collective-permute-start.15 = (f32[3,36,2,256]{3,2,1,0:T(2,128)S(1)}, f32[3,36,2,256]{3,2,1,0:T(2,128)S(1)}, u32[]{:S(2)}, u32[]{:S(2)}) collective-permute-start(f32[3,36,2,256]{3,2,1,0:T(2,128)S(1)} %get-tuple-element.257), channel_id=1, source_target_pairs={{1,0},{2,1},{3,2},{5,4},{6,5},{7,6},{9,8},{10,9},{11,10},{13,12},{... | collective-permute-start | bytes 663560 | tf_op jit(solution)/shard_map/ppermute | solution.py:156
  226.0 3.2 %fusion.7 = f32[3072,256]{1,0:T(8,128)} fusion(s32[256]{0:T(256)S(1)} %get-tuple-element.287, f32[256]{0:T(256)S(1)} %bitcast.117, s32[256]{0:T(256)S(1)} %get-tuple-element.286), kind=kOutput, calls=%fused_computation.29 | convolution fusion | flops 2416836608 | bytes 3148800 | tf_op jit(solution)/shard_map/dot_general | solution.py:364
  229.3 13.1 %concatenate.35.up_ref = f32[3,36,48,256]{3,2,1,0:T(8,128)} concatenate(f32[3,36,6,256]{3,2,1,0:T(8,128)S(1)} %broadcast.438, f32[3,36,2,256]{3,2,1,0:T(2,128)S(1)} %collective-permute-done.14, f32[3,36,32,256]{3,2,1,0:T(8,128)} %copy-done.1, f32[3,36,2,256]{3,2,1,0:T(2,128)S(1)} %collective-permute-done.15, f32[3,36,6,256]{3,2,1,0:T(8,128)S(1)} %broadcast.438), dimensions={2} | concatenate | bytes 10616832 | tf_op jit(solution)/shard_map/concatenate | solution.py:158
  242.4 6.2 %shard_map.128.rest_0_ = f32[3,32,32,256]{3,2,1,0:T(8,128)} custom-call(f32[3,36,48,256]{3,2,1,0:T(8,128)} %concatenate.35.up_ref, f32[3,32,32,256]{3,2,1,0:T(8,128)} %shard_map.125.prev_ref, f32[2,32,32,256]{3,2,1,0:T(8,128)} %mod_ref.15, f32[3,32,32,256]{3,2,1,0:T(8,128)} %bitcast.109), custom_call_target="tpu_custom_call" | custom-call | tf_op jit(solution)/shard_map/pallas_call | solution.py:125
  248.5 11.5 %shard_map.129 = f32[3,32,32,256]{3,2,1,0:T(8,128)} custom-call(f32[3,36,48,256]{3,2,1,0:T(8,128)} %concatenate.35.up_ref, f32[3,32,32,256]{3,2,1,0:T(8,128)} %shard_map.125.prev_ref, f32[2,32,32,256]{3,2,1,0:T(8,128)} %mod_ref.15, f32[3,32,32,256]{3,2,1,0:T(8,128)} %bitcast.110, f32[3,32,32,256]{3,2,1,0:T(8,128)} %shard_map.128.rest_0_), custom_call_target="tpu_custom_call", output_to_operand_aliasing={{}: (4, {})} | custom-call | tf_op jit(solution)/shard_map/pallas_call | solution.py:125
  (115 shorter events, 16.9 us)
Async XLA Ops:
  15.9 5.4 %copy-start.5 = (s32[8192]{0:T(1024)S(1)}, s32[8192]{0:T(1024)}, u32[]{:S(2)}) copy-start(s32[8192]{0:T(1024)} %param.19) | copy-start | bytes 98308
  15.9 5.5 %copy-start.6 = (s32[8192]{0:T(1024)S(1)}, s32[8192]{0:T(1024)}, u32[]{:S(2)}) copy-start(s32[8192]{0:T(1024)} %param.20) | copy-start | bytes 98308
  25.8 23.1 %copy-start = (f32[3,32,32,256]{3,2,1,0:T(8,128)S(1)}, f32[3,32,32,256]{3,2,1,0:T(8,128)}, u32[]{:S(2)}) copy-start(f32[3,32,32,256]{3,2,1,0:T(8,128)} %prev_ref.7) | copy-start | bytes 9437188
  25.8 30.7 %copy-start.7 = (s32[256]{0:T(256)S(1)}, s32[256]{0:T(256)}, u32[]{:S(2)}) copy-start(s32[256]{0:T(256)} %param.21) | copy-start | bytes 3076
  42.9 27.7 %all-to-all-start = ((bf16[2,4,32,256]{3,1,0,2:T(4,128)(2,1)}), bf16[2,4,32,256]{3,1,0,2:T(4,128)(2,1)S(1)}, u32[]{:S(2)}, u32[]{:S(2)}) async-start(bf16[2,4,32,256]{3,1,0,2:T(4,128)(2,1)} %copy.31), calls=%async_computation | async-start | bytes 262144 | tf_op jit(solution)/shard_map/all_to_all | solution.py:340
  48.9 12.2 %collective-permute-start = (f32[3,2,32,256]{3,2,1,0:T(8,128)S(1)}, f32[3,2,32,256]{3,2,1,0:T(8,128)S(1)}, u32[]{:S(2)}, u32[]{:S(2)}) collective-permute-start(f32[3,2,32,256]{3,2,1,0:T(8,128)S(1)} %get-tuple-element.272), channel_id=1, source_target_pairs={{0,4},{4,8},{8,12},{12,16},{16,20},{20,24},{24,28},{1,5},{5,9},{9,... | collective-permute-start | bytes 589832 | tf_op jit(solution)/shard_map/ppermute | solution.py:149
  52.3 10.7 %collective-permute-start.1 = (f32[3,2,32,256]{3,2,1,0:T(8,128)S(1)}, f32[3,2,32,256]{3,2,1,0:T(8,128)S(1)}, u32[]{:S(2)}, u32[]{:S(2)}) collective-permute-start(f32[3,2,32,256]{3,2,1,0:T(8,128)S(1)} %get-tuple-element.271), channel_id=1, source_target_pairs={{4,0},{8,4},{12,8},{16,12},{20,16},{24,20},{28,24},{5,1},{9,5},{13... | collective-permute-start | bytes 589832 | tf_op jit(solution)/shard_map/ppermute | solution.py:150
  63.0 1.8 copy-start.4
  64.9 9.1 %collective-permute-start.2 = (f32[3,36,2,256]{3,2,1,0:T(2,128)S(1)}, f32[3,36,2,256]{3,2,1,0:T(2,128)S(1)}, u32[]{:S(2)}, u32[]{:S(2)}) collective-permute-start(f32[3,36,2,256]{3,2,1,0:T(2,128)S(1)} %get-tuple-element.264), channel_id=1, source_target_pairs={{0,1},{1,2},{2,3},{4,5},{5,6},{6,7},{8,9},{9,10},{10,11},{12,13},{... | collective-permute-start | bytes 663560 | tf_op jit(solution)/shard_map/ppermute | solution.py:155
  67.0 7.1 %collective-permute-start.3 = (f32[3,36,2,256]{3,2,1,0:T(2,128)S(1)}, f32[3,36,2,256]{3,2,1,0:T(2,128)S(1)}, u32[]{:S(2)}, u32[]{:S(2)}) collective-permute-start(f32[3,36,2,256]{3,2,1,0:T(2,128)S(1)} %get-tuple-element.263), channel_id=1, source_target_pairs={{1,0},{2,1},{3,2},{5,4},{6,5},{7,6},{9,8},{10,9},{11,10},{13,12},{... | collective-permute-start | bytes 663560 | tf_op jit(solution)/shard_map/ppermute | solution.py:156
  94.5 18.3 %collective-permute-start.4 = (f32[3,2,32,256]{3,2,1,0:T(8,128)S(1)}, f32[3,2,32,256]{3,2,1,0:T(8,128)S(1)}, u32[]{:S(2)}, u32[]{:S(2)}) collective-permute-start(f32[3,2,32,256]{3,2,1,0:T(8,128)S(1)} %get-tuple-element.269), channel_id=1, source_target_pairs={{0,4},{4,8},{8,12},{12,16},{16,20},{20,24},{24,28},{1,5},{5,9},{9,... | collective-permute-start | bytes 589832 | tf_op jit(solution)/shard_map/ppermute | solution.py:149
  97.3 15.4 %collective-permute-start.5 = (f32[3,2,32,256]{3,2,1,0:T(8,128)S(1)}, f32[3,2,32,256]{3,2,1,0:T(8,128)S(1)}, u32[]{:S(2)}, u32[]{:S(2)}) collective-permute-start(f32[3,2,32,256]{3,2,1,0:T(8,128)S(1)} %get-tuple-element.270), channel_id=1, source_target_pairs={{4,0},{8,4},{12,8},{16,12},{20,16},{24,20},{28,24},{5,1},{9,5},{13... | collective-permute-start | bytes 589832 | tf_op jit(solution)/shard_map/ppermute | solution.py:150
  114.9 1.8 copy-start.2
  116.8 8.8 %collective-permute-start.6 = (f32[3,36,2,256]{3,2,1,0:T(2,128)S(1)}, f32[3,36,2,256]{3,2,1,0:T(2,128)S(1)}, u32[]{:S(2)}, u32[]{:S(2)}) collective-permute-start(f32[3,36,2,256]{3,2,1,0:T(2,128)S(1)} %get-tuple-element.262), channel_id=1, source_target_pairs={{0,1},{1,2},{2,3},{4,5},{5,6},{6,7},{8,9},{9,10},{10,11},{12,13},{... | collective-permute-start | bytes 663560 | tf_op jit(solution)/shard_map/ppermute | solution.py:155
  118.8 7.1 %collective-permute-start.7 = (f32[3,36,2,256]{3,2,1,0:T(2,128)S(1)}, f32[3,36,2,256]{3,2,1,0:T(2,128)S(1)}, u32[]{:S(2)}, u32[]{:S(2)}) collective-permute-start(f32[3,36,2,256]{3,2,1,0:T(2,128)S(1)} %get-tuple-element.261), channel_id=1, source_target_pairs={{1,0},{2,1},{3,2},{5,4},{6,5},{7,6},{9,8},{10,9},{11,10},{13,12},{... | collective-permute-start | bytes 663560 | tf_op jit(solution)/shard_map/ppermute | solution.py:156
  146.2 18.3 %collective-permute-start.8 = (f32[3,2,32,256]{3,2,1,0:T(8,128)S(1)}, f32[3,2,32,256]{3,2,1,0:T(8,128)S(1)}, u32[]{:S(2)}, u32[]{:S(2)}) collective-permute-start(f32[3,2,32,256]{3,2,1,0:T(8,128)S(1)} %get-tuple-element.267), channel_id=1, source_target_pairs={{0,4},{4,8},{8,12},{12,16},{16,20},{20,24},{24,28},{1,5},{5,9},{9,... | collective-permute-start | bytes 589832 | tf_op jit(solution)/shard_map/ppermute | solution.py:149
  148.2 16.3 %collective-permute-start.9 = (f32[3,2,32,256]{3,2,1,0:T(8,128)S(1)}, f32[3,2,32,256]{3,2,1,0:T(8,128)S(1)}, u32[]{:S(2)}, u32[]{:S(2)}) collective-permute-start(f32[3,2,32,256]{3,2,1,0:T(8,128)S(1)} %get-tuple-element.268), channel_id=1, source_target_pairs={{4,0},{8,4},{12,8},{16,12},{20,16},{24,20},{28,24},{5,1},{9,5},{13... | collective-permute-start | bytes 589832 | tf_op jit(solution)/shard_map/ppermute | solution.py:150
  166.6 1.8 copy-start.3
  168.5 8.8 %collective-permute-start.10 = (f32[3,36,2,256]{3,2,1,0:T(2,128)S(1)}, f32[3,36,2,256]{3,2,1,0:T(2,128)S(1)}, u32[]{:S(2)}, u32[]{:S(2)}) collective-permute-start(f32[3,36,2,256]{3,2,1,0:T(2,128)S(1)} %get-tuple-element.260), channel_id=1, source_target_pairs={{0,1},{1,2},{2,3},{4,5},{5,6},{6,7},{8,9},{9,10},{10,11},{12,13},{... | collective-permute-start | bytes 663560 | tf_op jit(solution)/shard_map/ppermute | solution.py:155
  170.5 7.1 %collective-permute-start.11 = (f32[3,36,2,256]{3,2,1,0:T(2,128)S(1)}, f32[3,36,2,256]{3,2,1,0:T(2,128)S(1)}, u32[]{:S(2)}, u32[]{:S(2)}) collective-permute-start(f32[3,36,2,256]{3,2,1,0:T(2,128)S(1)} %get-tuple-element.259), channel_id=1, source_target_pairs={{1,0},{2,1},{3,2},{5,4},{6,5},{7,6},{9,8},{10,9},{11,10},{13,12},{... | collective-permute-start | bytes 663560 | tf_op jit(solution)/shard_map/ppermute | solution.py:156
  197.9 18.2 %collective-permute-start.12 = (f32[3,2,32,256]{3,2,1,0:T(8,128)S(1)}, f32[3,2,32,256]{3,2,1,0:T(8,128)S(1)}, u32[]{:S(2)}, u32[]{:S(2)}) collective-permute-start(f32[3,2,32,256]{3,2,1,0:T(8,128)S(1)} %get-tuple-element.265), channel_id=1, source_target_pairs={{0,4},{4,8},{8,12},{12,16},{16,20},{20,24},{24,28},{1,5},{5,9},{9,... | collective-permute-start | bytes 589832 | tf_op jit(solution)/shard_map/ppermute | solution.py:149
  199.8 16.3 %collective-permute-start.13 = (f32[3,2,32,256]{3,2,1,0:T(8,128)S(1)}, f32[3,2,32,256]{3,2,1,0:T(8,128)S(1)}, u32[]{:S(2)}, u32[]{:S(2)}) collective-permute-start(f32[3,2,32,256]{3,2,1,0:T(8,128)S(1)} %get-tuple-element.266), channel_id=1, source_target_pairs={{4,0},{8,4},{12,8},{16,12},{20,16},{24,20},{28,24},{5,1},{9,5},{13... | collective-permute-start | bytes 589832 | tf_op jit(solution)/shard_map/ppermute | solution.py:150
  218.3 1.8 copy-start.1
  220.2 9.0 %collective-permute-start.14 = (f32[3,36,2,256]{3,2,1,0:T(2,128)S(1)}, f32[3,36,2,256]{3,2,1,0:T(2,128)S(1)}, u32[]{:S(2)}, u32[]{:S(2)}) collective-permute-start(f32[3,36,2,256]{3,2,1,0:T(2,128)S(1)} %get-tuple-element.258), channel_id=1, source_target_pairs={{0,1},{1,2},{2,3},{4,5},{5,6},{6,7},{8,9},{9,10},{10,11},{12,13},{... | collective-permute-start | bytes 663560 | tf_op jit(solution)/shard_map/ppermute | solution.py:155
  222.2 7.1 %collective-permute-start.15 = (f32[3,36,2,256]{3,2,1,0:T(2,128)S(1)}, f32[3,36,2,256]{3,2,1,0:T(2,128)S(1)}, u32[]{:S(2)}, u32[]{:S(2)}) collective-permute-start(f32[3,36,2,256]{3,2,1,0:T(2,128)S(1)} %get-tuple-element.257), channel_id=1, source_target_pairs={{1,0},{2,1},{3,2},{5,4},{6,5},{7,6},{9,8},{10,9},{11,10},{13,12},{... | collective-permute-start | bytes 663560 | tf_op jit(solution)/shard_map/ppermute | solution.py:156

commit v4 on v2

--- a/solution.py
+++ b/solution.py
@@ -276,6 +276,8 @@
         kernel.reshape(2 * per_device * ND, NK), cosines, preferred_element_type=jnp.float32
     )
     table_rounded = spectrum_table.astype(jnp.bfloat16)
+    first_padded = padded_2(field_now, (("gx", 1),), 2)
+    first_padded, table_rounded = lax.optimization_barrier((first_padded, table_rounded))
     all_slots = slot_offset.shape[0]
     width = math.gcd(all_slots, 4096)
     count_blocks = all_slots // width
@@ -301,6 +303,8 @@
     )
     slots_dev = slot_target.shape[0]
     occupied = (jnp.arange(slots_dev, dtype=jnp.int32) < live_count[0]).astype(jnp.float32)
+    first_padded = padded_2(first_padded, (("gy", 2),), 2)
+    first_padded, spectra = lax.optimization_barrier((first_padded, spectra))
     parcel = spectra.reshape(2, per_device, groups, slots_dev)
     arrived = lax.all_to_all(parcel, ("gx", "gy"), split_axis=2, concat_axis=1, tiled=True)
     freq_order = jnp.arange(F, dtype=jnp.int32)
@@ -327,7 +331,7 @@
         spread = weighted[instant][:, None] * depth_hot
         source = jnp.dot(column_hot, spread, precision=lax.Precision.HIGHEST)
         source = source.reshape(3, block_x, block_y, depth)
-        padded = padded_2(current, (("gx", 1), ("gy", 2)), 2)
+        padded = first_padded if instant == 0 else padded_2(current, (("gx", 1), ("gy", 2)), 2)
         padded = jnp.pad(padded, ((0, 0), (0, 0), (YPAD - 2, YPAD - 2), (0, 0)))
         advanced = elastic_step(padded, previous, moduli, source)
         previous, current = (current, advanced)

time: 225 us -> 228 us (1.013)
  local copies, waits for them, and re-layouts: 12.1 us -> 19 us
  waiting for transfers between devices: 24.1 us -> 19.6 us
    pad x0 -> x1, local copies, waits for them, and re-layouts: none -> 5.45 us  [shards(): padded = jnp.pad(padded, ((0, 0), (0, 0), (YPAD - 2, YPAD - 2), (0, 0)))]
    ppermute x8, waiting for transfers between devices: 9.97 us -> 6.69 us  [padded_2(): lax.ppermute(lax.slice_in_dim(block, block.shape[dim] - width, None, axis...]
    concatenate x4 -> x5, other arithmetic: 11.8 us -> 14.3 us  [padded_2(): block = jnp.concatenate([low, block, high], axis=dim)]
    slice x4 -> x5, local copies, waits for them, and re-layouts: 4.5 us -> 6.34 us  [padded_2(): lax.slice_in_dim(block, block.shape[dim] - width, None, axis=dim)]
  transfers between devices with their start and end apart: 17 -> 17, of which waited for: 11 -> 9; matrix products, arithmetic and copies ran while one was open for 9% -> 27% of each run, Pallas kernels for 0% -> 0%
where the time goes in v4:
time: 228 us; the launch traced here: 225 us
  Pallas kernels  57.3 us (25%)
  starting transfers between devices  55.4 us (24%)
  other arithmetic  38.6 us (17%)
  matrix products  33.1 us (15%)
  waiting for transfers between devices  19.6 us (9%)
  local copies, waits for them, and re-layouts  19 us (8%)
    pallas_call x4, Pallas kernels, elastic_step(): pl.pallas_call(kernel, grid=(nx // bx,), in_specs=[pl.BlockSpec((3, px, p...  57.3 us
    ppermute x8, starting transfers between devices, padded_2(): lax.ppermute(lax.slice_in_dim(block, 0, width, axis=dim), axis, backward)  31.1 us
    ppermute x8, starting transfers between devices, padded_2(): lax.ppermute(lax.slice_in_dim(block, block.shape[dim] - width, None, axis...  18.5 us
    dot_general x2, matrix products, select_block(): jnp.dot(table_rounded, offset_hot, preferred_element_type=jnp.float32)  15.6 us
    concatenate x5, other arithmetic, padded_2(): block = jnp.concatenate([low, block, high], axis=dim)  14.3 us
    dot_general x4, matrix products, shards(): source = jnp.dot(column_hot, spread, precision=lax.Precision.HIGHEST)  12.9 us
    ppermute x8, waiting for transfers between devices, padded_2(): lax.ppermute(lax.slice_in_dim(block, 0, width, axis=dim), axis, backward)  12.6 us
    ppermute x8, waiting for transfers between devices, padded_2(): lax.ppermute(lax.slice_in_dim(block, block.shape[dim] - width, None, axis...  6.69 us
  transfers between devices with their start and end apart: 17, of which 9 were waited for; matrix products, arithmetic and copies ran while one was open for 27% of the time, Pallas kernels for 0%

profile of v4, /device:TPU:12, one launch (start us, length us, event | category | flops | bytes accessed | tf_op | source)
XLA Modules:
  0.0 225.2 jit_solution(3915200609737980326)
XLA Ops:
  0.6 1.8 fusion.83
  2.5 3.4 %collective-permute-start = (f32[3,2,32,256]{3,2,1,0:T(8,128)}, f32[3,2,32,256]{3,2,1,0:T(8,128)S(1)}, u32[]{:S(2)}, u32[]{:S(2)}) collective-permute-start(f32[3,2,32,256]{3,2,1,0:T(8,128)} %get-tuple-element.279), channel_id=1, source_target_pairs={{0,4},{4,8},{8,12},{12,16},{16,20},{20,24},{24,28},{1,5},{5,9},{9,... | collective-permute-start | bytes 589832 | tf_op jit(solution)/shard_map/ppermute | solution.py:27
  5.8 3.3 %collective-permute-start.1 = (f32[3,2,32,256]{3,2,1,0:T(8,128)}, f32[3,2,32,256]{3,2,1,0:T(8,128)}, u32[]{:S(2)}, u32[]{:S(2)}) collective-permute-start(f32[3,2,32,256]{3,2,1,0:T(8,128)} %get-tuple-element.280), channel_id=1, source_target_pairs={{4,0},{8,4},{12,8},{16,12},{20,16},{24,20},{28,24},{5,1},{9,5},{13... | collective-permute-start | bytes 589832 | tf_op jit(solution)/shard_map/ppermute | solution.py:30
  11.5 4.9 %sine_multiply_fusion.1 = (f32[32,4,1024]{2,1,0:T(4,128)S(1)}, f32[32,4,1024]{2,1,0:T(4,128)S(1)}, f32[32,4,1024]{2,1,0:T(4,128)S(1)}) fusion(f32[32]{0:T(128)S(1)} %get-tuple-element.299, f32[32,4]{1,0:T(8,128)S(1)} %copy.24, f32[1024]{0:T(1024)S(1)} %multiply_multiply_fusion, f32[1,4,1024]{2,1,0:T(4,128)S(1)} %slice.89, f32[31,4,1024]{2,1,0:T(4,128)S(1)} %slice.88, ...), kind=kLoop, calls=%fused_computation.58 | loop fusion | flops 1441792 | bytes 2102016 | tf_op jit(solution)/shard_map/mul | solution.py:143
  16.7 2.2 while.32
  19.8 4.3 %fusion.44 = (bf16[1,32,4,1024]{3,2,1,0:T(4,128)(2,1)S(1)}, bf16[1,32,4,1024]{3,2,1,0:T(4,128)(2,1)S(1)}) fusion(f32[32,4,1024]{2,1,0:T(4,128)S(1)} %get-tuple-element.195, f32[32,4,1024]{2,1,0:T(4,128)S(1)} %get-tuple-element.194, f32[32,4,1024]{2,1,0:T(4,128)S(1)} %negate_exponential_fusion, f32[32,4,1024]{2,1,0:T(4,128)S(1)} %fusion.24), kind=kLoop, calls=%fused_computation.91 | loop fusion | flops 1835008 | bytes 2621440 | tf_op jit(solution)/shard_map/stack | solution.py:172
  26.3 3.6 %subtract_convert_fusion = bf16[1024,32,64]{0,2,1:T(8,128)(2,1)} fusion(f32[1024,64]{0,1:T(8,128)S(1)} %get-tuple-element.293, f32[1024,32]{0,1:T(8,128)S(1)} %get-tuple-element.287, f32[1024,64]{0,1:T(8,128)S(1)} %get-tuple-element.292, f32[1024,32]{0,1:T(8,128)S(1)} %get-tuple-element.286), kind=kLoop, calls=%fused_computation.24 | loop fusion | flops 8388608 | bytes 4980736 | tf_op jit(solution)/shard_map/convert_element_type | solution.py:187
  31.8 4.4 %convolution_convert_fusion = bf16[256,2048]{1,0:T(8,128)(2,1)} fusion(bf16[256,1024]{1,0:T(8,128)(2,1)S(1)} %bitcast.115, bf16[1024,2048]{0,1:T(8,128)(2,1)} %bitcast.113), kind=kOutput, calls=%fused_computation.47 | convolution fusion | flops 1074266112 | bytes 5767168 | tf_op jit(solution)/shard_map/dot_general | solution.py:275
  37.0 2.3 %pad_maximum_fusion.1 = f32[3,36,32,256]{3,2,1,0:T(8,128)S(1)} fusion(f32[3,2,32,256]{3,2,1,0:T(8,128)} %collective-permute-done.1, f32[3,32,32,256]{3,2,1,0:T(8,128)} %prev_ref.3, f32[3,2,32,256]{3,2,1,0:T(8,128)} %copy-done.3), kind=kLoop, calls=%fused_computation.41 | loop fusion | flops 1769472 | bytes 7077888 | tf_op jit(solution)/shard_map/concatenate | solution.py:31
  40.2 1.9 collective-permute-start.2
  42.1 3.8 %collective-permute-start.3 = (f32[3,36,2,256]{3,2,1,0:T(2,128)}, f32[3,36,2,256]{3,2,1,0:T(2,128)}, u32[]{:S(2)}, u32[]{:S(2)}) collective-permute-start(f32[3,36,2,256]{3,2,1,0:T(2,128)} %get-tuple-element.272), channel_id=1, source_target_pairs={{1,0},{2,1},{3,2},{5,4},{6,5},{7,6},{9,8},{10,9},{11,10},{13,12},{... | collective-permute-start | bytes 663560 | tf_op jit(solution)/shard_map/ppermute | solution.py:30
  45.9 18.7 %while.31 = (s32[]{:T(128)}, bf16[2,2,4,4096]{3,2,1,0:T(4,128)(2,1)}, s32[2,4096]{1,0:T(2,128)}, bf16[256,2048]{1,0:T(8,128)(2,1)}, s32[2,4096]{1,0:T(2,128)}, /*index=5*/s32[]{:T(128)}) while((s32[]{:T(128)}, bf16[2,2,4,4096]{3,2,1,0:T(4,128)(2,1)}, s32[2,4096]{1,0:T(2,128)}, bf16[256,2048]{1,0:T(8,128)(2,1)}, s32[2,4096]{1,0:T(2,128)}, ...), condition=%wide.region_9.10_spmd, body=%wide.region_7.9_spmd.sunk | while | flops 4305682432 | bytes 2392649 | solution.py:300
  46.8 7.8 %multiply_reduce_fusion.2 = bf16[2,4,4096]{2,1,0:T(4,128)(2,1)S(1)} fusion(f32[32,4096]{1,0:T(8,128)S(1)} %fusion.92, bf16[256,2048]{1,0:T(8,128)(2,1)} %get-tuple-element.440, s32[4096]{0:T(1024)S(1)} %bitcast.118), kind=kOutput, calls=%fused_computation.3.clone.1 | convolution fusion | flops 4305420288 | bytes 1654784 | tf_op jit(solution)/shard_map/while/body/eval_jaxpr/dot_general | solution.py:292
  56.1 7.8 %multiply_reduce_fusion.2 = bf16[2,4,4096]{2,1,0:T(4,128)(2,1)S(1)} fusion(f32[32,4096]{1,0:T(8,128)S(1)} %fusion.92, bf16[256,2048]{1,0:T(8,128)(2,1)} %get-tuple-element.440, s32[4096]{0:T(1024)S(1)} %bitcast.118), kind=kOutput, calls=%fused_computation.3.clone.1 | convolution fusion | flops 4305420288 | bytes 1654784 | tf_op jit(solution)/shard_map/while/body/eval_jaxpr/dot_general | solution.py:292
  65.5 3.9 %pad_maximum_fusion = f32[3,36,36,256]{3,2,1,0:T(8,128)} fusion(f32[3,36,2,256]{3,2,1,0:T(2,128)} %collective-permute-done.3, f32[3,36,32,256]{3,2,1,0:T(8,128)S(1)} %pad_maximum_fusion.1, f32[3,36,2,256]{3,2,1,0:T(2,128)} %collective-permute-done.2), kind=kLoop, calls=%fused_computation.40 | loop fusion | flops 1990656 | bytes 7962624 | tf_op jit(solution)/shard_map/concatenate | solution.py:31
  70.1 5.8 %all-to-all-start = ((bf16[2,4,32,256]{3,1,0,2:T(4,128)(2,1)}), bf16[2,4,32,256]{3,1,0,2:T(4,128)(2,1)S(1)}, u32[]{:S(2)}, u32[]{:S(2)}) async-start(bf16[2,4,32,256]{3,1,0,2:T(4,128)(2,1)} %bitcast.95), calls=%async_computation | async-start | bytes 262144 | tf_op jit(solution)/shard_map/all_to_all | solution.py:309
  76.0 5.5 %pad.13.up_ref = f32[3,36,48,256]{3,2,1,0:T(8,128)} pad(f32[3,36,36,256]{3,2,1,0:T(8,128)} %pad_maximum_fusion, f32[]{:T(128)} %constant.161.clone.1), padding=0_0x0_0x6_6x0_0 | pad | bytes 9289732 | tf_op jit(solution)/shard_map/jit(_pad)/pad | solution.py:335
  82.1 3.2 %fusion.11 = f32[3072,256]{1,0:T(8,128)} fusion(s32[256]{0:T(256)S(1)} %get-tuple-element.295, f32[256]{0:T(256)S(1)} %bitcast.122, s32[256]{0:T(256)S(1)} %get-tuple-element.294), kind=kOutput, calls=%fused_computation.46 | convolution fusion | flops 2416836608 | bytes 3148800 | tf_op jit(solution)/shard_map/dot_general | solution.py:332
  85.3 14.4 %shard_map.122.prev_ref = f32[3,32,32,256]{3,2,1,0:T(8,128)} custom-call(f32[3,36,48,256]{3,2,1,0:T(8,128)} %pad.13.up_ref, f32[3,32,32,256]{3,2,1,0:T(8,128)} %prev_ref.2, f32[2,32,32,256]{3,2,1,0:T(8,128)} %mod_ref.7, f32[3,32,32,256]{3,2,1,0:T(8,128)} %bitcast.112), custom_call_target="tpu_custom_call" | custom-call | tf_op jit(solution)/shard_map/pallas_call | solution.py:112
  100.8 3.1 %collective-permute-start.4 = (f32[3,2,32,256]{3,2,1,0:T(8,128)S(1)}, f32[3,2,32,256]{3,2,1,0:T(8,128)S(1)}, u32[]{:S(2)}, u32[]{:S(2)}) collective-permute-start(f32[3,2,32,256]{3,2,1,0:T(8,128)S(1)} %get-tuple-element.277), channel_id=1, source_target_pairs={{0,4},{4,8},{8,12},{12,16},{16,20},{20,24},{24,28},{1,5},{5,9},{9,... | collective-permute-start | bytes 589832 | tf_op jit(solution)/shard_map/ppermute | solution.py:27
  104.0 3.6 %collective-permute-start.5 = (f32[3,2,32,256]{3,2,1,0:T(8,128)S(1)}, f32[3,2,32,256]{3,2,1,0:T(8,128)S(1)}, u32[]{:S(2)}, u32[]{:S(2)}) collective-permute-start(f32[3,2,32,256]{3,2,1,0:T(8,128)S(1)} %get-tuple-element.278), channel_id=1, source_target_pairs={{4,0},{8,4},{12,8},{16,12},{20,16},{24,20},{28,24},{5,1},{9,5},{13... | collective-permute-start | bytes 589832 | tf_op jit(solution)/shard_map/ppermute | solution.py:30
  107.6 3.2 %collective-permute-done.4 = f32[3,2,32,256]{3,2,1,0:T(8,128)S(1)} collective-permute-done((f32[3,2,32,256]{3,2,1,0:T(8,128)S(1)}, f32[3,2,32,256]{3,2,1,0:T(8,128)S(1)}, u32[]{:S(2)}, u32[]{:S(2)}) %collective-permute-start.4) | collective-permute-done | bytes 196640 | tf_op jit(solution)/shard_map/ppermute | solution.py:27
  110.9 4.1 %collective-permute-done.5 = f32[3,2,32,256]{3,2,1,0:T(8,128)S(1)} collective-permute-done((f32[3,2,32,256]{3,2,1,0:T(8,128)S(1)}, f32[3,2,32,256]{3,2,1,0:T(8,128)S(1)}, u32[]{:S(2)}, u32[]{:S(2)}) %collective-permute-start.5) | collective-permute-done | bytes 196640 | tf_op jit(solution)/shard_map/ppermute | solution.py:30
  115.0 1.5 pad_maximum_fusion.11
  116.5 1.9 collective-permute-start.6
  118.4 3.6 %collective-permute-start.7 = (f32[3,36,2,256]{3,2,1,0:T(2,128)S(1)}, f32[3,36,2,256]{3,2,1,0:T(2,128)S(1)}, u32[]{:S(2)}, u32[]{:S(2)}) collective-permute-start(f32[3,36,2,256]{3,2,1,0:T(2,128)S(1)} %get-tuple-element.270), channel_id=1, source_target_pairs={{1,0},{2,1},{3,2},{5,4},{6,5},{7,6},{9,8},{10,9},{11,10},{13,12},{... | collective-permute-start | bytes 663560 | tf_op jit(solution)/shard_map/ppermute | solution.py:30
  122.1 3.2 %fusion.10 = f32[3072,256]{1,0:T(8,128)} fusion(s32[256]{0:T(256)S(1)} %get-tuple-element.295, f32[256]{0:T(256)S(1)} %bitcast.121, s32[256]{0:T(256)S(1)} %get-tuple-element.294), kind=kOutput, calls=%fused_computation.45 | convolution fusion | flops 2416836608 | bytes 3148800 | tf_op jit(solution)/shard_map/dot_general | solution.py:332
  125.5 2.7 %select_maximum_fusion.8.up_ref = f32[3,36,48,256]{3,2,1,0:T(8,128)} fusion(f32[3,36,2,256]{3,2,1,0:T(2,128)S(1)} %collective-permute-done.7, f32[3,36,2,256]{3,2,1,0:T(2,128)S(1)} %collective-permute-done.6, f32[3,2,32,256]{3,2,1,0:T(8,128)S(1)} %collective-permute-done.5, f32[3,32,32,256]{3,2,1,0:T(8,128)S(1)} %copy-done.1, ...), kind=kLoop, calls=%fused_computation.35 | loop fusion | flops 15925248 | bytes 9289728 | tf_op jit(solution)/shard_map/concatenate | solution.py:31
  128.2 14.3 %shard_map.123.prev_ref = f32[3,32,32,256]{3,2,1,0:T(8,128)} custom-call(f32[3,36,48,256]{3,2,1,0:T(8,128)} %select_maximum_fusion.8.up_ref, f32[3,32,32,256]{3,2,1,0:T(8,128)} %prev_ref.3, f32[2,32,32,256]{3,2,1,0:T(8,128)} %mod_ref.7, f32[3,32,32,256]{3,2,1,0:T(8,128)} %bitcast.111), custom_call_target="tpu_custom_call" | custom-call | tf_op jit(solution)/shard_map/pallas_call | solution.py:112
  143.8 2.0 collective-permute-start.8
  145.8 4.7 %collective-permute-start.9 = (f32[3,2,32,256]{3,2,1,0:T(8,128)S(1)}, f32[3,2,32,256]{3,2,1,0:T(8,128)S(1)}, u32[]{:S(2)}, u32[]{:S(2)}) collective-permute-start(f32[3,2,32,256]{3,2,1,0:T(8,128)S(1)} %get-tuple-element.276), channel_id=1, source_target_pairs={{4,0},{8,4},{12,8},{16,12},{20,16},{24,20},{28,24},{5,1},{9,5},{13... | collective-permute-start | bytes 589832 | tf_op jit(solution)/shard_map/ppermute | solution.py:30
  150.5 1.7 collective-permute-done.8
  152.2 4.0 %collective-permute-done.9 = f32[3,2,32,256]{3,2,1,0:T(8,128)S(1)} collective-permute-done((f32[3,2,32,256]{3,2,1,0:T(8,128)S(1)}, f32[3,2,32,256]{3,2,1,0:T(8,128)S(1)}, u32[]{:S(2)}, u32[]{:S(2)}) %collective-permute-start.9) | collective-permute-done | bytes 196640 | tf_op jit(solution)/shard_map/ppermute | solution.py:30
  156.2 1.5 pad_maximum_fusion.8
  157.7 1.9 collective-permute-start.10
  159.7 3.9 %collective-permute-start.11 = (f32[3,36,2,256]{3,2,1,0:T(2,128)S(1)}, f32[3,36,2,256]{3,2,1,0:T(2,128)S(1)}, u32[]{:S(2)}, u32[]{:S(2)}) collective-permute-start(f32[3,36,2,256]{3,2,1,0:T(2,128)S(1)} %get-tuple-element.268), channel_id=1, source_target_pairs={{1,0},{2,1},{3,2},{5,4},{6,5},{7,6},{9,8},{10,9},{11,10},{13,12},{... | collective-permute-start | bytes 663560 | tf_op jit(solution)/shard_map/ppermute | solution.py:30
  163.5 3.2 %fusion.9 = f32[3072,256]{1,0:T(8,128)} fusion(s32[256]{0:T(256)S(1)} %get-tuple-element.295, f32[256]{0:T(256)S(1)} %bitcast.120, s32[256]{0:T(256)S(1)} %get-tuple-element.294), kind=kOutput, calls=%fused_computation.44 | convolution fusion | flops 2416836608 | bytes 3148800 | tf_op jit(solution)/shard_map/dot_general | solution.py:332
  166.8 2.7 %select_maximum_fusion.4.up_ref = f32[3,36,48,256]{3,2,1,0:T(8,128)} fusion(f32[3,36,2,256]{3,2,1,0:T(2,128)S(1)} %collective-permute-done.11, f32[3,36,2,256]{3,2,1,0:T(2,128)S(1)} %collective-permute-done.10, f32[3,2,32,256]{3,2,1,0:T(8,128)S(1)} %collective-permute-done.9, f32[3,32,32,256]{3,2,1,0:T(8,128)S(1)} %copy-done, ...), kind=kLoop, calls=%fused_computation.31 | loop fusion | flops 15925248 | bytes 9289728 | tf_op jit(solution)/shard_map/concatenate | solution.py:31
  169.5 14.3 %shard_map.124 = f32[3,32,32,256]{3,2,1,0:T(8,128)} custom-call(f32[3,36,48,256]{3,2,1,0:T(8,128)} %select_maximum_fusion.4.up_ref, f32[3,32,32,256]{3,2,1,0:T(8,128)} %shard_map.122.prev_ref, f32[2,32,32,256]{3,2,1,0:T(8,128)} %mod_ref.7, f32[3,32,32,256]{3,2,1,0:T(8,128)} %bitcast.110), custom_call_target="tpu_custom_call" | custom-call | tf_op jit(solution)/shard_map/pallas_call | solution.py:112
  185.0 2.3 %collective-permute-start.12 = (f32[3,2,32,256]{3,2,1,0:T(8,128)S(1)}, f32[3,2,32,256]{3,2,1,0:T(8,128)S(1)}, u32[]{:S(2)}, u32[]{:S(2)}) collective-permute-start(f32[3,2,32,256]{3,2,1,0:T(8,128)S(1)} %get-tuple-element.273), channel_id=1, source_target_pairs={{0,4},{4,8},{8,12},{12,16},{16,20},{20,24},{24,28},{1,5},{5,9},{9,... | collective-permute-start | bytes 589832 | tf_op jit(solution)/shard_map/ppermute | solution.py:27
  187.4 4.4 %collective-permute-start.13 = (f32[3,2,32,256]{3,2,1,0:T(8,128)S(1)}, f32[3,2,32,256]{3,2,1,0:T(8,128)S(1)}, u32[]{:S(2)}, u32[]{:S(2)}) collective-permute-start(f32[3,2,32,256]{3,2,1,0:T(8,128)S(1)} %get-tuple-element.274), channel_id=1, source_target_pairs={{4,0},{8,4},{12,8},{16,12},{20,16},{24,20},{28,24},{5,1},{9,5},{13... | collective-permute-start | bytes 589832 | tf_op jit(solution)/shard_map/ppermute | solution.py:30
  191.8 1.7 collective-permute-done.12
  193.5 4.1 %collective-permute-done.13 = f32[3,2,32,256]{3,2,1,0:T(8,128)S(1)} collective-permute-done((f32[3,2,32,256]{3,2,1,0:T(8,128)S(1)}, f32[3,2,32,256]{3,2,1,0:T(8,128)S(1)}, u32[]{:S(2)}, u32[]{:S(2)}) %collective-permute-start.13) | collective-permute-done | bytes 196640 | tf_op jit(solution)/shard_map/ppermute | solution.py:30
  199.2 1.9 collective-permute-start.14
  201.1 3.6 %collective-permute-start.15 = (f32[3,36,2,256]{3,2,1,0:T(2,128)S(1)}, f32[3,36,2,256]{3,2,1,0:T(2,128)S(1)}, u32[]{:S(2)}, u32[]{:S(2)}) collective-permute-start(f32[3,36,2,256]{3,2,1,0:T(2,128)S(1)} %get-tuple-element.266), channel_id=1, source_target_pairs={{1,0},{2,1},{3,2},{5,4},{6,5},{7,6},{9,8},{10,9},{11,10},{13,12},{... | collective-permute-start | bytes 663560 | tf_op jit(solution)/shard_map/ppermute | solution.py:30
  204.7 3.2 %fusion.8 = f32[3072,256]{1,0:T(8,128)} fusion(s32[256]{0:T(256)S(1)} %get-tuple-element.295, f32[256]{0:T(256)S(1)} %bitcast.119, s32[256]{0:T(256)S(1)} %get-tuple-element.294), kind=kOutput, calls=%fused_computation.43 | convolution fusion | flops 2416836608 | bytes 3148800 | tf_op jit(solution)/shard_map/dot_general | solution.py:332
  208.2 2.7 %select_maximum_fusion.up_ref = f32[3,36,48,256]{3,2,1,0:T(8,128)} fusion(f32[3,36,2,256]{3,2,1,0:T(2,128)S(1)} %collective-permute-done.15, f32[3,36,2,256]{3,2,1,0:T(2,128)S(1)} %collective-permute-done.14, f32[3,2,32,256]{3,2,1,0:T(8,128)S(1)} %collective-permute-done.13, f32[3,32,32,256]{3,2,1,0:T(8,128)S(1)} %copy-done.2, ...), kind=kLoop, calls=%fused_computation.27 | loop fusion | flops 15925248 | bytes 9289728 | tf_op jit(solution)/shard_map/concatenate | solution.py:31
  210.9 14.3 %shard_map.125 = f32[3,32,32,256]{3,2,1,0:T(8,128)} custom-call(f32[3,36,48,256]{3,2,1,0:T(8,128)} %select_maximum_fusion.up_ref, f32[3,32,32,256]{3,2,1,0:T(8,128)} %shard_map.123.prev_ref, f32[2,32,32,256]{3,2,1,0:T(8,128)} %mod_ref.7, f32[3,32,32,256]{3,2,1,0:T(8,128)} %bitcast.109), custom_call_target="tpu_custom_call" | custom-call | tf_op jit(solution)/shard_map/pallas_call | solution.py:112
  (103 shorter events, 21.0 us)
Async XLA Ops:
  2.5 33.8 %collective-permute-start = (f32[3,2,32,256]{3,2,1,0:T(8,128)}, f32[3,2,32,256]{3,2,1,0:T(8,128)S(1)}, u32[]{:S(2)}, u32[]{:S(2)}) collective-permute-start(f32[3,2,32,256]{3,2,1,0:T(8,128)} %get-tuple-element.279), channel_id=1, source_target_pairs={{0,4},{4,8},{8,12},{12,16},{16,20},{20,24},{24,28},{1,5},{5,9},{9,... | collective-permute-start | bytes 589832 | tf_op jit(solution)/shard_map/ppermute | solution.py:27
  5.8 31.1 %collective-permute-start.1 = (f32[3,2,32,256]{3,2,1,0:T(8,128)}, f32[3,2,32,256]{3,2,1,0:T(8,128)}, u32[]{:S(2)}, u32[]{:S(2)}) collective-permute-start(f32[3,2,32,256]{3,2,1,0:T(8,128)} %get-tuple-element.280), channel_id=1, source_target_pairs={{4,0},{8,4},{12,8},{16,12},{20,16},{24,20},{28,24},{5,1},{9,5},{13... | collective-permute-start | bytes 589832 | tf_op jit(solution)/shard_map/ppermute | solution.py:30
  19.8 10.1 %copy-start.4 = (s32[8192]{0:T(1024)S(1)}, s32[8192]{0:T(1024)}, u32[]{:S(2)}) copy-start(s32[8192]{0:T(1024)} %param.19) | copy-start | bytes 98308
  19.8 10.7 %copy-start.5 = (s32[8192]{0:T(1024)S(1)}, s32[8192]{0:T(1024)}, u32[]{:S(2)}) copy-start(s32[8192]{0:T(1024)} %param.20) | copy-start | bytes 98308
  26.3 10.0 %copy-start.6 = (s32[256]{0:T(256)S(1)}, s32[256]{0:T(256)}, u32[]{:S(2)}) copy-start(s32[256]{0:T(256)} %param.21) | copy-start | bytes 3076
  36.3 0.7 copy-start.3
  40.2 25.4 %collective-permute-start.2 = (f32[3,36,2,256]{3,2,1,0:T(2,128)}, f32[3,36,2,256]{3,2,1,0:T(2,128)}, u32[]{:S(2)}, u32[]{:S(2)}) collective-permute-start(f32[3,36,2,256]{3,2,1,0:T(2,128)} %get-tuple-element.271), channel_id=1, source_target_pairs={{0,1},{1,2},{2,3},{4,5},{5,6},{6,7},{8,9},{9,10},{10,11},{12,13},{... | collective-permute-start | bytes 663560 | tf_op jit(solution)/shard_map/ppermute | solution.py:27
  42.1 23.5 %collective-permute-start.3 = (f32[3,36,2,256]{3,2,1,0:T(2,128)}, f32[3,36,2,256]{3,2,1,0:T(2,128)}, u32[]{:S(2)}, u32[]{:S(2)}) collective-permute-start(f32[3,36,2,256]{3,2,1,0:T(2,128)} %get-tuple-element.272), channel_id=1, source_target_pairs={{1,0},{2,1},{3,2},{5,4},{6,5},{7,6},{9,8},{10,9},{11,10},{13,12},{... | collective-permute-start | bytes 663560 | tf_op jit(solution)/shard_map/ppermute | solution.py:30
  70.1 11.6 %all-to-all-start = ((bf16[2,4,32,256]{3,1,0,2:T(4,128)(2,1)}), bf16[2,4,32,256]{3,1,0,2:T(4,128)(2,1)S(1)}, u32[]{:S(2)}, u32[]{:S(2)}) async-start(bf16[2,4,32,256]{3,1,0,2:T(4,128)(2,1)} %bitcast.95), calls=%async_computation | async-start | bytes 262144 | tf_op jit(solution)/shard_map/all_to_all | solution.py:309
  99.6 25.9 %copy-start.1 = (f32[3,32,32,256]{3,2,1,0:T(8,128)S(1)}, f32[3,32,32,256]{3,2,1,0:T(8,128)}, u32[]{:S(2)}) copy-start(f32[3,32,32,256]{3,2,1,0:T(8,128)} %shard_map.122.prev_ref) | copy-start | bytes 9437188
  100.8 10.0 %collective-permute-start.4 = (f32[3,2,32,256]{3,2,1,0:T(8,128)S(1)}, f32[3,2,32,256]{3,2,1,0:T(8,128)S(1)}, u32[]{:S(2)}, u32[]{:S(2)}) collective-permute-start(f32[3,2,32,256]{3,2,1,0:T(8,128)S(1)} %get-tuple-element.277), channel_id=1, source_target_pairs={{0,4},{4,8},{8,12},{12,16},{16,20},{20,24},{24,28},{1,5},{5,9},{9,... | collective-permute-start | bytes 589832 | tf_op jit(solution)/shard_map/ppermute | solution.py:27
  104.0 11.0 %collective-permute-start.5 = (f32[3,2,32,256]{3,2,1,0:T(8,128)S(1)}, f32[3,2,32,256]{3,2,1,0:T(8,128)S(1)}, u32[]{:S(2)}, u32[]{:S(2)}) collective-permute-start(f32[3,2,32,256]{3,2,1,0:T(8,128)S(1)} %get-tuple-element.278), channel_id=1, source_target_pairs={{4,0},{8,4},{12,8},{16,12},{20,16},{24,20},{28,24},{5,1},{9,5},{13... | collective-permute-start | bytes 589832 | tf_op jit(solution)/shard_map/ppermute | solution.py:30
  116.5 8.8 %collective-permute-start.6 = (f32[3,36,2,256]{3,2,1,0:T(2,128)S(1)}, f32[3,36,2,256]{3,2,1,0:T(2,128)S(1)}, u32[]{:S(2)}, u32[]{:S(2)}) collective-permute-start(f32[3,36,2,256]{3,2,1,0:T(2,128)S(1)} %get-tuple-element.269), channel_id=1, source_target_pairs={{0,1},{1,2},{2,3},{4,5},{5,6},{6,7},{8,9},{9,10},{10,11},{12,13},{... | collective-permute-start | bytes 663560 | tf_op jit(solution)/shard_map/ppermute | solution.py:27
  118.4 7.1 %collective-permute-start.7 = (f32[3,36,2,256]{3,2,1,0:T(2,128)S(1)}, f32[3,36,2,256]{3,2,1,0:T(2,128)S(1)}, u32[]{:S(2)}, u32[]{:S(2)}) collective-permute-start(f32[3,36,2,256]{3,2,1,0:T(2,128)S(1)} %get-tuple-element.270), channel_id=1, source_target_pairs={{1,0},{2,1},{3,2},{5,4},{6,5},{7,6},{9,8},{10,9},{11,10},{13,12},{... | collective-permute-start | bytes 663560 | tf_op jit(solution)/shard_map/ppermute | solution.py:30
  142.6 24.2 %copy-start = (f32[3,32,32,256]{3,2,1,0:T(8,128)S(1)}, f32[3,32,32,256]{3,2,1,0:T(8,128)}, u32[]{:S(2)}) copy-start(f32[3,32,32,256]{3,2,1,0:T(8,128)} %shard_map.123.prev_ref) | copy-start | bytes 9437188
  143.8 8.5 %collective-permute-start.8 = (f32[3,2,32,256]{3,2,1,0:T(8,128)S(1)}, f32[3,2,32,256]{3,2,1,0:T(8,128)S(1)}, u32[]{:S(2)}, u32[]{:S(2)}) collective-permute-start(f32[3,2,32,256]{3,2,1,0:T(8,128)S(1)} %get-tuple-element.275), channel_id=1, source_target_pairs={{0,4},{4,8},{8,12},{12,16},{16,20},{20,24},{24,28},{1,5},{5,9},{9,... | collective-permute-start | bytes 589832 | tf_op jit(solution)/shard_map/ppermute | solution.py:27
  145.8 10.4 %collective-permute-start.9 = (f32[3,2,32,256]{3,2,1,0:T(8,128)S(1)}, f32[3,2,32,256]{3,2,1,0:T(8,128)S(1)}, u32[]{:S(2)}, u32[]{:S(2)}) collective-permute-start(f32[3,2,32,256]{3,2,1,0:T(8,128)S(1)} %get-tuple-element.276), channel_id=1, source_target_pairs={{4,0},{8,4},{12,8},{16,12},{20,16},{24,20},{28,24},{5,1},{9,5},{13... | collective-permute-start | bytes 589832 | tf_op jit(solution)/shard_map/ppermute | solution.py:30
  157.7 9.0 %collective-permute-start.10 = (f32[3,36,2,256]{3,2,1,0:T(2,128)S(1)}, f32[3,36,2,256]{3,2,1,0:T(2,128)S(1)}, u32[]{:S(2)}, u32[]{:S(2)}) collective-permute-start(f32[3,36,2,256]{3,2,1,0:T(2,128)S(1)} %get-tuple-element.267), channel_id=1, source_target_pairs={{0,1},{1,2},{2,3},{4,5},{5,6},{6,7},{8,9},{9,10},{10,11},{12,13},{... | collective-permute-start | bytes 663560 | tf_op jit(solution)/shard_map/ppermute | solution.py:27
  159.7 7.1 %collective-permute-start.11 = (f32[3,36,2,256]{3,2,1,0:T(2,128)S(1)}, f32[3,36,2,256]{3,2,1,0:T(2,128)S(1)}, u32[]{:S(2)}, u32[]{:S(2)}) collective-permute-start(f32[3,36,2,256]{3,2,1,0:T(2,128)S(1)} %get-tuple-element.268), channel_id=1, source_target_pairs={{1,0},{2,1},{3,2},{5,4},{6,5},{7,6},{9,8},{10,9},{11,10},{13,12},{... | collective-permute-start | bytes 663560 | tf_op jit(solution)/shard_map/ppermute | solution.py:30
  183.8 24.4 %copy-start.2 = (f32[3,32,32,256]{3,2,1,0:T(8,128)S(1)}, f32[3,32,32,256]{3,2,1,0:T(8,128)}, u32[]{:S(2)}) copy-start(f32[3,32,32,256]{3,2,1,0:T(8,128)} %shard_map.124) | copy-start | bytes 9437188
  185.0 8.5 %collective-permute-start.12 = (f32[3,2,32,256]{3,2,1,0:T(8,128)S(1)}, f32[3,2,32,256]{3,2,1,0:T(8,128)S(1)}, u32[]{:S(2)}, u32[]{:S(2)}) collective-permute-start(f32[3,2,32,256]{3,2,1,0:T(8,128)S(1)} %get-tuple-element.273), channel_id=1, source_target_pairs={{0,4},{4,8},{8,12},{12,16},{16,20},{20,24},{24,28},{1,5},{5,9},{9,... | collective-permute-start | bytes 589832 | tf_op jit(solution)/shard_map/ppermute | solution.py:27
  187.4 10.3 %collective-permute-start.13 = (f32[3,2,32,256]{3,2,1,0:T(8,128)S(1)}, f32[3,2,32,256]{3,2,1,0:T(8,128)S(1)}, u32[]{:S(2)}, u32[]{:S(2)}) collective-permute-start(f32[3,2,32,256]{3,2,1,0:T(8,128)S(1)} %get-tuple-element.274), channel_id=1, source_target_pairs={{4,0},{8,4},{12,8},{16,12},{20,16},{24,20},{28,24},{5,1},{9,5},{13... | collective-permute-start | bytes 589832 | tf_op jit(solution)/shard_map/ppermute | solution.py:30
  199.2 8.8 %collective-permute-start.14 = (f32[3,36,2,256]{3,2,1,0:T(2,128)S(1)}, f32[3,36,2,256]{3,2,1,0:T(2,128)S(1)}, u32[]{:S(2)}, u32[]{:S(2)}) collective-permute-start(f32[3,36,2,256]{3,2,1,0:T(2,128)S(1)} %get-tuple-element.265), channel_id=1, source_target_pairs={{0,1},{1,2},{2,3},{4,5},{5,6},{6,7},{8,9},{9,10},{10,11},{12,13},{... | collective-permute-start | bytes 663560 | tf_op jit(solution)/shard_map/ppermute | solution.py:27
  201.1 7.1 %collective-permute-start.15 = (f32[3,36,2,256]{3,2,1,0:T(2,128)S(1)}, f32[3,36,2,256]{3,2,1,0:T(2,128)S(1)}, u32[]{:S(2)}, u32[]{:S(2)}) collective-permute-start(f32[3,36,2,256]{3,2,1,0:T(2,128)S(1)} %get-tuple-element.266), channel_id=1, source_target_pairs={{1,0},{2,1},{3,2},{5,4},{6,5},{7,6},{9,8},{10,9},{11,10},{13,12},{... | collective-permute-start | bytes 663560 | tf_op jit(solution)/shard_map/ppermute | solution.py:30

commit v5 on v2

--- a/solution.py
+++ b/solution.py
@@ -35,8 +35,23 @@
 YPAD = 8
 
 
-def step_kernel(up_ref, prev_ref, mod_ref, src_ref, out_ref, *, bx):
+def step_kernel(u_ref, xlo_ref, xhi_ref, ylo_ref, yhi_ref, prev_ref, mod_ref, src_ref, out_ref, up_ref, *, bx):
     i = pl.program_id(0)
+    nx, ny = u_ref.shape[1], u_ref.shape[2]
+
+    @pl.when(i == 0)
+    def _():
+        for c in range(3):
+            def fill(x, carry):
+                up_ref[c, x + 2, pl.ds(YPAD, ny), :] = u_ref[c, x]
+                return carry
+
+            lax.fori_loop(0, nx, fill, 0)
+        up_ref[:, 0:2, pl.ds(YPAD, ny), :] = xlo_ref[...]
+        up_ref[:, nx + 2:nx + 4, pl.ds(YPAD, ny), :] = xhi_ref[...]
+        up_ref[:, :, pl.ds(YPAD - 2, 2), :] = ylo_ref[...]
+        up_ref[:, :, pl.ds(YPAD + ny, 2), :] = yhi_ref[...]
+
     depth = out_ref.shape[3]
     lane = lax.broadcasted_iota(jnp.int32, (8, depth), 1)
     masks = {dz: (lane + dz >= 0) & (lane + dz < depth) for dz in (-2, -1, 1, 2)}
@@ -104,23 +119,45 @@
     lax.fori_loop(0, bx, plane, 0)
 
 
-def elastic_step(upad, prev, moduli, sources, bx=8):
-    _, px, py, depth = upad.shape
-    nx, ny = px - 4, py - 2 * YPAD
+def elastic_step(u, xlo, xhi, ylo, yhi, prev, moduli, sources, bx=8):
+    _, nx, ny, depth = u.shape
     kernel = functools.partial(step_kernel, bx=bx)
     block = lambda i: (0, i, 0, 0)
+    whole = lambda i: (0, 0, 0, 0)
     return pl.pallas_call(
         kernel,
         grid=(nx // bx,),
         in_specs=[
-            pl.BlockSpec((3, px, py, depth), lambda i: (0, 0, 0, 0)),
+            pl.BlockSpec(u.shape, whole),
+            pl.BlockSpec(xlo.shape, whole),
+            pl.BlockSpec(xhi.shape, whole),
+            pl.BlockSpec(ylo.shape, whole),
+            pl.BlockSpec(yhi.shape, whole),
             pl.BlockSpec((3, bx, ny, depth), block),
             pl.BlockSpec((2, bx, ny, depth), block),
             pl.BlockSpec((3, bx, ny, depth), block),
         ],
         out_specs=pl.BlockSpec((3, bx, ny, depth), block),
         out_shape=jax.ShapeDtypeStruct((3, nx, ny, depth), jnp.float32),
-    )(upad, prev, moduli, sources)
+        scratch_shapes=[pltpu.VMEM((3, nx + 4, ny + 2 * YPAD, depth), jnp.float32)],
+        compiler_params=pltpu.CompilerParams(dimension_semantics=("arbitrary",)),
+    )(u, xlo, xhi, ylo, yhi, prev, moduli, sources)
+
+
+def halos(block, width):
+    size_x = lax.axis_size("gx")
+    size_y = lax.axis_size("gy")
+    nx, ny = block.shape[1], block.shape[2]
+    forward_x = [(i, i + 1) for i in range(size_x - 1)]
+    backward_x = [(t, s) for s, t in forward_x]
+    xlo = lax.ppermute(block[:, nx - width:], "gx", forward_x)
+    xhi = lax.ppermute(block[:, :width], "gx", backward_x)
+    forward_y = [(i, i + 1) for i in range(size_y - 1)]
+    backward_y = [(t, s) for s, t in forward_y]
+    rows = lambda sl: jnp.concatenate([xlo[:, :, sl], block[:, :, sl], xhi[:, :, sl]], axis=1)
+    ylo = lax.ppermute(rows(slice(ny - width, ny)), "gy", forward_y)
+    yhi = lax.ppermute(rows(slice(0, width)), "gy", backward_y)
+    return xlo, xhi, ylo, yhi
 
 
 def level_table(values, layer_of_level):
@@ -327,9 +364,8 @@
         spread = weighted[instant][:, None] * depth_hot
         source = jnp.dot(column_hot, spread, precision=lax.Precision.HIGHEST)
         source = source.reshape(3, block_x, block_y, depth)
-        padded = padded_2(current, (("gx", 1), ("gy", 2)), 2)
-        padded = jnp.pad(padded, ((0, 0), (0, 0), (YPAD - 2, YPAD - 2), (0, 0)))
-        advanced = elastic_step(padded, previous, moduli, source)
+        xlo, xhi, ylo, yhi = halos(current, 2)
+        advanced = elastic_step(current, xlo, xhi, ylo, yhi, previous, moduli, source)
         previous, current = (current, advanced)
     return (current, previous)
 

time: 225 us -> 203 us (0.902); the launches traced: 222 us -> 203 us
  other arithmetic: 36.8 us -> 20.6 us
  matrix products: 34.2 us -> 29.6 us
  waiting for transfers between devices: 24.1 us -> 20.6 us
  local copies, waits for them, and re-layouts: 12.1 us -> 15 us
    concatenate x4 -> x8, other arithmetic: 11.8 us -> 0.83 us  [halos(): jnp.concatenate([xlo[:, :, sl], block[:, :, sl], xhi[:, :, sl]], axis=1)]
    slice x5 -> x16, local copies, waits for them, and re-layouts: 4.53 us -> 10.3 us  [the longest x4 6.06 us: halos(): block[:, :, sl]]
    slice x3 -> x0, other arithmetic: 4.63 us -> none  [padded_2(): lax.slice_in_dim(block, block.shape[dim] - width, None, axis=dim)]
    ppermute x16, waiting for transfers between devices: 24.1 us -> 20.6 us  [the longest x4 11.5 us: halos(): xhi = lax.ppermute(block[:, :width], 'gx', backward_x)]
    dot_general x2, matrix products: 15.8 us -> 13.1 us  [select_block(): jnp.dot(table_rounded, offset_hot, preferred_element_type=jnp.float32)]
  transfers between devices with their start and end apart: 17 -> 17, of which waited for: 11 -> 12; matrix products, arithmetic and copies ran while one was open for 9% -> 10% of each run, Pallas kernels for 0% -> 0%
where the time goes in v5:
time: 203 us
  Pallas kernels  58.5 us (29%)
  starting transfers between devices  55.9 us (28%)
  matrix products  29.6 us (15%)
  other arithmetic  20.6 us (10%)
  waiting for transfers between devices  20.6 us (10%)
  local copies, waits for them, and re-layouts  15 us (7%)
    pallas_call x4, Pallas kernels, elastic_step(): pl.pallas_call(kernel, grid=(nx // bx,), in_specs=[pl.BlockSpec(u.shape,...  58.5 us
    ppermute x4, starting transfers between devices, halos(): xhi = lax.ppermute(block[:, :width], 'gx', backward_x)  16.3 us
    ppermute x4, starting transfers between devices, halos(): yhi = lax.ppermute(rows(slice(0, width)), 'gy', backward_y)  15.1 us
    dot_general x2, matrix products, select_block(): jnp.dot(table_rounded, offset_hot, preferred_element_type=jnp.float32)  13.1 us
    dot_general x4, matrix products, shards(): source = jnp.dot(column_hot, spread, precision=lax.Precision.HIGHEST)  12.9 us
    ppermute x4, waiting for transfers between devices, halos(): xhi = lax.ppermute(block[:, :width], 'gx', backward_x)  11.5 us
    ppermute x4, starting transfers between devices, halos(): xlo = lax.ppermute(block[:, nx - width:], 'gx', forward_x)  10.7 us
    ppermute x4, starting transfers between devices, halos(): ylo = lax.ppermute(rows(slice(ny - width, ny)), 'gy', forward_y)  7.91 us
  transfers between devices with their start and end apart: 17, of which 12 were waited for; matrix products, arithmetic and copies ran while one was open for 10% of the time, Pallas kernels for 0%

profile of v5, /device:TPU:12, one launch (start us, length us, event | category | flops | bytes accessed | tf_op | source)
XLA Modules:
  0.0 202.6 jit_solution(2531469600852223828)
XLA Ops:
  2.9 4.9 %sine_multiply_fusion.1 = (f32[32,4,1024]{2,1,0:T(4,128)S(1)}, f32[32,4,1024]{2,1,0:T(4,128)S(1)}, f32[32,4,1024]{2,1,0:T(4,128)S(1)}) fusion(f32[32]{0:T(128)S(1)} %get-tuple-element.307, f32[32,4]{1,0:T(8,128)S(1)} %copy.24, f32[1024]{0:T(1024)S(1)} %multiply_multiply_fusion, f32[1,4,1024]{2,1,0:T(4,128)S(1)} %slice.157, f32[31,4,1024]{2,1,0:T(4,128)S(1)} %slice.156, ...), kind=kLoop, calls=%fused_computation.41 | loop fusion | flops 1441792 | bytes 2102016 | tf_op jit(solution)/shard_map/mul | solution.py:180
  8.1 2.2 %while.32 = (s32[]{:T(128)}, f32[4,1024]{1,0:T(4,128)S(1)}, f32[4,1024]{1,0:T(4,128)S(1)}, f32[32,4,1024]{2,1,0:T(4,128)S(1)}, f32[32,4,1024]{2,1,0:T(4,128)S(1)...) while((s32[]{:T(128)}, f32[4,1024]{1,0:T(4,128)S(1)}, ...), condition=%wide.region_6.7_spmd.clone, body=%wide.region_5.6_spmd.clone.sunk | while | flops 94212 | bytes 147591 | solution.py:196
  11.2 4.3 %fusion.43 = (bf16[1,32,4,1024]{3,2,1,0:T(4,128)(2,1)S(1)}, bf16[1,32,4,1024]{3,2,1,0:T(4,128)(2,1)S(1)}) fusion(f32[32,4,1024]{2,1,0:T(4,128)S(1)} %get-tuple-element.191, f32[32,4,1024]{2,1,0:T(4,128)S(1)} %get-tuple-element.190, f32[32,4,1024]{2,1,0:T(4,128)S(1)} %negate_exponential_fusion, f32[32,4,1024]{2,1,0:T(4,128)S(1)} %fusion.23), kind=kLoop, calls=%fused_computation.74 | loop fusion | flops 1835008 | bytes 2621440 | tf_op jit(solution)/shard_map/stack | solution.py:209
  17.7 3.6 %subtract_convert_fusion = bf16[1024,32,64]{0,2,1:T(8,128)(2,1)} fusion(f32[1024,64]{0,1:T(8,128)S(1)} %get-tuple-element.301, f32[1024,32]{0,1:T(8,128)S(1)} %get-tuple-element.295, f32[1024,64]{0,1:T(8,128)S(1)} %get-tuple-element.300, f32[1024,32]{0,1:T(8,128)S(1)} %get-tuple-element.294), kind=kLoop, calls=%fused_computation.24 | loop fusion | flops 8388608 | bytes 4980736 | tf_op jit(solution)/shard_map/convert_element_type | solution.py:224
  21.4 3.5 %convolution_convert_fusion = bf16[256,2048]{1,0:T(8,128)(2,1)S(1)} fusion(bf16[256,1024]{1,0:T(8,128)(2,1)S(1)} %bitcast.109, bf16[1024,2048]{0,1:T(8,128)(2,1)} %bitcast.107), kind=kOutput, calls=%fused_computation.30 | convolution fusion | flops 1074266112 | bytes 5767168 | tf_op jit(solution)/shard_map/dot_general | solution.py:312
  24.9 13.4 %while.31 = (s32[]{:T(128)}, bf16[2,2,4,4096]{3,2,1,0:T(4,128)(2,1)S(1)}, s32[2,4096]{1,0:T(2,128)S(1)}, bf16[256,2048]{1,0:T(8,128)(2,1)S(1)}, s32[2,4096]{1,0:T(2,128)S(1)}, /*index=5*/s32[]{:T(128)}) while((s32[]{:T(128)}, bf16[2,2,4,4096]{3,2,1,0:T(4,128)(2,1)S(1)}, s32[2,4096]{1,0:T(2,128)S(1)}, bf16[256,2048]{1,0:T(8,128)(2,1)S(1)}, ...), condition=%wide.region_9.10_spmd, body=%wide.region_7.9_spmd.sunk | while | flops 4305682432 | bytes 2392141 | solution.py:335
  25.0 6.5 %multiply_reduce_fusion.2 = bf16[2,4,4096]{2,1,0:T(4,128)(2,1)S(1)} fusion(f32[32,4096]{1,0:T(8,128)S(1)} %fusion.102, bf16[256,2048]{1,0:T(8,128)(2,1)S(1)} %get-tuple-element.448, s32[4096]{0:T(1024)S(1)} %bitcast.111), kind=kOutput, calls=%fused_computation.3.clone.1 | convolution fusion | flops 4305420288 | bytes 1654784 | tf_op jit(solution)/shard_map/while/body/eval_jaxpr/dot_general | solution.py:327
  31.7 6.5 %multiply_reduce_fusion.2 = bf16[2,4,4096]{2,1,0:T(4,128)(2,1)S(1)} fusion(f32[32,4096]{1,0:T(8,128)S(1)} %fusion.102, bf16[256,2048]{1,0:T(8,128)(2,1)S(1)} %get-tuple-element.448, s32[4096]{0:T(1024)S(1)} %bitcast.111), kind=kOutput, calls=%fused_computation.3.clone.1 | convolution fusion | flops 4305420288 | bytes 1654784 | tf_op jit(solution)/shard_map/while/body/eval_jaxpr/dot_general | solution.py:327
  39.3 6.0 %all-to-all-start = ((bf16[2,4,32,256]{3,1,0,2:T(4,128)(2,1)}), bf16[2,4,32,256]{3,1,0,2:T(4,128)(2,1)S(1)}, u32[]{:S(2)}, u32[]{:S(2)}) async-start(bf16[2,4,32,256]{3,1,0,2:T(4,128)(2,1)} %copy.27), calls=%async_computation | async-start | bytes 262144 | tf_op jit(solution)/shard_map/all_to_all | solution.py:342
  45.3 1.1 fusion.85
  46.3 3.4 %collective-permute-start = (f32[3,2,32,256]{3,2,1,0:T(8,128)S(1)}, f32[3,2,32,256]{3,2,1,0:T(8,128)S(1)}, u32[]{:S(2)}, u32[]{:S(2)}) collective-permute-start(f32[3,2,32,256]{3,2,1,0:T(8,128)S(1)} %get-tuple-element.272), channel_id=1, source_target_pairs={{0,4},{4,8},{8,12},{12,16},{16,20},{20,24},{24,28},{1,5},{5,9},{9,... | collective-permute-start | bytes 589832 | tf_op jit(solution)/shard_map/ppermute | solution.py:153
  49.7 3.4 %collective-permute-start.1 = (f32[3,2,32,256]{3,2,1,0:T(8,128)S(1)}, f32[3,2,32,256]{3,2,1,0:T(8,128)S(1)}, u32[]{:S(2)}, u32[]{:S(2)}) collective-permute-start(f32[3,2,32,256]{3,2,1,0:T(8,128)S(1)} %get-tuple-element.271), channel_id=1, source_target_pairs={{4,0},{8,4},{12,8},{16,12},{20,16},{24,20},{28,24},{5,1},{9,5},{13... | collective-permute-start | bytes 589832 | tf_op jit(solution)/shard_map/ppermute | solution.py:154
  53.1 1.5 fusion.84
  56.0 4.2 %collective-permute-done.1.xhi_ref = f32[3,2,32,256]{3,2,1,0:T(8,128)S(1)} collective-permute-done((f32[3,2,32,256]{3,2,1,0:T(8,128)S(1)}, f32[3,2,32,256]{3,2,1,0:T(8,128)S(1)}, u32[]{:S(2)}, u32[]{:S(2)}) %collective-permute-start.1) | collective-permute-done | bytes 196640 | tf_op jit(solution)/shard_map/ppermute | solution.py:154
  60.4 2.2 %collective-permute-start.3 = (f32[3,36,2,256]{3,2,1,0:T(2,128)S(1)}, f32[3,36,2,256]{3,2,1,0:T(2,128)S(1)}, u32[]{:S(2)}, u32[]{:S(2)}) collective-permute-start(f32[3,36,2,256]{3,2,1,0:T(2,128)S(1)} %pad_maximum_fusion.2), channel_id=1, source_target_pairs={{1,0},{2,1},{3,2},{5,4},{6,5},{7,6},{9,8},{10,9},{11,10},{13,12},{... | collective-permute-start | bytes 663560 | tf_op jit(solution)/shard_map/ppermute | solution.py:159
  62.7 2.1 %collective-permute-start.2 = (f32[3,36,2,256]{3,2,1,0:T(2,128)S(1)}, f32[3,36,2,256]{3,2,1,0:T(2,128)S(1)}, u32[]{:S(2)}, u32[]{:S(2)}) collective-permute-start(f32[3,36,2,256]{3,2,1,0:T(2,128)S(1)} %pad_maximum_fusion.1), channel_id=1, source_target_pairs={{0,1},{1,2},{2,3},{4,5},{5,6},{6,7},{8,9},{9,10},{10,11},{12,13},{... | collective-permute-start | bytes 663560 | tf_op jit(solution)/shard_map/ppermute | solution.py:158
  65.1 3.2 %fusion.10 = f32[3072,256]{1,0:T(8,128)} fusion(s32[256]{0:T(256)S(1)} %get-tuple-element.303, f32[256]{0:T(256)S(1)} %bitcast.116, s32[256]{0:T(256)S(1)} %get-tuple-element.302), kind=kOutput, calls=%fused_computation.29 | convolution fusion | flops 2416836608 | bytes 3148800 | tf_op jit(solution)/shard_map/dot_general | solution.py:365
  68.4 1.6 collective-permute-done.2.ylo_ref
  70.6 14.6 %shard_map.122.u_ref.prev_ref = f32[3,32,32,256]{3,2,1,0:T(8,128)} custom-call(f32[3,32,32,256]{3,2,1,0:T(8,128)} %prev_ref.3, f32[3,2,32,256]{3,2,1,0:T(8,128)} %copy-done, f32[3,2,32,256]{3,2,1,0:T(8,128)} %copy-done.1, f32[3,36,2,256]{3,2,1,0:T(2,128)} %copy-done.9, f32[3,36,2,256]{3,2,1,0:T(2,128)} %copy-done.8, f32[3,32,32,256]{3,2,1,0:T(8,128)} %prev_ref.2, ...), custom_call_target="tpu_custom_call" | custom-call | tf_op jit(solution)/shard_map/pallas_call | solution.py:127
  85.3 1.0 fusion.83
  86.3 2.2 %collective-permute-start.4 = (f32[3,2,32,256]{3,2,1,0:T(8,128)S(1)}, f32[3,2,32,256]{3,2,1,0:T(8,128)S(1)}, u32[]{:S(2)}, u32[]{:S(2)}) collective-permute-start(f32[3,2,32,256]{3,2,1,0:T(8,128)S(1)} %get-tuple-element.268), channel_id=1, source_target_pairs={{0,4},{4,8},{8,12},{12,16},{16,20},{20,24},{24,28},{1,5},{5,9},{9,... | collective-permute-start | bytes 589832 | tf_op jit(solution)/shard_map/ppermute | solution.py:153
  88.6 4.5 %collective-permute-start.5 = (f32[3,2,32,256]{3,2,1,0:T(8,128)S(1)}, f32[3,2,32,256]{3,2,1,0:T(8,128)S(1)}, u32[]{:S(2)}, u32[]{:S(2)}) collective-permute-start(f32[3,2,32,256]{3,2,1,0:T(8,128)S(1)} %get-tuple-element.267), channel_id=1, source_target_pairs={{4,0},{8,4},{12,8},{16,12},{20,16},{24,20},{28,24},{5,1},{9,5},{13... | collective-permute-start | bytes 589832 | tf_op jit(solution)/shard_map/ppermute | solution.py:154
  93.1 1.5 fusion.82
  94.9 3.1 %collective-permute-done.5.xhi_ref = f32[3,2,32,256]{3,2,1,0:T(8,128)S(1)} collective-permute-done((f32[3,2,32,256]{3,2,1,0:T(8,128)S(1)}, f32[3,2,32,256]{3,2,1,0:T(8,128)S(1)}, u32[]{:S(2)}, u32[]{:S(2)}) %collective-permute-start.5) | collective-permute-done | bytes 196640 | tf_op jit(solution)/shard_map/ppermute | solution.py:154
  98.1 3.8 %collective-permute-start.7 = (f32[3,36,2,256]{3,2,1,0:T(2,128)S(1)}, f32[3,36,2,256]{3,2,1,0:T(2,128)S(1)}, u32[]{:S(2)}, u32[]{:S(2)}) collective-permute-start(f32[3,36,2,256]{3,2,1,0:T(2,128)S(1)} %pad_maximum_fusion.4), channel_id=1, source_target_pairs={{1,0},{2,1},{3,2},{5,4},{6,5},{7,6},{9,8},{10,9},{11,10},{13,12},{... | collective-permute-start | bytes 663560 | tf_op jit(solution)/shard_map/ppermute | solution.py:159
  102.0 1.9 collective-permute-start.6
  103.9 3.2 %fusion.9 = f32[3072,256]{1,0:T(8,128)} fusion(s32[256]{0:T(256)S(1)} %get-tuple-element.303, f32[256]{0:T(256)S(1)} %bitcast.115, s32[256]{0:T(256)S(1)} %get-tuple-element.302), kind=kOutput, calls=%fused_computation.28 | convolution fusion | flops 2416836608 | bytes 3148800 | tf_op jit(solution)/shard_map/dot_general | solution.py:365
  107.1 2.1 %collective-permute-done.6.ylo_ref = f32[3,36,2,256]{3,2,1,0:T(2,128)S(1)} collective-permute-done((f32[3,36,2,256]{3,2,1,0:T(2,128)S(1)}, f32[3,36,2,256]{3,2,1,0:T(2,128)S(1)}, u32[]{:S(2)}, u32[]{:S(2)}) %collective-permute-start.6) | collective-permute-done | bytes 221216 | tf_op jit(solution)/shard_map/ppermute | solution.py:158
  109.9 14.6 %shard_map.123.u_ref.prev_ref = f32[3,32,32,256]{3,2,1,0:T(8,128)} custom-call(f32[3,32,32,256]{3,2,1,0:T(8,128)} %shard_map.122.u_ref.prev_ref, f32[3,2,32,256]{3,2,1,0:T(8,128)} %copy-done.4, f32[3,2,32,256]{3,2,1,0:T(8,128)} %copy-done.7, f32[3,36,2,256]{3,2,1,0:T(2,128)} %copy-done.15, f32[3,36,2,256]{3,2,1,0:T(2,128)} %copy-done.12, ...), custom_call_target="tpu_custom_call" | custom-call | tf_op jit(solution)/shard_map/pallas_call | solution.py:127
  125.6 2.5 %collective-permute-start.8 = (f32[3,2,32,256]{3,2,1,0:T(8,128)S(1)}, f32[3,2,32,256]{3,2,1,0:T(8,128)S(1)}, u32[]{:S(2)}, u32[]{:S(2)}) collective-permute-start(f32[3,2,32,256]{3,2,1,0:T(8,128)S(1)} %get-tuple-element.264), channel_id=1, source_target_pairs={{0,4},{4,8},{8,12},{12,16},{16,20},{20,24},{24,28},{1,5},{5,9},{9,... | collective-permute-start | bytes 589832 | tf_op jit(solution)/shard_map/ppermute | solution.py:153
  128.2 4.2 %collective-permute-start.9 = (f32[3,2,32,256]{3,2,1,0:T(8,128)S(1)}, f32[3,2,32,256]{3,2,1,0:T(8,128)S(1)}, u32[]{:S(2)}, u32[]{:S(2)}) collective-permute-start(f32[3,2,32,256]{3,2,1,0:T(8,128)S(1)} %get-tuple-element.263), channel_id=1, source_target_pairs={{4,0},{8,4},{12,8},{16,12},{20,16},{24,20},{28,24},{5,1},{9,5},{13... | collective-permute-start | bytes 589832 | tf_op jit(solution)/shard_map/ppermute | solution.py:154
  132.4 1.5 fusion.80
  134.1 2.1 %collective-permute-done.9.xhi_ref = f32[3,2,32,256]{3,2,1,0:T(8,128)S(1)} collective-permute-done((f32[3,2,32,256]{3,2,1,0:T(8,128)S(1)}, f32[3,2,32,256]{3,2,1,0:T(8,128)S(1)}, u32[]{:S(2)}, u32[]{:S(2)}) %collective-permute-start.9) | collective-permute-done | bytes 196640 | tf_op jit(solution)/shard_map/ppermute | solution.py:154
  136.3 4.6 %collective-permute-start.11 = (f32[3,36,2,256]{3,2,1,0:T(2,128)S(1)}, f32[3,36,2,256]{3,2,1,0:T(2,128)S(1)}, u32[]{:S(2)}, u32[]{:S(2)}) collective-permute-start(f32[3,36,2,256]{3,2,1,0:T(2,128)S(1)} %pad_maximum_fusion.6), channel_id=1, source_target_pairs={{1,0},{2,1},{3,2},{5,4},{6,5},{7,6},{9,8},{10,9},{11,10},{13,12},{... | collective-permute-start | bytes 663560 | tf_op jit(solution)/shard_map/ppermute | solution.py:159
  141.0 1.9 collective-permute-start.10
  142.9 3.2 %fusion.8 = f32[3072,256]{1,0:T(8,128)} fusion(s32[256]{0:T(256)S(1)} %get-tuple-element.303, f32[256]{0:T(256)S(1)} %bitcast.114, s32[256]{0:T(256)S(1)} %get-tuple-element.302), kind=kOutput, calls=%fused_computation.27 | convolution fusion | flops 2416836608 | bytes 3148800 | tf_op jit(solution)/shard_map/dot_general | solution.py:365
  146.1 2.1 %collective-permute-done.10.ylo_ref = f32[3,36,2,256]{3,2,1,0:T(2,128)S(1)} collective-permute-done((f32[3,36,2,256]{3,2,1,0:T(2,128)S(1)}, f32[3,36,2,256]{3,2,1,0:T(2,128)S(1)}, u32[]{:S(2)}, u32[]{:S(2)}) %collective-permute-start.10) | collective-permute-done | bytes 221216 | tf_op jit(solution)/shard_map/ppermute | solution.py:158
  148.9 14.6 %shard_map.124.u_ref = f32[3,32,32,256]{3,2,1,0:T(8,128)} custom-call(f32[3,32,32,256]{3,2,1,0:T(8,128)} %shard_map.123.u_ref.prev_ref, f32[3,2,32,256]{3,2,1,0:T(8,128)} %copy-done.3, f32[3,2,32,256]{3,2,1,0:T(8,128)} %copy-done.6, f32[3,36,2,256]{3,2,1,0:T(2,128)} %copy-done.14, f32[3,36,2,256]{3,2,1,0:T(2,128)} %copy-done.11, ...), custom_call_target="tpu_custom_call" | custom-call | tf_op jit(solution)/shard_map/pallas_call | solution.py:127
  163.6 1.0 fusion.79
  164.6 2.5 %collective-permute-start.12 = (f32[3,2,32,256]{3,2,1,0:T(8,128)S(1)}, f32[3,2,32,256]{3,2,1,0:T(8,128)S(1)}, u32[]{:S(2)}, u32[]{:S(2)}) collective-permute-start(f32[3,2,32,256]{3,2,1,0:T(8,128)S(1)} %get-tuple-element.260), channel_id=1, source_target_pairs={{0,4},{4,8},{8,12},{12,16},{16,20},{20,24},{24,28},{1,5},{5,9},{9,... | collective-permute-start | bytes 589832 | tf_op jit(solution)/shard_map/ppermute | solution.py:153
  167.1 4.3 %collective-permute-start.13 = (f32[3,2,32,256]{3,2,1,0:T(8,128)S(1)}, f32[3,2,32,256]{3,2,1,0:T(8,128)S(1)}, u32[]{:S(2)}, u32[]{:S(2)}) collective-permute-start(f32[3,2,32,256]{3,2,1,0:T(8,128)S(1)} %get-tuple-element.259), channel_id=1, source_target_pairs={{4,0},{8,4},{12,8},{16,12},{20,16},{24,20},{28,24},{5,1},{9,5},{13... | collective-permute-start | bytes 589832 | tf_op jit(solution)/shard_map/ppermute | solution.py:154
  171.4 1.5 fusion.78
  173.1 2.1 %collective-permute-done.13.xhi_ref = f32[3,2,32,256]{3,2,1,0:T(8,128)S(1)} collective-permute-done((f32[3,2,32,256]{3,2,1,0:T(8,128)S(1)}, f32[3,2,32,256]{3,2,1,0:T(8,128)S(1)}, u32[]{:S(2)}, u32[]{:S(2)}) %collective-permute-start.13) | collective-permute-done | bytes 196640 | tf_op jit(solution)/shard_map/ppermute | solution.py:154
  175.3 4.6 %collective-permute-start.15 = (f32[3,36,2,256]{3,2,1,0:T(2,128)S(1)}, f32[3,36,2,256]{3,2,1,0:T(2,128)S(1)}, u32[]{:S(2)}, u32[]{:S(2)}) collective-permute-start(f32[3,36,2,256]{3,2,1,0:T(2,128)S(1)} %pad_maximum_fusion.8), channel_id=1, source_target_pairs={{1,0},{2,1},{3,2},{5,4},{6,5},{7,6},{9,8},{10,9},{11,10},{13,12},{... | collective-permute-start | bytes 663560 | tf_op jit(solution)/shard_map/ppermute | solution.py:159
  180.0 1.9 collective-permute-start.14
  181.9 3.2 %fusion.7 = f32[3072,256]{1,0:T(8,128)} fusion(s32[256]{0:T(256)S(1)} %get-tuple-element.303, f32[256]{0:T(256)S(1)} %bitcast.113, s32[256]{0:T(256)S(1)} %get-tuple-element.302), kind=kOutput, calls=%fused_computation.26 | convolution fusion | flops 2416836608 | bytes 3148800 | tf_op jit(solution)/shard_map/dot_general | solution.py:365
  185.1 2.1 %collective-permute-done.14.ylo_ref = f32[3,36,2,256]{3,2,1,0:T(2,128)S(1)} collective-permute-done((f32[3,36,2,256]{3,2,1,0:T(2,128)S(1)}, f32[3,36,2,256]{3,2,1,0:T(2,128)S(1)}, u32[]{:S(2)}, u32[]{:S(2)}) %collective-permute-start.14) | collective-permute-done | bytes 221216 | tf_op jit(solution)/shard_map/ppermute | solution.py:158
  188.0 14.6 %shard_map.125 = f32[3,32,32,256]{3,2,1,0:T(8,128)} custom-call(f32[3,32,32,256]{3,2,1,0:T(8,128)} %shard_map.124.u_ref, f32[3,2,32,256]{3,2,1,0:T(8,128)} %copy-done.2, f32[3,2,32,256]{3,2,1,0:T(8,128)} %copy-done.5, f32[3,36,2,256]{3,2,1,0:T(2,128)} %copy-done.13, f32[3,36,2,256]{3,2,1,0:T(2,128)} %copy-done.10, ...), custom_call_target="tpu_custom_call" | custom-call | tf_op jit(solution)/shard_map/pallas_call | solution.py:127
  (138 shorter events, 14.9 us)
Async XLA Ops:
  16.0 5.3 %copy-start.16 = (s32[8192]{0:T(1024)S(1)}, s32[8192]{0:T(1024)}, u32[]{:S(2)}) copy-start(s32[8192]{0:T(1024)} %param.19) | copy-start | bytes 98308
  16.0 5.3 %copy-start.17 = (s32[8192]{0:T(1024)S(1)}, s32[8192]{0:T(1024)}, u32[]{:S(2)}) copy-start(s32[8192]{0:T(1024)} %param.20) | copy-start | bytes 98308
  24.8 30.6 %copy-start.18 = (s32[256]{0:T(256)S(1)}, s32[256]{0:T(256)}, u32[]{:S(2)}) copy-start(s32[256]{0:T(256)} %param.21) | copy-start | bytes 3076
  39.3 25.6 %all-to-all-start = ((bf16[2,4,32,256]{3,1,0,2:T(4,128)(2,1)}), bf16[2,4,32,256]{3,1,0,2:T(4,128)(2,1)S(1)}, u32[]{:S(2)}, u32[]{:S(2)}) async-start(bf16[2,4,32,256]{3,1,0,2:T(4,128)(2,1)} %copy.27), calls=%async_computation | async-start | bytes 262144 | tf_op jit(solution)/shard_map/all_to_all | solution.py:342
  46.3 9.7 %collective-permute-start = (f32[3,2,32,256]{3,2,1,0:T(8,128)S(1)}, f32[3,2,32,256]{3,2,1,0:T(8,128)S(1)}, u32[]{:S(2)}, u32[]{:S(2)}) collective-permute-start(f32[3,2,32,256]{3,2,1,0:T(8,128)S(1)} %get-tuple-element.272), channel_id=1, source_target_pairs={{0,4},{4,8},{8,12},{12,16},{16,20},{20,24},{24,28},{1,5},{5,9},{9,... | collective-permute-start | bytes 589832 | tf_op jit(solution)/shard_map/ppermute | solution.py:153
  49.7 10.5 %collective-permute-start.1 = (f32[3,2,32,256]{3,2,1,0:T(8,128)S(1)}, f32[3,2,32,256]{3,2,1,0:T(8,128)S(1)}, u32[]{:S(2)}, u32[]{:S(2)}) collective-permute-start(f32[3,2,32,256]{3,2,1,0:T(8,128)S(1)} %get-tuple-element.271), channel_id=1, source_target_pairs={{4,0},{8,4},{12,8},{16,12},{20,16},{24,20},{28,24},{5,1},{9,5},{13... | collective-permute-start | bytes 589832 | tf_op jit(solution)/shard_map/ppermute | solution.py:154
  56.0 13.9 %copy-start = (f32[3,2,32,256]{3,2,1,0:T(8,128)}, f32[3,2,32,256]{3,2,1,0:T(8,128)S(1)}, u32[]{:S(2)}) copy-start(f32[3,2,32,256]{3,2,1,0:T(8,128)S(1)} %collective-permute-done.xlo_ref) | copy-start | bytes 589828
  60.2 9.7 %copy-start.1 = (f32[3,2,32,256]{3,2,1,0:T(8,128)}, f32[3,2,32,256]{3,2,1,0:T(8,128)S(1)}, u32[]{:S(2)}) copy-start(f32[3,2,32,256]{3,2,1,0:T(8,128)S(1)} %collective-permute-done.1.xhi_ref) | copy-start | bytes 589828
  60.4 8.0 %collective-permute-start.3 = (f32[3,36,2,256]{3,2,1,0:T(2,128)S(1)}, f32[3,36,2,256]{3,2,1,0:T(2,128)S(1)}, u32[]{:S(2)}, u32[]{:S(2)}) collective-permute-start(f32[3,36,2,256]{3,2,1,0:T(2,128)S(1)} %pad_maximum_fusion.2), channel_id=1, source_target_pairs={{1,0},{2,1},{3,2},{5,4},{6,5},{7,6},{9,8},{10,9},{11,10},{13,12},{... | collective-permute-start | bytes 663560 | tf_op jit(solution)/shard_map/ppermute | solution.py:159
  62.7 7.3 %collective-permute-start.2 = (f32[3,36,2,256]{3,2,1,0:T(2,128)S(1)}, f32[3,36,2,256]{3,2,1,0:T(2,128)S(1)}, u32[]{:S(2)}, u32[]{:S(2)}) collective-permute-start(f32[3,36,2,256]{3,2,1,0:T(2,128)S(1)} %pad_maximum_fusion.1), channel_id=1, source_target_pairs={{0,1},{1,2},{2,3},{4,5},{5,6},{6,7},{8,9},{9,10},{10,11},{12,13},{... | collective-permute-start | bytes 663560 | tf_op jit(solution)/shard_map/ppermute | solution.py:158
  68.4 1.6 copy-start.8
  69.9 0.7 copy-start.9
  86.3 8.6 %collective-permute-start.4 = (f32[3,2,32,256]{3,2,1,0:T(8,128)S(1)}, f32[3,2,32,256]{3,2,1,0:T(8,128)S(1)}, u32[]{:S(2)}, u32[]{:S(2)}) collective-permute-start(f32[3,2,32,256]{3,2,1,0:T(8,128)S(1)} %get-tuple-element.268), channel_id=1, source_target_pairs={{0,4},{4,8},{8,12},{12,16},{16,20},{20,24},{24,28},{1,5},{5,9},{9,... | collective-permute-start | bytes 589832 | tf_op jit(solution)/shard_map/ppermute | solution.py:153
  88.6 9.4 %collective-permute-start.5 = (f32[3,2,32,256]{3,2,1,0:T(8,128)S(1)}, f32[3,2,32,256]{3,2,1,0:T(8,128)S(1)}, u32[]{:S(2)}, u32[]{:S(2)}) collective-permute-start(f32[3,2,32,256]{3,2,1,0:T(8,128)S(1)} %get-tuple-element.267), channel_id=1, source_target_pairs={{4,0},{8,4},{12,8},{16,12},{20,16},{24,20},{28,24},{5,1},{9,5},{13... | collective-permute-start | bytes 589832 | tf_op jit(solution)/shard_map/ppermute | solution.py:154
  94.9 14.4 %copy-start.4 = (f32[3,2,32,256]{3,2,1,0:T(8,128)}, f32[3,2,32,256]{3,2,1,0:T(8,128)S(1)}, u32[]{:S(2)}) copy-start(f32[3,2,32,256]{3,2,1,0:T(8,128)S(1)} %collective-permute-done.4.xlo_ref) | copy-start | bytes 589828
  98.0 11.3 %copy-start.7 = (f32[3,2,32,256]{3,2,1,0:T(8,128)}, f32[3,2,32,256]{3,2,1,0:T(8,128)S(1)}, u32[]{:S(2)}) copy-start(f32[3,2,32,256]{3,2,1,0:T(8,128)S(1)} %collective-permute-done.5.xhi_ref) | copy-start | bytes 589828
  98.1 9.0 %collective-permute-start.7 = (f32[3,36,2,256]{3,2,1,0:T(2,128)S(1)}, f32[3,36,2,256]{3,2,1,0:T(2,128)S(1)}, u32[]{:S(2)}, u32[]{:S(2)}) collective-permute-start(f32[3,36,2,256]{3,2,1,0:T(2,128)S(1)} %pad_maximum_fusion.4), channel_id=1, source_target_pairs={{1,0},{2,1},{3,2},{5,4},{6,5},{7,6},{9,8},{10,9},{11,10},{13,12},{... | collective-permute-start | bytes 663560 | tf_op jit(solution)/shard_map/ppermute | solution.py:159
  102.0 7.3 %collective-permute-start.6 = (f32[3,36,2,256]{3,2,1,0:T(2,128)S(1)}, f32[3,36,2,256]{3,2,1,0:T(2,128)S(1)}, u32[]{:S(2)}, u32[]{:S(2)}) collective-permute-start(f32[3,36,2,256]{3,2,1,0:T(2,128)S(1)} %pad_maximum_fusion.3), channel_id=1, source_target_pairs={{0,1},{1,2},{2,3},{4,5},{5,6},{6,7},{8,9},{9,10},{10,11},{12,13},{... | collective-permute-start | bytes 663560 | tf_op jit(solution)/shard_map/ppermute | solution.py:158
  107.1 2.1 %copy-start.12 = (f32[3,36,2,256]{3,2,1,0:T(2,128)}, f32[3,36,2,256]{3,2,1,0:T(2,128)S(1)}, u32[]{:S(2)}) copy-start(f32[3,36,2,256]{3,2,1,0:T(2,128)S(1)} %collective-permute-done.7.yhi_ref) | copy-start | bytes 663556
  109.2 0.7 copy-start.15
  125.6 8.5 %collective-permute-start.8 = (f32[3,2,32,256]{3,2,1,0:T(8,128)S(1)}, f32[3,2,32,256]{3,2,1,0:T(8,128)S(1)}, u32[]{:S(2)}, u32[]{:S(2)}) collective-permute-start(f32[3,2,32,256]{3,2,1,0:T(8,128)S(1)} %get-tuple-element.264), channel_id=1, source_target_pairs={{0,4},{4,8},{8,12},{12,16},{16,20},{20,24},{24,28},{1,5},{5,9},{9,... | collective-permute-start | bytes 589832 | tf_op jit(solution)/shard_map/ppermute | solution.py:153
  128.2 8.0 %collective-permute-start.9 = (f32[3,2,32,256]{3,2,1,0:T(8,128)S(1)}, f32[3,2,32,256]{3,2,1,0:T(8,128)S(1)}, u32[]{:S(2)}, u32[]{:S(2)}) collective-permute-start(f32[3,2,32,256]{3,2,1,0:T(8,128)S(1)} %get-tuple-element.263), channel_id=1, source_target_pairs={{4,0},{8,4},{12,8},{16,12},{20,16},{24,20},{28,24},{5,1},{9,5},{13... | collective-permute-start | bytes 589832 | tf_op jit(solution)/shard_map/ppermute | solution.py:154
  134.1 14.2 %copy-start.3 = (f32[3,2,32,256]{3,2,1,0:T(8,128)}, f32[3,2,32,256]{3,2,1,0:T(8,128)S(1)}, u32[]{:S(2)}) copy-start(f32[3,2,32,256]{3,2,1,0:T(8,128)S(1)} %collective-permute-done.8.xlo_ref) | copy-start | bytes 589828
  136.2 12.1 %copy-start.6 = (f32[3,2,32,256]{3,2,1,0:T(8,128)}, f32[3,2,32,256]{3,2,1,0:T(8,128)S(1)}, u32[]{:S(2)}) copy-start(f32[3,2,32,256]{3,2,1,0:T(8,128)S(1)} %collective-permute-done.9.xhi_ref) | copy-start | bytes 589828
  136.3 9.8 %collective-permute-start.11 = (f32[3,36,2,256]{3,2,1,0:T(2,128)S(1)}, f32[3,36,2,256]{3,2,1,0:T(2,128)S(1)}, u32[]{:S(2)}, u32[]{:S(2)}) collective-permute-start(f32[3,36,2,256]{3,2,1,0:T(2,128)S(1)} %pad_maximum_fusion.6), channel_id=1, source_target_pairs={{1,0},{2,1},{3,2},{5,4},{6,5},{7,6},{9,8},{10,9},{11,10},{13,12},{... | collective-permute-start | bytes 663560 | tf_op jit(solution)/shard_map/ppermute | solution.py:159
  141.0 7.3 %collective-permute-start.10 = (f32[3,36,2,256]{3,2,1,0:T(2,128)S(1)}, f32[3,36,2,256]{3,2,1,0:T(2,128)S(1)}, u32[]{:S(2)}, u32[]{:S(2)}) collective-permute-start(f32[3,36,2,256]{3,2,1,0:T(2,128)S(1)} %pad_maximum_fusion.5), channel_id=1, source_target_pairs={{0,1},{1,2},{2,3},{4,5},{5,6},{6,7},{8,9},{9,10},{10,11},{12,13},{... | collective-permute-start | bytes 663560 | tf_op jit(solution)/shard_map/ppermute | solution.py:158
  146.1 2.1 %copy-start.11 = (f32[3,36,2,256]{3,2,1,0:T(2,128)}, f32[3,36,2,256]{3,2,1,0:T(2,128)S(1)}, u32[]{:S(2)}) copy-start(f32[3,36,2,256]{3,2,1,0:T(2,128)S(1)} %collective-permute-done.11.yhi_ref) | copy-start | bytes 663556
  148.2 0.7 copy-start.14
  164.6 8.5 %collective-permute-start.12 = (f32[3,2,32,256]{3,2,1,0:T(8,128)S(1)}, f32[3,2,32,256]{3,2,1,0:T(8,128)S(1)}, u32[]{:S(2)}, u32[]{:S(2)}) collective-permute-start(f32[3,2,32,256]{3,2,1,0:T(8,128)S(1)} %get-tuple-element.260), channel_id=1, source_target_pairs={{0,4},{4,8},{8,12},{12,16},{16,20},{20,24},{24,28},{1,5},{5,9},{9,... | collective-permute-start | bytes 589832 | tf_op jit(solution)/shard_map/ppermute | solution.py:153
  167.1 8.1 %collective-permute-start.13 = (f32[3,2,32,256]{3,2,1,0:T(8,128)S(1)}, f32[3,2,32,256]{3,2,1,0:T(8,128)S(1)}, u32[]{:S(2)}, u32[]{:S(2)}) collective-permute-start(f32[3,2,32,256]{3,2,1,0:T(8,128)S(1)} %get-tuple-element.259), channel_id=1, source_target_pairs={{4,0},{8,4},{12,8},{16,12},{20,16},{24,20},{28,24},{5,1},{9,5},{13... | collective-permute-start | bytes 589832 | tf_op jit(solution)/shard_map/ppermute | solution.py:154
  173.1 14.2 %copy-start.2 = (f32[3,2,32,256]{3,2,1,0:T(8,128)}, f32[3,2,32,256]{3,2,1,0:T(8,128)S(1)}, u32[]{:S(2)}) copy-start(f32[3,2,32,256]{3,2,1,0:T(8,128)S(1)} %collective-permute-done.12.xlo_ref) | copy-start | bytes 589828
  175.2 12.1 %copy-start.5 = (f32[3,2,32,256]{3,2,1,0:T(8,128)}, f32[3,2,32,256]{3,2,1,0:T(8,128)S(1)}, u32[]{:S(2)}) copy-start(f32[3,2,32,256]{3,2,1,0:T(8,128)S(1)} %collective-permute-done.13.xhi_ref) | copy-start | bytes 589828
  175.3 9.8 %collective-permute-start.15 = (f32[3,36,2,256]{3,2,1,0:T(2,128)S(1)}, f32[3,36,2,256]{3,2,1,0:T(2,128)S(1)}, u32[]{:S(2)}, u32[]{:S(2)}) collective-permute-start(f32[3,36,2,256]{3,2,1,0:T(2,128)S(1)} %pad_maximum_fusion.8), channel_id=1, source_target_pairs={{1,0},{2,1},{3,2},{5,4},{6,5},{7,6},{9,8},{10,9},{11,10},{13,12},{... | collective-permute-start | bytes 663560 | tf_op jit(solution)/shard_map/ppermute | solution.py:159
  180.0 7.3 %collective-permute-start.14 = (f32[3,36,2,256]{3,2,1,0:T(2,128)S(1)}, f32[3,36,2,256]{3,2,1,0:T(2,128)S(1)}, u32[]{:S(2)}, u32[]{:S(2)}) collective-permute-start(f32[3,36,2,256]{3,2,1,0:T(2,128)S(1)} %pad_maximum_fusion.7), channel_id=1, source_target_pairs={{0,1},{1,2},{2,3},{4,5},{5,6},{6,7},{8,9},{9,10},{10,11},{12,13},{... | collective-permute-start | bytes 663560 | tf_op jit(solution)/shard_map/ppermute | solution.py:158
  185.1 2.1 %copy-start.10 = (f32[3,36,2,256]{3,2,1,0:T(2,128)}, f32[3,36,2,256]{3,2,1,0:T(2,128)S(1)}, u32[]{:S(2)}) copy-start(f32[3,36,2,256]{3,2,1,0:T(2,128)S(1)} %collective-permute-done.15.yhi_ref) | copy-start | bytes 663556
  187.2 0.7 copy-start.13

commit v6 on v5

--- a/solution.py
+++ b/solution.py
@@ -91,6 +91,14 @@
                 return 16.0 * near - far - 30.0 * center
 
             def mixed(p_c, a, b):
+                if 2 in (a, b):
+                    n = a + b - 2
+                    d = [0, 0]
+                    d[n] = 1
+                    step = load(p_c, d[0], d[1])
+                    d[n] = -1
+                    diff = step - load(p_c, d[0], d[1])
+                    return zs(diff, 1) - zs(diff, -1)
                 acc = None
                 for sa in (1, -1):
                     for sb in (1, -1):

time: 203 us -> 197 us (0.970)
  Pallas kernels: 58.5 us -> 52 us
    pallas_call x4, Pallas kernels: 58.5 us -> 52 us  [elastic_step(): pl.pallas_call(kernel, grid=(nx // bx,), in_specs=[pl.BlockSpec(u.shape,...]
  transfers between devices with their start and end apart: 17 -> 17, of which waited for: 12 -> 12; matrix products, arithmetic and copies ran while one was open for 10% -> 11% of each run, Pallas kernels for 0% -> 0%
where the time goes in v6:
time: 197 us; the launch traced here: 196 us
  starting transfers between devices  55.9 us (28%)
  Pallas kernels  52 us (26%)
  matrix products  29.6 us (15%)
  other arithmetic  20.6 us (10%)
  waiting for transfers between devices  20.6 us (10%)
  local copies, waits for them, and re-layouts  15 us (8%)
    pallas_call x4, Pallas kernels, elastic_step(): pl.pallas_call(kernel, grid=(nx // bx,), in_specs=[pl.BlockSpec(u.shape,...  52 us
    ppermute x4, starting transfers between devices, halos(): xhi = lax.ppermute(block[:, :width], 'gx', backward_x)  16.3 us
    ppermute x4, starting transfers between devices, halos(): yhi = lax.ppermute(rows(slice(0, width)), 'gy', backward_y)  15.1 us
    dot_general x2, matrix products, select_block(): jnp.dot(table_rounded, offset_hot, preferred_element_type=jnp.float32)  13.1 us
    dot_general x4, matrix products, shards(): source = jnp.dot(column_hot, spread, precision=lax.Precision.HIGHEST)  12.9 us
    ppermute x4, waiting for transfers between devices, halos(): xhi = lax.ppermute(block[:, :width], 'gx', backward_x)  11.5 us
    ppermute x4, starting transfers between devices, halos(): xlo = lax.ppermute(block[:, nx - width:], 'gx', forward_x)  10.7 us
    ppermute x4, starting transfers between devices, halos(): ylo = lax.ppermute(rows(slice(ny - width, ny)), 'gy', forward_y)  7.91 us
  transfers between devices with their start and end apart: 17, of which 12 were waited for; matrix products, arithmetic and copies ran while one was open for 11% of the time, Pallas kernels for 0%

profile of v6, /device:TPU:12, one launch (start us, length us, event | category | flops | bytes accessed | tf_op | source)
XLA Modules:
  0.0 196.1 jit_solution(8608686874190558782)
XLA Ops:
  2.9 4.9 %sine_multiply_fusion.1 = (f32[32,4,1024]{2,1,0:T(4,128)S(1)}, f32[32,4,1024]{2,1,0:T(4,128)S(1)}, f32[32,4,1024]{2,1,0:T(4,128)S(1)}) fusion(f32[32]{0:T(128)S(1)} %get-tuple-element.307, f32[32,4]{1,0:T(8,128)S(1)} %copy.24, f32[1024]{0:T(1024)S(1)} %multiply_multiply_fusion, f32[1,4,1024]{2,1,0:T(4,128)S(1)} %slice.157, f32[31,4,1024]{2,1,0:T(4,128)S(1)} %slice.156, ...), kind=kLoop, calls=%fused_computation.41 | loop fusion | flops 1441792 | bytes 2102016 | tf_op jit(solution)/shard_map/mul | solution.py:188
  8.1 2.2 %while.32 = (s32[]{:T(128)}, f32[4,1024]{1,0:T(4,128)S(1)}, f32[4,1024]{1,0:T(4,128)S(1)}, f32[32,4,1024]{2,1,0:T(4,128)S(1)}, f32[32,4,1024]{2,1,0:T(4,128)S(1)...) while((s32[]{:T(128)}, f32[4,1024]{1,0:T(4,128)S(1)}, ...), condition=%wide.region_6.7_spmd.clone, body=%wide.region_5.6_spmd.clone.sunk | while | flops 94212 | bytes 147591 | solution.py:204
  11.2 4.3 %fusion.43 = (bf16[1,32,4,1024]{3,2,1,0:T(4,128)(2,1)S(1)}, bf16[1,32,4,1024]{3,2,1,0:T(4,128)(2,1)S(1)}) fusion(f32[32,4,1024]{2,1,0:T(4,128)S(1)} %get-tuple-element.191, f32[32,4,1024]{2,1,0:T(4,128)S(1)} %get-tuple-element.190, f32[32,4,1024]{2,1,0:T(4,128)S(1)} %negate_exponential_fusion, f32[32,4,1024]{2,1,0:T(4,128)S(1)} %fusion.23), kind=kLoop, calls=%fused_computation.74 | loop fusion | flops 1835008 | bytes 2621440 | tf_op jit(solution)/shard_map/stack | solution.py:217
  17.7 3.6 %subtract_convert_fusion = bf16[1024,32,64]{0,2,1:T(8,128)(2,1)} fusion(f32[1024,64]{0,1:T(8,128)S(1)} %get-tuple-element.301, f32[1024,32]{0,1:T(8,128)S(1)} %get-tuple-element.295, f32[1024,64]{0,1:T(8,128)S(1)} %get-tuple-element.300, f32[1024,32]{0,1:T(8,128)S(1)} %get-tuple-element.294), kind=kLoop, calls=%fused_computation.24 | loop fusion | flops 8388608 | bytes 4980736 | tf_op jit(solution)/shard_map/convert_element_type | solution.py:232
  21.4 3.5 %convolution_convert_fusion = bf16[256,2048]{1,0:T(8,128)(2,1)S(1)} fusion(bf16[256,1024]{1,0:T(8,128)(2,1)S(1)} %bitcast.109, bf16[1024,2048]{0,1:T(8,128)(2,1)} %bitcast.107), kind=kOutput, calls=%fused_computation.30 | convolution fusion | flops 1074266112 | bytes 5767168 | tf_op jit(solution)/shard_map/dot_general | solution.py:320
  24.9 13.4 %while.31 = (s32[]{:T(128)}, bf16[2,2,4,4096]{3,2,1,0:T(4,128)(2,1)S(1)}, s32[2,4096]{1,0:T(2,128)S(1)}, bf16[256,2048]{1,0:T(8,128)(2,1)S(1)}, s32[2,4096]{1,0:T(2,128)S(1)}, /*index=5*/s32[]{:T(128)}) while((s32[]{:T(128)}, bf16[2,2,4,4096]{3,2,1,0:T(4,128)(2,1)S(1)}, s32[2,4096]{1,0:T(2,128)S(1)}, bf16[256,2048]{1,0:T(8,128)(2,1)S(1)}, ...), condition=%wide.region_9.10_spmd, body=%wide.region_7.9_spmd.sunk | while | flops 4305682432 | bytes 2392141 | solution.py:343
  25.0 6.5 %multiply_reduce_fusion.2 = bf16[2,4,4096]{2,1,0:T(4,128)(2,1)S(1)} fusion(f32[32,4096]{1,0:T(8,128)S(1)} %fusion.102, bf16[256,2048]{1,0:T(8,128)(2,1)S(1)} %get-tuple-element.448, s32[4096]{0:T(1024)S(1)} %bitcast.111), kind=kOutput, calls=%fused_computation.3.clone.1 | convolution fusion | flops 4305420288 | bytes 1654784 | tf_op jit(solution)/shard_map/while/body/eval_jaxpr/dot_general | solution.py:335
  31.7 6.5 %multiply_reduce_fusion.2 = bf16[2,4,4096]{2,1,0:T(4,128)(2,1)S(1)} fusion(f32[32,4096]{1,0:T(8,128)S(1)} %fusion.102, bf16[256,2048]{1,0:T(8,128)(2,1)S(1)} %get-tuple-element.448, s32[4096]{0:T(1024)S(1)} %bitcast.111), kind=kOutput, calls=%fused_computation.3.clone.1 | convolution fusion | flops 4305420288 | bytes 1654784 | tf_op jit(solution)/shard_map/while/body/eval_jaxpr/dot_general | solution.py:335
  39.3 6.0 %all-to-all-start = ((bf16[2,4,32,256]{3,1,0,2:T(4,128)(2,1)}), bf16[2,4,32,256]{3,1,0,2:T(4,128)(2,1)S(1)}, u32[]{:S(2)}, u32[]{:S(2)}) async-start(bf16[2,4,32,256]{3,1,0,2:T(4,128)(2,1)} %copy.27), calls=%async_computation | async-start | bytes 262144 | tf_op jit(solution)/shard_map/all_to_all | solution.py:350
  45.3 1.1 fusion.85
  46.3 3.4 %collective-permute-start = (f32[3,2,32,256]{3,2,1,0:T(8,128)S(1)}, f32[3,2,32,256]{3,2,1,0:T(8,128)S(1)}, u32[]{:S(2)}, u32[]{:S(2)}) collective-permute-start(f32[3,2,32,256]{3,2,1,0:T(8,128)S(1)} %get-tuple-element.272), channel_id=1, source_target_pairs={{0,4},{4,8},{8,12},{12,16},{16,20},{20,24},{24,28},{1,5},{5,9},{9,... | collective-permute-start | bytes 589832 | tf_op jit(solution)/shard_map/ppermute | solution.py:161
  49.7 3.4 %collective-permute-start.1 = (f32[3,2,32,256]{3,2,1,0:T(8,128)S(1)}, f32[3,2,32,256]{3,2,1,0:T(8,128)S(1)}, u32[]{:S(2)}, u32[]{:S(2)}) collective-permute-start(f32[3,2,32,256]{3,2,1,0:T(8,128)S(1)} %get-tuple-element.271), channel_id=1, source_target_pairs={{4,0},{8,4},{12,8},{16,12},{20,16},{24,20},{28,24},{5,1},{9,5},{13... | collective-permute-start | bytes 589832 | tf_op jit(solution)/shard_map/ppermute | solution.py:162
  53.1 1.5 fusion.84
  56.0 4.2 %collective-permute-done.1.xhi_ref = f32[3,2,32,256]{3,2,1,0:T(8,128)S(1)} collective-permute-done((f32[3,2,32,256]{3,2,1,0:T(8,128)S(1)}, f32[3,2,32,256]{3,2,1,0:T(8,128)S(1)}, u32[]{:S(2)}, u32[]{:S(2)}) %collective-permute-start.1) | collective-permute-done | bytes 196640 | tf_op jit(solution)/shard_map/ppermute | solution.py:162
  60.4 2.2 %collective-permute-start.3 = (f32[3,36,2,256]{3,2,1,0:T(2,128)S(1)}, f32[3,36,2,256]{3,2,1,0:T(2,128)S(1)}, u32[]{:S(2)}, u32[]{:S(2)}) collective-permute-start(f32[3,36,2,256]{3,2,1,0:T(2,128)S(1)} %pad_maximum_fusion.2), channel_id=1, source_target_pairs={{1,0},{2,1},{3,2},{5,4},{6,5},{7,6},{9,8},{10,9},{11,10},{13,12},{... | collective-permute-start | bytes 663560 | tf_op jit(solution)/shard_map/ppermute | solution.py:167
  62.7 2.1 %collective-permute-start.2 = (f32[3,36,2,256]{3,2,1,0:T(2,128)S(1)}, f32[3,36,2,256]{3,2,1,0:T(2,128)S(1)}, u32[]{:S(2)}, u32[]{:S(2)}) collective-permute-start(f32[3,36,2,256]{3,2,1,0:T(2,128)S(1)} %pad_maximum_fusion.1), channel_id=1, source_target_pairs={{0,1},{1,2},{2,3},{4,5},{5,6},{6,7},{8,9},{9,10},{10,11},{12,13},{... | collective-permute-start | bytes 663560 | tf_op jit(solution)/shard_map/ppermute | solution.py:166
  65.1 3.2 %fusion.10 = f32[3072,256]{1,0:T(8,128)} fusion(s32[256]{0:T(256)S(1)} %get-tuple-element.303, f32[256]{0:T(256)S(1)} %bitcast.116, s32[256]{0:T(256)S(1)} %get-tuple-element.302), kind=kOutput, calls=%fused_computation.29 | convolution fusion | flops 2416836608 | bytes 3148800 | tf_op jit(solution)/shard_map/dot_general | solution.py:373
  68.4 1.6 collective-permute-done.2.ylo_ref
  70.6 13.0 %shard_map.122.u_ref.prev_ref = f32[3,32,32,256]{3,2,1,0:T(8,128)} custom-call(f32[3,32,32,256]{3,2,1,0:T(8,128)} %prev_ref.3, f32[3,2,32,256]{3,2,1,0:T(8,128)} %copy-done, f32[3,2,32,256]{3,2,1,0:T(8,128)} %copy-done.1, f32[3,36,2,256]{3,2,1,0:T(2,128)} %copy-done.9, f32[3,36,2,256]{3,2,1,0:T(2,128)} %copy-done.8, f32[3,32,32,256]{3,2,1,0:T(8,128)} %prev_ref.2, ...), custom_call_target="tpu_custom_call" | custom-call | tf_op jit(solution)/shard_map/pallas_call | solution.py:135
  83.6 1.0 fusion.83
  84.7 2.2 %collective-permute-start.4 = (f32[3,2,32,256]{3,2,1,0:T(8,128)S(1)}, f32[3,2,32,256]{3,2,1,0:T(8,128)S(1)}, u32[]{:S(2)}, u32[]{:S(2)}) collective-permute-start(f32[3,2,32,256]{3,2,1,0:T(8,128)S(1)} %get-tuple-element.268), channel_id=1, source_target_pairs={{0,4},{4,8},{8,12},{12,16},{16,20},{20,24},{24,28},{1,5},{5,9},{9,... | collective-permute-start | bytes 589832 | tf_op jit(solution)/shard_map/ppermute | solution.py:161
  86.9 4.5 %collective-permute-start.5 = (f32[3,2,32,256]{3,2,1,0:T(8,128)S(1)}, f32[3,2,32,256]{3,2,1,0:T(8,128)S(1)}, u32[]{:S(2)}, u32[]{:S(2)}) collective-permute-start(f32[3,2,32,256]{3,2,1,0:T(8,128)S(1)} %get-tuple-element.267), channel_id=1, source_target_pairs={{4,0},{8,4},{12,8},{16,12},{20,16},{24,20},{28,24},{5,1},{9,5},{13... | collective-permute-start | bytes 589832 | tf_op jit(solution)/shard_map/ppermute | solution.py:162
  91.4 1.5 fusion.82
  93.3 3.1 %collective-permute-done.5.xhi_ref = f32[3,2,32,256]{3,2,1,0:T(8,128)S(1)} collective-permute-done((f32[3,2,32,256]{3,2,1,0:T(8,128)S(1)}, f32[3,2,32,256]{3,2,1,0:T(8,128)S(1)}, u32[]{:S(2)}, u32[]{:S(2)}) %collective-permute-start.5) | collective-permute-done | bytes 196640 | tf_op jit(solution)/shard_map/ppermute | solution.py:162
  96.5 3.8 %collective-permute-start.7 = (f32[3,36,2,256]{3,2,1,0:T(2,128)S(1)}, f32[3,36,2,256]{3,2,1,0:T(2,128)S(1)}, u32[]{:S(2)}, u32[]{:S(2)}) collective-permute-start(f32[3,36,2,256]{3,2,1,0:T(2,128)S(1)} %pad_maximum_fusion.4), channel_id=1, source_target_pairs={{1,0},{2,1},{3,2},{5,4},{6,5},{7,6},{9,8},{10,9},{11,10},{13,12},{... | collective-permute-start | bytes 663560 | tf_op jit(solution)/shard_map/ppermute | solution.py:167
  100.4 1.9 collective-permute-start.6
  102.3 3.2 %fusion.9 = f32[3072,256]{1,0:T(8,128)} fusion(s32[256]{0:T(256)S(1)} %get-tuple-element.303, f32[256]{0:T(256)S(1)} %bitcast.115, s32[256]{0:T(256)S(1)} %get-tuple-element.302), kind=kOutput, calls=%fused_computation.28 | convolution fusion | flops 2416836608 | bytes 3148800 | tf_op jit(solution)/shard_map/dot_general | solution.py:373
  105.5 2.1 %collective-permute-done.6.ylo_ref = f32[3,36,2,256]{3,2,1,0:T(2,128)S(1)} collective-permute-done((f32[3,36,2,256]{3,2,1,0:T(2,128)S(1)}, f32[3,36,2,256]{3,2,1,0:T(2,128)S(1)}, u32[]{:S(2)}, u32[]{:S(2)}) %collective-permute-start.6) | collective-permute-done | bytes 221216 | tf_op jit(solution)/shard_map/ppermute | solution.py:166
  108.3 13.0 %shard_map.123.u_ref.prev_ref = f32[3,32,32,256]{3,2,1,0:T(8,128)} custom-call(f32[3,32,32,256]{3,2,1,0:T(8,128)} %shard_map.122.u_ref.prev_ref, f32[3,2,32,256]{3,2,1,0:T(8,128)} %copy-done.4, f32[3,2,32,256]{3,2,1,0:T(8,128)} %copy-done.7, f32[3,36,2,256]{3,2,1,0:T(2,128)} %copy-done.15, f32[3,36,2,256]{3,2,1,0:T(2,128)} %copy-done.12, ...), custom_call_target="tpu_custom_call" | custom-call | tf_op jit(solution)/shard_map/pallas_call | solution.py:135
  121.3 1.0 fusion.81
  122.3 2.5 %collective-permute-start.8 = (f32[3,2,32,256]{3,2,1,0:T(8,128)S(1)}, f32[3,2,32,256]{3,2,1,0:T(8,128)S(1)}, u32[]{:S(2)}, u32[]{:S(2)}) collective-permute-start(f32[3,2,32,256]{3,2,1,0:T(8,128)S(1)} %get-tuple-element.264), channel_id=1, source_target_pairs={{0,4},{4,8},{8,12},{12,16},{16,20},{20,24},{24,28},{1,5},{5,9},{9,... | collective-permute-start | bytes 589832 | tf_op jit(solution)/shard_map/ppermute | solution.py:161
  124.9 4.2 %collective-permute-start.9 = (f32[3,2,32,256]{3,2,1,0:T(8,128)S(1)}, f32[3,2,32,256]{3,2,1,0:T(8,128)S(1)}, u32[]{:S(2)}, u32[]{:S(2)}) collective-permute-start(f32[3,2,32,256]{3,2,1,0:T(8,128)S(1)} %get-tuple-element.263), channel_id=1, source_target_pairs={{4,0},{8,4},{12,8},{16,12},{20,16},{24,20},{28,24},{5,1},{9,5},{13... | collective-permute-start | bytes 589832 | tf_op jit(solution)/shard_map/ppermute | solution.py:162
  129.1 1.5 fusion.80
  130.8 2.1 %collective-permute-done.9.xhi_ref = f32[3,2,32,256]{3,2,1,0:T(8,128)S(1)} collective-permute-done((f32[3,2,32,256]{3,2,1,0:T(8,128)S(1)}, f32[3,2,32,256]{3,2,1,0:T(8,128)S(1)}, u32[]{:S(2)}, u32[]{:S(2)}) %collective-permute-start.9) | collective-permute-done | bytes 196640 | tf_op jit(solution)/shard_map/ppermute | solution.py:162
  133.0 4.6 %collective-permute-start.11 = (f32[3,36,2,256]{3,2,1,0:T(2,128)S(1)}, f32[3,36,2,256]{3,2,1,0:T(2,128)S(1)}, u32[]{:S(2)}, u32[]{:S(2)}) collective-permute-start(f32[3,36,2,256]{3,2,1,0:T(2,128)S(1)} %pad_maximum_fusion.6), channel_id=1, source_target_pairs={{1,0},{2,1},{3,2},{5,4},{6,5},{7,6},{9,8},{10,9},{11,10},{13,12},{... | collective-permute-start | bytes 663560 | tf_op jit(solution)/shard_map/ppermute | solution.py:167
  137.7 1.9 collective-permute-start.10
  139.7 3.2 %fusion.8 = f32[3072,256]{1,0:T(8,128)} fusion(s32[256]{0:T(256)S(1)} %get-tuple-element.303, f32[256]{0:T(256)S(1)} %bitcast.114, s32[256]{0:T(256)S(1)} %get-tuple-element.302), kind=kOutput, calls=%fused_computation.27 | convolution fusion | flops 2416836608 | bytes 3148800 | tf_op jit(solution)/shard_map/dot_general | solution.py:373
  142.9 2.1 %collective-permute-done.10.ylo_ref = f32[3,36,2,256]{3,2,1,0:T(2,128)S(1)} collective-permute-done((f32[3,36,2,256]{3,2,1,0:T(2,128)S(1)}, f32[3,36,2,256]{3,2,1,0:T(2,128)S(1)}, u32[]{:S(2)}, u32[]{:S(2)}) %collective-permute-start.10) | collective-permute-done | bytes 221216 | tf_op jit(solution)/shard_map/ppermute | solution.py:166
  145.7 13.0 %shard_map.124.u_ref = f32[3,32,32,256]{3,2,1,0:T(8,128)} custom-call(f32[3,32,32,256]{3,2,1,0:T(8,128)} %shard_map.123.u_ref.prev_ref, f32[3,2,32,256]{3,2,1,0:T(8,128)} %copy-done.3, f32[3,2,32,256]{3,2,1,0:T(8,128)} %copy-done.6, f32[3,36,2,256]{3,2,1,0:T(2,128)} %copy-done.14, f32[3,36,2,256]{3,2,1,0:T(2,128)} %copy-done.11, ...), custom_call_target="tpu_custom_call" | custom-call | tf_op jit(solution)/shard_map/pallas_call | solution.py:135
  159.7 2.5 %collective-permute-start.12 = (f32[3,2,32,256]{3,2,1,0:T(8,128)S(1)}, f32[3,2,32,256]{3,2,1,0:T(8,128)S(1)}, u32[]{:S(2)}, u32[]{:S(2)}) collective-permute-start(f32[3,2,32,256]{3,2,1,0:T(8,128)S(1)} %get-tuple-element.260), channel_id=1, source_target_pairs={{0,4},{4,8},{8,12},{12,16},{16,20},{20,24},{24,28},{1,5},{5,9},{9,... | collective-permute-start | bytes 589832 | tf_op jit(solution)/shard_map/ppermute | solution.py:161
  162.2 4.3 %collective-permute-start.13 = (f32[3,2,32,256]{3,2,1,0:T(8,128)S(1)}, f32[3,2,32,256]{3,2,1,0:T(8,128)S(1)}, u32[]{:S(2)}, u32[]{:S(2)}) collective-permute-start(f32[3,2,32,256]{3,2,1,0:T(8,128)S(1)} %get-tuple-element.259), channel_id=1, source_target_pairs={{4,0},{8,4},{12,8},{16,12},{20,16},{24,20},{28,24},{5,1},{9,5},{13... | collective-permute-start | bytes 589832 | tf_op jit(solution)/shard_map/ppermute | solution.py:162
  166.5 1.5 fusion.78
  168.2 2.1 %collective-permute-done.13.xhi_ref = f32[3,2,32,256]{3,2,1,0:T(8,128)S(1)} collective-permute-done((f32[3,2,32,256]{3,2,1,0:T(8,128)S(1)}, f32[3,2,32,256]{3,2,1,0:T(8,128)S(1)}, u32[]{:S(2)}, u32[]{:S(2)}) %collective-permute-start.13) | collective-permute-done | bytes 196640 | tf_op jit(solution)/shard_map/ppermute | solution.py:162
  170.4 4.6 %collective-permute-start.15 = (f32[3,36,2,256]{3,2,1,0:T(2,128)S(1)}, f32[3,36,2,256]{3,2,1,0:T(2,128)S(1)}, u32[]{:S(2)}, u32[]{:S(2)}) collective-permute-start(f32[3,36,2,256]{3,2,1,0:T(2,128)S(1)} %pad_maximum_fusion.8), channel_id=1, source_target_pairs={{1,0},{2,1},{3,2},{5,4},{6,5},{7,6},{9,8},{10,9},{11,10},{13,12},{... | collective-permute-start | bytes 663560 | tf_op jit(solution)/shard_map/ppermute | solution.py:167
  175.1 1.9 collective-permute-start.14
  177.0 3.2 %fusion.7 = f32[3072,256]{1,0:T(8,128)} fusion(s32[256]{0:T(256)S(1)} %get-tuple-element.303, f32[256]{0:T(256)S(1)} %bitcast.113, s32[256]{0:T(256)S(1)} %get-tuple-element.302), kind=kOutput, calls=%fused_computation.26 | convolution fusion | flops 2416836608 | bytes 3148800 | tf_op jit(solution)/shard_map/dot_general | solution.py:373
  180.3 2.1 %collective-permute-done.14.ylo_ref = f32[3,36,2,256]{3,2,1,0:T(2,128)S(1)} collective-permute-done((f32[3,36,2,256]{3,2,1,0:T(2,128)S(1)}, f32[3,36,2,256]{3,2,1,0:T(2,128)S(1)}, u32[]{:S(2)}, u32[]{:S(2)}) %collective-permute-start.14) | collective-permute-done | bytes 221216 | tf_op jit(solution)/shard_map/ppermute | solution.py:166
  183.1 13.0 %shard_map.125 = f32[3,32,32,256]{3,2,1,0:T(8,128)} custom-call(f32[3,32,32,256]{3,2,1,0:T(8,128)} %shard_map.124.u_ref, f32[3,2,32,256]{3,2,1,0:T(8,128)} %copy-done.2, f32[3,2,32,256]{3,2,1,0:T(8,128)} %copy-done.5, f32[3,36,2,256]{3,2,1,0:T(2,128)} %copy-done.13, f32[3,36,2,256]{3,2,1,0:T(2,128)} %copy-done.10, ...), custom_call_target="tpu_custom_call" | custom-call | tf_op jit(solution)/shard_map/pallas_call | solution.py:135
  (138 shorter events, 14.9 us)
Async XLA Ops:
  16.0 5.3 %copy-start.16 = (s32[8192]{0:T(1024)S(1)}, s32[8192]{0:T(1024)}, u32[]{:S(2)}) copy-start(s32[8192]{0:T(1024)} %param.19) | copy-start | bytes 98308
  16.0 5.3 %copy-start.17 = (s32[8192]{0:T(1024)S(1)}, s32[8192]{0:T(1024)}, u32[]{:S(2)}) copy-start(s32[8192]{0:T(1024)} %param.20) | copy-start | bytes 98308
  24.8 30.6 %copy-start.18 = (s32[256]{0:T(256)S(1)}, s32[256]{0:T(256)}, u32[]{:S(2)}) copy-start(s32[256]{0:T(256)} %param.21) | copy-start | bytes 3076
  39.3 25.6 %all-to-all-start = ((bf16[2,4,32,256]{3,1,0,2:T(4,128)(2,1)}), bf16[2,4,32,256]{3,1,0,2:T(4,128)(2,1)S(1)}, u32[]{:S(2)}, u32[]{:S(2)}) async-start(bf16[2,4,32,256]{3,1,0,2:T(4,128)(2,1)} %copy.27), calls=%async_computation | async-start | bytes 262144 | tf_op jit(solution)/shard_map/all_to_all | solution.py:350
  46.3 9.7 %collective-permute-start = (f32[3,2,32,256]{3,2,1,0:T(8,128)S(1)}, f32[3,2,32,256]{3,2,1,0:T(8,128)S(1)}, u32[]{:S(2)}, u32[]{:S(2)}) collective-permute-start(f32[3,2,32,256]{3,2,1,0:T(8,128)S(1)} %get-tuple-element.272), channel_id=1, source_target_pairs={{0,4},{4,8},{8,12},{12,16},{16,20},{20,24},{24,28},{1,5},{5,9},{9,... | collective-permute-start | bytes 589832 | tf_op jit(solution)/shard_map/ppermute | solution.py:161
  49.7 10.5 %collective-permute-start.1 = (f32[3,2,32,256]{3,2,1,0:T(8,128)S(1)}, f32[3,2,32,256]{3,2,1,0:T(8,128)S(1)}, u32[]{:S(2)}, u32[]{:S(2)}) collective-permute-start(f32[3,2,32,256]{3,2,1,0:T(8,128)S(1)} %get-tuple-element.271), channel_id=1, source_target_pairs={{4,0},{8,4},{12,8},{16,12},{20,16},{24,20},{28,24},{5,1},{9,5},{13... | collective-permute-start | bytes 589832 | tf_op jit(solution)/shard_map/ppermute | solution.py:162
  56.0 13.9 %copy-start = (f32[3,2,32,256]{3,2,1,0:T(8,128)}, f32[3,2,32,256]{3,2,1,0:T(8,128)S(1)}, u32[]{:S(2)}) copy-start(f32[3,2,32,256]{3,2,1,0:T(8,128)S(1)} %collective-permute-done.xlo_ref) | copy-start | bytes 589828
  60.2 9.7 %copy-start.1 = (f32[3,2,32,256]{3,2,1,0:T(8,128)}, f32[3,2,32,256]{3,2,1,0:T(8,128)S(1)}, u32[]{:S(2)}) copy-start(f32[3,2,32,256]{3,2,1,0:T(8,128)S(1)} %collective-permute-done.1.xhi_ref) | copy-start | bytes 589828
  60.4 8.0 %collective-permute-start.3 = (f32[3,36,2,256]{3,2,1,0:T(2,128)S(1)}, f32[3,36,2,256]{3,2,1,0:T(2,128)S(1)}, u32[]{:S(2)}, u32[]{:S(2)}) collective-permute-start(f32[3,36,2,256]{3,2,1,0:T(2,128)S(1)} %pad_maximum_fusion.2), channel_id=1, source_target_pairs={{1,0},{2,1},{3,2},{5,4},{6,5},{7,6},{9,8},{10,9},{11,10},{13,12},{... | collective-permute-start | bytes 663560 | tf_op jit(solution)/shard_map/ppermute | solution.py:167
  62.7 7.3 %collective-permute-start.2 = (f32[3,36,2,256]{3,2,1,0:T(2,128)S(1)}, f32[3,36,2,256]{3,2,1,0:T(2,128)S(1)}, u32[]{:S(2)}, u32[]{:S(2)}) collective-permute-start(f32[3,36,2,256]{3,2,1,0:T(2,128)S(1)} %pad_maximum_fusion.1), channel_id=1, source_target_pairs={{0,1},{1,2},{2,3},{4,5},{5,6},{6,7},{8,9},{9,10},{10,11},{12,13},{... | collective-permute-start | bytes 663560 | tf_op jit(solution)/shard_map/ppermute | solution.py:166
  68.4 1.6 copy-start.8
  69.9 0.7 copy-start.9
  84.7 8.6 %collective-permute-start.4 = (f32[3,2,32,256]{3,2,1,0:T(8,128)S(1)}, f32[3,2,32,256]{3,2,1,0:T(8,128)S(1)}, u32[]{:S(2)}, u32[]{:S(2)}) collective-permute-start(f32[3,2,32,256]{3,2,1,0:T(8,128)S(1)} %get-tuple-element.268), channel_id=1, source_target_pairs={{0,4},{4,8},{8,12},{12,16},{16,20},{20,24},{24,28},{1,5},{5,9},{9,... | collective-permute-start | bytes 589832 | tf_op jit(solution)/shard_map/ppermute | solution.py:161
  86.9 9.4 %collective-permute-start.5 = (f32[3,2,32,256]{3,2,1,0:T(8,128)S(1)}, f32[3,2,32,256]{3,2,1,0:T(8,128)S(1)}, u32[]{:S(2)}, u32[]{:S(2)}) collective-permute-start(f32[3,2,32,256]{3,2,1,0:T(8,128)S(1)} %get-tuple-element.267), channel_id=1, source_target_pairs={{4,0},{8,4},{12,8},{16,12},{20,16},{24,20},{28,24},{5,1},{9,5},{13... | collective-permute-start | bytes 589832 | tf_op jit(solution)/shard_map/ppermute | solution.py:162
  93.2 14.4 %copy-start.4 = (f32[3,2,32,256]{3,2,1,0:T(8,128)}, f32[3,2,32,256]{3,2,1,0:T(8,128)S(1)}, u32[]{:S(2)}) copy-start(f32[3,2,32,256]{3,2,1,0:T(8,128)S(1)} %collective-permute-done.4.xlo_ref) | copy-start | bytes 589828
  96.4 11.3 %copy-start.7 = (f32[3,2,32,256]{3,2,1,0:T(8,128)}, f32[3,2,32,256]{3,2,1,0:T(8,128)S(1)}, u32[]{:S(2)}) copy-start(f32[3,2,32,256]{3,2,1,0:T(8,128)S(1)} %collective-permute-done.5.xhi_ref) | copy-start | bytes 589828
  96.5 9.0 %collective-permute-start.7 = (f32[3,36,2,256]{3,2,1,0:T(2,128)S(1)}, f32[3,36,2,256]{3,2,1,0:T(2,128)S(1)}, u32[]{:S(2)}, u32[]{:S(2)}) collective-permute-start(f32[3,36,2,256]{3,2,1,0:T(2,128)S(1)} %pad_maximum_fusion.4), channel_id=1, source_target_pairs={{1,0},{2,1},{3,2},{5,4},{6,5},{7,6},{9,8},{10,9},{11,10},{13,12},{... | collective-permute-start | bytes 663560 | tf_op jit(solution)/shard_map/ppermute | solution.py:167
  100.4 7.3 %collective-permute-start.6 = (f32[3,36,2,256]{3,2,1,0:T(2,128)S(1)}, f32[3,36,2,256]{3,2,1,0:T(2,128)S(1)}, u32[]{:S(2)}, u32[]{:S(2)}) collective-permute-start(f32[3,36,2,256]{3,2,1,0:T(2,128)S(1)} %pad_maximum_fusion.3), channel_id=1, source_target_pairs={{0,1},{1,2},{2,3},{4,5},{5,6},{6,7},{8,9},{9,10},{10,11},{12,13},{... | collective-permute-start | bytes 663560 | tf_op jit(solution)/shard_map/ppermute | solution.py:166
  105.5 2.1 %copy-start.12 = (f32[3,36,2,256]{3,2,1,0:T(2,128)}, f32[3,36,2,256]{3,2,1,0:T(2,128)S(1)}, u32[]{:S(2)}) copy-start(f32[3,36,2,256]{3,2,1,0:T(2,128)S(1)} %collective-permute-done.7.yhi_ref) | copy-start | bytes 663556
  107.6 0.7 copy-start.15
  122.3 8.5 %collective-permute-start.8 = (f32[3,2,32,256]{3,2,1,0:T(8,128)S(1)}, f32[3,2,32,256]{3,2,1,0:T(8,128)S(1)}, u32[]{:S(2)}, u32[]{:S(2)}) collective-permute-start(f32[3,2,32,256]{3,2,1,0:T(8,128)S(1)} %get-tuple-element.264), channel_id=1, source_target_pairs={{0,4},{4,8},{8,12},{12,16},{16,20},{20,24},{24,28},{1,5},{5,9},{9,... | collective-permute-start | bytes 589832 | tf_op jit(solution)/shard_map/ppermute | solution.py:161
  124.9 8.0 %collective-permute-start.9 = (f32[3,2,32,256]{3,2,1,0:T(8,128)S(1)}, f32[3,2,32,256]{3,2,1,0:T(8,128)S(1)}, u32[]{:S(2)}, u32[]{:S(2)}) collective-permute-start(f32[3,2,32,256]{3,2,1,0:T(8,128)S(1)} %get-tuple-element.263), channel_id=1, source_target_pairs={{4,0},{8,4},{12,8},{16,12},{20,16},{24,20},{28,24},{5,1},{9,5},{13... | collective-permute-start | bytes 589832 | tf_op jit(solution)/shard_map/ppermute | solution.py:162
  130.8 14.2 %copy-start.3 = (f32[3,2,32,256]{3,2,1,0:T(8,128)}, f32[3,2,32,256]{3,2,1,0:T(8,128)S(1)}, u32[]{:S(2)}) copy-start(f32[3,2,32,256]{3,2,1,0:T(8,128)S(1)} %collective-permute-done.8.xlo_ref) | copy-start | bytes 589828
  132.9 12.1 %copy-start.6 = (f32[3,2,32,256]{3,2,1,0:T(8,128)}, f32[3,2,32,256]{3,2,1,0:T(8,128)S(1)}, u32[]{:S(2)}) copy-start(f32[3,2,32,256]{3,2,1,0:T(8,128)S(1)} %collective-permute-done.9.xhi_ref) | copy-start | bytes 589828
  133.0 9.8 %collective-permute-start.11 = (f32[3,36,2,256]{3,2,1,0:T(2,128)S(1)}, f32[3,36,2,256]{3,2,1,0:T(2,128)S(1)}, u32[]{:S(2)}, u32[]{:S(2)}) collective-permute-start(f32[3,36,2,256]{3,2,1,0:T(2,128)S(1)} %pad_maximum_fusion.6), channel_id=1, source_target_pairs={{1,0},{2,1},{3,2},{5,4},{6,5},{7,6},{9,8},{10,9},{11,10},{13,12},{... | collective-permute-start | bytes 663560 | tf_op jit(solution)/shard_map/ppermute | solution.py:167
  137.7 7.3 %collective-permute-start.10 = (f32[3,36,2,256]{3,2,1,0:T(2,128)S(1)}, f32[3,36,2,256]{3,2,1,0:T(2,128)S(1)}, u32[]{:S(2)}, u32[]{:S(2)}) collective-permute-start(f32[3,36,2,256]{3,2,1,0:T(2,128)S(1)} %pad_maximum_fusion.5), channel_id=1, source_target_pairs={{0,1},{1,2},{2,3},{4,5},{5,6},{6,7},{8,9},{9,10},{10,11},{12,13},{... | collective-permute-start | bytes 663560 | tf_op jit(solution)/shard_map/ppermute | solution.py:166
  142.9 2.1 %copy-start.11 = (f32[3,36,2,256]{3,2,1,0:T(2,128)}, f32[3,36,2,256]{3,2,1,0:T(2,128)S(1)}, u32[]{:S(2)}) copy-start(f32[3,36,2,256]{3,2,1,0:T(2,128)S(1)} %collective-permute-done.11.yhi_ref) | copy-start | bytes 663556
  145.0 0.7 copy-start.14
  159.7 8.5 %collective-permute-start.12 = (f32[3,2,32,256]{3,2,1,0:T(8,128)S(1)}, f32[3,2,32,256]{3,2,1,0:T(8,128)S(1)}, u32[]{:S(2)}, u32[]{:S(2)}) collective-permute-start(f32[3,2,32,256]{3,2,1,0:T(8,128)S(1)} %get-tuple-element.260), channel_id=1, source_target_pairs={{0,4},{4,8},{8,12},{12,16},{16,20},{20,24},{24,28},{1,5},{5,9},{9,... | collective-permute-start | bytes 589832 | tf_op jit(solution)/shard_map/ppermute | solution.py:161
  162.2 8.1 %collective-permute-start.13 = (f32[3,2,32,256]{3,2,1,0:T(8,128)S(1)}, f32[3,2,32,256]{3,2,1,0:T(8,128)S(1)}, u32[]{:S(2)}, u32[]{:S(2)}) collective-permute-start(f32[3,2,32,256]{3,2,1,0:T(8,128)S(1)} %get-tuple-element.259), channel_id=1, source_target_pairs={{4,0},{8,4},{12,8},{16,12},{20,16},{24,20},{28,24},{5,1},{9,5},{13... | collective-permute-start | bytes 589832 | tf_op jit(solution)/shard_map/ppermute | solution.py:162
  168.2 14.2 %copy-start.2 = (f32[3,2,32,256]{3,2,1,0:T(8,128)}, f32[3,2,32,256]{3,2,1,0:T(8,128)S(1)}, u32[]{:S(2)}) copy-start(f32[3,2,32,256]{3,2,1,0:T(8,128)S(1)} %collective-permute-done.12.xlo_ref) | copy-start | bytes 589828
  170.3 12.1 %copy-start.5 = (f32[3,2,32,256]{3,2,1,0:T(8,128)}, f32[3,2,32,256]{3,2,1,0:T(8,128)S(1)}, u32[]{:S(2)}) copy-start(f32[3,2,32,256]{3,2,1,0:T(8,128)S(1)} %collective-permute-done.13.xhi_ref) | copy-start | bytes 589828
  170.4 9.8 %collective-permute-start.15 = (f32[3,36,2,256]{3,2,1,0:T(2,128)S(1)}, f32[3,36,2,256]{3,2,1,0:T(2,128)S(1)}, u32[]{:S(2)}, u32[]{:S(2)}) collective-permute-start(f32[3,36,2,256]{3,2,1,0:T(2,128)S(1)} %pad_maximum_fusion.8), channel_id=1, source_target_pairs={{1,0},{2,1},{3,2},{5,4},{6,5},{7,6},{9,8},{10,9},{11,10},{13,12},{... | collective-permute-start | bytes 663560 | tf_op jit(solution)/shard_map/ppermute | solution.py:167
  175.1 7.3 %collective-permute-start.14 = (f32[3,36,2,256]{3,2,1,0:T(2,128)S(1)}, f32[3,36,2,256]{3,2,1,0:T(2,128)S(1)}, u32[]{:S(2)}, u32[]{:S(2)}) collective-permute-start(f32[3,36,2,256]{3,2,1,0:T(2,128)S(1)} %pad_maximum_fusion.7), channel_id=1, source_target_pairs={{0,1},{1,2},{2,3},{4,5},{5,6},{6,7},{8,9},{9,10},{10,11},{12,13},{... | collective-permute-start | bytes 663560 | tf_op jit(solution)/shard_map/ppermute | solution.py:166
  180.3 2.1 %copy-start.10 = (f32[3,36,2,256]{3,2,1,0:T(2,128)}, f32[3,36,2,256]{3,2,1,0:T(2,128)S(1)}, u32[]{:S(2)}) copy-start(f32[3,36,2,256]{3,2,1,0:T(2,128)S(1)} %collective-permute-done.15.yhi_ref) | copy-start | bytes 663556
  182.4 0.7 copy-start.13

commit v7 on v6

--- a/solution.py
+++ b/solution.py
@@ -156,15 +156,19 @@
     size_x = lax.axis_size("gx")
     size_y = lax.axis_size("gy")
     nx, ny = block.shape[1], block.shape[2]
+
+    def send(piece, axis, pairs):
+        return lax.ppermute(piece.astype(jnp.bfloat16), axis, pairs).astype(jnp.float32)
+
     forward_x = [(i, i + 1) for i in range(size_x - 1)]
     backward_x = [(t, s) for s, t in forward_x]
-    xlo = lax.ppermute(block[:, nx - width:], "gx", forward_x)
-    xhi = lax.ppermute(block[:, :width], "gx", backward_x)
+    xlo = send(block[:, nx - width:], "gx", forward_x)
+    xhi = send(block[:, :width], "gx", backward_x)
     forward_y = [(i, i + 1) for i in range(size_y - 1)]
     backward_y = [(t, s) for s, t in forward_y]
     rows = lambda sl: jnp.concatenate([xlo[:, :, sl], block[:, :, sl], xhi[:, :, sl]], axis=1)
-    ylo = lax.ppermute(rows(slice(ny - width, ny)), "gy", forward_y)
-    yhi = lax.ppermute(rows(slice(0, width)), "gy", backward_y)
+    ylo = send(rows(slice(ny - width, ny)), "gy", forward_y)
+    yhi = send(rows(slice(0, width)), "gy", backward_y)
     return xlo, xhi, ylo, yhi
 
 

time: 197 us -> 199 us (1.010); the launches traced: 196 us -> 195 us
  other arithmetic: 20.6 us -> 39.3 us
  local copies, waits for them, and re-layouts: 15 us -> 2.64 us
  waiting for transfers between devices: 20.6 us -> 14.9 us
  starting transfers between devices: 55.9 us -> 50.9 us
  matrix products: 29.6 us -> 33.2 us
    convert_element_type x0 -> x16, other arithmetic: none -> 11.7 us  [send(): lax.ppermute(piece.astype(jnp.bfloat16), axis, pairs).astype(jnp.float32)]
    another operation x0 -> x4, other arithmetic: none -> 6.6 us
    ppermute x16, waiting for transfers between devices: 20.6 us -> 14.9 us  [send(): lax.ppermute(piece.astype(jnp.bfloat16), axis, pairs).astype(jnp.float32)]
    slice x4, local copies, waits for them, and re-layouts: 6.06 us -> 0.63 us  [halos(): block[:, :, sl]]
    ppermute x16, starting transfers between devices: 49.9 us -> 44.9 us  [send(): lax.ppermute(piece.astype(jnp.bfloat16), axis, pairs).astype(jnp.float32)]
    slice x4, local copies, waits for them, and re-layouts: 4.2 us -> 0.06 us  [halos(): xhi = send(block[:, :width], 'gx', backward_x)]
    unnamed x38 -> x8, local copies, waits for them, and re-layouts: 2.81 us -> 0.02 us
    dot_general x2, matrix products: 13.1 us -> 15.8 us  [select_block(): jnp.dot(table_rounded, offset_hot, preferred_element_type=jnp.float32)]
  transfers between devices with their start and end apart: 17 -> 17, of which waited for: 12 -> 8; matrix products, arithmetic and copies ran while one was open for 11% -> 11% of each run, Pallas kernels for 0% -> 0%
where the time goes in v7:
time: 199 us; the launch traced here: 195 us
  Pallas kernels  52 us (26%)
  starting transfers between devices  50.9 us (26%)
  other arithmetic  39.3 us (20%)
  matrix products  33.2 us (17%)
  waiting for transfers between devices  14.9 us (7%)
  local copies, waits for them, and re-layouts  2.64 us (1%)
    pallas_call x4, Pallas kernels, elastic_step(): pl.pallas_call(kernel, grid=(nx // bx,), in_specs=[pl.BlockSpec(u.shape,...  52 us
    ppermute x16, starting transfers between devices, send(): lax.ppermute(piece.astype(jnp.bfloat16), axis, pairs).astype(jnp.float32)  44.9 us
    dot_general x2, matrix products, select_block(): jnp.dot(table_rounded, offset_hot, preferred_element_type=jnp.float32)  15.8 us
    ppermute x16, waiting for transfers between devices, send(): lax.ppermute(piece.astype(jnp.bfloat16), axis, pairs).astype(jnp.float32)  14.9 us
    dot_general x4, matrix products, shards(): source = jnp.dot(column_hot, spread, precision=lax.Precision.HIGHEST)  12.9 us
    convert_element_type x16, other arithmetic, send(): lax.ppermute(piece.astype(jnp.bfloat16), axis, pairs).astype(jnp.float32)  11.7 us
    another operation x4, other arithmetic  6.6 us
    all_to_all x1, starting transfers between devices, shards(): lax.all_to_all(parcel, ('gx', 'gy'), split_axis=2, concat_axis=1, tiled=T...  6 us
  transfers between devices with their start and end apart: 17, of which 8 were waited for; matrix products, arithmetic and copies ran while one was open for 11% of the time, Pallas kernels for 0%

profile of v7, /device:TPU:12, one launch (start us, length us, event | category | flops | bytes accessed | tf_op | source)
XLA Modules:
  0.0 195.4 jit_solution(6604564857777974028)
XLA Ops:
  0.7 0.8 select_reduce_fusion
  2.9 4.9 %sine_multiply_fusion.1 = (f32[32,4,1024]{2,1,0:T(4,128)S(1)}, f32[32,4,1024]{2,1,0:T(4,128)S(1)}, f32[32,4,1024]{2,1,0:T(4,128)S(1)}) fusion(f32[32]{0:T(128)S(1)} %get-tuple-element.307, f32[32,4]{1,0:T(8,128)S(1)} %copy.24, f32[1024]{0:T(1024)S(1)} %multiply_multiply_fusion, f32[1,4,1024]{2,1,0:T(4,128)S(1)} %slice.193, f32[31,4,1024]{2,1,0:T(4,128)S(1)} %slice.192, ...), kind=kLoop, calls=%fused_computation.41 | loop fusion | flops 1441792 | bytes 2102016 | tf_op jit(solution)/shard_map/mul | solution.py:192
  8.1 2.2 %while.32 = (s32[]{:T(128)}, f32[4,1024]{1,0:T(4,128)S(1)}, f32[4,1024]{1,0:T(4,128)S(1)}, f32[32,4,1024]{2,1,0:T(4,128)S(1)}, f32[32,4,1024]{2,1,0:T(4,128)S(1)...) while((s32[]{:T(128)}, f32[4,1024]{1,0:T(4,128)S(1)}, ...), condition=%wide.region_6.7_spmd.clone, body=%wide.region_5.6_spmd.clone.sunk | while | flops 94212 | bytes 147591 | solution.py:208
  10.3 0.9 negate_exponential_fusion
  11.2 4.3 %fusion.43 = (bf16[1,32,4,1024]{3,2,1,0:T(4,128)(2,1)S(1)}, bf16[1,32,4,1024]{3,2,1,0:T(4,128)(2,1)S(1)}) fusion(f32[32,4,1024]{2,1,0:T(4,128)S(1)} %get-tuple-element.191, f32[32,4,1024]{2,1,0:T(4,128)S(1)} %get-tuple-element.190, f32[32,4,1024]{2,1,0:T(4,128)S(1)} %negate_exponential_fusion, f32[32,4,1024]{2,1,0:T(4,128)S(1)} %fusion.23), kind=kLoop, calls=%fused_computation.74 | loop fusion | flops 1835008 | bytes 2621440 | tf_op jit(solution)/shard_map/stack | solution.py:221
  16.0 1.0 fusion.58
  17.7 3.6 %subtract_convert_fusion = bf16[1024,32,64]{0,2,1:T(8,128)(2,1)} fusion(f32[1024,64]{0,1:T(8,128)S(1)} %get-tuple-element.301, f32[1024,32]{0,1:T(8,128)S(1)} %get-tuple-element.295, f32[1024,64]{0,1:T(8,128)S(1)} %get-tuple-element.300, f32[1024,32]{0,1:T(8,128)S(1)} %get-tuple-element.294), kind=kLoop, calls=%fused_computation.24 | loop fusion | flops 8388608 | bytes 4980736 | tf_op jit(solution)/shard_map/convert_element_type | solution.py:236
  21.4 4.4 %convolution_convert_fusion = bf16[256,2048]{1,0:T(8,128)(2,1)} fusion(bf16[256,1024]{1,0:T(8,128)(2,1)S(1)} %bitcast.109, bf16[1024,2048]{0,1:T(8,128)(2,1)} %bitcast.107), kind=kOutput, calls=%fused_computation.30 | convolution fusion | flops 1074266112 | bytes 5767168 | tf_op jit(solution)/shard_map/dot_general | solution.py:324
  25.8 16.0 %while.31 = (s32[]{:T(128)}, bf16[2,2,4,4096]{3,2,1,0:T(4,128)(2,1)S(1)}, s32[2,4096]{1,0:T(2,128)S(1)}, bf16[256,2048]{1,0:T(8,128)(2,1)}, s32[2,4096]{1,0:T(2,128)S(1)}, /*index=5*/s32[]{:T(128)}) while((s32[]{:T(128)}, bf16[2,2,4,4096]{3,2,1,0:T(4,128)(2,1)S(1)}, s32[2,4096]{1,0:T(2,128)S(1)}, bf16[256,2048]{1,0:T(8,128)(2,1)}, ...), condition=%wide.region_9.10_spmd, body=%wide.region_7.9_spmd.sunk | while | flops 4305682432 | bytes 2392141 | solution.py:347
  25.9 8.0 %multiply_reduce_fusion.2 = bf16[2,4,4096]{2,1,0:T(4,128)(2,1)S(1)} fusion(f32[32,4096]{1,0:T(8,128)S(1)} %fusion.102, bf16[256,2048]{1,0:T(8,128)(2,1)} %get-tuple-element.448, s32[4096]{0:T(1024)S(1)} %bitcast.111), kind=kOutput, calls=%fused_computation.3.clone.1 | convolution fusion | flops 4305420288 | bytes 1654784 | tf_op jit(solution)/shard_map/while/body/eval_jaxpr/dot_general | solution.py:339
  34.0 7.8 %multiply_reduce_fusion.2 = bf16[2,4,4096]{2,1,0:T(4,128)(2,1)S(1)} fusion(f32[32,4096]{1,0:T(8,128)S(1)} %fusion.102, bf16[256,2048]{1,0:T(8,128)(2,1)} %get-tuple-element.448, s32[4096]{0:T(1024)S(1)} %bitcast.111), kind=kOutput, calls=%fused_computation.3.clone.1 | convolution fusion | flops 4305420288 | bytes 1654784 | tf_op jit(solution)/shard_map/while/body/eval_jaxpr/dot_general | solution.py:339
  42.9 6.0 %all-to-all-start = ((bf16[2,4,32,256]{3,1,0,2:T(4,128)(2,1)}), bf16[2,4,32,256]{3,1,0,2:T(4,128)(2,1)S(1)}, u32[]{:S(2)}, u32[]{:S(2)}) async-start(bf16[2,4,32,256]{3,1,0,2:T(4,128)(2,1)} %copy.27), calls=%async_computation | async-start | bytes 262144 | tf_op jit(solution)/shard_map/all_to_all | solution.py:354
  49.1 3.4 %collective-permute-start = (bf16[3,2,32,256]{3,2,1,0:T(8,128)(2,1)S(1)}, bf16[3,2,32,256]{3,2,1,0:T(8,128)(2,1)S(1)}, u32[]{:S(2)}, u32[]{:S(2)}) collective-permute-start(bf16[3,2,32,256]{3,2,1,0:T(8,128)(2,1)S(1)} %get-tuple-element.274), channel_id=1, source_target_pairs={{0,4},{4,8},{8,12},{12,16},{16,20},{20,24},{24,28},{1,5},{5,9},{9,... | collective-permute-start | bytes 294920 | tf_op jit(solution)/shard_map/ppermute | solution.py:161
  52.5 3.4 %collective-permute-start.1 = (bf16[3,2,32,256]{3,2,1,0:T(8,128)(2,1)S(1)}, bf16[3,2,32,256]{3,2,1,0:T(8,128)(2,1)S(1)}, u32[]{:S(2)}, u32[]{:S(2)}) collective-permute-start(bf16[3,2,32,256]{3,2,1,0:T(8,128)(2,1)S(1)} %get-tuple-element.273), channel_id=1, source_target_pairs={{4,0},{8,4},{12,8},{16,12},{20,16},{24,20},{28,24},{5,1},{9,5},{13... | collective-permute-start | bytes 294920 | tf_op jit(solution)/shard_map/ppermute | solution.py:161
  56.9 2.1 %collective-permute-done.1 = bf16[3,2,32,256]{3,2,1,0:T(8,128)(2,1)S(1)} collective-permute-done((bf16[3,2,32,256]{3,2,1,0:T(8,128)(2,1)S(1)}, bf16[3,2,32,256]{3,2,1,0:T(8,128)(2,1)S(1)}, u32[]{:S(2)}, u32[]{:S(2)}) %collective-permute-start.1) | collective-permute-done | bytes 98336 | tf_op jit(solution)/shard_map/ppermute | solution.py:161
  59.2 1.9 collective-permute-start.3
  61.3 2.4 %collective-permute-start.2 = (bf16[3,36,2,256]{3,2,1,0:T(2,128)(2,1)S(1)}, bf16[3,36,2,256]{3,2,1,0:T(2,128)(2,1)S(1)}, u32[]{:S(2)}, u32[]{:S(2)}) collective-permute-start(bf16[3,36,2,256]{3,2,1,0:T(2,128)(2,1)S(1)} %pad_maximum_fusion.1), channel_id=1, source_target_pairs={{0,1},{1,2},{2,3},{4,5},{5,6},{6,7},{8,9},{9,10},{10,11},{12,13},{... | collective-permute-start | bytes 331784 | tf_op jit(solution)/shard_map/ppermute | solution.py:161
  65.9 1.5 collective-permute-done.2
  68.4 3.2 %fusion.10 = f32[3072,256]{1,0:T(8,128)} fusion(s32[256]{0:T(256)S(1)} %get-tuple-element.303, f32[256]{0:T(256)S(1)} %bitcast.116, s32[256]{0:T(256)S(1)} %get-tuple-element.302), kind=kOutput, calls=%fused_computation.29 | convolution fusion | flops 2416836608 | bytes 3148800 | tf_op jit(solution)/shard_map/dot_general | solution.py:377
  71.7 13.0 %shard_map.122.u_ref.prev_ref = f32[3,32,32,256]{3,2,1,0:T(8,128)} custom-call(f32[3,32,32,256]{3,2,1,0:T(8,128)} %prev_ref.3, f32[3,2,32,256]{3,2,1,0:T(8,128)} %convert_element_type.151.xlo_ref, f32[3,2,32,256]{3,2,1,0:T(8,128)} %convert_element_type.152.xhi_ref, f32[3,36,2,256]{3,2,1,0:T(2,128)} %convert_element_type.153.ylo_ref, ...), custom_call_target="tpu_custom_call" | custom-call | tf_op jit(solution)/shard_map/pallas_call | solution.py:135
  84.7 2.1 %convert.75 = bf16[3,32,32,256]{3,2,1,0:T(8,128)(2,1)S(1)} convert(f32[3,32,32,256]{3,2,1,0:T(8,128)} %shard_map.122.u_ref.prev_ref) | non-fusion elementwise | flops 786432 | bytes 4718592 | tf_op jit(solution)/shard_map/convert.41
  86.8 4.3 %collective-permute-start.4 = (bf16[3,2,32,256]{3,2,1,0:T(8,128)(2,1)S(1)}, bf16[3,2,32,256]{3,2,1,0:T(8,128)(2,1)S(1)}, u32[]{:S(2)}, u32[]{:S(2)}) collective-permute-start(bf16[3,2,32,256]{3,2,1,0:T(8,128)(2,1)S(1)} %get-tuple-element.270), channel_id=1, source_target_pairs={{0,4},{4,8},{8,12},{12,16},{16,20},{20,24},{24,28},{1,5},{5,9},{9,... | collective-permute-start | bytes 294920 | tf_op jit(solution)/shard_map/ppermute | solution.py:161
  91.3 2.5 %collective-permute-start.5 = (bf16[3,2,32,256]{3,2,1,0:T(8,128)(2,1)S(1)}, bf16[3,2,32,256]{3,2,1,0:T(8,128)(2,1)S(1)}, u32[]{:S(2)}, u32[]{:S(2)}) collective-permute-start(bf16[3,2,32,256]{3,2,1,0:T(8,128)(2,1)S(1)} %get-tuple-element.269), channel_id=1, source_target_pairs={{4,0},{8,4},{12,8},{16,12},{20,16},{24,20},{28,24},{5,1},{9,5},{13... | collective-permute-start | bytes 294920 | tf_op jit(solution)/shard_map/ppermute | solution.py:161
  94.3 3.4 %collective-permute-done.5 = bf16[3,2,32,256]{3,2,1,0:T(8,128)(2,1)S(1)} collective-permute-done((bf16[3,2,32,256]{3,2,1,0:T(8,128)(2,1)S(1)}, bf16[3,2,32,256]{3,2,1,0:T(8,128)(2,1)S(1)}, u32[]{:S(2)}, u32[]{:S(2)}) %collective-permute-start.5) | collective-permute-done | bytes 98336 | tf_op jit(solution)/shard_map/ppermute | solution.py:161
  98.0 1.9 collective-permute-start.7
  100.1 2.4 %collective-permute-start.6 = (bf16[3,36,2,256]{3,2,1,0:T(2,128)(2,1)S(1)}, bf16[3,36,2,256]{3,2,1,0:T(2,128)(2,1)S(1)}, u32[]{:S(2)}, u32[]{:S(2)}) collective-permute-start(bf16[3,36,2,256]{3,2,1,0:T(2,128)(2,1)S(1)} %pad_maximum_fusion.3), channel_id=1, source_target_pairs={{0,1},{1,2},{2,3},{4,5},{5,6},{6,7},{8,9},{9,10},{10,11},{12,13},{... | collective-permute-start | bytes 331784 | tf_op jit(solution)/shard_map/ppermute | solution.py:161
  102.5 3.2 %fusion.9 = f32[3072,256]{1,0:T(8,128)} fusion(s32[256]{0:T(256)S(1)} %get-tuple-element.303, f32[256]{0:T(256)S(1)} %bitcast.115, s32[256]{0:T(256)S(1)} %get-tuple-element.302), kind=kOutput, calls=%fused_computation.28 | convolution fusion | flops 2416836608 | bytes 3148800 | tf_op jit(solution)/shard_map/dot_general | solution.py:377
  107.1 0.8 convert_element_type.170.yhi_ref
  108.6 13.0 %shard_map.123.u_ref.prev_ref = f32[3,32,32,256]{3,2,1,0:T(8,128)} custom-call(f32[3,32,32,256]{3,2,1,0:T(8,128)} %shard_map.122.u_ref.prev_ref, f32[3,2,32,256]{3,2,1,0:T(8,128)} %convert_element_type.167.xlo_ref, f32[3,2,32,256]{3,2,1,0:T(8,128)} %convert_element_type.168.xhi_ref, f32[3,36,2,256]{3,2,1,0:T(2,128)} %convert_element_type.169.ylo_ref, ...), custom_call_target="tpu_custom_call" | custom-call | tf_op jit(solution)/shard_map/pallas_call | solution.py:135
  121.7 2.1 %convert.76 = bf16[3,32,32,256]{3,2,1,0:T(8,128)(2,1)S(1)} convert(f32[3,32,32,256]{3,2,1,0:T(8,128)} %shard_map.123.u_ref.prev_ref) | non-fusion elementwise | flops 786432 | bytes 4718592 | tf_op jit(solution)/shard_map/convert.27
  123.8 3.4 %collective-permute-start.8 = (bf16[3,2,32,256]{3,2,1,0:T(8,128)(2,1)S(1)}, bf16[3,2,32,256]{3,2,1,0:T(8,128)(2,1)S(1)}, u32[]{:S(2)}, u32[]{:S(2)}) collective-permute-start(bf16[3,2,32,256]{3,2,1,0:T(8,128)(2,1)S(1)} %get-tuple-element.266), channel_id=1, source_target_pairs={{0,4},{4,8},{8,12},{12,16},{16,20},{20,24},{24,28},{1,5},{5,9},{9,... | collective-permute-start | bytes 294920 | tf_op jit(solution)/shard_map/ppermute | solution.py:161
  127.4 3.4 %collective-permute-start.9 = (bf16[3,2,32,256]{3,2,1,0:T(8,128)(2,1)S(1)}, bf16[3,2,32,256]{3,2,1,0:T(8,128)(2,1)S(1)}, u32[]{:S(2)}, u32[]{:S(2)}) collective-permute-start(bf16[3,2,32,256]{3,2,1,0:T(8,128)(2,1)S(1)} %get-tuple-element.265), channel_id=1, source_target_pairs={{4,0},{8,4},{12,8},{16,12},{20,16},{24,20},{28,24},{5,1},{9,5},{13... | collective-permute-start | bytes 294920 | tf_op jit(solution)/shard_map/ppermute | solution.py:161
  131.3 2.6 %collective-permute-done.9 = bf16[3,2,32,256]{3,2,1,0:T(8,128)(2,1)S(1)} collective-permute-done((bf16[3,2,32,256]{3,2,1,0:T(8,128)(2,1)S(1)}, bf16[3,2,32,256]{3,2,1,0:T(8,128)(2,1)S(1)}, u32[]{:S(2)}, u32[]{:S(2)}) %collective-permute-start.9) | collective-permute-done | bytes 98336 | tf_op jit(solution)/shard_map/ppermute | solution.py:161
  134.1 2.3 %collective-permute-start.11 = (bf16[3,36,2,256]{3,2,1,0:T(2,128)(2,1)S(1)}, bf16[3,36,2,256]{3,2,1,0:T(2,128)(2,1)S(1)}, u32[]{:S(2)}, u32[]{:S(2)}) collective-permute-start(bf16[3,36,2,256]{3,2,1,0:T(2,128)(2,1)S(1)} %pad_maximum_fusion.6), channel_id=1, source_target_pairs={{1,0},{2,1},{3,2},{5,4},{6,5},{7,6},{9,8},{10,9},{11,10},{13,12},{... | collective-permute-start | bytes 331784 | tf_op jit(solution)/shard_map/ppermute | solution.py:161
  136.6 2.0 %collective-permute-start.10 = (bf16[3,36,2,256]{3,2,1,0:T(2,128)(2,1)S(1)}, bf16[3,36,2,256]{3,2,1,0:T(2,128)(2,1)S(1)}, u32[]{:S(2)}, u32[]{:S(2)}) collective-permute-start(bf16[3,36,2,256]{3,2,1,0:T(2,128)(2,1)S(1)} %pad_maximum_fusion.5), channel_id=1, source_target_pairs={{0,1},{1,2},{2,3},{4,5},{5,6},{6,7},{8,9},{9,10},{10,11},{12,13},{... | collective-permute-start | bytes 331784 | tf_op jit(solution)/shard_map/ppermute | solution.py:161
  138.6 3.2 %fusion.8 = f32[3072,256]{1,0:T(8,128)} fusion(s32[256]{0:T(256)S(1)} %get-tuple-element.303, f32[256]{0:T(256)S(1)} %bitcast.114, s32[256]{0:T(256)S(1)} %get-tuple-element.302), kind=kOutput, calls=%fused_computation.27 | convolution fusion | flops 2416836608 | bytes 3148800 | tf_op jit(solution)/shard_map/dot_general | solution.py:377
  143.2 0.8 convert_element_type.174.yhi_ref
  144.0 0.8 convert_element_type.173.ylo_ref
  144.8 13.0 %shard_map.124.u_ref = f32[3,32,32,256]{3,2,1,0:T(8,128)} custom-call(f32[3,32,32,256]{3,2,1,0:T(8,128)} %shard_map.123.u_ref.prev_ref, f32[3,2,32,256]{3,2,1,0:T(8,128)} %convert_element_type.171.xlo_ref, f32[3,2,32,256]{3,2,1,0:T(8,128)} %convert_element_type.172.xhi_ref, f32[3,36,2,256]{3,2,1,0:T(2,128)} %convert_element_type.173.ylo_ref, ...), custom_call_target="tpu_custom_call" | custom-call | tf_op jit(solution)/shard_map/pallas_call | solution.py:135
  157.8 2.1 %convert.77 = bf16[3,32,32,256]{3,2,1,0:T(8,128)(2,1)S(1)} convert(f32[3,32,32,256]{3,2,1,0:T(8,128)} %shard_map.124.u_ref) | non-fusion elementwise | flops 786432 | bytes 4718592 | tf_op jit(solution)/shard_map/convert.13
  159.9 4.3 %collective-permute-start.12 = (bf16[3,2,32,256]{3,2,1,0:T(8,128)(2,1)S(1)}, bf16[3,2,32,256]{3,2,1,0:T(8,128)(2,1)S(1)}, u32[]{:S(2)}, u32[]{:S(2)}) collective-permute-start(bf16[3,2,32,256]{3,2,1,0:T(8,128)(2,1)S(1)} %get-tuple-element.262), channel_id=1, source_target_pairs={{0,4},{4,8},{8,12},{12,16},{16,20},{20,24},{24,28},{1,5},{5,9},{9,... | collective-permute-start | bytes 294920 | tf_op jit(solution)/shard_map/ppermute | solution.py:161
  164.4 2.4 %collective-permute-start.13 = (bf16[3,2,32,256]{3,2,1,0:T(8,128)(2,1)S(1)}, bf16[3,2,32,256]{3,2,1,0:T(8,128)(2,1)S(1)}, u32[]{:S(2)}, u32[]{:S(2)}) collective-permute-start(bf16[3,2,32,256]{3,2,1,0:T(8,128)(2,1)S(1)} %get-tuple-element.261), channel_id=1, source_target_pairs={{4,0},{8,4},{12,8},{16,12},{20,16},{24,20},{28,24},{5,1},{9,5},{13... | collective-permute-start | bytes 294920 | tf_op jit(solution)/shard_map/ppermute | solution.py:161
  167.3 3.6 %collective-permute-done.13 = bf16[3,2,32,256]{3,2,1,0:T(8,128)(2,1)S(1)} collective-permute-done((bf16[3,2,32,256]{3,2,1,0:T(8,128)(2,1)S(1)}, bf16[3,2,32,256]{3,2,1,0:T(8,128)(2,1)S(1)}, u32[]{:S(2)}, u32[]{:S(2)}) %collective-permute-start.13) | collective-permute-done | bytes 98336 | tf_op jit(solution)/shard_map/ppermute | solution.py:161
  171.1 3.0 %collective-permute-start.15 = (bf16[3,36,2,256]{3,2,1,0:T(2,128)(2,1)S(1)}, bf16[3,36,2,256]{3,2,1,0:T(2,128)(2,1)S(1)}, u32[]{:S(2)}, u32[]{:S(2)}) collective-permute-start(bf16[3,36,2,256]{3,2,1,0:T(2,128)(2,1)S(1)} %pad_maximum_fusion.8), channel_id=1, source_target_pairs={{1,0},{2,1},{3,2},{5,4},{6,5},{7,6},{9,8},{10,9},{11,10},{13,12},{... | collective-permute-start | bytes 331784 | tf_op jit(solution)/shard_map/ppermute | solution.py:161
  174.3 1.9 collective-permute-start.14
  176.2 3.2 %fusion.7 = f32[3072,256]{1,0:T(8,128)} fusion(s32[256]{0:T(256)S(1)} %get-tuple-element.303, f32[256]{0:T(256)S(1)} %bitcast.113, s32[256]{0:T(256)S(1)} %get-tuple-element.302), kind=kOutput, calls=%fused_computation.26 | convolution fusion | flops 2416836608 | bytes 3148800 | tf_op jit(solution)/shard_map/dot_general | solution.py:377
  181.6 0.8 convert_element_type.177.ylo_ref
  182.4 13.0 %shard_map.125 = f32[3,32,32,256]{3,2,1,0:T(8,128)} custom-call(f32[3,32,32,256]{3,2,1,0:T(8,128)} %shard_map.124.u_ref, f32[3,2,32,256]{3,2,1,0:T(8,128)} %convert_element_type.175.xlo_ref, f32[3,2,32,256]{3,2,1,0:T(8,128)} %convert_element_type.176.xhi_ref, f32[3,36,2,256]{3,2,1,0:T(2,128)} %convert_element_type.177.ylo_ref, ...), custom_call_target="tpu_custom_call" | custom-call | tf_op jit(solution)/shard_map/pallas_call | solution.py:135
  (128 shorter events, 18.7 us)
Async XLA Ops:
  16.0 5.3 %copy-start.1 = (s32[8192]{0:T(1024)S(1)}, s32[8192]{0:T(1024)}, u32[]{:S(2)}) copy-start(s32[8192]{0:T(1024)} %param.19) | copy-start | bytes 98308
  16.0 5.3 %copy-start.2 = (s32[8192]{0:T(1024)S(1)}, s32[8192]{0:T(1024)}, u32[]{:S(2)}) copy-start(s32[8192]{0:T(1024)} %param.20) | copy-start | bytes 98308
  25.8 23.1 %copy-start = (f32[3,32,32,256]{3,2,1,0:T(8,128)S(1)}, f32[3,32,32,256]{3,2,1,0:T(8,128)}, u32[]{:S(2)}) copy-start(f32[3,32,32,256]{3,2,1,0:T(8,128)} %prev_ref.3) | copy-start | bytes 9437188
  42.0 14.2 %copy-start.3 = (s32[256]{0:T(256)S(1)}, s32[256]{0:T(256)}, u32[]{:S(2)}) copy-start(s32[256]{0:T(256)} %param.21) | copy-start | bytes 3076
  42.9 25.3 %all-to-all-start = ((bf16[2,4,32,256]{3,1,0,2:T(4,128)(2,1)}), bf16[2,4,32,256]{3,1,0,2:T(4,128)(2,1)S(1)}, u32[]{:S(2)}, u32[]{:S(2)}) async-start(bf16[2,4,32,256]{3,1,0,2:T(4,128)(2,1)} %copy.27), calls=%async_computation | async-start | bytes 262144 | tf_op jit(solution)/shard_map/all_to_all | solution.py:354
  49.1 7.7 %collective-permute-start = (bf16[3,2,32,256]{3,2,1,0:T(8,128)(2,1)S(1)}, bf16[3,2,32,256]{3,2,1,0:T(8,128)(2,1)S(1)}, u32[]{:S(2)}, u32[]{:S(2)}) collective-permute-start(bf16[3,2,32,256]{3,2,1,0:T(8,128)(2,1)S(1)} %get-tuple-element.274), channel_id=1, source_target_pairs={{0,4},{4,8},{8,12},{12,16},{16,20},{20,24},{24,28},{1,5},{5,9},{9,... | collective-permute-start | bytes 294920 | tf_op jit(solution)/shard_map/ppermute | solution.py:161
  52.5 6.5 %collective-permute-start.1 = (bf16[3,2,32,256]{3,2,1,0:T(8,128)(2,1)S(1)}, bf16[3,2,32,256]{3,2,1,0:T(8,128)(2,1)S(1)}, u32[]{:S(2)}, u32[]{:S(2)}) collective-permute-start(bf16[3,2,32,256]{3,2,1,0:T(8,128)(2,1)S(1)} %get-tuple-element.273), channel_id=1, source_target_pairs={{4,0},{8,4},{12,8},{16,12},{20,16},{24,20},{28,24},{5,1},{9,5},{13... | collective-permute-start | bytes 294920 | tf_op jit(solution)/shard_map/ppermute | solution.py:161
  59.2 5.9 %collective-permute-start.3 = (bf16[3,36,2,256]{3,2,1,0:T(2,128)(2,1)S(1)}, bf16[3,36,2,256]{3,2,1,0:T(2,128)(2,1)S(1)}, u32[]{:S(2)}, u32[]{:S(2)}) collective-permute-start(bf16[3,36,2,256]{3,2,1,0:T(2,128)(2,1)S(1)} %pad_maximum_fusion.2), channel_id=1, source_target_pairs={{1,0},{2,1},{3,2},{5,4},{6,5},{7,6},{9,8},{10,9},{11,10},{13,12},{... | collective-permute-start | bytes 331784 | tf_op jit(solution)/shard_map/ppermute | solution.py:161
  61.3 6.1 %collective-permute-start.2 = (bf16[3,36,2,256]{3,2,1,0:T(2,128)(2,1)S(1)}, bf16[3,36,2,256]{3,2,1,0:T(2,128)(2,1)S(1)}, u32[]{:S(2)}, u32[]{:S(2)}) collective-permute-start(bf16[3,36,2,256]{3,2,1,0:T(2,128)(2,1)S(1)} %pad_maximum_fusion.1), channel_id=1, source_target_pairs={{0,1},{1,2},{2,3},{4,5},{5,6},{6,7},{8,9},{9,10},{10,11},{12,13},{... | collective-permute-start | bytes 331784 | tf_op jit(solution)/shard_map/ppermute | solution.py:161
  86.8 7.5 %collective-permute-start.4 = (bf16[3,2,32,256]{3,2,1,0:T(8,128)(2,1)S(1)}, bf16[3,2,32,256]{3,2,1,0:T(8,128)(2,1)S(1)}, u32[]{:S(2)}, u32[]{:S(2)}) collective-permute-start(bf16[3,2,32,256]{3,2,1,0:T(8,128)(2,1)S(1)} %get-tuple-element.270), channel_id=1, source_target_pairs={{0,4},{4,8},{8,12},{12,16},{16,20},{20,24},{24,28},{1,5},{5,9},{9,... | collective-permute-start | bytes 294920 | tf_op jit(solution)/shard_map/ppermute | solution.py:161
  91.3 6.5 %collective-permute-start.5 = (bf16[3,2,32,256]{3,2,1,0:T(8,128)(2,1)S(1)}, bf16[3,2,32,256]{3,2,1,0:T(8,128)(2,1)S(1)}, u32[]{:S(2)}, u32[]{:S(2)}) collective-permute-start(bf16[3,2,32,256]{3,2,1,0:T(8,128)(2,1)S(1)} %get-tuple-element.269), channel_id=1, source_target_pairs={{4,0},{8,4},{12,8},{16,12},{20,16},{24,20},{28,24},{5,1},{9,5},{13... | collective-permute-start | bytes 294920 | tf_op jit(solution)/shard_map/ppermute | solution.py:161
  98.0 9.1 %collective-permute-start.7 = (bf16[3,36,2,256]{3,2,1,0:T(2,128)(2,1)S(1)}, bf16[3,36,2,256]{3,2,1,0:T(2,128)(2,1)S(1)}, u32[]{:S(2)}, u32[]{:S(2)}) collective-permute-start(bf16[3,36,2,256]{3,2,1,0:T(2,128)(2,1)S(1)} %pad_maximum_fusion.4), channel_id=1, source_target_pairs={{1,0},{2,1},{3,2},{5,4},{6,5},{7,6},{9,8},{10,9},{11,10},{13,12},{... | collective-permute-start | bytes 331784 | tf_op jit(solution)/shard_map/ppermute | solution.py:161
  100.1 7.8 %collective-permute-start.6 = (bf16[3,36,2,256]{3,2,1,0:T(2,128)(2,1)S(1)}, bf16[3,36,2,256]{3,2,1,0:T(2,128)(2,1)S(1)}, u32[]{:S(2)}, u32[]{:S(2)}) collective-permute-start(bf16[3,36,2,256]{3,2,1,0:T(2,128)(2,1)S(1)} %pad_maximum_fusion.3), channel_id=1, source_target_pairs={{0,1},{1,2},{2,3},{4,5},{5,6},{6,7},{8,9},{9,10},{10,11},{12,13},{... | collective-permute-start | bytes 331784 | tf_op jit(solution)/shard_map/ppermute | solution.py:161
  123.8 7.4 %collective-permute-start.8 = (bf16[3,2,32,256]{3,2,1,0:T(8,128)(2,1)S(1)}, bf16[3,2,32,256]{3,2,1,0:T(8,128)(2,1)S(1)}, u32[]{:S(2)}, u32[]{:S(2)}) collective-permute-start(bf16[3,2,32,256]{3,2,1,0:T(8,128)(2,1)S(1)} %get-tuple-element.266), channel_id=1, source_target_pairs={{0,4},{4,8},{8,12},{12,16},{16,20},{20,24},{24,28},{1,5},{5,9},{9,... | collective-permute-start | bytes 294920 | tf_op jit(solution)/shard_map/ppermute | solution.py:161
  127.4 6.5 %collective-permute-start.9 = (bf16[3,2,32,256]{3,2,1,0:T(8,128)(2,1)S(1)}, bf16[3,2,32,256]{3,2,1,0:T(8,128)(2,1)S(1)}, u32[]{:S(2)}, u32[]{:S(2)}) collective-permute-start(bf16[3,2,32,256]{3,2,1,0:T(8,128)(2,1)S(1)} %get-tuple-element.265), channel_id=1, source_target_pairs={{4,0},{8,4},{12,8},{16,12},{20,16},{24,20},{28,24},{5,1},{9,5},{13... | collective-permute-start | bytes 294920 | tf_op jit(solution)/shard_map/ppermute | solution.py:161
  134.1 9.1 %collective-permute-start.11 = (bf16[3,36,2,256]{3,2,1,0:T(2,128)(2,1)S(1)}, bf16[3,36,2,256]{3,2,1,0:T(2,128)(2,1)S(1)}, u32[]{:S(2)}, u32[]{:S(2)}) collective-permute-start(bf16[3,36,2,256]{3,2,1,0:T(2,128)(2,1)S(1)} %pad_maximum_fusion.6), channel_id=1, source_target_pairs={{1,0},{2,1},{3,2},{5,4},{6,5},{7,6},{9,8},{10,9},{11,10},{13,12},{... | collective-permute-start | bytes 331784 | tf_op jit(solution)/shard_map/ppermute | solution.py:161
  136.6 7.4 %collective-permute-start.10 = (bf16[3,36,2,256]{3,2,1,0:T(2,128)(2,1)S(1)}, bf16[3,36,2,256]{3,2,1,0:T(2,128)(2,1)S(1)}, u32[]{:S(2)}, u32[]{:S(2)}) collective-permute-start(bf16[3,36,2,256]{3,2,1,0:T(2,128)(2,1)S(1)} %pad_maximum_fusion.5), channel_id=1, source_target_pairs={{0,1},{1,2},{2,3},{4,5},{5,6},{6,7},{8,9},{9,10},{10,11},{12,13},{... | collective-permute-start | bytes 331784 | tf_op jit(solution)/shard_map/ppermute | solution.py:161
  159.9 7.4 %collective-permute-start.12 = (bf16[3,2,32,256]{3,2,1,0:T(8,128)(2,1)S(1)}, bf16[3,2,32,256]{3,2,1,0:T(8,128)(2,1)S(1)}, u32[]{:S(2)}, u32[]{:S(2)}) collective-permute-start(bf16[3,2,32,256]{3,2,1,0:T(8,128)(2,1)S(1)} %get-tuple-element.262), channel_id=1, source_target_pairs={{0,4},{4,8},{8,12},{12,16},{16,20},{20,24},{24,28},{1,5},{5,9},{9,... | collective-permute-start | bytes 294920 | tf_op jit(solution)/shard_map/ppermute | solution.py:161
  164.4 6.5 %collective-permute-start.13 = (bf16[3,2,32,256]{3,2,1,0:T(8,128)(2,1)S(1)}, bf16[3,2,32,256]{3,2,1,0:T(8,128)(2,1)S(1)}, u32[]{:S(2)}, u32[]{:S(2)}) collective-permute-start(bf16[3,2,32,256]{3,2,1,0:T(8,128)(2,1)S(1)} %get-tuple-element.261), channel_id=1, source_target_pairs={{4,0},{8,4},{12,8},{16,12},{20,16},{24,20},{28,24},{5,1},{9,5},{13... | collective-permute-start | bytes 294920 | tf_op jit(solution)/shard_map/ppermute | solution.py:161
  171.1 9.7 %collective-permute-start.15 = (bf16[3,36,2,256]{3,2,1,0:T(2,128)(2,1)S(1)}, bf16[3,36,2,256]{3,2,1,0:T(2,128)(2,1)S(1)}, u32[]{:S(2)}, u32[]{:S(2)}) collective-permute-start(bf16[3,36,2,256]{3,2,1,0:T(2,128)(2,1)S(1)} %pad_maximum_fusion.8), channel_id=1, source_target_pairs={{1,0},{2,1},{3,2},{5,4},{6,5},{7,6},{9,8},{10,9},{11,10},{13,12},{... | collective-permute-start | bytes 331784 | tf_op jit(solution)/shard_map/ppermute | solution.py:161
  174.3 7.3 %collective-permute-start.14 = (bf16[3,36,2,256]{3,2,1,0:T(2,128)(2,1)S(1)}, bf16[3,36,2,256]{3,2,1,0:T(2,128)(2,1)S(1)}, u32[]{:S(2)}, u32[]{:S(2)}) collective-permute-start(bf16[3,36,2,256]{3,2,1,0:T(2,128)(2,1)S(1)} %pad_maximum_fusion.7), channel_id=1, source_target_pairs={{0,1},{1,2},{2,3},{4,5},{5,6},{6,7},{8,9},{9,10},{10,11},{12,13},{... | collective-permute-start | bytes 331784 | tf_op jit(solution)/shard_map/ppermute | solution.py:161

commit v8 on v6

--- a/solution.py
+++ b/solution.py
@@ -35,7 +35,8 @@
 YPAD = 8
 
 
-def step_kernel(u_ref, xlo_ref, xhi_ref, ylo_ref, yhi_ref, prev_ref, mod_ref, src_ref, out_ref, up_ref, *, bx):
+def step_kernel(u_ref, xlo_ref, xhi_ref, ylo_ref, yhi_ref, prev_ref, mod_ref, src_ref, out_ref,
+                fxlo_ref, fxhi_ref, rylo_ref, ryhi_ref, up_ref, *, bx):
     i = pl.program_id(0)
     nx, ny = u_ref.shape[1], u_ref.shape[2]
 
@@ -61,9 +62,12 @@
             return v
         return jnp.where(masks[dz], pltpu.roll(v, (-dz) % depth, 1), 0.0)
 
+    groups = out_ref.shape[2] // 8
+
     def plane(p, carry):
-        xp = i * bx + p + 2
-        for g in range(out_ref.shape[2] // 8):
+        xg = i * bx + p
+        xp = xg + 2
+        for g in range(groups):
             def load(c, dx, dy):
                 return up_ref[c, xp + dx, pl.ds(8 * g + YPAD + dy, 8), :]
 
@@ -121,7 +125,20 @@
                 upd = second * (1.0 / 12.0) + coup * (cross * 0.25)
                 prev = prev_ref[c, p, pl.ds(8 * g, 8), :]
                 src = src_ref[c, p, pl.ds(8 * g, 8), :]
-                out_ref[c, p, pl.ds(8 * g, 8), :] = (2.0 * centers[c] - prev + upd) + src
+                fresh = (2.0 * centers[c] - prev + upd) + src
+                out_ref[c, p, pl.ds(8 * g, 8), :] = fresh
+                if g == 0:
+                    rylo_ref[c, xg] = fresh[0:2]
+                if g == groups - 1:
+                    ryhi_ref[c, xg] = fresh[6:8]
+
+                @pl.when(xg < 2)
+                def _():
+                    fxlo_ref[c, jnp.minimum(xg, 1), pl.ds(8 * g, 8), :] = fresh
+
+                @pl.when(xg >= nx - 2)
+                def _():
+                    fxhi_ref[c, jnp.maximum(xg - (nx - 2), 0), pl.ds(8 * g, 8), :] = fresh
         return carry
 
     lax.fori_loop(0, bx, plane, 0)
@@ -145,26 +162,44 @@
             pl.BlockSpec((2, bx, ny, depth), block),
             pl.BlockSpec((3, bx, ny, depth), block),
         ],
-        out_specs=pl.BlockSpec((3, bx, ny, depth), block),
-        out_shape=jax.ShapeDtypeStruct((3, nx, ny, depth), jnp.float32),
+        out_specs=[
+            pl.BlockSpec((3, bx, ny, depth), block),
+            pl.BlockSpec((3, 2, ny, depth), whole),
+            pl.BlockSpec((3, 2, ny, depth), whole),
+            pl.BlockSpec((3, nx, 2, depth), whole),
+            pl.BlockSpec((3, nx, 2, depth), whole),
+        ],
+        out_shape=[
+            jax.ShapeDtypeStruct((3, nx, ny, depth), jnp.float32),
+            jax.ShapeDtypeStruct((3, 2, ny, depth), jnp.float32),
+            jax.ShapeDtypeStruct((3, 2, ny, depth), jnp.float32),
+            jax.ShapeDtypeStruct((3, nx, 2, depth), jnp.float32),
+            jax.ShapeDtypeStruct((3, nx, 2, depth), jnp.float32),
+        ],
         scratch_shapes=[pltpu.VMEM((3, nx + 4, ny + 2 * YPAD, depth), jnp.float32)],
         compiler_params=pltpu.CompilerParams(dimension_semantics=("arbitrary",)),
     )(u, xlo, xhi, ylo, yhi, prev, moduli, sources)
 
 
-def halos(block, width):
+def faces_of(block, width):
+    nx, ny = block.shape[1], block.shape[2]
+    return (block[:, :width], block[:, nx - width:], block[:, :, :width], block[:, :, ny - width:])
+
+
+def halos(faces, width):
     size_x = lax.axis_size("gx")
     size_y = lax.axis_size("gy")
-    nx, ny = block.shape[1], block.shape[2]
+    face_xlo, face_xhi, row_lo, row_hi = faces
+    ny = face_xlo.shape[2]
     forward_x = [(i, i + 1) for i in range(size_x - 1)]
     backward_x = [(t, s) for s, t in forward_x]
-    xlo = lax.ppermute(block[:, nx - width:], "gx", forward_x)
-    xhi = lax.ppermute(block[:, :width], "gx", backward_x)
+    xlo = lax.ppermute(face_xhi, "gx", forward_x)
+    xhi = lax.ppermute(face_xlo, "gx", backward_x)
     forward_y = [(i, i + 1) for i in range(size_y - 1)]
     backward_y = [(t, s) for s, t in forward_y]
-    rows = lambda sl: jnp.concatenate([xlo[:, :, sl], block[:, :, sl], xhi[:, :, sl]], axis=1)
-    ylo = lax.ppermute(rows(slice(ny - width, ny)), "gy", forward_y)
-    yhi = lax.ppermute(rows(slice(0, width)), "gy", backward_y)
+    rows = lambda sl, mid: jnp.concatenate([xlo[:, :, sl], mid, xhi[:, :, sl]], axis=1)
+    ylo = lax.ppermute(rows(slice(ny - width, ny), row_hi), "gy", forward_y)
+    yhi = lax.ppermute(rows(slice(0, width), row_lo), "gy", backward_y)
     return xlo, xhi, ylo, yhi
 
 
@@ -368,12 +403,13 @@
         jnp.float32
     )
     previous, current = (field_old, field_now)
+    faces = faces_of(field_now, 2)
     for instant in range(STEPS):
         spread = weighted[instant][:, None] * depth_hot
         source = jnp.dot(column_hot, spread, precision=lax.Precision.HIGHEST)
         source = source.reshape(3, block_x, block_y, depth)
-        xlo, xhi, ylo, yhi = halos(current, 2)
-        advanced = elastic_step(current, xlo, xhi, ylo, yhi, previous, moduli, source)
+        xlo, xhi, ylo, yhi = halos(faces, 2)
+        advanced, *faces = elastic_step(current, xlo, xhi, ylo, yhi, previous, moduli, source)
         previous, current = (current, advanced)
     return (current, previous)
 

time: 197 us -> 309 us (1.57)
  Pallas kernels: 52 us -> 161 us
  local copies, waits for them, and re-layouts: 15 us -> 7.27 us
  other arithmetic: 20.6 us -> 26.3 us
  waiting for transfers between devices: 20.6 us -> 25.8 us
    pallas_call x4, Pallas kernels: 52 us -> 161 us  [elastic_step(): pl.pallas_call(kernel, grid=(nx // bx,), in_specs=[pl.BlockSpec(u.shape,...]
    slice x8 -> x2, local copies, waits for them, and re-layouts: 10.3 us -> 2.57 us  [the longest x1 1.52 us: faces_of(): block[:, :, :width]]
    concatenate x8, other arithmetic: 0.83 us -> 6.58 us  [halos(): jnp.concatenate([xlo[:, :, sl], mid, xhi[:, :, sl]], axis=1)]
    ppermute x16, waiting for transfers between devices: 20.6 us -> 25.8 us  [the longest x4 11.5 us: halos(): xhi = lax.ppermute(face_xlo, 'gx', backward_x)]
  transfers between devices with their start and end apart: 17 -> 17, of which waited for: 12 -> 12; matrix products, arithmetic and copies ran while one was open for 11% -> 6% of each run, Pallas kernels for 0% -> 0%
where the time goes in v8:
time: 309 us; the launch traced here: 308 us
  Pallas kernels  161 us (52%)
  starting transfers between devices  55.9 us (18%)
  matrix products  29.6 us (10%)
  other arithmetic  26.3 us (9%)
  waiting for transfers between devices  25.8 us (8%)
  local copies, waits for them, and re-layouts  7.27 us (2%)
    pallas_call x4, Pallas kernels, elastic_step(): pl.pallas_call(kernel, grid=(nx // bx,), in_specs=[pl.BlockSpec(u.shape,...  161 us
    ppermute x4, starting transfers between devices, halos(): xhi = lax.ppermute(face_xlo, 'gx', backward_x)  16.3 us
    ppermute x4, starting transfers between devices, halos(): yhi = lax.ppermute(rows(slice(0, width), row_lo), 'gy', backward_y)  15.1 us
    dot_general x2, matrix products, select_block(): jnp.dot(table_rounded, offset_hot, preferred_element_type=jnp.float32)  13.1 us
    dot_general x4, matrix products, shards(): source = jnp.dot(column_hot, spread, precision=lax.Precision.HIGHEST)  12.9 us
    ppermute x4, waiting for transfers between devices, halos(): xhi = lax.ppermute(face_xlo, 'gx', backward_x)  11.5 us
    ppermute x4, starting transfers between devices, halos(): xlo = lax.ppermute(face_xhi, 'gx', forward_x)  10.6 us
    ppermute x4, starting transfers between devices, halos(): ylo = lax.ppermute(rows(slice(ny - width, ny), row_hi), 'gy', forward_y)  7.91 us
  transfers between devices with their start and end apart: 17, of which 12 were waited for; matrix products, arithmetic and copies ran while one was open for 6% of the time, Pallas kernels for 0%

profile of v8, /device:TPU:12, one launch (start us, length us, event | category | flops | bytes accessed | tf_op | source)
XLA Modules:
  0.0 308.2 jit_solution(10058800701616572015)
XLA Ops:
  2.9 4.9 %sine_multiply_fusion.1 = (f32[32,4,1024]{2,1,0:T(4,128)S(1)}, f32[32,4,1024]{2,1,0:T(4,128)S(1)}, f32[32,4,1024]{2,1,0:T(4,128)S(1)}) fusion(f32[32]{0:T(128)S(1)} %get-tuple-element.327, f32[32,4]{1,0:T(8,128)S(1)} %copy.24, f32[1024]{0:T(1024)S(1)} %multiply_multiply_fusion, f32[1,4,1024]{2,1,0:T(4,128)S(1)} %slice.109, f32[31,4,1024]{2,1,0:T(4,128)S(1)} %slice.108, ...), kind=kLoop, calls=%fused_computation.41 | loop fusion | flops 1441792 | bytes 2102016 | tf_op jit(solution)/shard_map/mul | solution.py:223
  8.1 2.2 while.32
  11.2 4.3 %fusion.43 = (bf16[1,32,4,1024]{3,2,1,0:T(4,128)(2,1)S(1)}, bf16[1,32,4,1024]{3,2,1,0:T(4,128)(2,1)S(1)}) fusion(f32[32,4,1024]{2,1,0:T(4,128)S(1)} %get-tuple-element.207, f32[32,4,1024]{2,1,0:T(4,128)S(1)} %get-tuple-element.206, f32[32,4,1024]{2,1,0:T(4,128)S(1)} %negate_exponential_fusion, f32[32,4,1024]{2,1,0:T(4,128)S(1)} %fusion.23), kind=kLoop, calls=%fused_computation.74 | loop fusion | flops 1835008 | bytes 2621440 | tf_op jit(solution)/shard_map/stack | solution.py:252
  17.7 3.6 %subtract_convert_fusion = bf16[1024,32,64]{0,2,1:T(8,128)(2,1)} fusion(f32[1024,64]{0,1:T(8,128)S(1)} %get-tuple-element.321, f32[1024,32]{0,1:T(8,128)S(1)} %get-tuple-element.315, f32[1024,64]{0,1:T(8,128)S(1)} %get-tuple-element.320, f32[1024,32]{0,1:T(8,128)S(1)} %get-tuple-element.314), kind=kLoop, calls=%fused_computation.24 | loop fusion | flops 8388608 | bytes 4980736 | tf_op jit(solution)/shard_map/convert_element_type | solution.py:267
  21.3 3.5 %convolution_convert_fusion = bf16[256,2048]{1,0:T(8,128)(2,1)S(1)} fusion(bf16[256,1024]{1,0:T(8,128)(2,1)S(1)} %bitcast.109, bf16[1024,2048]{0,1:T(8,128)(2,1)} %bitcast.107), kind=kOutput, calls=%fused_computation.30 | convolution fusion | flops 1074266112 | bytes 5767168 | tf_op jit(solution)/shard_map/dot_general | solution.py:355
  24.8 13.4 %while.31 = (s32[]{:T(128)}, bf16[2,2,4,4096]{3,2,1,0:T(4,128)(2,1)S(1)}, s32[2,4096]{1,0:T(2,128)S(1)}, bf16[256,2048]{1,0:T(8,128)(2,1)S(1)}, s32[2,4096]{1,0:T(2,128)S(1)}, /*index=5*/s32[]{:T(128)}) while((s32[]{:T(128)}, bf16[2,2,4,4096]{3,2,1,0:T(4,128)(2,1)S(1)}, s32[2,4096]{1,0:T(2,128)S(1)}, bf16[256,2048]{1,0:T(8,128)(2,1)S(1)}, ...), condition=%wide.region_9.10_spmd, body=%wide.region_7.9_spmd.sunk | while | flops 4305682432 | bytes 2392141 | solution.py:378
  24.9 6.5 %multiply_reduce_fusion.2 = bf16[2,4,4096]{2,1,0:T(4,128)(2,1)S(1)} fusion(f32[32,4096]{1,0:T(8,128)S(1)} %fusion.96, bf16[256,2048]{1,0:T(8,128)(2,1)S(1)} %get-tuple-element.468, s32[4096]{0:T(1024)S(1)} %bitcast.111), kind=kOutput, calls=%fused_computation.3.clone.1 | convolution fusion | flops 4305420288 | bytes 1654784 | tf_op jit(solution)/shard_map/while/body/eval_jaxpr/dot_general | solution.py:370
  31.6 6.5 %multiply_reduce_fusion.2 = bf16[2,4,4096]{2,1,0:T(4,128)(2,1)S(1)} fusion(f32[32,4096]{1,0:T(8,128)S(1)} %fusion.96, bf16[256,2048]{1,0:T(8,128)(2,1)S(1)} %get-tuple-element.468, s32[4096]{0:T(1024)S(1)} %bitcast.111), kind=kOutput, calls=%fused_computation.3.clone.1 | convolution fusion | flops 4305420288 | bytes 1654784 | tf_op jit(solution)/shard_map/while/body/eval_jaxpr/dot_general | solution.py:370
  39.2 6.0 %all-to-all-start = ((bf16[2,4,32,256]{3,1,0,2:T(4,128)(2,1)}), bf16[2,4,32,256]{3,1,0,2:T(4,128)(2,1)S(1)}, u32[]{:S(2)}, u32[]{:S(2)}) async-start(bf16[2,4,32,256]{3,1,0,2:T(4,128)(2,1)} %copy.27), calls=%async_computation | async-start | bytes 262144 | tf_op jit(solution)/shard_map/all_to_all | solution.py:385
  46.3 3.4 %collective-permute-start = (f32[3,2,32,256]{3,2,1,0:T(8,128)S(1)}, f32[3,2,32,256]{3,2,1,0:T(8,128)S(1)}, u32[]{:S(2)}, u32[]{:S(2)}) collective-permute-start(f32[3,2,32,256]{3,2,1,0:T(8,128)S(1)} %get-tuple-element.292), channel_id=1, source_target_pairs={{0,4},{4,8},{8,12},{12,16},{16,20},{20,24},{24,28},{1,5},{5,9},{9,... | collective-permute-start | bytes 589832 | tf_op jit(solution)/shard_map/ppermute | solution.py:196
  49.7 3.4 %collective-permute-start.1 = (f32[3,2,32,256]{3,2,1,0:T(8,128)S(1)}, f32[3,2,32,256]{3,2,1,0:T(8,128)S(1)}, u32[]{:S(2)}, u32[]{:S(2)}) collective-permute-start(f32[3,2,32,256]{3,2,1,0:T(8,128)S(1)} %get-tuple-element.291), channel_id=1, source_target_pairs={{4,0},{8,4},{12,8},{16,12},{20,16},{24,20},{28,24},{5,1},{9,5},{13... | collective-permute-start | bytes 589832 | tf_op jit(solution)/shard_map/ppermute | solution.py:197
  53.1 1.5 fusion.78
  56.0 4.2 %collective-permute-done.1.xhi_ref = f32[3,2,32,256]{3,2,1,0:T(8,128)S(1)} collective-permute-done((f32[3,2,32,256]{3,2,1,0:T(8,128)S(1)}, f32[3,2,32,256]{3,2,1,0:T(8,128)S(1)}, u32[]{:S(2)}, u32[]{:S(2)}) %collective-permute-start.1) | collective-permute-done | bytes 196640 | tf_op jit(solution)/shard_map/ppermute | solution.py:197
  60.4 2.2 collective-permute-start.3
  62.7 2.1 collective-permute-start.2
  65.1 3.2 %fusion.10 = f32[3072,256]{1,0:T(8,128)} fusion(s32[256]{0:T(256)S(1)} %get-tuple-element.323, f32[256]{0:T(256)S(1)} %bitcast.116, s32[256]{0:T(256)S(1)} %get-tuple-element.322), kind=kOutput, calls=%fused_computation.29 | convolution fusion | flops 2416836608 | bytes 3148800 | tf_op jit(solution)/shard_map/dot_general | solution.py:409
  68.3 1.6 collective-permute-done.2.ylo_ref
  70.6 40.2 %shard_map.122 = (f32[3,32,32,256]{3,2,1,0:T(8,128)}, f32[3,2,32,256]{3,2,1,0:T(8,128)}, f32[3,2,32,256]{3,2,1,0:T(8,128)}, f32[3,32,2,256]{3,2,1,0:T(2,128)}, f32[3,32,2,256]{3,2,1,0:T(2,128)}) custom-call(f32[3,32,32,256]{3,2,1,0:T(8,128)} %prev_ref.3, f32[3,2,32,256]{3,2,1,0:T(8,128)} %copy-done, f32[3,2,32,256]{3,2,1,0:T(8,128)} %copy-done.1, ...), custom_call_target="tpu_custom_call" | custom-call | tf_op jit(solution)/shard_map/pallas_call | solution.py:152
  110.8 2.2 collective-permute-start.4
  113.1 4.5 %collective-permute-start.5 = (f32[3,2,32,256]{3,2,1,0:T(8,128)}, f32[3,2,32,256]{3,2,1,0:T(8,128)S(1)}, u32[]{:S(2)}, u32[]{:S(2)}) collective-permute-start(f32[3,2,32,256]{3,2,1,0:T(8,128)} %get-tuple-element.211), channel_id=1, source_target_pairs={{4,0},{8,4},{12,8},{16,12},{20,16},{24,20},{28,24},{5,1},{9,5},{13... | collective-permute-start | bytes 589832 | tf_op jit(solution)/shard_map/ppermute | solution.py:197
  117.6 2.0 collective-permute-done.4.xlo_ref
  119.6 3.1 %collective-permute-done.5.xhi_ref = f32[3,2,32,256]{3,2,1,0:T(8,128)S(1)} collective-permute-done((f32[3,2,32,256]{3,2,1,0:T(8,128)}, f32[3,2,32,256]{3,2,1,0:T(8,128)S(1)}, u32[]{:S(2)}, u32[]{:S(2)}) %collective-permute-start.5) | collective-permute-done | bytes 196640 | tf_op jit(solution)/shard_map/ppermute | solution.py:197
  122.7 1.1 pad_maximum_fusion.4
  123.8 3.8 %collective-permute-start.7 = (f32[3,36,2,256]{3,2,1,0:T(2,128)S(1)}, f32[3,36,2,256]{3,2,1,0:T(2,128)S(1)}, u32[]{:S(2)}, u32[]{:S(2)}) collective-permute-start(f32[3,36,2,256]{3,2,1,0:T(2,128)S(1)} %pad_maximum_fusion.4), channel_id=1, source_target_pairs={{1,0},{2,1},{3,2},{5,4},{6,5},{7,6},{9,8},{10,9},{11,10},{13,12},{... | collective-permute-start | bytes 663560 | tf_op jit(solution)/shard_map/ppermute | solution.py:202
  128.6 1.9 collective-permute-start.6
  130.6 3.2 %fusion.9 = f32[3072,256]{1,0:T(8,128)} fusion(s32[256]{0:T(256)S(1)} %get-tuple-element.323, f32[256]{0:T(256)S(1)} %bitcast.115, s32[256]{0:T(256)S(1)} %get-tuple-element.322), kind=kOutput, calls=%fused_computation.28 | convolution fusion | flops 2416836608 | bytes 3148800 | tf_op jit(solution)/shard_map/dot_general | solution.py:409
  133.8 2.1 collective-permute-done.6.ylo_ref
  136.6 40.2 %shard_map.123 = (f32[3,32,32,256]{3,2,1,0:T(8,128)}, f32[3,2,32,256]{3,2,1,0:T(8,128)}, f32[3,2,32,256]{3,2,1,0:T(8,128)}, f32[3,32,2,256]{3,2,1,0:T(2,128)}, f32[3,32,2,256]{3,2,1,0:T(2,128)}) custom-call(f32[3,32,32,256]{3,2,1,0:T(8,128)} %get-tuple-element.209.u_ref.prev_ref, f32[3,2,32,256]{3,2,1,0:T(8,128)} %copy-done.5, f32[3,2,32,256]{3,2,1,0:T(8,128)} %copy-done.7, ...), custom_call_target="tpu_custom_call" | custom-call | tf_op jit(solution)/shard_map/pallas_call | solution.py:152
  176.8 2.5 collective-permute-start.8
  179.4 4.2 %collective-permute-start.9 = (f32[3,2,32,256]{3,2,1,0:T(8,128)}, f32[3,2,32,256]{3,2,1,0:T(8,128)S(1)}, u32[]{:S(2)}, u32[]{:S(2)}) collective-permute-start(f32[3,2,32,256]{3,2,1,0:T(8,128)} %get-tuple-element.216), channel_id=1, source_target_pairs={{4,0},{8,4},{12,8},{16,12},{20,16},{24,20},{28,24},{5,1},{9,5},{13... | collective-permute-start | bytes 589832 | tf_op jit(solution)/shard_map/ppermute | solution.py:197
  183.6 1.9 collective-permute-done.8.xlo_ref
  185.5 2.1 collective-permute-done.9.xhi_ref
  187.6 1.1 pad_maximum_fusion.6
  188.7 4.6 %collective-permute-start.11 = (f32[3,36,2,256]{3,2,1,0:T(2,128)S(1)}, f32[3,36,2,256]{3,2,1,0:T(2,128)S(1)}, u32[]{:S(2)}, u32[]{:S(2)}) collective-permute-start(f32[3,36,2,256]{3,2,1,0:T(2,128)S(1)} %pad_maximum_fusion.6), channel_id=1, source_target_pairs={{1,0},{2,1},{3,2},{5,4},{6,5},{7,6},{9,8},{10,9},{11,10},{13,12},{... | collective-permute-start | bytes 663560 | tf_op jit(solution)/shard_map/ppermute | solution.py:202
  194.3 1.9 collective-permute-start.10
  196.2 3.2 %fusion.8 = f32[3072,256]{1,0:T(8,128)} fusion(s32[256]{0:T(256)S(1)} %get-tuple-element.323, f32[256]{0:T(256)S(1)} %bitcast.114, s32[256]{0:T(256)S(1)} %get-tuple-element.322), kind=kOutput, calls=%fused_computation.27 | convolution fusion | flops 2416836608 | bytes 3148800 | tf_op jit(solution)/shard_map/dot_general | solution.py:409
  199.5 2.1 collective-permute-done.10.ylo_ref
  202.3 40.2 %shard_map.124 = (f32[3,32,32,256]{3,2,1,0:T(8,128)}, f32[3,2,32,256]{3,2,1,0:T(8,128)}, f32[3,2,32,256]{3,2,1,0:T(8,128)}, f32[3,32,2,256]{3,2,1,0:T(2,128)}, f32[3,32,2,256]{3,2,1,0:T(2,128)}) custom-call(f32[3,32,32,256]{3,2,1,0:T(8,128)} %get-tuple-element.214.u_ref.prev_ref, f32[3,2,32,256]{3,2,1,0:T(8,128)} %copy-done.3, f32[3,2,32,256]{3,2,1,0:T(8,128)} %copy-done.6, ...), custom_call_target="tpu_custom_call" | custom-call | tf_op jit(solution)/shard_map/pallas_call | solution.py:152
  242.5 2.5 collective-permute-start.12
  244.9 4.3 %collective-permute-start.13 = (f32[3,2,32,256]{3,2,1,0:T(8,128)}, f32[3,2,32,256]{3,2,1,0:T(8,128)S(1)}, u32[]{:S(2)}, u32[]{:S(2)}) collective-permute-start(f32[3,2,32,256]{3,2,1,0:T(8,128)} %get-tuple-element.221), channel_id=1, source_target_pairs={{4,0},{8,4},{12,8},{16,12},{20,16},{24,20},{28,24},{5,1},{9,5},{13... | collective-permute-start | bytes 589832 | tf_op jit(solution)/shard_map/ppermute | solution.py:197
  249.2 1.9 collective-permute-done.12.xlo_ref
  251.2 2.1 collective-permute-done.13.xhi_ref
  253.2 1.1 pad_maximum_fusion.8
  254.3 4.6 %collective-permute-start.15 = (f32[3,36,2,256]{3,2,1,0:T(2,128)S(1)}, f32[3,36,2,256]{3,2,1,0:T(2,128)S(1)}, u32[]{:S(2)}, u32[]{:S(2)}) collective-permute-start(f32[3,36,2,256]{3,2,1,0:T(2,128)S(1)} %pad_maximum_fusion.8), channel_id=1, source_target_pairs={{1,0},{2,1},{3,2},{5,4},{6,5},{7,6},{9,8},{10,9},{11,10},{13,12},{... | collective-permute-start | bytes 663560 | tf_op jit(solution)/shard_map/ppermute | solution.py:202
  259.9 1.9 collective-permute-start.14
  261.9 3.2 %fusion.7 = f32[3072,256]{1,0:T(8,128)} fusion(s32[256]{0:T(256)S(1)} %get-tuple-element.323, f32[256]{0:T(256)S(1)} %bitcast.113, s32[256]{0:T(256)S(1)} %get-tuple-element.322), kind=kOutput, calls=%fused_computation.26 | convolution fusion | flops 2416836608 | bytes 3148800 | tf_op jit(solution)/shard_map/dot_general | solution.py:409
  265.1 2.1 collective-permute-done.14.ylo_ref
  267.9 40.2 %shard_map.125 = (f32[3,32,32,256]{3,2,1,0:T(8,128)}, f32[3,2,32,256]{3,2,1,0:T(8,128)}, f32[3,2,32,256]{3,2,1,0:T(8,128)}, f32[3,32,2,256]{3,2,1,0:T(2,128)}, f32[3,32,2,256]{3,2,1,0:T(2,128)}) custom-call(f32[3,32,32,256]{3,2,1,0:T(8,128)} %get-tuple-element.205.u_ref, f32[3,2,32,256]{3,2,1,0:T(8,128)} %copy-done.2, f32[3,2,32,256]{3,2,1,0:T(8,128)} %copy-done.4, ...), custom_call_target="tpu_custom_call" | custom-call | tf_op jit(solution)/shard_map/pallas_call | solution.py:152
  (132 shorter events, 16.7 us)
Async XLA Ops:
  16.0 5.3 %copy-start.16 = (s32[8192]{0:T(1024)S(1)}, s32[8192]{0:T(1024)}, u32[]{:S(2)}) copy-start(s32[8192]{0:T(1024)} %param.19) | copy-start | bytes 98308
  16.0 5.3 %copy-start.17 = (s32[8192]{0:T(1024)S(1)}, s32[8192]{0:T(1024)}, u32[]{:S(2)}) copy-start(s32[8192]{0:T(1024)} %param.20) | copy-start | bytes 98308
  24.8 30.6 %copy-start.18 = (s32[256]{0:T(256)S(1)}, s32[256]{0:T(256)}, u32[]{:S(2)}) copy-start(s32[256]{0:T(256)} %param.21) | copy-start | bytes 3076
  39.2 25.6 %all-to-all-start = ((bf16[2,4,32,256]{3,1,0,2:T(4,128)(2,1)}), bf16[2,4,32,256]{3,1,0,2:T(4,128)(2,1)S(1)}, u32[]{:S(2)}, u32[]{:S(2)}) async-start(bf16[2,4,32,256]{3,1,0,2:T(4,128)(2,1)} %copy.27), calls=%async_computation | async-start | bytes 262144 | tf_op jit(solution)/shard_map/all_to_all | solution.py:385
  46.3 9.7 %collective-permute-start = (f32[3,2,32,256]{3,2,1,0:T(8,128)S(1)}, f32[3,2,32,256]{3,2,1,0:T(8,128)S(1)}, u32[]{:S(2)}, u32[]{:S(2)}) collective-permute-start(f32[3,2,32,256]{3,2,1,0:T(8,128)S(1)} %get-tuple-element.292), channel_id=1, source_target_pairs={{0,4},{4,8},{8,12},{12,16},{16,20},{20,24},{24,28},{1,5},{5,9},{9,... | collective-permute-start | bytes 589832 | tf_op jit(solution)/shard_map/ppermute | solution.py:196
  49.7 10.5 %collective-permute-start.1 = (f32[3,2,32,256]{3,2,1,0:T(8,128)S(1)}, f32[3,2,32,256]{3,2,1,0:T(8,128)S(1)}, u32[]{:S(2)}, u32[]{:S(2)}) collective-permute-start(f32[3,2,32,256]{3,2,1,0:T(8,128)S(1)} %get-tuple-element.291), channel_id=1, source_target_pairs={{4,0},{8,4},{12,8},{16,12},{20,16},{24,20},{28,24},{5,1},{9,5},{13... | collective-permute-start | bytes 589832 | tf_op jit(solution)/shard_map/ppermute | solution.py:197
  56.0 13.9 %copy-start = (f32[3,2,32,256]{3,2,1,0:T(8,128)}, f32[3,2,32,256]{3,2,1,0:T(8,128)S(1)}, u32[]{:S(2)}) copy-start(f32[3,2,32,256]{3,2,1,0:T(8,128)S(1)} %collective-permute-done.xlo_ref) | copy-start | bytes 589828
  60.2 9.7 %copy-start.1 = (f32[3,2,32,256]{3,2,1,0:T(8,128)}, f32[3,2,32,256]{3,2,1,0:T(8,128)S(1)}, u32[]{:S(2)}) copy-start(f32[3,2,32,256]{3,2,1,0:T(8,128)S(1)} %collective-permute-done.1.xhi_ref) | copy-start | bytes 589828
  60.4 8.0 %collective-permute-start.3 = (f32[3,36,2,256]{3,2,1,0:T(2,128)S(1)}, f32[3,36,2,256]{3,2,1,0:T(2,128)S(1)}, u32[]{:S(2)}, u32[]{:S(2)}) collective-permute-start(f32[3,36,2,256]{3,2,1,0:T(2,128)S(1)} %pad_maximum_fusion.2), channel_id=1, source_target_pairs={{1,0},{2,1},{3,2},{5,4},{6,5},{7,6},{9,8},{10,9},{11,10},{13,12},{... | collective-permute-start | bytes 663560 | tf_op jit(solution)/shard_map/ppermute | solution.py:202
  62.7 7.3 %collective-permute-start.2 = (f32[3,36,2,256]{3,2,1,0:T(2,128)S(1)}, f32[3,36,2,256]{3,2,1,0:T(2,128)S(1)}, u32[]{:S(2)}, u32[]{:S(2)}) collective-permute-start(f32[3,36,2,256]{3,2,1,0:T(2,128)S(1)} %pad_maximum_fusion.1), channel_id=1, source_target_pairs={{0,1},{1,2},{2,3},{4,5},{5,6},{6,7},{8,9},{9,10},{10,11},{12,13},{... | collective-permute-start | bytes 663560 | tf_op jit(solution)/shard_map/ppermute | solution.py:201
  68.3 1.6 copy-start.8
  69.9 0.7 copy-start.9
  110.8 8.8 %collective-permute-start.4 = (f32[3,2,32,256]{3,2,1,0:T(8,128)}, f32[3,2,32,256]{3,2,1,0:T(8,128)S(1)}, u32[]{:S(2)}, u32[]{:S(2)}) collective-permute-start(f32[3,2,32,256]{3,2,1,0:T(8,128)} %get-tuple-element.210), channel_id=1, source_target_pairs={{0,4},{4,8},{8,12},{12,16},{16,20},{20,24},{24,28},{1,5},{5,9},{9,... | collective-permute-start | bytes 589832 | tf_op jit(solution)/shard_map/ppermute | solution.py:196
  113.1 9.6 %collective-permute-start.5 = (f32[3,2,32,256]{3,2,1,0:T(8,128)}, f32[3,2,32,256]{3,2,1,0:T(8,128)S(1)}, u32[]{:S(2)}, u32[]{:S(2)}) collective-permute-start(f32[3,2,32,256]{3,2,1,0:T(8,128)} %get-tuple-element.211), channel_id=1, source_target_pairs={{4,0},{8,4},{12,8},{16,12},{20,16},{24,20},{28,24},{5,1},{9,5},{13... | collective-permute-start | bytes 589832 | tf_op jit(solution)/shard_map/ppermute | solution.py:197
  119.6 16.3 %copy-start.5 = (f32[3,2,32,256]{3,2,1,0:T(8,128)}, f32[3,2,32,256]{3,2,1,0:T(8,128)S(1)}, u32[]{:S(2)}) copy-start(f32[3,2,32,256]{3,2,1,0:T(8,128)S(1)} %collective-permute-done.4.xlo_ref) | copy-start | bytes 589828
  122.7 13.2 %copy-start.7 = (f32[3,2,32,256]{3,2,1,0:T(8,128)}, f32[3,2,32,256]{3,2,1,0:T(8,128)S(1)}, u32[]{:S(2)}) copy-start(f32[3,2,32,256]{3,2,1,0:T(8,128)S(1)} %collective-permute-done.5.xhi_ref) | copy-start | bytes 589828
  123.8 9.9 %collective-permute-start.7 = (f32[3,36,2,256]{3,2,1,0:T(2,128)S(1)}, f32[3,36,2,256]{3,2,1,0:T(2,128)S(1)}, u32[]{:S(2)}, u32[]{:S(2)}) collective-permute-start(f32[3,36,2,256]{3,2,1,0:T(2,128)S(1)} %pad_maximum_fusion.4), channel_id=1, source_target_pairs={{1,0},{2,1},{3,2},{5,4},{6,5},{7,6},{9,8},{10,9},{11,10},{13,12},{... | collective-permute-start | bytes 663560 | tf_op jit(solution)/shard_map/ppermute | solution.py:202
  128.6 7.3 %collective-permute-start.6 = (f32[3,36,2,256]{3,2,1,0:T(2,128)S(1)}, f32[3,36,2,256]{3,2,1,0:T(2,128)S(1)}, u32[]{:S(2)}, u32[]{:S(2)}) collective-permute-start(f32[3,36,2,256]{3,2,1,0:T(2,128)S(1)} %pad_maximum_fusion.3), channel_id=1, source_target_pairs={{0,1},{1,2},{2,3},{4,5},{5,6},{6,7},{8,9},{9,10},{10,11},{12,13},{... | collective-permute-start | bytes 663560 | tf_op jit(solution)/shard_map/ppermute | solution.py:201
  133.8 2.1 copy-start.12
  135.9 0.7 copy-start.15
  176.8 8.7 %collective-permute-start.8 = (f32[3,2,32,256]{3,2,1,0:T(8,128)}, f32[3,2,32,256]{3,2,1,0:T(8,128)S(1)}, u32[]{:S(2)}, u32[]{:S(2)}) collective-permute-start(f32[3,2,32,256]{3,2,1,0:T(8,128)} %get-tuple-element.215), channel_id=1, source_target_pairs={{0,4},{4,8},{8,12},{12,16},{16,20},{20,24},{24,28},{1,5},{5,9},{9,... | collective-permute-start | bytes 589832 | tf_op jit(solution)/shard_map/ppermute | solution.py:196
  179.4 8.2 %collective-permute-start.9 = (f32[3,2,32,256]{3,2,1,0:T(8,128)}, f32[3,2,32,256]{3,2,1,0:T(8,128)S(1)}, u32[]{:S(2)}, u32[]{:S(2)}) collective-permute-start(f32[3,2,32,256]{3,2,1,0:T(8,128)} %get-tuple-element.216), channel_id=1, source_target_pairs={{4,0},{8,4},{12,8},{16,12},{20,16},{24,20},{28,24},{5,1},{9,5},{13... | collective-permute-start | bytes 589832 | tf_op jit(solution)/shard_map/ppermute | solution.py:197
  185.5 16.1 %copy-start.3 = (f32[3,2,32,256]{3,2,1,0:T(8,128)}, f32[3,2,32,256]{3,2,1,0:T(8,128)S(1)}, u32[]{:S(2)}) copy-start(f32[3,2,32,256]{3,2,1,0:T(8,128)S(1)} %collective-permute-done.8.xlo_ref) | copy-start | bytes 589828
  187.6 14.0 %copy-start.6 = (f32[3,2,32,256]{3,2,1,0:T(8,128)}, f32[3,2,32,256]{3,2,1,0:T(8,128)S(1)}, u32[]{:S(2)}) copy-start(f32[3,2,32,256]{3,2,1,0:T(8,128)S(1)} %collective-permute-done.9.xhi_ref) | copy-start | bytes 589828
  188.7 10.8 %collective-permute-start.11 = (f32[3,36,2,256]{3,2,1,0:T(2,128)S(1)}, f32[3,36,2,256]{3,2,1,0:T(2,128)S(1)}, u32[]{:S(2)}, u32[]{:S(2)}) collective-permute-start(f32[3,36,2,256]{3,2,1,0:T(2,128)S(1)} %pad_maximum_fusion.6), channel_id=1, source_target_pairs={{1,0},{2,1},{3,2},{5,4},{6,5},{7,6},{9,8},{10,9},{11,10},{13,12},{... | collective-permute-start | bytes 663560 | tf_op jit(solution)/shard_map/ppermute | solution.py:202
  194.3 7.3 %collective-permute-start.10 = (f32[3,36,2,256]{3,2,1,0:T(2,128)S(1)}, f32[3,36,2,256]{3,2,1,0:T(2,128)S(1)}, u32[]{:S(2)}, u32[]{:S(2)}) collective-permute-start(f32[3,36,2,256]{3,2,1,0:T(2,128)S(1)} %pad_maximum_fusion.5), channel_id=1, source_target_pairs={{0,1},{1,2},{2,3},{4,5},{5,6},{6,7},{8,9},{9,10},{10,11},{12,13},{... | collective-permute-start | bytes 663560 | tf_op jit(solution)/shard_map/ppermute | solution.py:201
  199.5 2.1 copy-start.11
  201.6 0.7 copy-start.14
  242.5 8.7 %collective-permute-start.12 = (f32[3,2,32,256]{3,2,1,0:T(8,128)}, f32[3,2,32,256]{3,2,1,0:T(8,128)S(1)}, u32[]{:S(2)}, u32[]{:S(2)}) collective-permute-start(f32[3,2,32,256]{3,2,1,0:T(8,128)} %get-tuple-element.220), channel_id=1, source_target_pairs={{0,4},{4,8},{8,12},{12,16},{16,20},{20,24},{24,28},{1,5},{5,9},{9,... | collective-permute-start | bytes 589832 | tf_op jit(solution)/shard_map/ppermute | solution.py:196
  244.9 8.3 %collective-permute-start.13 = (f32[3,2,32,256]{3,2,1,0:T(8,128)}, f32[3,2,32,256]{3,2,1,0:T(8,128)S(1)}, u32[]{:S(2)}, u32[]{:S(2)}) collective-permute-start(f32[3,2,32,256]{3,2,1,0:T(8,128)} %get-tuple-element.221), channel_id=1, source_target_pairs={{4,0},{8,4},{12,8},{16,12},{20,16},{24,20},{28,24},{5,1},{9,5},{13... | collective-permute-start | bytes 589832 | tf_op jit(solution)/shard_map/ppermute | solution.py:197
  251.1 16.1 %copy-start.2 = (f32[3,2,32,256]{3,2,1,0:T(8,128)}, f32[3,2,32,256]{3,2,1,0:T(8,128)S(1)}, u32[]{:S(2)}) copy-start(f32[3,2,32,256]{3,2,1,0:T(8,128)S(1)} %collective-permute-done.12.xlo_ref) | copy-start | bytes 589828
  253.2 14.0 %copy-start.4 = (f32[3,2,32,256]{3,2,1,0:T(8,128)}, f32[3,2,32,256]{3,2,1,0:T(8,128)S(1)}, u32[]{:S(2)}) copy-start(f32[3,2,32,256]{3,2,1,0:T(8,128)S(1)} %collective-permute-done.13.xhi_ref) | copy-start | bytes 589828
  254.3 10.8 %collective-permute-start.15 = (f32[3,36,2,256]{3,2,1,0:T(2,128)S(1)}, f32[3,36,2,256]{3,2,1,0:T(2,128)S(1)}, u32[]{:S(2)}, u32[]{:S(2)}) collective-permute-start(f32[3,36,2,256]{3,2,1,0:T(2,128)S(1)} %pad_maximum_fusion.8), channel_id=1, source_target_pairs={{1,0},{2,1},{3,2},{5,4},{6,5},{7,6},{9,8},{10,9},{11,10},{13,12},{... | collective-permute-start | bytes 663560 | tf_op jit(solution)/shard_map/ppermute | solution.py:202
  259.9 7.3 %collective-permute-start.14 = (f32[3,36,2,256]{3,2,1,0:T(2,128)S(1)}, f32[3,36,2,256]{3,2,1,0:T(2,128)S(1)}, u32[]{:S(2)}, u32[]{:S(2)}) collective-permute-start(f32[3,36,2,256]{3,2,1,0:T(2,128)S(1)} %pad_maximum_fusion.7), channel_id=1, source_target_pairs={{0,1},{1,2},{2,3},{4,5},{5,6},{6,7},{8,9},{9,10},{10,11},{12,13},{... | collective-permute-start | bytes 663560 | tf_op jit(solution)/shard_map/ppermute | solution.py:201
  265.1 2.1 copy-start.10
  267.2 0.7 copy-start.13

commit v9 on v8

--- a/solution.py
+++ b/solution.py
@@ -65,8 +65,7 @@
     groups = out_ref.shape[2] // 8
 
     def plane(p, carry):
-        xg = i * bx + p
-        xp = xg + 2
+        xp = i * bx + p + 2
         for g in range(groups):
             def load(c, dx, dy):
                 return up_ref[c, xp + dx, pl.ds(8 * g + YPAD + dy, 8), :]
@@ -125,23 +124,21 @@
                 upd = second * (1.0 / 12.0) + coup * (cross * 0.25)
                 prev = prev_ref[c, p, pl.ds(8 * g, 8), :]
                 src = src_ref[c, p, pl.ds(8 * g, 8), :]
-                fresh = (2.0 * centers[c] - prev + upd) + src
-                out_ref[c, p, pl.ds(8 * g, 8), :] = fresh
-                if g == 0:
-                    rylo_ref[c, xg] = fresh[0:2]
-                if g == groups - 1:
-                    ryhi_ref[c, xg] = fresh[6:8]
-
-                @pl.when(xg < 2)
-                def _():
-                    fxlo_ref[c, jnp.minimum(xg, 1), pl.ds(8 * g, 8), :] = fresh
-
-                @pl.when(xg >= nx - 2)
-                def _():
-                    fxhi_ref[c, jnp.maximum(xg - (nx - 2), 0), pl.ds(8 * g, 8), :] = fresh
+                out_ref[c, p, pl.ds(8 * g, 8), :] = (2.0 * centers[c] - prev + upd) + src
         return carry
 
     lax.fori_loop(0, bx, plane, 0)
+    ny = out_ref.shape[2]
+    rylo_ref[:, pl.ds(i * bx, bx)] = out_ref[:, :, 0:2, :]
+    ryhi_ref[:, pl.ds(i * bx, bx)] = out_ref[:, :, ny - 2:ny, :]
+
+    @pl.when(i == 0)
+    def _():
+        fxlo_ref[...] = out_ref[:, 0:2]
+
+    @pl.when(i == pl.num_programs(0) - 1)
+    def _():
+        fxhi_ref[...] = out_ref[:, bx - 2:bx]
 
 
 def elastic_step(u, xlo, xhi, ylo, yhi, prev, moduli, sources, bx=8):

time: 309 us -> 202 us (0.65)
  Pallas kernels: 161 us -> 53.8 us
    pallas_call x4, Pallas kernels: 161 us -> 53.8 us  [elastic_step(): pl.pallas_call(kernel, grid=(nx // bx,), in_specs=[pl.BlockSpec(u.shape,...]
  transfers between devices with their start and end apart: 17 -> 17, of which waited for: 12 -> 12; matrix products, arithmetic and copies ran while one was open for 6% -> 10% of each run, Pallas kernels for 0% -> 0%
where the time goes in v9:
time: 202 us; the launch traced here: 201 us
  starting transfers between devices  55.9 us (28%)
  Pallas kernels  53.8 us (27%)
  matrix products  29.6 us (15%)
  other arithmetic  26.3 us (13%)
  waiting for transfers between devices  25.8 us (13%)
  local copies, waits for them, and re-layouts  7.27 us (4%)
    pallas_call x4, Pallas kernels, elastic_step(): pl.pallas_call(kernel, grid=(nx // bx,), in_specs=[pl.BlockSpec(u.shape,...  53.8 us
    ppermute x4, starting transfers between devices, halos(): xhi = lax.ppermute(face_xlo, 'gx', backward_x)  16.3 us
    ppermute x4, starting transfers between devices, halos(): yhi = lax.ppermute(rows(slice(0, width), row_lo), 'gy', backward_y)  15.1 us
    dot_general x2, matrix products, select_block(): jnp.dot(table_rounded, offset_hot, preferred_element_type=jnp.float32)  13.1 us
    dot_general x4, matrix products, shards(): source = jnp.dot(column_hot, spread, precision=lax.Precision.HIGHEST)  12.9 us
    ppermute x4, waiting for transfers between devices, halos(): xhi = lax.ppermute(face_xlo, 'gx', backward_x)  11.5 us
    ppermute x4, starting transfers between devices, halos(): xlo = lax.ppermute(face_xhi, 'gx', forward_x)  10.6 us
    ppermute x4, starting transfers between devices, halos(): ylo = lax.ppermute(rows(slice(ny - width, ny), row_hi), 'gy', forward_y)  7.91 us
  transfers between devices with their start and end apart: 17, of which 12 were waited for; matrix products, arithmetic and copies ran while one was open for 10% of the time, Pallas kernels for 0%

profile of v9, /device:TPU:12, one launch (start us, length us, event | category | flops | bytes accessed | tf_op | source)
XLA Modules:
  0.0 201.2 jit_solution(13303439896045926930)
XLA Ops:
  2.9 4.9 %sine_multiply_fusion.1 = (f32[32,4,1024]{2,1,0:T(4,128)S(1)}, f32[32,4,1024]{2,1,0:T(4,128)S(1)}, f32[32,4,1024]{2,1,0:T(4,128)S(1)}) fusion(f32[32]{0:T(128)S(1)} %get-tuple-element.327, f32[32,4]{1,0:T(8,128)S(1)} %copy.24, f32[1024]{0:T(1024)S(1)} %multiply_multiply_fusion, f32[1,4,1024]{2,1,0:T(4,128)S(1)} %slice.109, f32[31,4,1024]{2,1,0:T(4,128)S(1)} %slice.108, ...), kind=kLoop, calls=%fused_computation.41 | loop fusion | flops 1441792 | bytes 2102016 | tf_op jit(solution)/shard_map/mul | solution.py:220
  8.1 2.2 %while.32 = (s32[]{:T(128)}, f32[4,1024]{1,0:T(4,128)S(1)}, f32[4,1024]{1,0:T(4,128)S(1)}, f32[32,4,1024]{2,1,0:T(4,128)S(1)}, f32[32,4,1024]{2,1,0:T(4,128)S(1)...) while((s32[]{:T(128)}, f32[4,1024]{1,0:T(4,128)S(1)}, ...), condition=%wide.region_6.7_spmd.clone, body=%wide.region_5.6_spmd.clone.sunk | while | flops 94212 | bytes 147591 | solution.py:236
  11.2 4.3 %fusion.43 = (bf16[1,32,4,1024]{3,2,1,0:T(4,128)(2,1)S(1)}, bf16[1,32,4,1024]{3,2,1,0:T(4,128)(2,1)S(1)}) fusion(f32[32,4,1024]{2,1,0:T(4,128)S(1)} %get-tuple-element.207, f32[32,4,1024]{2,1,0:T(4,128)S(1)} %get-tuple-element.206, f32[32,4,1024]{2,1,0:T(4,128)S(1)} %negate_exponential_fusion, f32[32,4,1024]{2,1,0:T(4,128)S(1)} %fusion.23), kind=kLoop, calls=%fused_computation.74 | loop fusion | flops 1835008 | bytes 2621440 | tf_op jit(solution)/shard_map/stack | solution.py:249
  17.7 3.6 %subtract_convert_fusion = bf16[1024,32,64]{0,2,1:T(8,128)(2,1)} fusion(f32[1024,64]{0,1:T(8,128)S(1)} %get-tuple-element.321, f32[1024,32]{0,1:T(8,128)S(1)} %get-tuple-element.315, f32[1024,64]{0,1:T(8,128)S(1)} %get-tuple-element.320, f32[1024,32]{0,1:T(8,128)S(1)} %get-tuple-element.314), kind=kLoop, calls=%fused_computation.24 | loop fusion | flops 8388608 | bytes 4980736 | tf_op jit(solution)/shard_map/convert_element_type | solution.py:264
  21.3 3.5 %convolution_convert_fusion = bf16[256,2048]{1,0:T(8,128)(2,1)S(1)} fusion(bf16[256,1024]{1,0:T(8,128)(2,1)S(1)} %bitcast.109, bf16[1024,2048]{0,1:T(8,128)(2,1)} %bitcast.107), kind=kOutput, calls=%fused_computation.30 | convolution fusion | flops 1074266112 | bytes 5767168 | tf_op jit(solution)/shard_map/dot_general | solution.py:352
  24.8 13.4 %while.31 = (s32[]{:T(128)}, bf16[2,2,4,4096]{3,2,1,0:T(4,128)(2,1)S(1)}, s32[2,4096]{1,0:T(2,128)S(1)}, bf16[256,2048]{1,0:T(8,128)(2,1)S(1)}, s32[2,4096]{1,0:T(2,128)S(1)}, /*index=5*/s32[]{:T(128)}) while((s32[]{:T(128)}, bf16[2,2,4,4096]{3,2,1,0:T(4,128)(2,1)S(1)}, s32[2,4096]{1,0:T(2,128)S(1)}, bf16[256,2048]{1,0:T(8,128)(2,1)S(1)}, ...), condition=%wide.region_9.10_spmd, body=%wide.region_7.9_spmd.sunk | while | flops 4305682432 | bytes 2392141 | solution.py:375
  24.9 6.5 %multiply_reduce_fusion.2 = bf16[2,4,4096]{2,1,0:T(4,128)(2,1)S(1)} fusion(f32[32,4096]{1,0:T(8,128)S(1)} %fusion.96, bf16[256,2048]{1,0:T(8,128)(2,1)S(1)} %get-tuple-element.468, s32[4096]{0:T(1024)S(1)} %bitcast.111), kind=kOutput, calls=%fused_computation.3.clone.1 | convolution fusion | flops 4305420288 | bytes 1654784 | tf_op jit(solution)/shard_map/while/body/eval_jaxpr/dot_general | solution.py:367
  31.6 6.5 %multiply_reduce_fusion.2 = bf16[2,4,4096]{2,1,0:T(4,128)(2,1)S(1)} fusion(f32[32,4096]{1,0:T(8,128)S(1)} %fusion.96, bf16[256,2048]{1,0:T(8,128)(2,1)S(1)} %get-tuple-element.468, s32[4096]{0:T(1024)S(1)} %bitcast.111), kind=kOutput, calls=%fused_computation.3.clone.1 | convolution fusion | flops 4305420288 | bytes 1654784 | tf_op jit(solution)/shard_map/while/body/eval_jaxpr/dot_general | solution.py:367
  39.2 6.0 %all-to-all-start = ((bf16[2,4,32,256]{3,1,0,2:T(4,128)(2,1)}), bf16[2,4,32,256]{3,1,0,2:T(4,128)(2,1)S(1)}, u32[]{:S(2)}, u32[]{:S(2)}) async-start(bf16[2,4,32,256]{3,1,0,2:T(4,128)(2,1)} %copy.27), calls=%async_computation | async-start | bytes 262144 | tf_op jit(solution)/shard_map/all_to_all | solution.py:382
  46.3 3.4 %collective-permute-start = (f32[3,2,32,256]{3,2,1,0:T(8,128)S(1)}, f32[3,2,32,256]{3,2,1,0:T(8,128)S(1)}, u32[]{:S(2)}, u32[]{:S(2)}) collective-permute-start(f32[3,2,32,256]{3,2,1,0:T(8,128)S(1)} %get-tuple-element.292), channel_id=1, source_target_pairs={{0,4},{4,8},{8,12},{12,16},{16,20},{20,24},{24,28},{1,5},{5,9},{9,... | collective-permute-start | bytes 589832 | tf_op jit(solution)/shard_map/ppermute | solution.py:193
  49.7 3.4 %collective-permute-start.1 = (f32[3,2,32,256]{3,2,1,0:T(8,128)S(1)}, f32[3,2,32,256]{3,2,1,0:T(8,128)S(1)}, u32[]{:S(2)}, u32[]{:S(2)}) collective-permute-start(f32[3,2,32,256]{3,2,1,0:T(8,128)S(1)} %get-tuple-element.291), channel_id=1, source_target_pairs={{4,0},{8,4},{12,8},{16,12},{20,16},{24,20},{28,24},{5,1},{9,5},{13... | collective-permute-start | bytes 589832 | tf_op jit(solution)/shard_map/ppermute | solution.py:194
  53.1 1.5 fusion.78
  56.0 4.2 %collective-permute-done.1.xhi_ref = f32[3,2,32,256]{3,2,1,0:T(8,128)S(1)} collective-permute-done((f32[3,2,32,256]{3,2,1,0:T(8,128)S(1)}, f32[3,2,32,256]{3,2,1,0:T(8,128)S(1)}, u32[]{:S(2)}, u32[]{:S(2)}) %collective-permute-start.1) | collective-permute-done | bytes 196640 | tf_op jit(solution)/shard_map/ppermute | solution.py:194
  60.4 2.2 %collective-permute-start.3 = (f32[3,36,2,256]{3,2,1,0:T(2,128)S(1)}, f32[3,36,2,256]{3,2,1,0:T(2,128)S(1)}, u32[]{:S(2)}, u32[]{:S(2)}) collective-permute-start(f32[3,36,2,256]{3,2,1,0:T(2,128)S(1)} %pad_maximum_fusion.2), channel_id=1, source_target_pairs={{1,0},{2,1},{3,2},{5,4},{6,5},{7,6},{9,8},{10,9},{11,10},{13,12},{... | collective-permute-start | bytes 663560 | tf_op jit(solution)/shard_map/ppermute | solution.py:199
  62.7 2.1 %collective-permute-start.2 = (f32[3,36,2,256]{3,2,1,0:T(2,128)S(1)}, f32[3,36,2,256]{3,2,1,0:T(2,128)S(1)}, u32[]{:S(2)}, u32[]{:S(2)}) collective-permute-start(f32[3,36,2,256]{3,2,1,0:T(2,128)S(1)} %pad_maximum_fusion.1), channel_id=1, source_target_pairs={{0,1},{1,2},{2,3},{4,5},{5,6},{6,7},{8,9},{9,10},{10,11},{12,13},{... | collective-permute-start | bytes 663560 | tf_op jit(solution)/shard_map/ppermute | solution.py:198
  65.1 3.2 %fusion.10 = f32[3072,256]{1,0:T(8,128)} fusion(s32[256]{0:T(256)S(1)} %get-tuple-element.323, f32[256]{0:T(256)S(1)} %bitcast.116, s32[256]{0:T(256)S(1)} %get-tuple-element.322), kind=kOutput, calls=%fused_computation.29 | convolution fusion | flops 2416836608 | bytes 3148800 | tf_op jit(solution)/shard_map/dot_general | solution.py:406
  68.3 1.6 collective-permute-done.2.ylo_ref
  70.6 13.5 %shard_map.122 = (f32[3,32,32,256]{3,2,1,0:T(8,128)}, f32[3,2,32,256]{3,2,1,0:T(8,128)}, f32[3,2,32,256]{3,2,1,0:T(8,128)}, f32[3,32,2,256]{3,2,1,0:T(2,128)}, f32[3,32,2,256]{3,2,1,0:T(2,128)}) custom-call(f32[3,32,32,256]{3,2,1,0:T(8,128)} %prev_ref.3, f32[3,2,32,256]{3,2,1,0:T(8,128)} %copy-done, f32[3,2,32,256]{3,2,1,0:T(8,128)} %copy-done.1, ...), custom_call_target="tpu_custom_call" | custom-call | tf_op jit(solution)/shard_map/pallas_call | solution.py:149
  84.1 2.2 %collective-permute-start.4 = (f32[3,2,32,256]{3,2,1,0:T(8,128)}, f32[3,2,32,256]{3,2,1,0:T(8,128)S(1)}, u32[]{:S(2)}, u32[]{:S(2)}) collective-permute-start(f32[3,2,32,256]{3,2,1,0:T(8,128)} %get-tuple-element.210), channel_id=1, source_target_pairs={{0,4},{4,8},{8,12},{12,16},{16,20},{20,24},{24,28},{1,5},{5,9},{9,... | collective-permute-start | bytes 589832 | tf_op jit(solution)/shard_map/ppermute | solution.py:193
  86.3 4.5 %collective-permute-start.5 = (f32[3,2,32,256]{3,2,1,0:T(8,128)}, f32[3,2,32,256]{3,2,1,0:T(8,128)S(1)}, u32[]{:S(2)}, u32[]{:S(2)}) collective-permute-start(f32[3,2,32,256]{3,2,1,0:T(8,128)} %get-tuple-element.211), channel_id=1, source_target_pairs={{4,0},{8,4},{12,8},{16,12},{20,16},{24,20},{28,24},{5,1},{9,5},{13... | collective-permute-start | bytes 589832 | tf_op jit(solution)/shard_map/ppermute | solution.py:194
  90.8 2.0 %collective-permute-done.4.xlo_ref = f32[3,2,32,256]{3,2,1,0:T(8,128)S(1)} collective-permute-done((f32[3,2,32,256]{3,2,1,0:T(8,128)}, f32[3,2,32,256]{3,2,1,0:T(8,128)S(1)}, u32[]{:S(2)}, u32[]{:S(2)}) %collective-permute-start.4) | collective-permute-done | bytes 196640 | tf_op jit(solution)/shard_map/ppermute | solution.py:193
  92.8 3.1 %collective-permute-done.5.xhi_ref = f32[3,2,32,256]{3,2,1,0:T(8,128)S(1)} collective-permute-done((f32[3,2,32,256]{3,2,1,0:T(8,128)}, f32[3,2,32,256]{3,2,1,0:T(8,128)S(1)}, u32[]{:S(2)}, u32[]{:S(2)}) %collective-permute-start.5) | collective-permute-done | bytes 196640 | tf_op jit(solution)/shard_map/ppermute | solution.py:194
  96.0 1.1 pad_maximum_fusion.4
  97.1 3.8 %collective-permute-start.7 = (f32[3,36,2,256]{3,2,1,0:T(2,128)S(1)}, f32[3,36,2,256]{3,2,1,0:T(2,128)S(1)}, u32[]{:S(2)}, u32[]{:S(2)}) collective-permute-start(f32[3,36,2,256]{3,2,1,0:T(2,128)S(1)} %pad_maximum_fusion.4), channel_id=1, source_target_pairs={{1,0},{2,1},{3,2},{5,4},{6,5},{7,6},{9,8},{10,9},{11,10},{13,12},{... | collective-permute-start | bytes 663560 | tf_op jit(solution)/shard_map/ppermute | solution.py:199
  101.9 1.9 collective-permute-start.6
  103.8 3.2 %fusion.9 = f32[3072,256]{1,0:T(8,128)} fusion(s32[256]{0:T(256)S(1)} %get-tuple-element.323, f32[256]{0:T(256)S(1)} %bitcast.115, s32[256]{0:T(256)S(1)} %get-tuple-element.322), kind=kOutput, calls=%fused_computation.28 | convolution fusion | flops 2416836608 | bytes 3148800 | tf_op jit(solution)/shard_map/dot_general | solution.py:406
  107.0 2.1 %collective-permute-done.6.ylo_ref = f32[3,36,2,256]{3,2,1,0:T(2,128)S(1)} collective-permute-done((f32[3,36,2,256]{3,2,1,0:T(2,128)S(1)}, f32[3,36,2,256]{3,2,1,0:T(2,128)S(1)}, u32[]{:S(2)}, u32[]{:S(2)}) %collective-permute-start.6) | collective-permute-done | bytes 221216 | tf_op jit(solution)/shard_map/ppermute | solution.py:198
  109.8 13.5 %shard_map.123 = (f32[3,32,32,256]{3,2,1,0:T(8,128)}, f32[3,2,32,256]{3,2,1,0:T(8,128)}, f32[3,2,32,256]{3,2,1,0:T(8,128)}, f32[3,32,2,256]{3,2,1,0:T(2,128)}, f32[3,32,2,256]{3,2,1,0:T(2,128)}) custom-call(f32[3,32,32,256]{3,2,1,0:T(8,128)} %get-tuple-element.209.u_ref.prev_ref, f32[3,2,32,256]{3,2,1,0:T(8,128)} %copy-done.5, f32[3,2,32,256]{3,2,1,0:T(8,128)} %copy-done.7, ...), custom_call_target="tpu_custom_call" | custom-call | tf_op jit(solution)/shard_map/pallas_call | solution.py:149
  123.3 2.5 %collective-permute-start.8 = (f32[3,2,32,256]{3,2,1,0:T(8,128)}, f32[3,2,32,256]{3,2,1,0:T(8,128)S(1)}, u32[]{:S(2)}, u32[]{:S(2)}) collective-permute-start(f32[3,2,32,256]{3,2,1,0:T(8,128)} %get-tuple-element.215), channel_id=1, source_target_pairs={{0,4},{4,8},{8,12},{12,16},{16,20},{20,24},{24,28},{1,5},{5,9},{9,... | collective-permute-start | bytes 589832 | tf_op jit(solution)/shard_map/ppermute | solution.py:193
  125.8 4.2 %collective-permute-start.9 = (f32[3,2,32,256]{3,2,1,0:T(8,128)}, f32[3,2,32,256]{3,2,1,0:T(8,128)S(1)}, u32[]{:S(2)}, u32[]{:S(2)}) collective-permute-start(f32[3,2,32,256]{3,2,1,0:T(8,128)} %get-tuple-element.216), channel_id=1, source_target_pairs={{4,0},{8,4},{12,8},{16,12},{20,16},{24,20},{28,24},{5,1},{9,5},{13... | collective-permute-start | bytes 589832 | tf_op jit(solution)/shard_map/ppermute | solution.py:194
  130.0 1.9 collective-permute-done.8.xlo_ref
  132.0 2.1 %collective-permute-done.9.xhi_ref = f32[3,2,32,256]{3,2,1,0:T(8,128)S(1)} collective-permute-done((f32[3,2,32,256]{3,2,1,0:T(8,128)}, f32[3,2,32,256]{3,2,1,0:T(8,128)S(1)}, u32[]{:S(2)}, u32[]{:S(2)}) %collective-permute-start.9) | collective-permute-done | bytes 196640 | tf_op jit(solution)/shard_map/ppermute | solution.py:194
  134.1 1.1 pad_maximum_fusion.6
  135.2 4.6 %collective-permute-start.11 = (f32[3,36,2,256]{3,2,1,0:T(2,128)S(1)}, f32[3,36,2,256]{3,2,1,0:T(2,128)S(1)}, u32[]{:S(2)}, u32[]{:S(2)}) collective-permute-start(f32[3,36,2,256]{3,2,1,0:T(2,128)S(1)} %pad_maximum_fusion.6), channel_id=1, source_target_pairs={{1,0},{2,1},{3,2},{5,4},{6,5},{7,6},{9,8},{10,9},{11,10},{13,12},{... | collective-permute-start | bytes 663560 | tf_op jit(solution)/shard_map/ppermute | solution.py:199
  140.8 1.9 collective-permute-start.10
  142.7 3.2 %fusion.8 = f32[3072,256]{1,0:T(8,128)} fusion(s32[256]{0:T(256)S(1)} %get-tuple-element.323, f32[256]{0:T(256)S(1)} %bitcast.114, s32[256]{0:T(256)S(1)} %get-tuple-element.322), kind=kOutput, calls=%fused_computation.27 | convolution fusion | flops 2416836608 | bytes 3148800 | tf_op jit(solution)/shard_map/dot_general | solution.py:406
  145.9 2.1 %collective-permute-done.10.ylo_ref = f32[3,36,2,256]{3,2,1,0:T(2,128)S(1)} collective-permute-done((f32[3,36,2,256]{3,2,1,0:T(2,128)S(1)}, f32[3,36,2,256]{3,2,1,0:T(2,128)S(1)}, u32[]{:S(2)}, u32[]{:S(2)}) %collective-permute-start.10) | collective-permute-done | bytes 221216 | tf_op jit(solution)/shard_map/ppermute | solution.py:198
  148.7 13.4 %shard_map.124 = (f32[3,32,32,256]{3,2,1,0:T(8,128)}, f32[3,2,32,256]{3,2,1,0:T(8,128)}, f32[3,2,32,256]{3,2,1,0:T(8,128)}, f32[3,32,2,256]{3,2,1,0:T(2,128)}, f32[3,32,2,256]{3,2,1,0:T(2,128)}) custom-call(f32[3,32,32,256]{3,2,1,0:T(8,128)} %get-tuple-element.214.u_ref.prev_ref, f32[3,2,32,256]{3,2,1,0:T(8,128)} %copy-done.3, f32[3,2,32,256]{3,2,1,0:T(8,128)} %copy-done.6, ...), custom_call_target="tpu_custom_call" | custom-call | tf_op jit(solution)/shard_map/pallas_call | solution.py:149
  162.2 2.5 %collective-permute-start.12 = (f32[3,2,32,256]{3,2,1,0:T(8,128)}, f32[3,2,32,256]{3,2,1,0:T(8,128)S(1)}, u32[]{:S(2)}, u32[]{:S(2)}) collective-permute-start(f32[3,2,32,256]{3,2,1,0:T(8,128)} %get-tuple-element.220), channel_id=1, source_target_pairs={{0,4},{4,8},{8,12},{12,16},{16,20},{20,24},{24,28},{1,5},{5,9},{9,... | collective-permute-start | bytes 589832 | tf_op jit(solution)/shard_map/ppermute | solution.py:193
  164.6 4.3 %collective-permute-start.13 = (f32[3,2,32,256]{3,2,1,0:T(8,128)}, f32[3,2,32,256]{3,2,1,0:T(8,128)S(1)}, u32[]{:S(2)}, u32[]{:S(2)}) collective-permute-start(f32[3,2,32,256]{3,2,1,0:T(8,128)} %get-tuple-element.221), channel_id=1, source_target_pairs={{4,0},{8,4},{12,8},{16,12},{20,16},{24,20},{28,24},{5,1},{9,5},{13... | collective-permute-start | bytes 589832 | tf_op jit(solution)/shard_map/ppermute | solution.py:194
  168.9 1.9 collective-permute-done.12.xlo_ref
  170.9 2.1 %collective-permute-done.13.xhi_ref = f32[3,2,32,256]{3,2,1,0:T(8,128)S(1)} collective-permute-done((f32[3,2,32,256]{3,2,1,0:T(8,128)}, f32[3,2,32,256]{3,2,1,0:T(8,128)S(1)}, u32[]{:S(2)}, u32[]{:S(2)}) %collective-permute-start.13) | collective-permute-done | bytes 196640 | tf_op jit(solution)/shard_map/ppermute | solution.py:194
  172.9 1.1 pad_maximum_fusion.8
  174.0 4.6 %collective-permute-start.15 = (f32[3,36,2,256]{3,2,1,0:T(2,128)S(1)}, f32[3,36,2,256]{3,2,1,0:T(2,128)S(1)}, u32[]{:S(2)}, u32[]{:S(2)}) collective-permute-start(f32[3,36,2,256]{3,2,1,0:T(2,128)S(1)} %pad_maximum_fusion.8), channel_id=1, source_target_pairs={{1,0},{2,1},{3,2},{5,4},{6,5},{7,6},{9,8},{10,9},{11,10},{13,12},{... | collective-permute-start | bytes 663560 | tf_op jit(solution)/shard_map/ppermute | solution.py:199
  179.6 1.9 collective-permute-start.14
  181.6 3.2 %fusion.7 = f32[3072,256]{1,0:T(8,128)} fusion(s32[256]{0:T(256)S(1)} %get-tuple-element.323, f32[256]{0:T(256)S(1)} %bitcast.113, s32[256]{0:T(256)S(1)} %get-tuple-element.322), kind=kOutput, calls=%fused_computation.26 | convolution fusion | flops 2416836608 | bytes 3148800 | tf_op jit(solution)/shard_map/dot_general | solution.py:406
  184.8 2.1 %collective-permute-done.14.ylo_ref = f32[3,36,2,256]{3,2,1,0:T(2,128)S(1)} collective-permute-done((f32[3,36,2,256]{3,2,1,0:T(2,128)S(1)}, f32[3,36,2,256]{3,2,1,0:T(2,128)S(1)}, u32[]{:S(2)}, u32[]{:S(2)}) %collective-permute-start.14) | collective-permute-done | bytes 221216 | tf_op jit(solution)/shard_map/ppermute | solution.py:198
  187.6 13.4 %shard_map.125 = (f32[3,32,32,256]{3,2,1,0:T(8,128)}, f32[3,2,32,256]{3,2,1,0:T(8,128)}, f32[3,2,32,256]{3,2,1,0:T(8,128)}, f32[3,32,2,256]{3,2,1,0:T(2,128)}, f32[3,32,2,256]{3,2,1,0:T(2,128)}) custom-call(f32[3,32,32,256]{3,2,1,0:T(8,128)} %get-tuple-element.205.u_ref, f32[3,2,32,256]{3,2,1,0:T(8,128)} %copy-done.2, f32[3,2,32,256]{3,2,1,0:T(8,128)} %copy-done.4, ...), custom_call_target="tpu_custom_call" | custom-call | tf_op jit(solution)/shard_map/pallas_call | solution.py:149
  (132 shorter events, 16.7 us)
Async XLA Ops:
  16.0 5.3 %copy-start.16 = (s32[8192]{0:T(1024)S(1)}, s32[8192]{0:T(1024)}, u32[]{:S(2)}) copy-start(s32[8192]{0:T(1024)} %param.19) | copy-start | bytes 98308
  16.0 5.3 %copy-start.17 = (s32[8192]{0:T(1024)S(1)}, s32[8192]{0:T(1024)}, u32[]{:S(2)}) copy-start(s32[8192]{0:T(1024)} %param.20) | copy-start | bytes 98308
  24.8 30.6 %copy-start.18 = (s32[256]{0:T(256)S(1)}, s32[256]{0:T(256)}, u32[]{:S(2)}) copy-start(s32[256]{0:T(256)} %param.21) | copy-start | bytes 3076
  39.2 25.6 %all-to-all-start = ((bf16[2,4,32,256]{3,1,0,2:T(4,128)(2,1)}), bf16[2,4,32,256]{3,1,0,2:T(4,128)(2,1)S(1)}, u32[]{:S(2)}, u32[]{:S(2)}) async-start(bf16[2,4,32,256]{3,1,0,2:T(4,128)(2,1)} %copy.27), calls=%async_computation | async-start | bytes 262144 | tf_op jit(solution)/shard_map/all_to_all | solution.py:382
  46.3 9.7 %collective-permute-start = (f32[3,2,32,256]{3,2,1,0:T(8,128)S(1)}, f32[3,2,32,256]{3,2,1,0:T(8,128)S(1)}, u32[]{:S(2)}, u32[]{:S(2)}) collective-permute-start(f32[3,2,32,256]{3,2,1,0:T(8,128)S(1)} %get-tuple-element.292), channel_id=1, source_target_pairs={{0,4},{4,8},{8,12},{12,16},{16,20},{20,24},{24,28},{1,5},{5,9},{9,... | collective-permute-start | bytes 589832 | tf_op jit(solution)/shard_map/ppermute | solution.py:193
  49.7 10.5 %collective-permute-start.1 = (f32[3,2,32,256]{3,2,1,0:T(8,128)S(1)}, f32[3,2,32,256]{3,2,1,0:T(8,128)S(1)}, u32[]{:S(2)}, u32[]{:S(2)}) collective-permute-start(f32[3,2,32,256]{3,2,1,0:T(8,128)S(1)} %get-tuple-element.291), channel_id=1, source_target_pairs={{4,0},{8,4},{12,8},{16,12},{20,16},{24,20},{28,24},{5,1},{9,5},{13... | collective-permute-start | bytes 589832 | tf_op jit(solution)/shard_map/ppermute | solution.py:194
  56.0 13.9 %copy-start = (f32[3,2,32,256]{3,2,1,0:T(8,128)}, f32[3,2,32,256]{3,2,1,0:T(8,128)S(1)}, u32[]{:S(2)}) copy-start(f32[3,2,32,256]{3,2,1,0:T(8,128)S(1)} %collective-permute-done.xlo_ref) | copy-start | bytes 589828
  60.2 9.7 %copy-start.1 = (f32[3,2,32,256]{3,2,1,0:T(8,128)}, f32[3,2,32,256]{3,2,1,0:T(8,128)S(1)}, u32[]{:S(2)}) copy-start(f32[3,2,32,256]{3,2,1,0:T(8,128)S(1)} %collective-permute-done.1.xhi_ref) | copy-start | bytes 589828
  60.4 8.0 %collective-permute-start.3 = (f32[3,36,2,256]{3,2,1,0:T(2,128)S(1)}, f32[3,36,2,256]{3,2,1,0:T(2,128)S(1)}, u32[]{:S(2)}, u32[]{:S(2)}) collective-permute-start(f32[3,36,2,256]{3,2,1,0:T(2,128)S(1)} %pad_maximum_fusion.2), channel_id=1, source_target_pairs={{1,0},{2,1},{3,2},{5,4},{6,5},{7,6},{9,8},{10,9},{11,10},{13,12},{... | collective-permute-start | bytes 663560 | tf_op jit(solution)/shard_map/ppermute | solution.py:199
  62.7 7.3 %collective-permute-start.2 = (f32[3,36,2,256]{3,2,1,0:T(2,128)S(1)}, f32[3,36,2,256]{3,2,1,0:T(2,128)S(1)}, u32[]{:S(2)}, u32[]{:S(2)}) collective-permute-start(f32[3,36,2,256]{3,2,1,0:T(2,128)S(1)} %pad_maximum_fusion.1), channel_id=1, source_target_pairs={{0,1},{1,2},{2,3},{4,5},{5,6},{6,7},{8,9},{9,10},{10,11},{12,13},{... | collective-permute-start | bytes 663560 | tf_op jit(solution)/shard_map/ppermute | solution.py:198
  68.3 1.6 copy-start.8
  69.9 0.7 copy-start.9
  84.1 8.8 %collective-permute-start.4 = (f32[3,2,32,256]{3,2,1,0:T(8,128)}, f32[3,2,32,256]{3,2,1,0:T(8,128)S(1)}, u32[]{:S(2)}, u32[]{:S(2)}) collective-permute-start(f32[3,2,32,256]{3,2,1,0:T(8,128)} %get-tuple-element.210), channel_id=1, source_target_pairs={{0,4},{4,8},{8,12},{12,16},{16,20},{20,24},{24,28},{1,5},{5,9},{9,... | collective-permute-start | bytes 589832 | tf_op jit(solution)/shard_map/ppermute | solution.py:193
  86.3 9.6 %collective-permute-start.5 = (f32[3,2,32,256]{3,2,1,0:T(8,128)}, f32[3,2,32,256]{3,2,1,0:T(8,128)S(1)}, u32[]{:S(2)}, u32[]{:S(2)}) collective-permute-start(f32[3,2,32,256]{3,2,1,0:T(8,128)} %get-tuple-element.211), channel_id=1, source_target_pairs={{4,0},{8,4},{12,8},{16,12},{20,16},{24,20},{28,24},{5,1},{9,5},{13... | collective-permute-start | bytes 589832 | tf_op jit(solution)/shard_map/ppermute | solution.py:194
  92.8 16.3 %copy-start.5 = (f32[3,2,32,256]{3,2,1,0:T(8,128)}, f32[3,2,32,256]{3,2,1,0:T(8,128)S(1)}, u32[]{:S(2)}) copy-start(f32[3,2,32,256]{3,2,1,0:T(8,128)S(1)} %collective-permute-done.4.xlo_ref) | copy-start | bytes 589828
  96.0 13.2 %copy-start.7 = (f32[3,2,32,256]{3,2,1,0:T(8,128)}, f32[3,2,32,256]{3,2,1,0:T(8,128)S(1)}, u32[]{:S(2)}) copy-start(f32[3,2,32,256]{3,2,1,0:T(8,128)S(1)} %collective-permute-done.5.xhi_ref) | copy-start | bytes 589828
  97.1 9.9 %collective-permute-start.7 = (f32[3,36,2,256]{3,2,1,0:T(2,128)S(1)}, f32[3,36,2,256]{3,2,1,0:T(2,128)S(1)}, u32[]{:S(2)}, u32[]{:S(2)}) collective-permute-start(f32[3,36,2,256]{3,2,1,0:T(2,128)S(1)} %pad_maximum_fusion.4), channel_id=1, source_target_pairs={{1,0},{2,1},{3,2},{5,4},{6,5},{7,6},{9,8},{10,9},{11,10},{13,12},{... | collective-permute-start | bytes 663560 | tf_op jit(solution)/shard_map/ppermute | solution.py:199
  101.9 7.3 %collective-permute-start.6 = (f32[3,36,2,256]{3,2,1,0:T(2,128)S(1)}, f32[3,36,2,256]{3,2,1,0:T(2,128)S(1)}, u32[]{:S(2)}, u32[]{:S(2)}) collective-permute-start(f32[3,36,2,256]{3,2,1,0:T(2,128)S(1)} %pad_maximum_fusion.3), channel_id=1, source_target_pairs={{0,1},{1,2},{2,3},{4,5},{5,6},{6,7},{8,9},{9,10},{10,11},{12,13},{... | collective-permute-start | bytes 663560 | tf_op jit(solution)/shard_map/ppermute | solution.py:198
  107.0 2.1 %copy-start.12 = (f32[3,36,2,256]{3,2,1,0:T(2,128)}, f32[3,36,2,256]{3,2,1,0:T(2,128)S(1)}, u32[]{:S(2)}) copy-start(f32[3,36,2,256]{3,2,1,0:T(2,128)S(1)} %collective-permute-done.7.yhi_ref) | copy-start | bytes 663556
  109.1 0.7 copy-start.15
  123.3 8.7 %collective-permute-start.8 = (f32[3,2,32,256]{3,2,1,0:T(8,128)}, f32[3,2,32,256]{3,2,1,0:T(8,128)S(1)}, u32[]{:S(2)}, u32[]{:S(2)}) collective-permute-start(f32[3,2,32,256]{3,2,1,0:T(8,128)} %get-tuple-element.215), channel_id=1, source_target_pairs={{0,4},{4,8},{8,12},{12,16},{16,20},{20,24},{24,28},{1,5},{5,9},{9,... | collective-permute-start | bytes 589832 | tf_op jit(solution)/shard_map/ppermute | solution.py:193
  125.8 8.2 %collective-permute-start.9 = (f32[3,2,32,256]{3,2,1,0:T(8,128)}, f32[3,2,32,256]{3,2,1,0:T(8,128)S(1)}, u32[]{:S(2)}, u32[]{:S(2)}) collective-permute-start(f32[3,2,32,256]{3,2,1,0:T(8,128)} %get-tuple-element.216), channel_id=1, source_target_pairs={{4,0},{8,4},{12,8},{16,12},{20,16},{24,20},{28,24},{5,1},{9,5},{13... | collective-permute-start | bytes 589832 | tf_op jit(solution)/shard_map/ppermute | solution.py:194
  132.0 16.1 %copy-start.3 = (f32[3,2,32,256]{3,2,1,0:T(8,128)}, f32[3,2,32,256]{3,2,1,0:T(8,128)S(1)}, u32[]{:S(2)}) copy-start(f32[3,2,32,256]{3,2,1,0:T(8,128)S(1)} %collective-permute-done.8.xlo_ref) | copy-start | bytes 589828
  134.0 14.0 %copy-start.6 = (f32[3,2,32,256]{3,2,1,0:T(8,128)}, f32[3,2,32,256]{3,2,1,0:T(8,128)S(1)}, u32[]{:S(2)}) copy-start(f32[3,2,32,256]{3,2,1,0:T(8,128)S(1)} %collective-permute-done.9.xhi_ref) | copy-start | bytes 589828
  135.2 10.8 %collective-permute-start.11 = (f32[3,36,2,256]{3,2,1,0:T(2,128)S(1)}, f32[3,36,2,256]{3,2,1,0:T(2,128)S(1)}, u32[]{:S(2)}, u32[]{:S(2)}) collective-permute-start(f32[3,36,2,256]{3,2,1,0:T(2,128)S(1)} %pad_maximum_fusion.6), channel_id=1, source_target_pairs={{1,0},{2,1},{3,2},{5,4},{6,5},{7,6},{9,8},{10,9},{11,10},{13,12},{... | collective-permute-start | bytes 663560 | tf_op jit(solution)/shard_map/ppermute | solution.py:199
  140.8 7.3 %collective-permute-start.10 = (f32[3,36,2,256]{3,2,1,0:T(2,128)S(1)}, f32[3,36,2,256]{3,2,1,0:T(2,128)S(1)}, u32[]{:S(2)}, u32[]{:S(2)}) collective-permute-start(f32[3,36,2,256]{3,2,1,0:T(2,128)S(1)} %pad_maximum_fusion.5), channel_id=1, source_target_pairs={{0,1},{1,2},{2,3},{4,5},{5,6},{6,7},{8,9},{9,10},{10,11},{12,13},{... | collective-permute-start | bytes 663560 | tf_op jit(solution)/shard_map/ppermute | solution.py:198
  145.9 2.1 %copy-start.11 = (f32[3,36,2,256]{3,2,1,0:T(2,128)}, f32[3,36,2,256]{3,2,1,0:T(2,128)S(1)}, u32[]{:S(2)}) copy-start(f32[3,36,2,256]{3,2,1,0:T(2,128)S(1)} %collective-permute-done.11.yhi_ref) | copy-start | bytes 663556
  148.0 0.7 copy-start.14
  162.2 8.7 %collective-permute-start.12 = (f32[3,2,32,256]{3,2,1,0:T(8,128)}, f32[3,2,32,256]{3,2,1,0:T(8,128)S(1)}, u32[]{:S(2)}, u32[]{:S(2)}) collective-permute-start(f32[3,2,32,256]{3,2,1,0:T(8,128)} %get-tuple-element.220), channel_id=1, source_target_pairs={{0,4},{4,8},{8,12},{12,16},{16,20},{20,24},{24,28},{1,5},{5,9},{9,... | collective-permute-start | bytes 589832 | tf_op jit(solution)/shard_map/ppermute | solution.py:193
  164.6 8.3 %collective-permute-start.13 = (f32[3,2,32,256]{3,2,1,0:T(8,128)}, f32[3,2,32,256]{3,2,1,0:T(8,128)S(1)}, u32[]{:S(2)}, u32[]{:S(2)}) collective-permute-start(f32[3,2,32,256]{3,2,1,0:T(8,128)} %get-tuple-element.221), channel_id=1, source_target_pairs={{4,0},{8,4},{12,8},{16,12},{20,16},{24,20},{28,24},{5,1},{9,5},{13... | collective-permute-start | bytes 589832 | tf_op jit(solution)/shard_map/ppermute | solution.py:194
  170.8 16.1 %copy-start.2 = (f32[3,2,32,256]{3,2,1,0:T(8,128)}, f32[3,2,32,256]{3,2,1,0:T(8,128)S(1)}, u32[]{:S(2)}) copy-start(f32[3,2,32,256]{3,2,1,0:T(8,128)S(1)} %collective-permute-done.12.xlo_ref) | copy-start | bytes 589828
  172.9 14.0 %copy-start.4 = (f32[3,2,32,256]{3,2,1,0:T(8,128)}, f32[3,2,32,256]{3,2,1,0:T(8,128)S(1)}, u32[]{:S(2)}) copy-start(f32[3,2,32,256]{3,2,1,0:T(8,128)S(1)} %collective-permute-done.13.xhi_ref) | copy-start | bytes 589828
  174.0 10.8 %collective-permute-start.15 = (f32[3,36,2,256]{3,2,1,0:T(2,128)S(1)}, f32[3,36,2,256]{3,2,1,0:T(2,128)S(1)}, u32[]{:S(2)}, u32[]{:S(2)}) collective-permute-start(f32[3,36,2,256]{3,2,1,0:T(2,128)S(1)} %pad_maximum_fusion.8), channel_id=1, source_target_pairs={{1,0},{2,1},{3,2},{5,4},{6,5},{7,6},{9,8},{10,9},{11,10},{13,12},{... | collective-permute-start | bytes 663560 | tf_op jit(solution)/shard_map/ppermute | solution.py:199
  179.6 7.3 %collective-permute-start.14 = (f32[3,36,2,256]{3,2,1,0:T(2,128)S(1)}, f32[3,36,2,256]{3,2,1,0:T(2,128)S(1)}, u32[]{:S(2)}, u32[]{:S(2)}) collective-permute-start(f32[3,36,2,256]{3,2,1,0:T(2,128)S(1)} %pad_maximum_fusion.7), channel_id=1, source_target_pairs={{0,1},{1,2},{2,3},{4,5},{5,6},{6,7},{8,9},{9,10},{10,11},{12,13},{... | collective-permute-start | bytes 663560 | tf_op jit(solution)/shard_map/ppermute | solution.py:198
  184.8 2.1 %copy-start.10 = (f32[3,36,2,256]{3,2,1,0:T(2,128)}, f32[3,36,2,256]{3,2,1,0:T(2,128)S(1)}, u32[]{:S(2)}) copy-start(f32[3,36,2,256]{3,2,1,0:T(2,128)S(1)} %collective-permute-done.15.yhi_ref) | copy-start | bytes 663556
  186.9 0.7 copy-start.13

commit v10 on v6

--- a/solution.py
+++ b/solution.py
@@ -35,22 +35,19 @@
 YPAD = 8
 
 
-def step_kernel(u_ref, xlo_ref, xhi_ref, ylo_ref, yhi_ref, prev_ref, mod_ref, src_ref, out_ref, up_ref, *, bx):
+def step_kernel(u_ref, xlo_ref, xhi_ref, ylo_ref, yhi_ref, prev_ref, mod_ref, src_ref, out_ref, up_ref, sem, *, bx):
     i = pl.program_id(0)
     nx, ny = u_ref.shape[1], u_ref.shape[2]
 
     @pl.when(i == 0)
     def _():
-        for c in range(3):
-            def fill(x, carry):
-                up_ref[c, x + 2, pl.ds(YPAD, ny), :] = u_ref[c, x]
-                return carry
-
-            lax.fori_loop(0, nx, fill, 0)
+        fill = pltpu.make_async_copy(u_ref, up_ref.at[:, pl.ds(2, nx), pl.ds(YPAD, ny), :], sem)
+        fill.start()
         up_ref[:, 0:2, pl.ds(YPAD, ny), :] = xlo_ref[...]
         up_ref[:, nx + 2:nx + 4, pl.ds(YPAD, ny), :] = xhi_ref[...]
         up_ref[:, :, pl.ds(YPAD - 2, 2), :] = ylo_ref[...]
         up_ref[:, :, pl.ds(YPAD + ny, 2), :] = yhi_ref[...]
+        fill.wait()
 
     depth = out_ref.shape[3]
     lane = lax.broadcasted_iota(jnp.int32, (8, depth), 1)
@@ -136,7 +133,7 @@
         kernel,
         grid=(nx // bx,),
         in_specs=[
-            pl.BlockSpec(u.shape, whole),
+            pl.BlockSpec(memory_space=pl.ANY),
             pl.BlockSpec(xlo.shape, whole),
             pl.BlockSpec(xhi.shape, whole),
             pl.BlockSpec(ylo.shape, whole),
@@ -147,7 +144,10 @@
         ],
         out_specs=pl.BlockSpec((3, bx, ny, depth), block),
         out_shape=jax.ShapeDtypeStruct((3, nx, ny, depth), jnp.float32),
-        scratch_shapes=[pltpu.VMEM((3, nx + 4, ny + 2 * YPAD, depth), jnp.float32)],
+        scratch_shapes=[
+            pltpu.VMEM((3, nx + 4, ny + 2 * YPAD, depth), jnp.float32),
+            pltpu.SemaphoreType.DMA(()),
+        ],
         compiler_params=pltpu.CompilerParams(dimension_semantics=("arbitrary",)),
     )(u, xlo, xhi, ylo, yhi, prev, moduli, sources)
 

time: 197 us -> 199 us (1.010)
  no operation moved by 1% of the time
where the time goes in v10:
time: 199 us; the launch traced here: 198 us
  starting transfers between devices  55.9 us (28%)
  Pallas kernels  53.4 us (27%)
  matrix products  29.6 us (15%)
  other arithmetic  20.6 us (10%)
  waiting for transfers between devices  20.6 us (10%)
  local copies, waits for them, and re-layouts  15 us (8%)
  between operations  2.05 us (1%)
    pallas_call x4, Pallas kernels, elastic_step(): pl.pallas_call(kernel, grid=(nx // bx,), in_specs=[pl.BlockSpec(memory_sp...  53.4 us
    ppermute x4, starting transfers between devices, halos(): xhi = lax.ppermute(block[:, :width], 'gx', backward_x)  16.3 us
    ppermute x4, starting transfers between devices, halos(): yhi = lax.ppermute(rows(slice(0, width)), 'gy', backward_y)  15.1 us
    dot_general x2, matrix products, select_block(): jnp.dot(table_rounded, offset_hot, preferred_element_type=jnp.float32)  13.1 us
    dot_general x4, matrix products, shards(): source = jnp.dot(column_hot, spread, precision=lax.Precision.HIGHEST)  12.9 us
    ppermute x4, waiting for transfers between devices, halos(): xhi = lax.ppermute(block[:, :width], 'gx', backward_x)  11.5 us
    ppermute x4, starting transfers between devices, halos(): xlo = lax.ppermute(block[:, nx - width:], 'gx', forward_x)  10.7 us
    ppermute x4, starting transfers between devices, halos(): ylo = lax.ppermute(rows(slice(ny - width, ny)), 'gy', forward_y)  7.91 us
  transfers between devices with their start and end apart: 17, of which 12 were waited for; matrix products, arithmetic and copies ran while one was open for 11% of the time, Pallas kernels for 0%

profile of v10, /device:TPU:12, one launch (start us, length us, event | category | flops | bytes accessed | tf_op | source)
XLA Modules:
  0.0 197.7 jit_solution(10015930181887496397)
XLA Ops:
  2.9 4.9 %sine_multiply_fusion.1 = (f32[32,4,1024]{2,1,0:T(4,128)S(1)}, f32[32,4,1024]{2,1,0:T(4,128)S(1)}, f32[32,4,1024]{2,1,0:T(4,128)S(1)}) fusion(f32[32]{0:T(128)S(1)} %get-tuple-element.307, f32[32,4]{1,0:T(8,128)S(1)} %copy.24, f32[1024]{0:T(1024)S(1)} %multiply_multiply_fusion, f32[1,4,1024]{2,1,0:T(4,128)S(1)} %slice.157, f32[31,4,1024]{2,1,0:T(4,128)S(1)} %slice.156, ...), kind=kLoop, calls=%fused_computation.41 | loop fusion | flops 1441792 | bytes 2102016 | tf_op jit(solution)/shard_map/mul | solution.py:188
  8.1 2.2 %while.32 = (s32[]{:T(128)}, f32[4,1024]{1,0:T(4,128)S(1)}, f32[4,1024]{1,0:T(4,128)S(1)}, f32[32,4,1024]{2,1,0:T(4,128)S(1)}, f32[32,4,1024]{2,1,0:T(4,128)S(1)...) while((s32[]{:T(128)}, f32[4,1024]{1,0:T(4,128)S(1)}, ...), condition=%wide.region_6.7_spmd.clone, body=%wide.region_5.6_spmd.clone.sunk | while | flops 94212 | bytes 147591 | solution.py:204
  11.2 4.3 %fusion.43 = (bf16[1,32,4,1024]{3,2,1,0:T(4,128)(2,1)S(1)}, bf16[1,32,4,1024]{3,2,1,0:T(4,128)(2,1)S(1)}) fusion(f32[32,4,1024]{2,1,0:T(4,128)S(1)} %get-tuple-element.191, f32[32,4,1024]{2,1,0:T(4,128)S(1)} %get-tuple-element.190, f32[32,4,1024]{2,1,0:T(4,128)S(1)} %negate_exponential_fusion, f32[32,4,1024]{2,1,0:T(4,128)S(1)} %fusion.23), kind=kLoop, calls=%fused_computation.74 | loop fusion | flops 1835008 | bytes 2621440 | tf_op jit(solution)/shard_map/stack | solution.py:217
  17.7 3.6 %subtract_convert_fusion = bf16[1024,32,64]{0,2,1:T(8,128)(2,1)} fusion(f32[1024,64]{0,1:T(8,128)S(1)} %get-tuple-element.301, f32[1024,32]{0,1:T(8,128)S(1)} %get-tuple-element.295, f32[1024,64]{0,1:T(8,128)S(1)} %get-tuple-element.300, f32[1024,32]{0,1:T(8,128)S(1)} %get-tuple-element.294), kind=kLoop, calls=%fused_computation.24 | loop fusion | flops 8388608 | bytes 4980736 | tf_op jit(solution)/shard_map/convert_element_type | solution.py:232
  21.4 3.5 %convolution_convert_fusion = bf16[256,2048]{1,0:T(8,128)(2,1)S(1)} fusion(bf16[256,1024]{1,0:T(8,128)(2,1)S(1)} %bitcast.109, bf16[1024,2048]{0,1:T(8,128)(2,1)} %bitcast.107), kind=kOutput, calls=%fused_computation.30 | convolution fusion | flops 1074266112 | bytes 5767168 | tf_op jit(solution)/shard_map/dot_general | solution.py:320
  24.9 13.4 %while.31 = (s32[]{:T(128)}, bf16[2,2,4,4096]{3,2,1,0:T(4,128)(2,1)S(1)}, s32[2,4096]{1,0:T(2,128)S(1)}, bf16[256,2048]{1,0:T(8,128)(2,1)S(1)}, s32[2,4096]{1,0:T(2,128)S(1)}, /*index=5*/s32[]{:T(128)}) while((s32[]{:T(128)}, bf16[2,2,4,4096]{3,2,1,0:T(4,128)(2,1)S(1)}, s32[2,4096]{1,0:T(2,128)S(1)}, bf16[256,2048]{1,0:T(8,128)(2,1)S(1)}, ...), condition=%wide.region_9.10_spmd, body=%wide.region_7.9_spmd.sunk | while | flops 4305682432 | bytes 2392141 | solution.py:343
  25.0 6.5 %multiply_reduce_fusion.2 = bf16[2,4,4096]{2,1,0:T(4,128)(2,1)S(1)} fusion(f32[32,4096]{1,0:T(8,128)S(1)} %fusion.102, bf16[256,2048]{1,0:T(8,128)(2,1)S(1)} %get-tuple-element.448, s32[4096]{0:T(1024)S(1)} %bitcast.111), kind=kOutput, calls=%fused_computation.3.clone.1 | convolution fusion | flops 4305420288 | bytes 1654784 | tf_op jit(solution)/shard_map/while/body/eval_jaxpr/dot_general | solution.py:335
  31.7 6.5 %multiply_reduce_fusion.2 = bf16[2,4,4096]{2,1,0:T(4,128)(2,1)S(1)} fusion(f32[32,4096]{1,0:T(8,128)S(1)} %fusion.102, bf16[256,2048]{1,0:T(8,128)(2,1)S(1)} %get-tuple-element.448, s32[4096]{0:T(1024)S(1)} %bitcast.111), kind=kOutput, calls=%fused_computation.3.clone.1 | convolution fusion | flops 4305420288 | bytes 1654784 | tf_op jit(solution)/shard_map/while/body/eval_jaxpr/dot_general | solution.py:335
  39.3 6.0 %all-to-all-start = ((bf16[2,4,32,256]{3,1,0,2:T(4,128)(2,1)}), bf16[2,4,32,256]{3,1,0,2:T(4,128)(2,1)S(1)}, u32[]{:S(2)}, u32[]{:S(2)}) async-start(bf16[2,4,32,256]{3,1,0,2:T(4,128)(2,1)} %copy.27), calls=%async_computation | async-start | bytes 262144 | tf_op jit(solution)/shard_map/all_to_all | solution.py:350
  45.3 1.1 fusion.85
  46.3 3.4 %collective-permute-start = (f32[3,2,32,256]{3,2,1,0:T(8,128)S(1)}, f32[3,2,32,256]{3,2,1,0:T(8,128)S(1)}, u32[]{:S(2)}, u32[]{:S(2)}) collective-permute-start(f32[3,2,32,256]{3,2,1,0:T(8,128)S(1)} %get-tuple-element.272), channel_id=1, source_target_pairs={{0,4},{4,8},{8,12},{12,16},{16,20},{20,24},{24,28},{1,5},{5,9},{9,... | collective-permute-start | bytes 589832 | tf_op jit(solution)/shard_map/ppermute | solution.py:161
  49.7 3.4 %collective-permute-start.1 = (f32[3,2,32,256]{3,2,1,0:T(8,128)S(1)}, f32[3,2,32,256]{3,2,1,0:T(8,128)S(1)}, u32[]{:S(2)}, u32[]{:S(2)}) collective-permute-start(f32[3,2,32,256]{3,2,1,0:T(8,128)S(1)} %get-tuple-element.271), channel_id=1, source_target_pairs={{4,0},{8,4},{12,8},{16,12},{20,16},{24,20},{28,24},{5,1},{9,5},{13... | collective-permute-start | bytes 589832 | tf_op jit(solution)/shard_map/ppermute | solution.py:162
  53.1 1.5 fusion.84
  56.0 4.2 %collective-permute-done.1.xhi_ref = f32[3,2,32,256]{3,2,1,0:T(8,128)S(1)} collective-permute-done((f32[3,2,32,256]{3,2,1,0:T(8,128)S(1)}, f32[3,2,32,256]{3,2,1,0:T(8,128)S(1)}, u32[]{:S(2)}, u32[]{:S(2)}) %collective-permute-start.1) | collective-permute-done | bytes 196640 | tf_op jit(solution)/shard_map/ppermute | solution.py:162
  60.4 2.2 %collective-permute-start.3 = (f32[3,36,2,256]{3,2,1,0:T(2,128)S(1)}, f32[3,36,2,256]{3,2,1,0:T(2,128)S(1)}, u32[]{:S(2)}, u32[]{:S(2)}) collective-permute-start(f32[3,36,2,256]{3,2,1,0:T(2,128)S(1)} %pad_maximum_fusion.2), channel_id=1, source_target_pairs={{1,0},{2,1},{3,2},{5,4},{6,5},{7,6},{9,8},{10,9},{11,10},{13,12},{... | collective-permute-start | bytes 663560 | tf_op jit(solution)/shard_map/ppermute | solution.py:167
  62.7 2.1 %collective-permute-start.2 = (f32[3,36,2,256]{3,2,1,0:T(2,128)S(1)}, f32[3,36,2,256]{3,2,1,0:T(2,128)S(1)}, u32[]{:S(2)}, u32[]{:S(2)}) collective-permute-start(f32[3,36,2,256]{3,2,1,0:T(2,128)S(1)} %pad_maximum_fusion.1), channel_id=1, source_target_pairs={{0,1},{1,2},{2,3},{4,5},{5,6},{6,7},{8,9},{9,10},{10,11},{12,13},{... | collective-permute-start | bytes 663560 | tf_op jit(solution)/shard_map/ppermute | solution.py:166
  65.1 3.2 %fusion.10 = f32[3072,256]{1,0:T(8,128)} fusion(s32[256]{0:T(256)S(1)} %get-tuple-element.303, f32[256]{0:T(256)S(1)} %bitcast.116, s32[256]{0:T(256)S(1)} %get-tuple-element.302), kind=kOutput, calls=%fused_computation.29 | convolution fusion | flops 2416836608 | bytes 3148800 | tf_op jit(solution)/shard_map/dot_general | solution.py:373
  68.4 1.6 collective-permute-done.2.ylo_ref
  70.6 13.4 %shard_map.122.u_ref.prev_ref = f32[3,32,32,256]{3,2,1,0:T(8,128)} custom-call(f32[3,32,32,256]{3,2,1,0:T(8,128)} %prev_ref.3, f32[3,2,32,256]{3,2,1,0:T(8,128)} %copy-done, f32[3,2,32,256]{3,2,1,0:T(8,128)} %copy-done.1, f32[3,36,2,256]{3,2,1,0:T(2,128)} %copy-done.9, f32[3,36,2,256]{3,2,1,0:T(2,128)} %copy-done.8, f32[3,32,32,256]{3,2,1,0:T(8,128)} %prev_ref.2, ...), custom_call_target="tpu_custom_call" | custom-call | tf_op jit(solution)/shard_map/pallas_call | solution.py:132
  84.0 1.1 fusion.83
  85.0 2.2 %collective-permute-start.4 = (f32[3,2,32,256]{3,2,1,0:T(8,128)S(1)}, f32[3,2,32,256]{3,2,1,0:T(8,128)S(1)}, u32[]{:S(2)}, u32[]{:S(2)}) collective-permute-start(f32[3,2,32,256]{3,2,1,0:T(8,128)S(1)} %get-tuple-element.268), channel_id=1, source_target_pairs={{0,4},{4,8},{8,12},{12,16},{16,20},{20,24},{24,28},{1,5},{5,9},{9,... | collective-permute-start | bytes 589832 | tf_op jit(solution)/shard_map/ppermute | solution.py:161
  87.3 4.5 %collective-permute-start.5 = (f32[3,2,32,256]{3,2,1,0:T(8,128)S(1)}, f32[3,2,32,256]{3,2,1,0:T(8,128)S(1)}, u32[]{:S(2)}, u32[]{:S(2)}) collective-permute-start(f32[3,2,32,256]{3,2,1,0:T(8,128)S(1)} %get-tuple-element.267), channel_id=1, source_target_pairs={{4,0},{8,4},{12,8},{16,12},{20,16},{24,20},{28,24},{5,1},{9,5},{13... | collective-permute-start | bytes 589832 | tf_op jit(solution)/shard_map/ppermute | solution.py:162
  91.8 1.5 fusion.82
  93.6 3.1 %collective-permute-done.5.xhi_ref = f32[3,2,32,256]{3,2,1,0:T(8,128)S(1)} collective-permute-done((f32[3,2,32,256]{3,2,1,0:T(8,128)S(1)}, f32[3,2,32,256]{3,2,1,0:T(8,128)S(1)}, u32[]{:S(2)}, u32[]{:S(2)}) %collective-permute-start.5) | collective-permute-done | bytes 196640 | tf_op jit(solution)/shard_map/ppermute | solution.py:162
  96.9 3.8 %collective-permute-start.7 = (f32[3,36,2,256]{3,2,1,0:T(2,128)S(1)}, f32[3,36,2,256]{3,2,1,0:T(2,128)S(1)}, u32[]{:S(2)}, u32[]{:S(2)}) collective-permute-start(f32[3,36,2,256]{3,2,1,0:T(2,128)S(1)} %pad_maximum_fusion.4), channel_id=1, source_target_pairs={{1,0},{2,1},{3,2},{5,4},{6,5},{7,6},{9,8},{10,9},{11,10},{13,12},{... | collective-permute-start | bytes 663560 | tf_op jit(solution)/shard_map/ppermute | solution.py:167
  100.7 1.9 collective-permute-start.6
  102.7 3.2 %fusion.9 = f32[3072,256]{1,0:T(8,128)} fusion(s32[256]{0:T(256)S(1)} %get-tuple-element.303, f32[256]{0:T(256)S(1)} %bitcast.115, s32[256]{0:T(256)S(1)} %get-tuple-element.302), kind=kOutput, calls=%fused_computation.28 | convolution fusion | flops 2416836608 | bytes 3148800 | tf_op jit(solution)/shard_map/dot_general | solution.py:373
  105.9 2.1 %collective-permute-done.6.ylo_ref = f32[3,36,2,256]{3,2,1,0:T(2,128)S(1)} collective-permute-done((f32[3,36,2,256]{3,2,1,0:T(2,128)S(1)}, f32[3,36,2,256]{3,2,1,0:T(2,128)S(1)}, u32[]{:S(2)}, u32[]{:S(2)}) %collective-permute-start.6) | collective-permute-done | bytes 221216 | tf_op jit(solution)/shard_map/ppermute | solution.py:166
  108.7 13.3 %shard_map.123.u_ref.prev_ref = f32[3,32,32,256]{3,2,1,0:T(8,128)} custom-call(f32[3,32,32,256]{3,2,1,0:T(8,128)} %shard_map.122.u_ref.prev_ref, f32[3,2,32,256]{3,2,1,0:T(8,128)} %copy-done.4, f32[3,2,32,256]{3,2,1,0:T(8,128)} %copy-done.7, f32[3,36,2,256]{3,2,1,0:T(2,128)} %copy-done.15, f32[3,36,2,256]{3,2,1,0:T(2,128)} %copy-done.12, ...), custom_call_target="tpu_custom_call" | custom-call | tf_op jit(solution)/shard_map/pallas_call | solution.py:132
  122.0 1.1 fusion.81
  123.1 2.5 %collective-permute-start.8 = (f32[3,2,32,256]{3,2,1,0:T(8,128)S(1)}, f32[3,2,32,256]{3,2,1,0:T(8,128)S(1)}, u32[]{:S(2)}, u32[]{:S(2)}) collective-permute-start(f32[3,2,32,256]{3,2,1,0:T(8,128)S(1)} %get-tuple-element.264), channel_id=1, source_target_pairs={{0,4},{4,8},{8,12},{12,16},{16,20},{20,24},{24,28},{1,5},{5,9},{9,... | collective-permute-start | bytes 589832 | tf_op jit(solution)/shard_map/ppermute | solution.py:161
  125.6 4.2 %collective-permute-start.9 = (f32[3,2,32,256]{3,2,1,0:T(8,128)S(1)}, f32[3,2,32,256]{3,2,1,0:T(8,128)S(1)}, u32[]{:S(2)}, u32[]{:S(2)}) collective-permute-start(f32[3,2,32,256]{3,2,1,0:T(8,128)S(1)} %get-tuple-element.263), channel_id=1, source_target_pairs={{4,0},{8,4},{12,8},{16,12},{20,16},{24,20},{28,24},{5,1},{9,5},{13... | collective-permute-start | bytes 589832 | tf_op jit(solution)/shard_map/ppermute | solution.py:162
  129.8 1.5 fusion.80
  131.6 2.1 %collective-permute-done.9.xhi_ref = f32[3,2,32,256]{3,2,1,0:T(8,128)S(1)} collective-permute-done((f32[3,2,32,256]{3,2,1,0:T(8,128)S(1)}, f32[3,2,32,256]{3,2,1,0:T(8,128)S(1)}, u32[]{:S(2)}, u32[]{:S(2)}) %collective-permute-start.9) | collective-permute-done | bytes 196640 | tf_op jit(solution)/shard_map/ppermute | solution.py:162
  133.8 4.6 %collective-permute-start.11 = (f32[3,36,2,256]{3,2,1,0:T(2,128)S(1)}, f32[3,36,2,256]{3,2,1,0:T(2,128)S(1)}, u32[]{:S(2)}, u32[]{:S(2)}) collective-permute-start(f32[3,36,2,256]{3,2,1,0:T(2,128)S(1)} %pad_maximum_fusion.6), channel_id=1, source_target_pairs={{1,0},{2,1},{3,2},{5,4},{6,5},{7,6},{9,8},{10,9},{11,10},{13,12},{... | collective-permute-start | bytes 663560 | tf_op jit(solution)/shard_map/ppermute | solution.py:167
  138.5 1.9 collective-permute-start.10
  140.4 3.2 %fusion.8 = f32[3072,256]{1,0:T(8,128)} fusion(s32[256]{0:T(256)S(1)} %get-tuple-element.303, f32[256]{0:T(256)S(1)} %bitcast.114, s32[256]{0:T(256)S(1)} %get-tuple-element.302), kind=kOutput, calls=%fused_computation.27 | convolution fusion | flops 2416836608 | bytes 3148800 | tf_op jit(solution)/shard_map/dot_general | solution.py:373
  143.6 2.1 %collective-permute-done.10.ylo_ref = f32[3,36,2,256]{3,2,1,0:T(2,128)S(1)} collective-permute-done((f32[3,36,2,256]{3,2,1,0:T(2,128)S(1)}, f32[3,36,2,256]{3,2,1,0:T(2,128)S(1)}, u32[]{:S(2)}, u32[]{:S(2)}) %collective-permute-start.10) | collective-permute-done | bytes 221216 | tf_op jit(solution)/shard_map/ppermute | solution.py:166
  146.4 13.3 %shard_map.124.u_ref = f32[3,32,32,256]{3,2,1,0:T(8,128)} custom-call(f32[3,32,32,256]{3,2,1,0:T(8,128)} %shard_map.123.u_ref.prev_ref, f32[3,2,32,256]{3,2,1,0:T(8,128)} %copy-done.3, f32[3,2,32,256]{3,2,1,0:T(8,128)} %copy-done.6, f32[3,36,2,256]{3,2,1,0:T(2,128)} %copy-done.14, f32[3,36,2,256]{3,2,1,0:T(2,128)} %copy-done.11, ...), custom_call_target="tpu_custom_call" | custom-call | tf_op jit(solution)/shard_map/pallas_call | solution.py:132
  160.8 2.5 %collective-permute-start.12 = (f32[3,2,32,256]{3,2,1,0:T(8,128)S(1)}, f32[3,2,32,256]{3,2,1,0:T(8,128)S(1)}, u32[]{:S(2)}, u32[]{:S(2)}) collective-permute-start(f32[3,2,32,256]{3,2,1,0:T(8,128)S(1)} %get-tuple-element.260), channel_id=1, source_target_pairs={{0,4},{4,8},{8,12},{12,16},{16,20},{20,24},{24,28},{1,5},{5,9},{9,... | collective-permute-start | bytes 589832 | tf_op jit(solution)/shard_map/ppermute | solution.py:161
  163.3 4.3 %collective-permute-start.13 = (f32[3,2,32,256]{3,2,1,0:T(8,128)S(1)}, f32[3,2,32,256]{3,2,1,0:T(8,128)S(1)}, u32[]{:S(2)}, u32[]{:S(2)}) collective-permute-start(f32[3,2,32,256]{3,2,1,0:T(8,128)S(1)} %get-tuple-element.259), channel_id=1, source_target_pairs={{4,0},{8,4},{12,8},{16,12},{20,16},{24,20},{28,24},{5,1},{9,5},{13... | collective-permute-start | bytes 589832 | tf_op jit(solution)/shard_map/ppermute | solution.py:162
  167.6 1.5 fusion.78
  169.3 2.1 %collective-permute-done.13.xhi_ref = f32[3,2,32,256]{3,2,1,0:T(8,128)S(1)} collective-permute-done((f32[3,2,32,256]{3,2,1,0:T(8,128)S(1)}, f32[3,2,32,256]{3,2,1,0:T(8,128)S(1)}, u32[]{:S(2)}, u32[]{:S(2)}) %collective-permute-start.13) | collective-permute-done | bytes 196640 | tf_op jit(solution)/shard_map/ppermute | solution.py:162
  171.5 4.6 %collective-permute-start.15 = (f32[3,36,2,256]{3,2,1,0:T(2,128)S(1)}, f32[3,36,2,256]{3,2,1,0:T(2,128)S(1)}, u32[]{:S(2)}, u32[]{:S(2)}) collective-permute-start(f32[3,36,2,256]{3,2,1,0:T(2,128)S(1)} %pad_maximum_fusion.8), channel_id=1, source_target_pairs={{1,0},{2,1},{3,2},{5,4},{6,5},{7,6},{9,8},{10,9},{11,10},{13,12},{... | collective-permute-start | bytes 663560 | tf_op jit(solution)/shard_map/ppermute | solution.py:167
  176.2 1.9 collective-permute-start.14
  178.1 3.2 %fusion.7 = f32[3072,256]{1,0:T(8,128)} fusion(s32[256]{0:T(256)S(1)} %get-tuple-element.303, f32[256]{0:T(256)S(1)} %bitcast.113, s32[256]{0:T(256)S(1)} %get-tuple-element.302), kind=kOutput, calls=%fused_computation.26 | convolution fusion | flops 2416836608 | bytes 3148800 | tf_op jit(solution)/shard_map/dot_general | solution.py:373
  181.4 2.1 %collective-permute-done.14.ylo_ref = f32[3,36,2,256]{3,2,1,0:T(2,128)S(1)} collective-permute-done((f32[3,36,2,256]{3,2,1,0:T(2,128)S(1)}, f32[3,36,2,256]{3,2,1,0:T(2,128)S(1)}, u32[]{:S(2)}, u32[]{:S(2)}) %collective-permute-start.14) | collective-permute-done | bytes 221216 | tf_op jit(solution)/shard_map/ppermute | solution.py:166
  184.2 13.3 %shard_map.125 = f32[3,32,32,256]{3,2,1,0:T(8,128)} custom-call(f32[3,32,32,256]{3,2,1,0:T(8,128)} %shard_map.124.u_ref, f32[3,2,32,256]{3,2,1,0:T(8,128)} %copy-done.2, f32[3,2,32,256]{3,2,1,0:T(8,128)} %copy-done.5, f32[3,36,2,256]{3,2,1,0:T(2,128)} %copy-done.13, f32[3,36,2,256]{3,2,1,0:T(2,128)} %copy-done.10, ...), custom_call_target="tpu_custom_call" | custom-call | tf_op jit(solution)/shard_map/pallas_call | solution.py:132
  (138 shorter events, 15.0 us)
Async XLA Ops:
  16.0 5.3 %copy-start.16 = (s32[8192]{0:T(1024)S(1)}, s32[8192]{0:T(1024)}, u32[]{:S(2)}) copy-start(s32[8192]{0:T(1024)} %param.19) | copy-start | bytes 98308
  16.0 5.3 %copy-start.17 = (s32[8192]{0:T(1024)S(1)}, s32[8192]{0:T(1024)}, u32[]{:S(2)}) copy-start(s32[8192]{0:T(1024)} %param.20) | copy-start | bytes 98308
  24.8 30.6 %copy-start.18 = (s32[256]{0:T(256)S(1)}, s32[256]{0:T(256)}, u32[]{:S(2)}) copy-start(s32[256]{0:T(256)} %param.21) | copy-start | bytes 3076
  39.3 25.6 %all-to-all-start = ((bf16[2,4,32,256]{3,1,0,2:T(4,128)(2,1)}), bf16[2,4,32,256]{3,1,0,2:T(4,128)(2,1)S(1)}, u32[]{:S(2)}, u32[]{:S(2)}) async-start(bf16[2,4,32,256]{3,1,0,2:T(4,128)(2,1)} %copy.27), calls=%async_computation | async-start | bytes 262144 | tf_op jit(solution)/shard_map/all_to_all | solution.py:350
  46.3 9.7 %collective-permute-start = (f32[3,2,32,256]{3,2,1,0:T(8,128)S(1)}, f32[3,2,32,256]{3,2,1,0:T(8,128)S(1)}, u32[]{:S(2)}, u32[]{:S(2)}) collective-permute-start(f32[3,2,32,256]{3,2,1,0:T(8,128)S(1)} %get-tuple-element.272), channel_id=1, source_target_pairs={{0,4},{4,8},{8,12},{12,16},{16,20},{20,24},{24,28},{1,5},{5,9},{9,... | collective-permute-start | bytes 589832 | tf_op jit(solution)/shard_map/ppermute | solution.py:161
  49.7 10.5 %collective-permute-start.1 = (f32[3,2,32,256]{3,2,1,0:T(8,128)S(1)}, f32[3,2,32,256]{3,2,1,0:T(8,128)S(1)}, u32[]{:S(2)}, u32[]{:S(2)}) collective-permute-start(f32[3,2,32,256]{3,2,1,0:T(8,128)S(1)} %get-tuple-element.271), channel_id=1, source_target_pairs={{4,0},{8,4},{12,8},{16,12},{20,16},{24,20},{28,24},{5,1},{9,5},{13... | collective-permute-start | bytes 589832 | tf_op jit(solution)/shard_map/ppermute | solution.py:162
  56.0 13.9 %copy-start = (f32[3,2,32,256]{3,2,1,0:T(8,128)}, f32[3,2,32,256]{3,2,1,0:T(8,128)S(1)}, u32[]{:S(2)}) copy-start(f32[3,2,32,256]{3,2,1,0:T(8,128)S(1)} %collective-permute-done.xlo_ref) | copy-start | bytes 589828
  60.2 9.7 %copy-start.1 = (f32[3,2,32,256]{3,2,1,0:T(8,128)}, f32[3,2,32,256]{3,2,1,0:T(8,128)S(1)}, u32[]{:S(2)}) copy-start(f32[3,2,32,256]{3,2,1,0:T(8,128)S(1)} %collective-permute-done.1.xhi_ref) | copy-start | bytes 589828
  60.4 8.0 %collective-permute-start.3 = (f32[3,36,2,256]{3,2,1,0:T(2,128)S(1)}, f32[3,36,2,256]{3,2,1,0:T(2,128)S(1)}, u32[]{:S(2)}, u32[]{:S(2)}) collective-permute-start(f32[3,36,2,256]{3,2,1,0:T(2,128)S(1)} %pad_maximum_fusion.2), channel_id=1, source_target_pairs={{1,0},{2,1},{3,2},{5,4},{6,5},{7,6},{9,8},{10,9},{11,10},{13,12},{... | collective-permute-start | bytes 663560 | tf_op jit(solution)/shard_map/ppermute | solution.py:167
  62.7 7.3 %collective-permute-start.2 = (f32[3,36,2,256]{3,2,1,0:T(2,128)S(1)}, f32[3,36,2,256]{3,2,1,0:T(2,128)S(1)}, u32[]{:S(2)}, u32[]{:S(2)}) collective-permute-start(f32[3,36,2,256]{3,2,1,0:T(2,128)S(1)} %pad_maximum_fusion.1), channel_id=1, source_target_pairs={{0,1},{1,2},{2,3},{4,5},{5,6},{6,7},{8,9},{9,10},{10,11},{12,13},{... | collective-permute-start | bytes 663560 | tf_op jit(solution)/shard_map/ppermute | solution.py:166
  68.4 1.6 copy-start.8
  69.9 0.7 copy-start.9
  85.0 8.6 %collective-permute-start.4 = (f32[3,2,32,256]{3,2,1,0:T(8,128)S(1)}, f32[3,2,32,256]{3,2,1,0:T(8,128)S(1)}, u32[]{:S(2)}, u32[]{:S(2)}) collective-permute-start(f32[3,2,32,256]{3,2,1,0:T(8,128)S(1)} %get-tuple-element.268), channel_id=1, source_target_pairs={{0,4},{4,8},{8,12},{12,16},{16,20},{20,24},{24,28},{1,5},{5,9},{9,... | collective-permute-start | bytes 589832 | tf_op jit(solution)/shard_map/ppermute | solution.py:161
  87.3 9.4 %collective-permute-start.5 = (f32[3,2,32,256]{3,2,1,0:T(8,128)S(1)}, f32[3,2,32,256]{3,2,1,0:T(8,128)S(1)}, u32[]{:S(2)}, u32[]{:S(2)}) collective-permute-start(f32[3,2,32,256]{3,2,1,0:T(8,128)S(1)} %get-tuple-element.267), channel_id=1, source_target_pairs={{4,0},{8,4},{12,8},{16,12},{20,16},{24,20},{28,24},{5,1},{9,5},{13... | collective-permute-start | bytes 589832 | tf_op jit(solution)/shard_map/ppermute | solution.py:162
  93.6 14.4 %copy-start.4 = (f32[3,2,32,256]{3,2,1,0:T(8,128)}, f32[3,2,32,256]{3,2,1,0:T(8,128)S(1)}, u32[]{:S(2)}) copy-start(f32[3,2,32,256]{3,2,1,0:T(8,128)S(1)} %collective-permute-done.4.xlo_ref) | copy-start | bytes 589828
  96.7 11.3 %copy-start.7 = (f32[3,2,32,256]{3,2,1,0:T(8,128)}, f32[3,2,32,256]{3,2,1,0:T(8,128)S(1)}, u32[]{:S(2)}) copy-start(f32[3,2,32,256]{3,2,1,0:T(8,128)S(1)} %collective-permute-done.5.xhi_ref) | copy-start | bytes 589828
  96.9 9.0 %collective-permute-start.7 = (f32[3,36,2,256]{3,2,1,0:T(2,128)S(1)}, f32[3,36,2,256]{3,2,1,0:T(2,128)S(1)}, u32[]{:S(2)}, u32[]{:S(2)}) collective-permute-start(f32[3,36,2,256]{3,2,1,0:T(2,128)S(1)} %pad_maximum_fusion.4), channel_id=1, source_target_pairs={{1,0},{2,1},{3,2},{5,4},{6,5},{7,6},{9,8},{10,9},{11,10},{13,12},{... | collective-permute-start | bytes 663560 | tf_op jit(solution)/shard_map/ppermute | solution.py:167
  100.7 7.3 %collective-permute-start.6 = (f32[3,36,2,256]{3,2,1,0:T(2,128)S(1)}, f32[3,36,2,256]{3,2,1,0:T(2,128)S(1)}, u32[]{:S(2)}, u32[]{:S(2)}) collective-permute-start(f32[3,36,2,256]{3,2,1,0:T(2,128)S(1)} %pad_maximum_fusion.3), channel_id=1, source_target_pairs={{0,1},{1,2},{2,3},{4,5},{5,6},{6,7},{8,9},{9,10},{10,11},{12,13},{... | collective-permute-start | bytes 663560 | tf_op jit(solution)/shard_map/ppermute | solution.py:166
  105.9 2.1 %copy-start.12 = (f32[3,36,2,256]{3,2,1,0:T(2,128)}, f32[3,36,2,256]{3,2,1,0:T(2,128)S(1)}, u32[]{:S(2)}) copy-start(f32[3,36,2,256]{3,2,1,0:T(2,128)S(1)} %collective-permute-done.7.yhi_ref) | copy-start | bytes 663556
  108.0 0.7 copy-start.15
  123.1 8.5 %collective-permute-start.8 = (f32[3,2,32,256]{3,2,1,0:T(8,128)S(1)}, f32[3,2,32,256]{3,2,1,0:T(8,128)S(1)}, u32[]{:S(2)}, u32[]{:S(2)}) collective-permute-start(f32[3,2,32,256]{3,2,1,0:T(8,128)S(1)} %get-tuple-element.264), channel_id=1, source_target_pairs={{0,4},{4,8},{8,12},{12,16},{16,20},{20,24},{24,28},{1,5},{5,9},{9,... | collective-permute-start | bytes 589832 | tf_op jit(solution)/shard_map/ppermute | solution.py:161
  125.6 8.0 %collective-permute-start.9 = (f32[3,2,32,256]{3,2,1,0:T(8,128)S(1)}, f32[3,2,32,256]{3,2,1,0:T(8,128)S(1)}, u32[]{:S(2)}, u32[]{:S(2)}) collective-permute-start(f32[3,2,32,256]{3,2,1,0:T(8,128)S(1)} %get-tuple-element.263), channel_id=1, source_target_pairs={{4,0},{8,4},{12,8},{16,12},{20,16},{24,20},{28,24},{5,1},{9,5},{13... | collective-permute-start | bytes 589832 | tf_op jit(solution)/shard_map/ppermute | solution.py:162
  131.6 14.2 %copy-start.3 = (f32[3,2,32,256]{3,2,1,0:T(8,128)}, f32[3,2,32,256]{3,2,1,0:T(8,128)S(1)}, u32[]{:S(2)}) copy-start(f32[3,2,32,256]{3,2,1,0:T(8,128)S(1)} %collective-permute-done.8.xlo_ref) | copy-start | bytes 589828
  133.7 12.1 %copy-start.6 = (f32[3,2,32,256]{3,2,1,0:T(8,128)}, f32[3,2,32,256]{3,2,1,0:T(8,128)S(1)}, u32[]{:S(2)}) copy-start(f32[3,2,32,256]{3,2,1,0:T(8,128)S(1)} %collective-permute-done.9.xhi_ref) | copy-start | bytes 589828
  133.8 9.8 %collective-permute-start.11 = (f32[3,36,2,256]{3,2,1,0:T(2,128)S(1)}, f32[3,36,2,256]{3,2,1,0:T(2,128)S(1)}, u32[]{:S(2)}, u32[]{:S(2)}) collective-permute-start(f32[3,36,2,256]{3,2,1,0:T(2,128)S(1)} %pad_maximum_fusion.6), channel_id=1, source_target_pairs={{1,0},{2,1},{3,2},{5,4},{6,5},{7,6},{9,8},{10,9},{11,10},{13,12},{... | collective-permute-start | bytes 663560 | tf_op jit(solution)/shard_map/ppermute | solution.py:167
  138.5 7.3 %collective-permute-start.10 = (f32[3,36,2,256]{3,2,1,0:T(2,128)S(1)}, f32[3,36,2,256]{3,2,1,0:T(2,128)S(1)}, u32[]{:S(2)}, u32[]{:S(2)}) collective-permute-start(f32[3,36,2,256]{3,2,1,0:T(2,128)S(1)} %pad_maximum_fusion.5), channel_id=1, source_target_pairs={{0,1},{1,2},{2,3},{4,5},{5,6},{6,7},{8,9},{9,10},{10,11},{12,13},{... | collective-permute-start | bytes 663560 | tf_op jit(solution)/shard_map/ppermute | solution.py:166
  143.6 2.1 %copy-start.11 = (f32[3,36,2,256]{3,2,1,0:T(2,128)}, f32[3,36,2,256]{3,2,1,0:T(2,128)S(1)}, u32[]{:S(2)}) copy-start(f32[3,36,2,256]{3,2,1,0:T(2,128)S(1)} %collective-permute-done.11.yhi_ref) | copy-start | bytes 663556
  145.7 0.7 copy-start.14
  160.8 8.5 %collective-permute-start.12 = (f32[3,2,32,256]{3,2,1,0:T(8,128)S(1)}, f32[3,2,32,256]{3,2,1,0:T(8,128)S(1)}, u32[]{:S(2)}, u32[]{:S(2)}) collective-permute-start(f32[3,2,32,256]{3,2,1,0:T(8,128)S(1)} %get-tuple-element.260), channel_id=1, source_target_pairs={{0,4},{4,8},{8,12},{12,16},{16,20},{20,24},{24,28},{1,5},{5,9},{9,... | collective-permute-start | bytes 589832 | tf_op jit(solution)/shard_map/ppermute | solution.py:161
  163.3 8.1 %collective-permute-start.13 = (f32[3,2,32,256]{3,2,1,0:T(8,128)S(1)}, f32[3,2,32,256]{3,2,1,0:T(8,128)S(1)}, u32[]{:S(2)}, u32[]{:S(2)}) collective-permute-start(f32[3,2,32,256]{3,2,1,0:T(8,128)S(1)} %get-tuple-element.259), channel_id=1, source_target_pairs={{4,0},{8,4},{12,8},{16,12},{20,16},{24,20},{28,24},{5,1},{9,5},{13... | collective-permute-start | bytes 589832 | tf_op jit(solution)/shard_map/ppermute | solution.py:162
  169.3 14.2 %copy-start.2 = (f32[3,2,32,256]{3,2,1,0:T(8,128)}, f32[3,2,32,256]{3,2,1,0:T(8,128)S(1)}, u32[]{:S(2)}) copy-start(f32[3,2,32,256]{3,2,1,0:T(8,128)S(1)} %collective-permute-done.12.xlo_ref) | copy-start | bytes 589828
  171.4 12.1 %copy-start.5 = (f32[3,2,32,256]{3,2,1,0:T(8,128)}, f32[3,2,32,256]{3,2,1,0:T(8,128)S(1)}, u32[]{:S(2)}) copy-start(f32[3,2,32,256]{3,2,1,0:T(8,128)S(1)} %collective-permute-done.13.xhi_ref) | copy-start | bytes 589828
  171.5 9.8 %collective-permute-start.15 = (f32[3,36,2,256]{3,2,1,0:T(2,128)S(1)}, f32[3,36,2,256]{3,2,1,0:T(2,128)S(1)}, u32[]{:S(2)}, u32[]{:S(2)}) collective-permute-start(f32[3,36,2,256]{3,2,1,0:T(2,128)S(1)} %pad_maximum_fusion.8), channel_id=1, source_target_pairs={{1,0},{2,1},{3,2},{5,4},{6,5},{7,6},{9,8},{10,9},{11,10},{13,12},{... | collective-permute-start | bytes 663560 | tf_op jit(solution)/shard_map/ppermute | solution.py:167
  176.2 7.3 %collective-permute-start.14 = (f32[3,36,2,256]{3,2,1,0:T(2,128)S(1)}, f32[3,36,2,256]{3,2,1,0:T(2,128)S(1)}, u32[]{:S(2)}, u32[]{:S(2)}) collective-permute-start(f32[3,36,2,256]{3,2,1,0:T(2,128)S(1)} %pad_maximum_fusion.7), channel_id=1, source_target_pairs={{0,1},{1,2},{2,3},{4,5},{5,6},{6,7},{8,9},{9,10},{10,11},{12,13},{... | collective-permute-start | bytes 663560 | tf_op jit(solution)/shard_map/ppermute | solution.py:166
  181.4 2.1 %copy-start.10 = (f32[3,36,2,256]{3,2,1,0:T(2,128)}, f32[3,36,2,256]{3,2,1,0:T(2,128)S(1)}, u32[]{:S(2)}) copy-start(f32[3,36,2,256]{3,2,1,0:T(2,128)S(1)} %collective-permute-done.15.yhi_ref) | copy-start | bytes 663556
  183.5 0.7 copy-start.13

commit v11 on v6

--- a/solution.py
+++ b/solution.py
@@ -69,11 +69,13 @@
 
             lam = mod_ref[0, p, pl.ds(8 * g, 8), :]
             mu = mod_ref[1, p, pl.ds(8 * g, 8), :]
-            stiff = lam + 2.0 * mu
-            coup = lam + mu
+            shear = mu * (1.0 / 12.0)
+            stiff = lam * (1.0 / 12.0) + 2.0 * shear
+            coup = (lam + mu) * 0.25
+            centre_weight = -30.0 * (stiff + 2.0 * shear)
             centers = [load(c, 0, 0) for c in range(3)]
 
-            def curv(c, axis):
+            def sums(c, axis):
                 center = centers[c]
                 near = None
                 far = None
@@ -88,7 +90,7 @@
                         near = t if near is None else near + t
                     else:
                         far = t if far is None else far + t
-                return 16.0 * near - far - 30.0 * center
+                return near, far
 
             def mixed(p_c, a, b):
                 if 2 in (a, b):
@@ -116,9 +118,14 @@
 
             for c in range(3):
                 others = [e for e in range(3) if e != c]
-                second = stiff * curv(c, c) + mu * (curv(c, others[0]) + curv(c, others[1]))
+                near_c, far_c = sums(c, c)
+                near_a, far_a = sums(c, others[0])
+                near_b, far_b = sums(c, others[1])
+                near = stiff * near_c + shear * (near_a + near_b)
+                far = stiff * far_c + shear * (far_a + far_b)
+                second = 16.0 * near - far + centre_weight * centers[c]
                 cross = mixed(others[0], c, others[0]) + mixed(others[1], c, others[1])
-                upd = second * (1.0 / 12.0) + coup * (cross * 0.25)
+                upd = second + coup * cross
                 prev = prev_ref[c, p, pl.ds(8 * g, 8), :]
                 src = src_ref[c, p, pl.ds(8 * g, 8), :]
                 out_ref[c, p, pl.ds(8 * g, 8), :] = (2.0 * centers[c] - prev + upd) + src

time: 197 us -> 196 us (level)
  no operation moved by 1% of the time
where the time goes in v11:
time: 196 us; the launch traced here: 195 us
  starting transfers between devices  55.9 us (29%)
  Pallas kernels  51.3 us (26%)
  matrix products  29.6 us (15%)
  other arithmetic  20.6 us (11%)
  waiting for transfers between devices  20.6 us (11%)
  local copies, waits for them, and re-layouts  15 us (8%)
    pallas_call x4, Pallas kernels, elastic_step(): pl.pallas_call(kernel, grid=(nx // bx,), in_specs=[pl.BlockSpec(u.shape,...  51.3 us
    ppermute x4, starting transfers between devices, halos(): xhi = lax.ppermute(block[:, :width], 'gx', backward_x)  16.3 us
    ppermute x4, starting transfers between devices, halos(): yhi = lax.ppermute(rows(slice(0, width)), 'gy', backward_y)  15.1 us
    dot_general x2, matrix products, select_block(): jnp.dot(table_rounded, offset_hot, preferred_element_type=jnp.float32)  13.1 us
    dot_general x4, matrix products, shards(): source = jnp.dot(column_hot, spread, precision=lax.Precision.HIGHEST)  12.9 us
    ppermute x4, waiting for transfers between devices, halos(): xhi = lax.ppermute(block[:, :width], 'gx', backward_x)  11.5 us
    ppermute x4, starting transfers between devices, halos(): xlo = lax.ppermute(block[:, nx - width:], 'gx', forward_x)  10.7 us
    ppermute x4, starting transfers between devices, halos(): ylo = lax.ppermute(rows(slice(ny - width, ny)), 'gy', forward_y)  7.91 us
  transfers between devices with their start and end apart: 17, of which 12 were waited for; matrix products, arithmetic and copies ran while one was open for 11% of the time, Pallas kernels for 0%

profile of v11, /device:TPU:12, one launch (start us, length us, event | category | flops | bytes accessed | tf_op | source)
XLA Modules:
  0.0 195.4 jit_solution(8587992093392193979)
XLA Ops:
  2.9 4.9 %sine_multiply_fusion.1 = (f32[32,4,1024]{2,1,0:T(4,128)S(1)}, f32[32,4,1024]{2,1,0:T(4,128)S(1)}, f32[32,4,1024]{2,1,0:T(4,128)S(1)}) fusion(f32[32]{0:T(128)S(1)} %get-tuple-element.307, f32[32,4]{1,0:T(8,128)S(1)} %copy.24, f32[1024]{0:T(1024)S(1)} %multiply_multiply_fusion, f32[1,4,1024]{2,1,0:T(4,128)S(1)} %slice.157, f32[31,4,1024]{2,1,0:T(4,128)S(1)} %slice.156, ...), kind=kLoop, calls=%fused_computation.41 | loop fusion | flops 1441792 | bytes 2102016 | tf_op jit(solution)/shard_map/mul | solution.py:195
  8.1 2.2 %while.32 = (s32[]{:T(128)}, f32[4,1024]{1,0:T(4,128)S(1)}, f32[4,1024]{1,0:T(4,128)S(1)}, f32[32,4,1024]{2,1,0:T(4,128)S(1)}, f32[32,4,1024]{2,1,0:T(4,128)S(1)...) while((s32[]{:T(128)}, f32[4,1024]{1,0:T(4,128)S(1)}, ...), condition=%wide.region_6.7_spmd.clone, body=%wide.region_5.6_spmd.clone.sunk | while | flops 94212 | bytes 147591 | solution.py:211
  11.2 4.3 %fusion.43 = (bf16[1,32,4,1024]{3,2,1,0:T(4,128)(2,1)S(1)}, bf16[1,32,4,1024]{3,2,1,0:T(4,128)(2,1)S(1)}) fusion(f32[32,4,1024]{2,1,0:T(4,128)S(1)} %get-tuple-element.191, f32[32,4,1024]{2,1,0:T(4,128)S(1)} %get-tuple-element.190, f32[32,4,1024]{2,1,0:T(4,128)S(1)} %negate_exponential_fusion, f32[32,4,1024]{2,1,0:T(4,128)S(1)} %fusion.23), kind=kLoop, calls=%fused_computation.74 | loop fusion | flops 1835008 | bytes 2621440 | tf_op jit(solution)/shard_map/stack | solution.py:224
  17.7 3.6 %subtract_convert_fusion = bf16[1024,32,64]{0,2,1:T(8,128)(2,1)} fusion(f32[1024,64]{0,1:T(8,128)S(1)} %get-tuple-element.301, f32[1024,32]{0,1:T(8,128)S(1)} %get-tuple-element.295, f32[1024,64]{0,1:T(8,128)S(1)} %get-tuple-element.300, f32[1024,32]{0,1:T(8,128)S(1)} %get-tuple-element.294), kind=kLoop, calls=%fused_computation.24 | loop fusion | flops 8388608 | bytes 4980736 | tf_op jit(solution)/shard_map/convert_element_type | solution.py:239
  21.4 3.5 %convolution_convert_fusion = bf16[256,2048]{1,0:T(8,128)(2,1)S(1)} fusion(bf16[256,1024]{1,0:T(8,128)(2,1)S(1)} %bitcast.109, bf16[1024,2048]{0,1:T(8,128)(2,1)} %bitcast.107), kind=kOutput, calls=%fused_computation.30 | convolution fusion | flops 1074266112 | bytes 5767168 | tf_op jit(solution)/shard_map/dot_general | solution.py:327
  24.9 13.4 %while.31 = (s32[]{:T(128)}, bf16[2,2,4,4096]{3,2,1,0:T(4,128)(2,1)S(1)}, s32[2,4096]{1,0:T(2,128)S(1)}, bf16[256,2048]{1,0:T(8,128)(2,1)S(1)}, s32[2,4096]{1,0:T(2,128)S(1)}, /*index=5*/s32[]{:T(128)}) while((s32[]{:T(128)}, bf16[2,2,4,4096]{3,2,1,0:T(4,128)(2,1)S(1)}, s32[2,4096]{1,0:T(2,128)S(1)}, bf16[256,2048]{1,0:T(8,128)(2,1)S(1)}, ...), condition=%wide.region_9.10_spmd, body=%wide.region_7.9_spmd.sunk | while | flops 4305682432 | bytes 2392141 | solution.py:350
  25.0 6.5 %multiply_reduce_fusion.2 = bf16[2,4,4096]{2,1,0:T(4,128)(2,1)S(1)} fusion(f32[32,4096]{1,0:T(8,128)S(1)} %fusion.102, bf16[256,2048]{1,0:T(8,128)(2,1)S(1)} %get-tuple-element.448, s32[4096]{0:T(1024)S(1)} %bitcast.111), kind=kOutput, calls=%fused_computation.3.clone.1 | convolution fusion | flops 4305420288 | bytes 1654784 | tf_op jit(solution)/shard_map/while/body/eval_jaxpr/dot_general | solution.py:342
  31.7 6.5 %multiply_reduce_fusion.2 = bf16[2,4,4096]{2,1,0:T(4,128)(2,1)S(1)} fusion(f32[32,4096]{1,0:T(8,128)S(1)} %fusion.102, bf16[256,2048]{1,0:T(8,128)(2,1)S(1)} %get-tuple-element.448, s32[4096]{0:T(1024)S(1)} %bitcast.111), kind=kOutput, calls=%fused_computation.3.clone.1 | convolution fusion | flops 4305420288 | bytes 1654784 | tf_op jit(solution)/shard_map/while/body/eval_jaxpr/dot_general | solution.py:342
  39.3 6.0 %all-to-all-start = ((bf16[2,4,32,256]{3,1,0,2:T(4,128)(2,1)}), bf16[2,4,32,256]{3,1,0,2:T(4,128)(2,1)S(1)}, u32[]{:S(2)}, u32[]{:S(2)}) async-start(bf16[2,4,32,256]{3,1,0,2:T(4,128)(2,1)} %copy.27), calls=%async_computation | async-start | bytes 262144 | tf_op jit(solution)/shard_map/all_to_all | solution.py:357
  45.3 1.1 fusion.85
  46.3 3.4 %collective-permute-start = (f32[3,2,32,256]{3,2,1,0:T(8,128)S(1)}, f32[3,2,32,256]{3,2,1,0:T(8,128)S(1)}, u32[]{:S(2)}, u32[]{:S(2)}) collective-permute-start(f32[3,2,32,256]{3,2,1,0:T(8,128)S(1)} %get-tuple-element.272), channel_id=1, source_target_pairs={{0,4},{4,8},{8,12},{12,16},{16,20},{20,24},{24,28},{1,5},{5,9},{9,... | collective-permute-start | bytes 589832 | tf_op jit(solution)/shard_map/ppermute | solution.py:168
  49.7 3.4 %collective-permute-start.1 = (f32[3,2,32,256]{3,2,1,0:T(8,128)S(1)}, f32[3,2,32,256]{3,2,1,0:T(8,128)S(1)}, u32[]{:S(2)}, u32[]{:S(2)}) collective-permute-start(f32[3,2,32,256]{3,2,1,0:T(8,128)S(1)} %get-tuple-element.271), channel_id=1, source_target_pairs={{4,0},{8,4},{12,8},{16,12},{20,16},{24,20},{28,24},{5,1},{9,5},{13... | collective-permute-start | bytes 589832 | tf_op jit(solution)/shard_map/ppermute | solution.py:169
  53.1 1.5 fusion.84
  56.0 4.2 %collective-permute-done.1.xhi_ref = f32[3,2,32,256]{3,2,1,0:T(8,128)S(1)} collective-permute-done((f32[3,2,32,256]{3,2,1,0:T(8,128)S(1)}, f32[3,2,32,256]{3,2,1,0:T(8,128)S(1)}, u32[]{:S(2)}, u32[]{:S(2)}) %collective-permute-start.1) | collective-permute-done | bytes 196640 | tf_op jit(solution)/shard_map/ppermute | solution.py:169
  60.4 2.2 %collective-permute-start.3 = (f32[3,36,2,256]{3,2,1,0:T(2,128)S(1)}, f32[3,36,2,256]{3,2,1,0:T(2,128)S(1)}, u32[]{:S(2)}, u32[]{:S(2)}) collective-permute-start(f32[3,36,2,256]{3,2,1,0:T(2,128)S(1)} %pad_maximum_fusion.2), channel_id=1, source_target_pairs={{1,0},{2,1},{3,2},{5,4},{6,5},{7,6},{9,8},{10,9},{11,10},{13,12},{... | collective-permute-start | bytes 663560 | tf_op jit(solution)/shard_map/ppermute | solution.py:174
  62.7 2.1 %collective-permute-start.2 = (f32[3,36,2,256]{3,2,1,0:T(2,128)S(1)}, f32[3,36,2,256]{3,2,1,0:T(2,128)S(1)}, u32[]{:S(2)}, u32[]{:S(2)}) collective-permute-start(f32[3,36,2,256]{3,2,1,0:T(2,128)S(1)} %pad_maximum_fusion.1), channel_id=1, source_target_pairs={{0,1},{1,2},{2,3},{4,5},{5,6},{6,7},{8,9},{9,10},{10,11},{12,13},{... | collective-permute-start | bytes 663560 | tf_op jit(solution)/shard_map/ppermute | solution.py:173
  65.1 3.2 %fusion.10 = f32[3072,256]{1,0:T(8,128)} fusion(s32[256]{0:T(256)S(1)} %get-tuple-element.303, f32[256]{0:T(256)S(1)} %bitcast.116, s32[256]{0:T(256)S(1)} %get-tuple-element.302), kind=kOutput, calls=%fused_computation.29 | convolution fusion | flops 2416836608 | bytes 3148800 | tf_op jit(solution)/shard_map/dot_general | solution.py:380
  68.4 1.6 collective-permute-done.2.ylo_ref
  70.6 12.9 %shard_map.122.u_ref.prev_ref = f32[3,32,32,256]{3,2,1,0:T(8,128)} custom-call(f32[3,32,32,256]{3,2,1,0:T(8,128)} %prev_ref.3, f32[3,2,32,256]{3,2,1,0:T(8,128)} %copy-done, f32[3,2,32,256]{3,2,1,0:T(8,128)} %copy-done.1, f32[3,36,2,256]{3,2,1,0:T(2,128)} %copy-done.9, f32[3,36,2,256]{3,2,1,0:T(2,128)} %copy-done.8, f32[3,32,32,256]{3,2,1,0:T(8,128)} %prev_ref.2, ...), custom_call_target="tpu_custom_call" | custom-call | tf_op jit(solution)/shard_map/pallas_call | solution.py:142
  83.5 1.0 fusion.83
  84.5 2.2 %collective-permute-start.4 = (f32[3,2,32,256]{3,2,1,0:T(8,128)S(1)}, f32[3,2,32,256]{3,2,1,0:T(8,128)S(1)}, u32[]{:S(2)}, u32[]{:S(2)}) collective-permute-start(f32[3,2,32,256]{3,2,1,0:T(8,128)S(1)} %get-tuple-element.268), channel_id=1, source_target_pairs={{0,4},{4,8},{8,12},{12,16},{16,20},{20,24},{24,28},{1,5},{5,9},{9,... | collective-permute-start | bytes 589832 | tf_op jit(solution)/shard_map/ppermute | solution.py:168
  86.8 4.5 %collective-permute-start.5 = (f32[3,2,32,256]{3,2,1,0:T(8,128)S(1)}, f32[3,2,32,256]{3,2,1,0:T(8,128)S(1)}, u32[]{:S(2)}, u32[]{:S(2)}) collective-permute-start(f32[3,2,32,256]{3,2,1,0:T(8,128)S(1)} %get-tuple-element.267), channel_id=1, source_target_pairs={{4,0},{8,4},{12,8},{16,12},{20,16},{24,20},{28,24},{5,1},{9,5},{13... | collective-permute-start | bytes 589832 | tf_op jit(solution)/shard_map/ppermute | solution.py:169
  91.3 1.5 fusion.82
  93.1 3.1 %collective-permute-done.5.xhi_ref = f32[3,2,32,256]{3,2,1,0:T(8,128)S(1)} collective-permute-done((f32[3,2,32,256]{3,2,1,0:T(8,128)S(1)}, f32[3,2,32,256]{3,2,1,0:T(8,128)S(1)}, u32[]{:S(2)}, u32[]{:S(2)}) %collective-permute-start.5) | collective-permute-done | bytes 196640 | tf_op jit(solution)/shard_map/ppermute | solution.py:169
  96.3 3.8 %collective-permute-start.7 = (f32[3,36,2,256]{3,2,1,0:T(2,128)S(1)}, f32[3,36,2,256]{3,2,1,0:T(2,128)S(1)}, u32[]{:S(2)}, u32[]{:S(2)}) collective-permute-start(f32[3,36,2,256]{3,2,1,0:T(2,128)S(1)} %pad_maximum_fusion.4), channel_id=1, source_target_pairs={{1,0},{2,1},{3,2},{5,4},{6,5},{7,6},{9,8},{10,9},{11,10},{13,12},{... | collective-permute-start | bytes 663560 | tf_op jit(solution)/shard_map/ppermute | solution.py:174
  100.2 1.9 collective-permute-start.6
  102.1 3.2 %fusion.9 = f32[3072,256]{1,0:T(8,128)} fusion(s32[256]{0:T(256)S(1)} %get-tuple-element.303, f32[256]{0:T(256)S(1)} %bitcast.115, s32[256]{0:T(256)S(1)} %get-tuple-element.302), kind=kOutput, calls=%fused_computation.28 | convolution fusion | flops 2416836608 | bytes 3148800 | tf_op jit(solution)/shard_map/dot_general | solution.py:380
  105.4 2.1 %collective-permute-done.6.ylo_ref = f32[3,36,2,256]{3,2,1,0:T(2,128)S(1)} collective-permute-done((f32[3,36,2,256]{3,2,1,0:T(2,128)S(1)}, f32[3,36,2,256]{3,2,1,0:T(2,128)S(1)}, u32[]{:S(2)}, u32[]{:S(2)}) %collective-permute-start.6) | collective-permute-done | bytes 221216 | tf_op jit(solution)/shard_map/ppermute | solution.py:173
  108.2 12.8 %shard_map.123.u_ref.prev_ref = f32[3,32,32,256]{3,2,1,0:T(8,128)} custom-call(f32[3,32,32,256]{3,2,1,0:T(8,128)} %shard_map.122.u_ref.prev_ref, f32[3,2,32,256]{3,2,1,0:T(8,128)} %copy-done.4, f32[3,2,32,256]{3,2,1,0:T(8,128)} %copy-done.7, f32[3,36,2,256]{3,2,1,0:T(2,128)} %copy-done.15, f32[3,36,2,256]{3,2,1,0:T(2,128)} %copy-done.12, ...), custom_call_target="tpu_custom_call" | custom-call | tf_op jit(solution)/shard_map/pallas_call | solution.py:142
  121.0 1.0 fusion.81
  122.0 2.5 %collective-permute-start.8 = (f32[3,2,32,256]{3,2,1,0:T(8,128)S(1)}, f32[3,2,32,256]{3,2,1,0:T(8,128)S(1)}, u32[]{:S(2)}, u32[]{:S(2)}) collective-permute-start(f32[3,2,32,256]{3,2,1,0:T(8,128)S(1)} %get-tuple-element.264), channel_id=1, source_target_pairs={{0,4},{4,8},{8,12},{12,16},{16,20},{20,24},{24,28},{1,5},{5,9},{9,... | collective-permute-start | bytes 589832 | tf_op jit(solution)/shard_map/ppermute | solution.py:168
  124.6 4.2 %collective-permute-start.9 = (f32[3,2,32,256]{3,2,1,0:T(8,128)S(1)}, f32[3,2,32,256]{3,2,1,0:T(8,128)S(1)}, u32[]{:S(2)}, u32[]{:S(2)}) collective-permute-start(f32[3,2,32,256]{3,2,1,0:T(8,128)S(1)} %get-tuple-element.263), channel_id=1, source_target_pairs={{4,0},{8,4},{12,8},{16,12},{20,16},{24,20},{28,24},{5,1},{9,5},{13... | collective-permute-start | bytes 589832 | tf_op jit(solution)/shard_map/ppermute | solution.py:169
  128.8 1.5 fusion.80
  130.5 2.1 %collective-permute-done.9.xhi_ref = f32[3,2,32,256]{3,2,1,0:T(8,128)S(1)} collective-permute-done((f32[3,2,32,256]{3,2,1,0:T(8,128)S(1)}, f32[3,2,32,256]{3,2,1,0:T(8,128)S(1)}, u32[]{:S(2)}, u32[]{:S(2)}) %collective-permute-start.9) | collective-permute-done | bytes 196640 | tf_op jit(solution)/shard_map/ppermute | solution.py:169
  132.7 4.6 %collective-permute-start.11 = (f32[3,36,2,256]{3,2,1,0:T(2,128)S(1)}, f32[3,36,2,256]{3,2,1,0:T(2,128)S(1)}, u32[]{:S(2)}, u32[]{:S(2)}) collective-permute-start(f32[3,36,2,256]{3,2,1,0:T(2,128)S(1)} %pad_maximum_fusion.6), channel_id=1, source_target_pairs={{1,0},{2,1},{3,2},{5,4},{6,5},{7,6},{9,8},{10,9},{11,10},{13,12},{... | collective-permute-start | bytes 663560 | tf_op jit(solution)/shard_map/ppermute | solution.py:174
  137.4 1.9 collective-permute-start.10
  139.3 3.2 %fusion.8 = f32[3072,256]{1,0:T(8,128)} fusion(s32[256]{0:T(256)S(1)} %get-tuple-element.303, f32[256]{0:T(256)S(1)} %bitcast.114, s32[256]{0:T(256)S(1)} %get-tuple-element.302), kind=kOutput, calls=%fused_computation.27 | convolution fusion | flops 2416836608 | bytes 3148800 | tf_op jit(solution)/shard_map/dot_general | solution.py:380
  142.6 2.1 %collective-permute-done.10.ylo_ref = f32[3,36,2,256]{3,2,1,0:T(2,128)S(1)} collective-permute-done((f32[3,36,2,256]{3,2,1,0:T(2,128)S(1)}, f32[3,36,2,256]{3,2,1,0:T(2,128)S(1)}, u32[]{:S(2)}, u32[]{:S(2)}) %collective-permute-start.10) | collective-permute-done | bytes 221216 | tf_op jit(solution)/shard_map/ppermute | solution.py:173
  145.4 12.8 %shard_map.124.u_ref = f32[3,32,32,256]{3,2,1,0:T(8,128)} custom-call(f32[3,32,32,256]{3,2,1,0:T(8,128)} %shard_map.123.u_ref.prev_ref, f32[3,2,32,256]{3,2,1,0:T(8,128)} %copy-done.3, f32[3,2,32,256]{3,2,1,0:T(8,128)} %copy-done.6, f32[3,36,2,256]{3,2,1,0:T(2,128)} %copy-done.14, f32[3,36,2,256]{3,2,1,0:T(2,128)} %copy-done.11, ...), custom_call_target="tpu_custom_call" | custom-call | tf_op jit(solution)/shard_map/pallas_call | solution.py:142
  159.3 2.5 %collective-permute-start.12 = (f32[3,2,32,256]{3,2,1,0:T(8,128)S(1)}, f32[3,2,32,256]{3,2,1,0:T(8,128)S(1)}, u32[]{:S(2)}, u32[]{:S(2)}) collective-permute-start(f32[3,2,32,256]{3,2,1,0:T(8,128)S(1)} %get-tuple-element.260), channel_id=1, source_target_pairs={{0,4},{4,8},{8,12},{12,16},{16,20},{20,24},{24,28},{1,5},{5,9},{9,... | collective-permute-start | bytes 589832 | tf_op jit(solution)/shard_map/ppermute | solution.py:168
  161.7 4.3 %collective-permute-start.13 = (f32[3,2,32,256]{3,2,1,0:T(8,128)S(1)}, f32[3,2,32,256]{3,2,1,0:T(8,128)S(1)}, u32[]{:S(2)}, u32[]{:S(2)}) collective-permute-start(f32[3,2,32,256]{3,2,1,0:T(8,128)S(1)} %get-tuple-element.259), channel_id=1, source_target_pairs={{4,0},{8,4},{12,8},{16,12},{20,16},{24,20},{28,24},{5,1},{9,5},{13... | collective-permute-start | bytes 589832 | tf_op jit(solution)/shard_map/ppermute | solution.py:169
  166.0 1.5 fusion.78
  167.7 2.1 %collective-permute-done.13.xhi_ref = f32[3,2,32,256]{3,2,1,0:T(8,128)S(1)} collective-permute-done((f32[3,2,32,256]{3,2,1,0:T(8,128)S(1)}, f32[3,2,32,256]{3,2,1,0:T(8,128)S(1)}, u32[]{:S(2)}, u32[]{:S(2)}) %collective-permute-start.13) | collective-permute-done | bytes 196640 | tf_op jit(solution)/shard_map/ppermute | solution.py:169
  170.0 4.6 %collective-permute-start.15 = (f32[3,36,2,256]{3,2,1,0:T(2,128)S(1)}, f32[3,36,2,256]{3,2,1,0:T(2,128)S(1)}, u32[]{:S(2)}, u32[]{:S(2)}) collective-permute-start(f32[3,36,2,256]{3,2,1,0:T(2,128)S(1)} %pad_maximum_fusion.8), channel_id=1, source_target_pairs={{1,0},{2,1},{3,2},{5,4},{6,5},{7,6},{9,8},{10,9},{11,10},{13,12},{... | collective-permute-start | bytes 663560 | tf_op jit(solution)/shard_map/ppermute | solution.py:174
  174.6 1.9 collective-permute-start.14
  176.6 3.2 %fusion.7 = f32[3072,256]{1,0:T(8,128)} fusion(s32[256]{0:T(256)S(1)} %get-tuple-element.303, f32[256]{0:T(256)S(1)} %bitcast.113, s32[256]{0:T(256)S(1)} %get-tuple-element.302), kind=kOutput, calls=%fused_computation.26 | convolution fusion | flops 2416836608 | bytes 3148800 | tf_op jit(solution)/shard_map/dot_general | solution.py:380
  179.8 2.1 %collective-permute-done.14.ylo_ref = f32[3,36,2,256]{3,2,1,0:T(2,128)S(1)} collective-permute-done((f32[3,36,2,256]{3,2,1,0:T(2,128)S(1)}, f32[3,36,2,256]{3,2,1,0:T(2,128)S(1)}, u32[]{:S(2)}, u32[]{:S(2)}) %collective-permute-start.14) | collective-permute-done | bytes 221216 | tf_op jit(solution)/shard_map/ppermute | solution.py:173
  182.6 12.8 %shard_map.125 = f32[3,32,32,256]{3,2,1,0:T(8,128)} custom-call(f32[3,32,32,256]{3,2,1,0:T(8,128)} %shard_map.124.u_ref, f32[3,2,32,256]{3,2,1,0:T(8,128)} %copy-done.2, f32[3,2,32,256]{3,2,1,0:T(8,128)} %copy-done.5, f32[3,36,2,256]{3,2,1,0:T(2,128)} %copy-done.13, f32[3,36,2,256]{3,2,1,0:T(2,128)} %copy-done.10, ...), custom_call_target="tpu_custom_call" | custom-call | tf_op jit(solution)/shard_map/pallas_call | solution.py:142
  (138 shorter events, 14.9 us)
Async XLA Ops:
  16.0 5.3 %copy-start.16 = (s32[8192]{0:T(1024)S(1)}, s32[8192]{0:T(1024)}, u32[]{:S(2)}) copy-start(s32[8192]{0:T(1024)} %param.19) | copy-start | bytes 98308
  16.0 5.3 %copy-start.17 = (s32[8192]{0:T(1024)S(1)}, s32[8192]{0:T(1024)}, u32[]{:S(2)}) copy-start(s32[8192]{0:T(1024)} %param.20) | copy-start | bytes 98308
  24.8 30.6 %copy-start.18 = (s32[256]{0:T(256)S(1)}, s32[256]{0:T(256)}, u32[]{:S(2)}) copy-start(s32[256]{0:T(256)} %param.21) | copy-start | bytes 3076
  39.3 25.6 %all-to-all-start = ((bf16[2,4,32,256]{3,1,0,2:T(4,128)(2,1)}), bf16[2,4,32,256]{3,1,0,2:T(4,128)(2,1)S(1)}, u32[]{:S(2)}, u32[]{:S(2)}) async-start(bf16[2,4,32,256]{3,1,0,2:T(4,128)(2,1)} %copy.27), calls=%async_computation | async-start | bytes 262144 | tf_op jit(solution)/shard_map/all_to_all | solution.py:357
  46.3 9.7 %collective-permute-start = (f32[3,2,32,256]{3,2,1,0:T(8,128)S(1)}, f32[3,2,32,256]{3,2,1,0:T(8,128)S(1)}, u32[]{:S(2)}, u32[]{:S(2)}) collective-permute-start(f32[3,2,32,256]{3,2,1,0:T(8,128)S(1)} %get-tuple-element.272), channel_id=1, source_target_pairs={{0,4},{4,8},{8,12},{12,16},{16,20},{20,24},{24,28},{1,5},{5,9},{9,... | collective-permute-start | bytes 589832 | tf_op jit(solution)/shard_map/ppermute | solution.py:168
  49.7 10.5 %collective-permute-start.1 = (f32[3,2,32,256]{3,2,1,0:T(8,128)S(1)}, f32[3,2,32,256]{3,2,1,0:T(8,128)S(1)}, u32[]{:S(2)}, u32[]{:S(2)}) collective-permute-start(f32[3,2,32,256]{3,2,1,0:T(8,128)S(1)} %get-tuple-element.271), channel_id=1, source_target_pairs={{4,0},{8,4},{12,8},{16,12},{20,16},{24,20},{28,24},{5,1},{9,5},{13... | collective-permute-start | bytes 589832 | tf_op jit(solution)/shard_map/ppermute | solution.py:169
  56.0 13.9 %copy-start = (f32[3,2,32,256]{3,2,1,0:T(8,128)}, f32[3,2,32,256]{3,2,1,0:T(8,128)S(1)}, u32[]{:S(2)}) copy-start(f32[3,2,32,256]{3,2,1,0:T(8,128)S(1)} %collective-permute-done.xlo_ref) | copy-start | bytes 589828
  60.2 9.7 %copy-start.1 = (f32[3,2,32,256]{3,2,1,0:T(8,128)}, f32[3,2,32,256]{3,2,1,0:T(8,128)S(1)}, u32[]{:S(2)}) copy-start(f32[3,2,32,256]{3,2,1,0:T(8,128)S(1)} %collective-permute-done.1.xhi_ref) | copy-start | bytes 589828
  60.4 8.0 %collective-permute-start.3 = (f32[3,36,2,256]{3,2,1,0:T(2,128)S(1)}, f32[3,36,2,256]{3,2,1,0:T(2,128)S(1)}, u32[]{:S(2)}, u32[]{:S(2)}) collective-permute-start(f32[3,36,2,256]{3,2,1,0:T(2,128)S(1)} %pad_maximum_fusion.2), channel_id=1, source_target_pairs={{1,0},{2,1},{3,2},{5,4},{6,5},{7,6},{9,8},{10,9},{11,10},{13,12},{... | collective-permute-start | bytes 663560 | tf_op jit(solution)/shard_map/ppermute | solution.py:174
  62.7 7.3 %collective-permute-start.2 = (f32[3,36,2,256]{3,2,1,0:T(2,128)S(1)}, f32[3,36,2,256]{3,2,1,0:T(2,128)S(1)}, u32[]{:S(2)}, u32[]{:S(2)}) collective-permute-start(f32[3,36,2,256]{3,2,1,0:T(2,128)S(1)} %pad_maximum_fusion.1), channel_id=1, source_target_pairs={{0,1},{1,2},{2,3},{4,5},{5,6},{6,7},{8,9},{9,10},{10,11},{12,13},{... | collective-permute-start | bytes 663560 | tf_op jit(solution)/shard_map/ppermute | solution.py:173
  68.4 1.6 copy-start.8
  69.9 0.7 copy-start.9
  84.5 8.6 %collective-permute-start.4 = (f32[3,2,32,256]{3,2,1,0:T(8,128)S(1)}, f32[3,2,32,256]{3,2,1,0:T(8,128)S(1)}, u32[]{:S(2)}, u32[]{:S(2)}) collective-permute-start(f32[3,2,32,256]{3,2,1,0:T(8,128)S(1)} %get-tuple-element.268), channel_id=1, source_target_pairs={{0,4},{4,8},{8,12},{12,16},{16,20},{20,24},{24,28},{1,5},{5,9},{9,... | collective-permute-start | bytes 589832 | tf_op jit(solution)/shard_map/ppermute | solution.py:168
  86.8 9.4 %collective-permute-start.5 = (f32[3,2,32,256]{3,2,1,0:T(8,128)S(1)}, f32[3,2,32,256]{3,2,1,0:T(8,128)S(1)}, u32[]{:S(2)}, u32[]{:S(2)}) collective-permute-start(f32[3,2,32,256]{3,2,1,0:T(8,128)S(1)} %get-tuple-element.267), channel_id=1, source_target_pairs={{4,0},{8,4},{12,8},{16,12},{20,16},{24,20},{28,24},{5,1},{9,5},{13... | collective-permute-start | bytes 589832 | tf_op jit(solution)/shard_map/ppermute | solution.py:169
  93.1 14.4 %copy-start.4 = (f32[3,2,32,256]{3,2,1,0:T(8,128)}, f32[3,2,32,256]{3,2,1,0:T(8,128)S(1)}, u32[]{:S(2)}) copy-start(f32[3,2,32,256]{3,2,1,0:T(8,128)S(1)} %collective-permute-done.4.xlo_ref) | copy-start | bytes 589828
  96.2 11.3 %copy-start.7 = (f32[3,2,32,256]{3,2,1,0:T(8,128)}, f32[3,2,32,256]{3,2,1,0:T(8,128)S(1)}, u32[]{:S(2)}) copy-start(f32[3,2,32,256]{3,2,1,0:T(8,128)S(1)} %collective-permute-done.5.xhi_ref) | copy-start | bytes 589828
  96.3 9.0 %collective-permute-start.7 = (f32[3,36,2,256]{3,2,1,0:T(2,128)S(1)}, f32[3,36,2,256]{3,2,1,0:T(2,128)S(1)}, u32[]{:S(2)}, u32[]{:S(2)}) collective-permute-start(f32[3,36,2,256]{3,2,1,0:T(2,128)S(1)} %pad_maximum_fusion.4), channel_id=1, source_target_pairs={{1,0},{2,1},{3,2},{5,4},{6,5},{7,6},{9,8},{10,9},{11,10},{13,12},{... | collective-permute-start | bytes 663560 | tf_op jit(solution)/shard_map/ppermute | solution.py:174
  100.2 7.3 %collective-permute-start.6 = (f32[3,36,2,256]{3,2,1,0:T(2,128)S(1)}, f32[3,36,2,256]{3,2,1,0:T(2,128)S(1)}, u32[]{:S(2)}, u32[]{:S(2)}) collective-permute-start(f32[3,36,2,256]{3,2,1,0:T(2,128)S(1)} %pad_maximum_fusion.3), channel_id=1, source_target_pairs={{0,1},{1,2},{2,3},{4,5},{5,6},{6,7},{8,9},{9,10},{10,11},{12,13},{... | collective-permute-start | bytes 663560 | tf_op jit(solution)/shard_map/ppermute | solution.py:173
  105.4 2.1 %copy-start.12 = (f32[3,36,2,256]{3,2,1,0:T(2,128)}, f32[3,36,2,256]{3,2,1,0:T(2,128)S(1)}, u32[]{:S(2)}) copy-start(f32[3,36,2,256]{3,2,1,0:T(2,128)S(1)} %collective-permute-done.7.yhi_ref) | copy-start | bytes 663556
  107.5 0.7 copy-start.15
  122.0 8.5 %collective-permute-start.8 = (f32[3,2,32,256]{3,2,1,0:T(8,128)S(1)}, f32[3,2,32,256]{3,2,1,0:T(8,128)S(1)}, u32[]{:S(2)}, u32[]{:S(2)}) collective-permute-start(f32[3,2,32,256]{3,2,1,0:T(8,128)S(1)} %get-tuple-element.264), channel_id=1, source_target_pairs={{0,4},{4,8},{8,12},{12,16},{16,20},{20,24},{24,28},{1,5},{5,9},{9,... | collective-permute-start | bytes 589832 | tf_op jit(solution)/shard_map/ppermute | solution.py:168
  124.6 8.0 %collective-permute-start.9 = (f32[3,2,32,256]{3,2,1,0:T(8,128)S(1)}, f32[3,2,32,256]{3,2,1,0:T(8,128)S(1)}, u32[]{:S(2)}, u32[]{:S(2)}) collective-permute-start(f32[3,2,32,256]{3,2,1,0:T(8,128)S(1)} %get-tuple-element.263), channel_id=1, source_target_pairs={{4,0},{8,4},{12,8},{16,12},{20,16},{24,20},{28,24},{5,1},{9,5},{13... | collective-permute-start | bytes 589832 | tf_op jit(solution)/shard_map/ppermute | solution.py:169
  130.5 14.2 %copy-start.3 = (f32[3,2,32,256]{3,2,1,0:T(8,128)}, f32[3,2,32,256]{3,2,1,0:T(8,128)S(1)}, u32[]{:S(2)}) copy-start(f32[3,2,32,256]{3,2,1,0:T(8,128)S(1)} %collective-permute-done.8.xlo_ref) | copy-start | bytes 589828
  132.6 12.1 %copy-start.6 = (f32[3,2,32,256]{3,2,1,0:T(8,128)}, f32[3,2,32,256]{3,2,1,0:T(8,128)S(1)}, u32[]{:S(2)}) copy-start(f32[3,2,32,256]{3,2,1,0:T(8,128)S(1)} %collective-permute-done.9.xhi_ref) | copy-start | bytes 589828
  132.7 9.8 %collective-permute-start.11 = (f32[3,36,2,256]{3,2,1,0:T(2,128)S(1)}, f32[3,36,2,256]{3,2,1,0:T(2,128)S(1)}, u32[]{:S(2)}, u32[]{:S(2)}) collective-permute-start(f32[3,36,2,256]{3,2,1,0:T(2,128)S(1)} %pad_maximum_fusion.6), channel_id=1, source_target_pairs={{1,0},{2,1},{3,2},{5,4},{6,5},{7,6},{9,8},{10,9},{11,10},{13,12},{... | collective-permute-start | bytes 663560 | tf_op jit(solution)/shard_map/ppermute | solution.py:174
  137.4 7.3 %collective-permute-start.10 = (f32[3,36,2,256]{3,2,1,0:T(2,128)S(1)}, f32[3,36,2,256]{3,2,1,0:T(2,128)S(1)}, u32[]{:S(2)}, u32[]{:S(2)}) collective-permute-start(f32[3,36,2,256]{3,2,1,0:T(2,128)S(1)} %pad_maximum_fusion.5), channel_id=1, source_target_pairs={{0,1},{1,2},{2,3},{4,5},{5,6},{6,7},{8,9},{9,10},{10,11},{12,13},{... | collective-permute-start | bytes 663560 | tf_op jit(solution)/shard_map/ppermute | solution.py:173
  142.6 2.1 %copy-start.11 = (f32[3,36,2,256]{3,2,1,0:T(2,128)}, f32[3,36,2,256]{3,2,1,0:T(2,128)S(1)}, u32[]{:S(2)}) copy-start(f32[3,36,2,256]{3,2,1,0:T(2,128)S(1)} %collective-permute-done.11.yhi_ref) | copy-start | bytes 663556
  144.7 0.7 copy-start.14
  159.3 8.5 %collective-permute-start.12 = (f32[3,2,32,256]{3,2,1,0:T(8,128)S(1)}, f32[3,2,32,256]{3,2,1,0:T(8,128)S(1)}, u32[]{:S(2)}, u32[]{:S(2)}) collective-permute-start(f32[3,2,32,256]{3,2,1,0:T(8,128)S(1)} %get-tuple-element.260), channel_id=1, source_target_pairs={{0,4},{4,8},{8,12},{12,16},{16,20},{20,24},{24,28},{1,5},{5,9},{9,... | collective-permute-start | bytes 589832 | tf_op jit(solution)/shard_map/ppermute | solution.py:168
  161.7 8.1 %collective-permute-start.13 = (f32[3,2,32,256]{3,2,1,0:T(8,128)S(1)}, f32[3,2,32,256]{3,2,1,0:T(8,128)S(1)}, u32[]{:S(2)}, u32[]{:S(2)}) collective-permute-start(f32[3,2,32,256]{3,2,1,0:T(8,128)S(1)} %get-tuple-element.259), channel_id=1, source_target_pairs={{4,0},{8,4},{12,8},{16,12},{20,16},{24,20},{28,24},{5,1},{9,5},{13... | collective-permute-start | bytes 589832 | tf_op jit(solution)/shard_map/ppermute | solution.py:169
  167.7 14.2 %copy-start.2 = (f32[3,2,32,256]{3,2,1,0:T(8,128)}, f32[3,2,32,256]{3,2,1,0:T(8,128)S(1)}, u32[]{:S(2)}) copy-start(f32[3,2,32,256]{3,2,1,0:T(8,128)S(1)} %collective-permute-done.12.xlo_ref) | copy-start | bytes 589828
  169.8 12.1 %copy-start.5 = (f32[3,2,32,256]{3,2,1,0:T(8,128)}, f32[3,2,32,256]{3,2,1,0:T(8,128)S(1)}, u32[]{:S(2)}) copy-start(f32[3,2,32,256]{3,2,1,0:T(8,128)S(1)} %collective-permute-done.13.xhi_ref) | copy-start | bytes 589828
  170.0 9.8 %collective-permute-start.15 = (f32[3,36,2,256]{3,2,1,0:T(2,128)S(1)}, f32[3,36,2,256]{3,2,1,0:T(2,128)S(1)}, u32[]{:S(2)}, u32[]{:S(2)}) collective-permute-start(f32[3,36,2,256]{3,2,1,0:T(2,128)S(1)} %pad_maximum_fusion.8), channel_id=1, source_target_pairs={{1,0},{2,1},{3,2},{5,4},{6,5},{7,6},{9,8},{10,9},{11,10},{13,12},{... | collective-permute-start | bytes 663560 | tf_op jit(solution)/shard_map/ppermute | solution.py:174
  174.6 7.3 %collective-permute-start.14 = (f32[3,36,2,256]{3,2,1,0:T(2,128)S(1)}, f32[3,36,2,256]{3,2,1,0:T(2,128)S(1)}, u32[]{:S(2)}, u32[]{:S(2)}) collective-permute-start(f32[3,36,2,256]{3,2,1,0:T(2,128)S(1)} %pad_maximum_fusion.7), channel_id=1, source_target_pairs={{0,1},{1,2},{2,3},{4,5},{5,6},{6,7},{8,9},{9,10},{10,11},{12,13},{... | collective-permute-start | bytes 663560 | tf_op jit(solution)/shard_map/ppermute | solution.py:173
  179.8 2.1 %copy-start.10 = (f32[3,36,2,256]{3,2,1,0:T(2,128)}, f32[3,36,2,256]{3,2,1,0:T(2,128)S(1)}, u32[]{:S(2)}) copy-start(f32[3,36,2,256]{3,2,1,0:T(2,128)S(1)} %collective-permute-done.15.yhi_ref) | copy-start | bytes 663556
  181.9 0.7 copy-start.13

commit v12 on v11

--- a/solution.py
+++ b/solution.py
@@ -35,11 +35,12 @@
 YPAD = 8
 
 
-def step_kernel(u_ref, xlo_ref, xhi_ref, ylo_ref, yhi_ref, prev_ref, mod_ref, src_ref, out_ref, up_ref, *, bx):
-    i = pl.program_id(0)
+def step_kernel(u_ref, xlo_ref, xhi_ref, ylo_ref, yhi_ref, prev_ref, mod_ref, src_ref, *rest, bx, first, stride):
+    out_ref, up_ref = rest[-2], rest[-1]
+    i = first + pl.program_id(0) * stride
     nx, ny = u_ref.shape[1], u_ref.shape[2]
 
-    @pl.when(i == 0)
+    @pl.when(pl.program_id(0) == 0)
     def _():
         for c in range(3):
             def fill(x, carry):
@@ -134,45 +135,66 @@
     lax.fori_loop(0, bx, plane, 0)
 
 
-def elastic_step(u, xlo, xhi, ylo, yhi, prev, moduli, sources, bx=8):
+def elastic_part(u, xlo, xhi, ylo, yhi, prev, moduli, sources, bx, first, stride, count, into=None):
     _, nx, ny, depth = u.shape
-    kernel = functools.partial(step_kernel, bx=bx)
-    block = lambda i: (0, i, 0, 0)
+    kernel = functools.partial(step_kernel, bx=bx, first=first, stride=stride)
+    block = lambda i: (0, first + i * stride, 0, 0)
     whole = lambda i: (0, 0, 0, 0)
+    in_specs = [
+        pl.BlockSpec(u.shape, whole),
+        pl.BlockSpec(xlo.shape, whole),
+        pl.BlockSpec(xhi.shape, whole),
+        pl.BlockSpec(ylo.shape, whole),
+        pl.BlockSpec(yhi.shape, whole),
+        pl.BlockSpec((3, bx, ny, depth), block),
+        pl.BlockSpec((2, bx, ny, depth), block),
+        pl.BlockSpec((3, bx, ny, depth), block),
+    ]
+    operands = [u, xlo, xhi, ylo, yhi, prev, moduli, sources]
+    aliases = {}
+    if into is not None:
+        in_specs.append(pl.BlockSpec(memory_space=pl.ANY))
+        operands.append(into)
+        aliases = {8: 0}
     return pl.pallas_call(
         kernel,
-        grid=(nx // bx,),
-        in_specs=[
-            pl.BlockSpec(u.shape, whole),
-            pl.BlockSpec(xlo.shape, whole),
-            pl.BlockSpec(xhi.shape, whole),
-            pl.BlockSpec(ylo.shape, whole),
-            pl.BlockSpec(yhi.shape, whole),
-            pl.BlockSpec((3, bx, ny, depth), block),
-            pl.BlockSpec((2, bx, ny, depth), block),
-            pl.BlockSpec((3, bx, ny, depth), block),
-        ],
+        grid=(count,),
+        in_specs=in_specs,
         out_specs=pl.BlockSpec((3, bx, ny, depth), block),
         out_shape=jax.ShapeDtypeStruct((3, nx, ny, depth), jnp.float32),
         scratch_shapes=[pltpu.VMEM((3, nx + 4, ny + 2 * YPAD, depth), jnp.float32)],
         compiler_params=pltpu.CompilerParams(dimension_semantics=("arbitrary",)),
-    )(u, xlo, xhi, ylo, yhi, prev, moduli, sources)
-
-
-def halos(block, width):
+        input_output_aliases=aliases,
+    )(*operands)
+
+
+def elastic_step(u, xlo, xhi, ylo, yhi, prev, moduli, sources, bx=4):
+    blocks = u.shape[1] // bx
+    args = (u, xlo, xhi, ylo, yhi, prev, moduli, sources, bx)
+    edge = elastic_part(*args, 0, blocks - 1, 2)
+    whole = elastic_part(*args, 1, 1, blocks - 2, into=edge)
+    return edge, whole
+
+
+def x_halos(block, width):
     size_x = lax.axis_size("gx")
-    size_y = lax.axis_size("gy")
-    nx, ny = block.shape[1], block.shape[2]
+    nx = block.shape[1]
     forward_x = [(i, i + 1) for i in range(size_x - 1)]
     backward_x = [(t, s) for s, t in forward_x]
     xlo = lax.ppermute(block[:, nx - width:], "gx", forward_x)
     xhi = lax.ppermute(block[:, :width], "gx", backward_x)
+    return xlo, xhi
+
+
+def y_halos(block, xlo, xhi, width):
+    size_y = lax.axis_size("gy")
+    ny = block.shape[2]
     forward_y = [(i, i + 1) for i in range(size_y - 1)]
     backward_y = [(t, s) for s, t in forward_y]
     rows = lambda sl: jnp.concatenate([xlo[:, :, sl], block[:, :, sl], xhi[:, :, sl]], axis=1)
     ylo = lax.ppermute(rows(slice(ny - width, ny)), "gy", forward_y)
     yhi = lax.ppermute(rows(slice(0, width)), "gy", backward_y)
-    return xlo, xhi, ylo, yhi
+    return ylo, yhi
 
 
 def level_table(values, layer_of_level):
@@ -375,12 +397,14 @@
         jnp.float32
     )
     previous, current = (field_old, field_now)
+    edge = field_now
     for instant in range(STEPS):
         spread = weighted[instant][:, None] * depth_hot
         source = jnp.dot(column_hot, spread, precision=lax.Precision.HIGHEST)
         source = source.reshape(3, block_x, block_y, depth)
-        xlo, xhi, ylo, yhi = halos(current, 2)
-        advanced = elastic_step(current, xlo, xhi, ylo, yhi, previous, moduli, source)
+        xlo, xhi = x_halos(edge, 2)
+        ylo, yhi = y_halos(current, xlo, xhi, 2)
+        edge, advanced = elastic_step(current, xlo, xhi, ylo, yhi, previous, moduli, source)
         previous, current = (current, advanced)
     return (current, previous)
 

time: 196 us -> 199 us (1.015)
  Pallas kernels: 51.3 us -> 68 us
  waiting for transfers between devices: 20.6 us -> 11 us
  starting transfers between devices: 55.9 us -> 50.5 us
    pallas_call x4 -> x8, Pallas kernels: 51.3 us -> 68 us  [elastic_part(): pl.pallas_call(kernel, grid=(count,), in_specs=in_specs, out_specs=pl.Blo...]
    ppermute x16, waiting for transfers between devices: 20.6 us -> 11 us  [the longest x4 6.2 us: y_halos(): ylo = lax.ppermute(rows(slice(ny - width, ny)), 'gy', forward_y)]
    ppermute x16, starting transfers between devices: 49.9 us -> 44.5 us  [the longest x4 17.5 us: x_halos(): xhi = lax.ppermute(block[:, :width], 'gx', backward_x)]
  transfers between devices with their start and end apart: 17 -> 17, of which waited for: 12 -> 6; matrix products, arithmetic and copies ran while one was open for 11% -> 11% of each run, Pallas kernels for 0% -> 17%
where the time goes in v12:
time: 199 us; the launch traced here: 197 us
  Pallas kernels  68 us (34%)
  starting transfers between devices  50.5 us (25%)
  matrix products  29.5 us (15%)
  other arithmetic  20.6 us (10%)
  local copies, waits for them, and re-layouts  15 us (8%)
  waiting for transfers between devices  11 us (6%)
  between operations  2 us (1%)
    pallas_call x8, Pallas kernels, elastic_part(): pl.pallas_call(kernel, grid=(count,), in_specs=in_specs, out_specs=pl.Blo...  68 us
    ppermute x4, starting transfers between devices, x_halos(): xhi = lax.ppermute(block[:, :width], 'gx', backward_x)  17.5 us
    dot_general x2, matrix products, select_block(): jnp.dot(table_rounded, offset_hot, preferred_element_type=jnp.float32)  13.1 us
    dot_general x4, matrix products, shards(): source = jnp.dot(column_hot, spread, precision=lax.Precision.HIGHEST)  12.8 us
    ppermute x4, starting transfers between devices, y_halos(): ylo = lax.ppermute(rows(slice(ny - width, ny)), 'gy', forward_y)  9.61 us
    ppermute x4, starting transfers between devices, x_halos(): xlo = lax.ppermute(block[:, nx - width:], 'gx', forward_x)  9.46 us
    ppermute x4, starting transfers between devices, y_halos(): yhi = lax.ppermute(rows(slice(0, width)), 'gy', backward_y)  7.95 us
    ppermute x4, waiting for transfers between devices, y_halos(): ylo = lax.ppermute(rows(slice(ny - width, ny)), 'gy', forward_y)  6.2 us
  transfers between devices with their start and end apart: 17, of which 6 were waited for; matrix products, arithmetic and copies ran while one was open for 11% of the time, Pallas kernels for 17%

profile of v12, /device:TPU:12, one launch (start us, length us, event | category | flops | bytes accessed | tf_op | source)
XLA Modules:
  0.0 197.2 jit_solution(17443778407361761101)
XLA Ops:
  2.9 4.9 %sine_multiply_fusion.1 = (f32[32,4,1024]{2,1,0:T(4,128)S(1)}, f32[32,4,1024]{2,1,0:T(4,128)S(1)}, f32[32,4,1024]{2,1,0:T(4,128)S(1)}) fusion(f32[32]{0:T(128)S(1)} %get-tuple-element.307, f32[32,4]{1,0:T(8,128)S(1)} %copy.28, f32[1024]{0:T(1024)S(1)} %multiply_multiply_fusion, f32[1,4,1024]{2,1,0:T(4,128)S(1)} %slice.157, f32[31,4,1024]{2,1,0:T(4,128)S(1)} %slice.156, ...), kind=kLoop, calls=%fused_computation.41 | loop fusion | flops 1441792 | bytes 2102016 | tf_op jit(solution)/shard_map/mul | solution.py:217
  8.1 2.2 %while.32 = (s32[]{:T(128)}, f32[4,1024]{1,0:T(4,128)S(1)}, f32[4,1024]{1,0:T(4,128)S(1)}, f32[32,4,1024]{2,1,0:T(4,128)S(1)}, f32[32,4,1024]{2,1,0:T(4,128)S(1)...) while((s32[]{:T(128)}, f32[4,1024]{1,0:T(4,128)S(1)}, ...), condition=%wide.region_6.7_spmd.clone, body=%wide.region_5.6_spmd.clone.sunk | while | flops 94212 | bytes 147591 | solution.py:233
  11.2 4.3 %fusion.43 = (bf16[1,32,4,1024]{3,2,1,0:T(4,128)(2,1)S(1)}, bf16[1,32,4,1024]{3,2,1,0:T(4,128)(2,1)S(1)}) fusion(f32[32,4,1024]{2,1,0:T(4,128)S(1)} %get-tuple-element.191, f32[32,4,1024]{2,1,0:T(4,128)S(1)} %get-tuple-element.190, f32[32,4,1024]{2,1,0:T(4,128)S(1)} %negate_exponential_fusion, f32[32,4,1024]{2,1,0:T(4,128)S(1)} %fusion.23), kind=kLoop, calls=%fused_computation.74 | loop fusion | flops 1835008 | bytes 2621440 | tf_op jit(solution)/shard_map/stack | solution.py:246
  17.7 3.6 %subtract_convert_fusion = bf16[1024,32,64]{0,2,1:T(8,128)(2,1)} fusion(f32[1024,64]{0,1:T(8,128)S(1)} %get-tuple-element.301, f32[1024,32]{0,1:T(8,128)S(1)} %get-tuple-element.295, f32[1024,64]{0,1:T(8,128)S(1)} %get-tuple-element.300, f32[1024,32]{0,1:T(8,128)S(1)} %get-tuple-element.294), kind=kLoop, calls=%fused_computation.24 | loop fusion | flops 8388608 | bytes 4980736 | tf_op jit(solution)/shard_map/convert_element_type | solution.py:261
  21.4 3.5 %convolution_convert_fusion = bf16[256,2048]{1,0:T(8,128)(2,1)S(1)} fusion(bf16[256,1024]{1,0:T(8,128)(2,1)S(1)} %bitcast.113, bf16[1024,2048]{0,1:T(8,128)(2,1)} %bitcast.111), kind=kOutput, calls=%fused_computation.30 | convolution fusion | flops 1074266112 | bytes 5767168 | tf_op jit(solution)/shard_map/dot_general | solution.py:349
  24.9 13.4 %while.31 = (s32[]{:T(128)}, bf16[2,2,4,4096]{3,2,1,0:T(4,128)(2,1)S(1)}, s32[2,4096]{1,0:T(2,128)S(1)}, bf16[256,2048]{1,0:T(8,128)(2,1)S(1)}, s32[2,4096]{1,0:T(2,128)S(1)}, /*index=5*/s32[]{:T(128)}) while((s32[]{:T(128)}, bf16[2,2,4,4096]{3,2,1,0:T(4,128)(2,1)S(1)}, s32[2,4096]{1,0:T(2,128)S(1)}, bf16[256,2048]{1,0:T(8,128)(2,1)S(1)}, ...), condition=%wide.region_9.10_spmd, body=%wide.region_7.9_spmd.sunk | while | flops 4305682432 | bytes 2392141 | solution.py:372
  25.0 6.5 %multiply_reduce_fusion.2 = bf16[2,4,4096]{2,1,0:T(4,128)(2,1)S(1)} fusion(f32[32,4096]{1,0:T(8,128)S(1)} %fusion.102, bf16[256,2048]{1,0:T(8,128)(2,1)S(1)} %get-tuple-element.448, s32[4096]{0:T(1024)S(1)} %bitcast.115), kind=kOutput, calls=%fused_computation.3.clone.1 | convolution fusion | flops 4305420288 | bytes 1654784 | tf_op jit(solution)/shard_map/while/body/eval_jaxpr/dot_general | solution.py:364
  31.7 6.5 %multiply_reduce_fusion.2 = bf16[2,4,4096]{2,1,0:T(4,128)(2,1)S(1)} fusion(f32[32,4096]{1,0:T(8,128)S(1)} %fusion.102, bf16[256,2048]{1,0:T(8,128)(2,1)S(1)} %get-tuple-element.448, s32[4096]{0:T(1024)S(1)} %bitcast.115), kind=kOutput, calls=%fused_computation.3.clone.1 | convolution fusion | flops 4305420288 | bytes 1654784 | tf_op jit(solution)/shard_map/while/body/eval_jaxpr/dot_general | solution.py:364
  39.3 6.0 %all-to-all-start = ((bf16[2,4,32,256]{3,1,0,2:T(4,128)(2,1)}), bf16[2,4,32,256]{3,1,0,2:T(4,128)(2,1)S(1)}, u32[]{:S(2)}, u32[]{:S(2)}) async-start(bf16[2,4,32,256]{3,1,0,2:T(4,128)(2,1)} %copy.31), calls=%async_computation | async-start | bytes 262144 | tf_op jit(solution)/shard_map/all_to_all | solution.py:379
  45.3 1.1 fusion.85
  46.3 3.4 %collective-permute-start = (f32[3,2,32,256]{3,2,1,0:T(8,128)S(1)}, f32[3,2,32,256]{3,2,1,0:T(8,128)S(1)}, u32[]{:S(2)}, u32[]{:S(2)}) collective-permute-start(f32[3,2,32,256]{3,2,1,0:T(8,128)S(1)} %get-tuple-element.272), channel_id=1, source_target_pairs={{0,4},{4,8},{8,12},{12,16},{16,20},{20,24},{24,28},{1,5},{5,9},{9,... | collective-permute-start | bytes 589832 | tf_op jit(solution)/shard_map/ppermute | solution.py:184
  49.7 3.4 %collective-permute-start.1 = (f32[3,2,32,256]{3,2,1,0:T(8,128)S(1)}, f32[3,2,32,256]{3,2,1,0:T(8,128)S(1)}, u32[]{:S(2)}, u32[]{:S(2)}) collective-permute-start(f32[3,2,32,256]{3,2,1,0:T(8,128)S(1)} %get-tuple-element.271), channel_id=1, source_target_pairs={{4,0},{8,4},{12,8},{16,12},{20,16},{24,20},{28,24},{5,1},{9,5},{13... | collective-permute-start | bytes 589832 | tf_op jit(solution)/shard_map/ppermute | solution.py:185
  53.1 1.5 fusion.84
  56.1 4.2 %collective-permute-done.1.xhi_ref = f32[3,2,32,256]{3,2,1,0:T(8,128)S(1)} collective-permute-done((f32[3,2,32,256]{3,2,1,0:T(8,128)S(1)}, f32[3,2,32,256]{3,2,1,0:T(8,128)S(1)}, u32[]{:S(2)}, u32[]{:S(2)}) %collective-permute-start.1) | collective-permute-done | bytes 196640 | tf_op jit(solution)/shard_map/ppermute | solution.py:185
  60.4 2.2 %collective-permute-start.3 = (f32[3,36,2,256]{3,2,1,0:T(2,128)S(1)}, f32[3,36,2,256]{3,2,1,0:T(2,128)S(1)}, u32[]{:S(2)}, u32[]{:S(2)}) collective-permute-start(f32[3,36,2,256]{3,2,1,0:T(2,128)S(1)} %pad_maximum_fusion.2), channel_id=1, source_target_pairs={{1,0},{2,1},{3,2},{5,4},{6,5},{7,6},{9,8},{10,9},{11,10},{13,12},{... | collective-permute-start | bytes 663560 | tf_op jit(solution)/shard_map/ppermute | solution.py:196
  62.7 2.1 %collective-permute-start.2 = (f32[3,36,2,256]{3,2,1,0:T(2,128)S(1)}, f32[3,36,2,256]{3,2,1,0:T(2,128)S(1)}, u32[]{:S(2)}, u32[]{:S(2)}) collective-permute-start(f32[3,36,2,256]{3,2,1,0:T(2,128)S(1)} %pad_maximum_fusion.1), channel_id=1, source_target_pairs={{0,1},{1,2},{2,3},{4,5},{5,6},{6,7},{8,9},{9,10},{10,11},{12,13},{... | collective-permute-start | bytes 663560 | tf_op jit(solution)/shard_map/ppermute | solution.py:195
  65.1 3.2 %fusion.10 = f32[3072,256]{1,0:T(8,128)} fusion(s32[256]{0:T(256)S(1)} %get-tuple-element.303, f32[256]{0:T(256)S(1)} %bitcast.120, s32[256]{0:T(256)S(1)} %get-tuple-element.302), kind=kOutput, calls=%fused_computation.29 | convolution fusion | flops 2416836608 | bytes 3148800 | tf_op jit(solution)/shard_map/dot_general | solution.py:403
  68.4 1.6 collective-permute-done.2.ylo_ref
  70.6 6.1 %shard_map.122.rest_0_ = f32[3,32,32,256]{3,2,1,0:T(8,128)} custom-call(f32[3,32,32,256]{3,2,1,0:T(8,128)} %prev_ref.7, f32[3,2,32,256]{3,2,1,0:T(8,128)} %copy-done, f32[3,2,32,256]{3,2,1,0:T(8,128)} %copy-done.1, f32[3,36,2,256]{3,2,1,0:T(2,128)} %copy-done.9, f32[3,36,2,256]{3,2,1,0:T(2,128)} %copy-done.8, f32[3,32,32,256]{3,2,1,0:T(8,128)} %prev_ref.5, ...), custom_call_target="tpu_custom_call" | custom-call | tf_op jit(solution)/shard_map/pallas_call | solution.py:159
  76.7 1.0 fusion.83
  77.7 2.2 %collective-permute-start.4 = (f32[3,2,32,256]{3,2,1,0:T(8,128)S(1)}, f32[3,2,32,256]{3,2,1,0:T(8,128)S(1)}, u32[]{:S(2)}, u32[]{:S(2)}) collective-permute-start(f32[3,2,32,256]{3,2,1,0:T(8,128)S(1)} %get-tuple-element.268), channel_id=1, source_target_pairs={{0,4},{4,8},{8,12},{12,16},{16,20},{20,24},{24,28},{1,5},{5,9},{9,... | collective-permute-start | bytes 589832 | tf_op jit(solution)/shard_map/ppermute | solution.py:184
  80.0 4.5 %collective-permute-start.5 = (f32[3,2,32,256]{3,2,1,0:T(8,128)S(1)}, f32[3,2,32,256]{3,2,1,0:T(8,128)S(1)}, u32[]{:S(2)}, u32[]{:S(2)}) collective-permute-start(f32[3,2,32,256]{3,2,1,0:T(8,128)S(1)} %get-tuple-element.267), channel_id=1, source_target_pairs={{4,0},{8,4},{12,8},{16,12},{20,16},{24,20},{28,24},{5,1},{9,5},{13... | collective-permute-start | bytes 589832 | tf_op jit(solution)/shard_map/ppermute | solution.py:185
  84.5 11.0 %shard_map.123.u_ref.prev_ref = f32[3,32,32,256]{3,2,1,0:T(8,128)} custom-call(f32[3,32,32,256]{3,2,1,0:T(8,128)} %prev_ref.7, f32[3,2,32,256]{3,2,1,0:T(8,128)} %copy-done, f32[3,2,32,256]{3,2,1,0:T(8,128)} %copy-done.1, f32[3,36,2,256]{3,2,1,0:T(2,128)} %copy-done.9, f32[3,36,2,256]{3,2,1,0:T(2,128)} %copy-done.8, ...), custom_call_target="tpu_custom_call", output_to_operand_aliasing={{}: (8, {})} | custom-call | tf_op jit(solution)/shard_map/pallas_call | solution.py:159
  95.5 1.5 fusion.82
  97.2 1.9 collective-permute-start.7
  99.2 2.4 %collective-permute-start.6 = (f32[3,36,2,256]{3,2,1,0:T(2,128)S(1)}, f32[3,36,2,256]{3,2,1,0:T(2,128)S(1)}, u32[]{:S(2)}, u32[]{:S(2)}) collective-permute-start(f32[3,36,2,256]{3,2,1,0:T(2,128)S(1)} %pad_maximum_fusion.3), channel_id=1, source_target_pairs={{0,1},{1,2},{2,3},{4,5},{5,6},{6,7},{8,9},{9,10},{10,11},{12,13},{... | collective-permute-start | bytes 663560 | tf_op jit(solution)/shard_map/ppermute | solution.py:195
  101.6 3.2 %fusion.9 = f32[3072,256]{1,0:T(8,128)} fusion(s32[256]{0:T(256)S(1)} %get-tuple-element.303, f32[256]{0:T(256)S(1)} %bitcast.119, s32[256]{0:T(256)S(1)} %get-tuple-element.302), kind=kOutput, calls=%fused_computation.28 | convolution fusion | flops 2416836608 | bytes 3148800 | tf_op jit(solution)/shard_map/dot_general | solution.py:403
  104.9 1.6 collective-permute-done.6.ylo_ref
  107.1 6.1 %shard_map.124.rest_0_ = f32[3,32,32,256]{3,2,1,0:T(8,128)} custom-call(f32[3,32,32,256]{3,2,1,0:T(8,128)} %shard_map.123.u_ref.prev_ref, f32[3,2,32,256]{3,2,1,0:T(8,128)} %copy-done.3, f32[3,2,32,256]{3,2,1,0:T(8,128)} %copy-done.5, f32[3,36,2,256]{3,2,1,0:T(2,128)} %copy-done.14, f32[3,36,2,256]{3,2,1,0:T(2,128)} %copy-done.11, ...), custom_call_target="tpu_custom_call" | custom-call | tf_op jit(solution)/shard_map/pallas_call | solution.py:159
  114.3 1.9 collective-permute-start.8
  116.2 4.8 %collective-permute-start.9 = (f32[3,2,32,256]{3,2,1,0:T(8,128)S(1)}, f32[3,2,32,256]{3,2,1,0:T(8,128)S(1)}, u32[]{:S(2)}, u32[]{:S(2)}) collective-permute-start(f32[3,2,32,256]{3,2,1,0:T(8,128)S(1)} %get-tuple-element.263), channel_id=1, source_target_pairs={{4,0},{8,4},{12,8},{16,12},{20,16},{24,20},{28,24},{5,1},{9,5},{13... | collective-permute-start | bytes 589832 | tf_op jit(solution)/shard_map/ppermute | solution.py:185
  121.0 11.0 %shard_map.125.u_ref.prev_ref = f32[3,32,32,256]{3,2,1,0:T(8,128)} custom-call(f32[3,32,32,256]{3,2,1,0:T(8,128)} %shard_map.123.u_ref.prev_ref, f32[3,2,32,256]{3,2,1,0:T(8,128)} %copy-done.3, f32[3,2,32,256]{3,2,1,0:T(8,128)} %copy-done.5, f32[3,36,2,256]{3,2,1,0:T(2,128)} %copy-done.14, ...), custom_call_target="tpu_custom_call", output_to_operand_aliasing={{}: (8, {})} | custom-call | tf_op jit(solution)/shard_map/pallas_call | solution.py:159
  132.0 1.5 fusion.80
  133.7 1.9 collective-permute-start.11
  135.7 2.4 %collective-permute-start.10 = (f32[3,36,2,256]{3,2,1,0:T(2,128)S(1)}, f32[3,36,2,256]{3,2,1,0:T(2,128)S(1)}, u32[]{:S(2)}, u32[]{:S(2)}) collective-permute-start(f32[3,36,2,256]{3,2,1,0:T(2,128)S(1)} %pad_maximum_fusion.5), channel_id=1, source_target_pairs={{0,1},{1,2},{2,3},{4,5},{5,6},{6,7},{8,9},{9,10},{10,11},{12,13},{... | collective-permute-start | bytes 663560 | tf_op jit(solution)/shard_map/ppermute | solution.py:195
  138.2 3.2 %fusion.8 = f32[3072,256]{1,0:T(8,128)} fusion(s32[256]{0:T(256)S(1)} %get-tuple-element.303, f32[256]{0:T(256)S(1)} %bitcast.118, s32[256]{0:T(256)S(1)} %get-tuple-element.302), kind=kOutput, calls=%fused_computation.27 | convolution fusion | flops 2416836608 | bytes 3148800 | tf_op jit(solution)/shard_map/dot_general | solution.py:403
  141.4 1.6 collective-permute-done.10.ylo_ref
  143.7 6.0 %shard_map.126.rest_0_ = f32[3,32,32,256]{3,2,1,0:T(8,128)} custom-call(f32[3,32,32,256]{3,2,1,0:T(8,128)} %shard_map.125.u_ref.prev_ref, f32[3,2,32,256]{3,2,1,0:T(8,128)} %copy-done.2, f32[3,2,32,256]{3,2,1,0:T(8,128)} %copy-done.4, f32[3,36,2,256]{3,2,1,0:T(2,128)} %copy-done.13, f32[3,36,2,256]{3,2,1,0:T(2,128)} %copy-done.10, ...), custom_call_target="tpu_custom_call" | custom-call | tf_op jit(solution)/shard_map/pallas_call | solution.py:159
  150.8 1.9 collective-permute-start.12
  152.7 4.8 %collective-permute-start.13 = (f32[3,2,32,256]{3,2,1,0:T(8,128)S(1)}, f32[3,2,32,256]{3,2,1,0:T(8,128)S(1)}, u32[]{:S(2)}, u32[]{:S(2)}) collective-permute-start(f32[3,2,32,256]{3,2,1,0:T(8,128)S(1)} %get-tuple-element.259), channel_id=1, source_target_pairs={{4,0},{8,4},{12,8},{16,12},{20,16},{24,20},{28,24},{5,1},{9,5},{13... | collective-permute-start | bytes 589832 | tf_op jit(solution)/shard_map/ppermute | solution.py:185
  157.5 11.0 %shard_map.127.u_ref = f32[3,32,32,256]{3,2,1,0:T(8,128)} custom-call(f32[3,32,32,256]{3,2,1,0:T(8,128)} %shard_map.125.u_ref.prev_ref, f32[3,2,32,256]{3,2,1,0:T(8,128)} %copy-done.2, f32[3,2,32,256]{3,2,1,0:T(8,128)} %copy-done.4, f32[3,36,2,256]{3,2,1,0:T(2,128)} %copy-done.13, f32[3,36,2,256]{3,2,1,0:T(2,128)} %copy-done.10, ...), custom_call_target="tpu_custom_call", output_to_operand_aliasing={{}: (8, {})} | custom-call | tf_op jit(solution)/shard_map/pallas_call | solution.py:159
  168.5 1.5 fusion.78
  170.2 1.9 collective-permute-start.15
  172.3 2.6 %collective-permute-start.14 = (f32[3,36,2,256]{3,2,1,0:T(2,128)S(1)}, f32[3,36,2,256]{3,2,1,0:T(2,128)S(1)}, u32[]{:S(2)}, u32[]{:S(2)}) collective-permute-start(f32[3,36,2,256]{3,2,1,0:T(2,128)S(1)} %pad_maximum_fusion.7), channel_id=1, source_target_pairs={{0,1},{1,2},{2,3},{4,5},{5,6},{6,7},{8,9},{9,10},{10,11},{12,13},{... | collective-permute-start | bytes 663560 | tf_op jit(solution)/shard_map/ppermute | solution.py:195
  174.9 3.2 %fusion.7 = f32[3072,256]{1,0:T(8,128)} fusion(s32[256]{0:T(256)S(1)} %get-tuple-element.303, f32[256]{0:T(256)S(1)} %bitcast.117, s32[256]{0:T(256)S(1)} %get-tuple-element.302), kind=kOutput, calls=%fused_computation.26 | convolution fusion | flops 2416836608 | bytes 3148800 | tf_op jit(solution)/shard_map/dot_general | solution.py:403
  178.1 1.4 collective-permute-done.14.ylo_ref
  180.2 6.0 %shard_map.128.rest_0_ = f32[3,32,32,256]{3,2,1,0:T(8,128)} custom-call(f32[3,32,32,256]{3,2,1,0:T(8,128)} %shard_map.127.u_ref, f32[3,2,32,256]{3,2,1,0:T(8,128)} %copy-done.6, f32[3,2,32,256]{3,2,1,0:T(8,128)} %copy-done.7, f32[3,36,2,256]{3,2,1,0:T(2,128)} %copy-done.15, f32[3,36,2,256]{3,2,1,0:T(2,128)} %copy-done.12, ...), custom_call_target="tpu_custom_call" | custom-call | tf_op jit(solution)/shard_map/pallas_call | solution.py:159
  186.3 11.0 %shard_map.129 = f32[3,32,32,256]{3,2,1,0:T(8,128)} custom-call(f32[3,32,32,256]{3,2,1,0:T(8,128)} %shard_map.127.u_ref, f32[3,2,32,256]{3,2,1,0:T(8,128)} %copy-done.6, f32[3,2,32,256]{3,2,1,0:T(8,128)} %copy-done.7, f32[3,36,2,256]{3,2,1,0:T(2,128)} %copy-done.15, f32[3,36,2,256]{3,2,1,0:T(2,128)} %copy-done.12, ...), custom_call_target="tpu_custom_call", output_to_operand_aliasing={{}: (8, {})} | custom-call | tf_op jit(solution)/shard_map/pallas_call | solution.py:159
  (142 shorter events, 15.3 us)
Async XLA Ops:
  16.0 5.3 %copy-start.16 = (s32[8192]{0:T(1024)S(1)}, s32[8192]{0:T(1024)}, u32[]{:S(2)}) copy-start(s32[8192]{0:T(1024)} %param.19) | copy-start | bytes 98308
  16.0 5.3 %copy-start.17 = (s32[8192]{0:T(1024)S(1)}, s32[8192]{0:T(1024)}, u32[]{:S(2)}) copy-start(s32[8192]{0:T(1024)} %param.20) | copy-start | bytes 98308
  24.8 30.6 %copy-start.18 = (s32[256]{0:T(256)S(1)}, s32[256]{0:T(256)}, u32[]{:S(2)}) copy-start(s32[256]{0:T(256)} %param.21) | copy-start | bytes 3076
  39.3 25.6 %all-to-all-start = ((bf16[2,4,32,256]{3,1,0,2:T(4,128)(2,1)}), bf16[2,4,32,256]{3,1,0,2:T(4,128)(2,1)S(1)}, u32[]{:S(2)}, u32[]{:S(2)}) async-start(bf16[2,4,32,256]{3,1,0,2:T(4,128)(2,1)} %copy.31), calls=%async_computation | async-start | bytes 262144 | tf_op jit(solution)/shard_map/all_to_all | solution.py:379
  46.3 9.7 %collective-permute-start = (f32[3,2,32,256]{3,2,1,0:T(8,128)S(1)}, f32[3,2,32,256]{3,2,1,0:T(8,128)S(1)}, u32[]{:S(2)}, u32[]{:S(2)}) collective-permute-start(f32[3,2,32,256]{3,2,1,0:T(8,128)S(1)} %get-tuple-element.272), channel_id=1, source_target_pairs={{0,4},{4,8},{8,12},{12,16},{16,20},{20,24},{24,28},{1,5},{5,9},{9,... | collective-permute-start | bytes 589832 | tf_op jit(solution)/shard_map/ppermute | solution.py:184
  49.7 10.5 %collective-permute-start.1 = (f32[3,2,32,256]{3,2,1,0:T(8,128)S(1)}, f32[3,2,32,256]{3,2,1,0:T(8,128)S(1)}, u32[]{:S(2)}, u32[]{:S(2)}) collective-permute-start(f32[3,2,32,256]{3,2,1,0:T(8,128)S(1)} %get-tuple-element.271), channel_id=1, source_target_pairs={{4,0},{8,4},{12,8},{16,12},{20,16},{24,20},{28,24},{5,1},{9,5},{13... | collective-permute-start | bytes 589832 | tf_op jit(solution)/shard_map/ppermute | solution.py:185
  56.0 13.9 %copy-start = (f32[3,2,32,256]{3,2,1,0:T(8,128)}, f32[3,2,32,256]{3,2,1,0:T(8,128)S(1)}, u32[]{:S(2)}) copy-start(f32[3,2,32,256]{3,2,1,0:T(8,128)S(1)} %collective-permute-done.xlo_ref) | copy-start | bytes 589828
  60.2 9.7 %copy-start.1 = (f32[3,2,32,256]{3,2,1,0:T(8,128)}, f32[3,2,32,256]{3,2,1,0:T(8,128)S(1)}, u32[]{:S(2)}) copy-start(f32[3,2,32,256]{3,2,1,0:T(8,128)S(1)} %collective-permute-done.1.xhi_ref) | copy-start | bytes 589828
  60.4 8.0 %collective-permute-start.3 = (f32[3,36,2,256]{3,2,1,0:T(2,128)S(1)}, f32[3,36,2,256]{3,2,1,0:T(2,128)S(1)}, u32[]{:S(2)}, u32[]{:S(2)}) collective-permute-start(f32[3,36,2,256]{3,2,1,0:T(2,128)S(1)} %pad_maximum_fusion.2), channel_id=1, source_target_pairs={{1,0},{2,1},{3,2},{5,4},{6,5},{7,6},{9,8},{10,9},{11,10},{13,12},{... | collective-permute-start | bytes 663560 | tf_op jit(solution)/shard_map/ppermute | solution.py:196
  62.7 7.3 %collective-permute-start.2 = (f32[3,36,2,256]{3,2,1,0:T(2,128)S(1)}, f32[3,36,2,256]{3,2,1,0:T(2,128)S(1)}, u32[]{:S(2)}, u32[]{:S(2)}) collective-permute-start(f32[3,36,2,256]{3,2,1,0:T(2,128)S(1)} %pad_maximum_fusion.1), channel_id=1, source_target_pairs={{0,1},{1,2},{2,3},{4,5},{5,6},{6,7},{8,9},{9,10},{10,11},{12,13},{... | collective-permute-start | bytes 663560 | tf_op jit(solution)/shard_map/ppermute | solution.py:195
  68.4 1.6 copy-start.8
  69.9 0.7 copy-start.9
  77.7 19.3 %collective-permute-start.4 = (f32[3,2,32,256]{3,2,1,0:T(8,128)S(1)}, f32[3,2,32,256]{3,2,1,0:T(8,128)S(1)}, u32[]{:S(2)}, u32[]{:S(2)}) collective-permute-start(f32[3,2,32,256]{3,2,1,0:T(8,128)S(1)} %get-tuple-element.268), channel_id=1, source_target_pairs={{0,4},{4,8},{8,12},{12,16},{16,20},{20,24},{24,28},{1,5},{5,9},{9,... | collective-permute-start | bytes 589832 | tf_op jit(solution)/shard_map/ppermute | solution.py:184
  80.0 17.0 %collective-permute-start.5 = (f32[3,2,32,256]{3,2,1,0:T(8,128)S(1)}, f32[3,2,32,256]{3,2,1,0:T(8,128)S(1)}, u32[]{:S(2)}, u32[]{:S(2)}) collective-permute-start(f32[3,2,32,256]{3,2,1,0:T(8,128)S(1)} %get-tuple-element.267), channel_id=1, source_target_pairs={{4,0},{8,4},{12,8},{16,12},{20,16},{24,20},{28,24},{5,1},{9,5},{13... | collective-permute-start | bytes 589832 | tf_op jit(solution)/shard_map/ppermute | solution.py:185
  97.0 9.5 %copy-start.3 = (f32[3,2,32,256]{3,2,1,0:T(8,128)}, f32[3,2,32,256]{3,2,1,0:T(8,128)S(1)}, u32[]{:S(2)}) copy-start(f32[3,2,32,256]{3,2,1,0:T(8,128)S(1)} %collective-permute-done.4.xlo_ref) | copy-start | bytes 589828
  97.0 9.4 %copy-start.5 = (f32[3,2,32,256]{3,2,1,0:T(8,128)}, f32[3,2,32,256]{3,2,1,0:T(8,128)S(1)}, u32[]{:S(2)}) copy-start(f32[3,2,32,256]{3,2,1,0:T(8,128)S(1)} %collective-permute-done.5.xhi_ref) | copy-start | bytes 589828
  97.2 7.7 %collective-permute-start.7 = (f32[3,36,2,256]{3,2,1,0:T(2,128)S(1)}, f32[3,36,2,256]{3,2,1,0:T(2,128)S(1)}, u32[]{:S(2)}, u32[]{:S(2)}) collective-permute-start(f32[3,36,2,256]{3,2,1,0:T(2,128)S(1)} %pad_maximum_fusion.4), channel_id=1, source_target_pairs={{1,0},{2,1},{3,2},{5,4},{6,5},{7,6},{9,8},{10,9},{11,10},{13,12},{... | collective-permute-start | bytes 663560 | tf_op jit(solution)/shard_map/ppermute | solution.py:196
  99.2 7.3 %collective-permute-start.6 = (f32[3,36,2,256]{3,2,1,0:T(2,128)S(1)}, f32[3,36,2,256]{3,2,1,0:T(2,128)S(1)}, u32[]{:S(2)}, u32[]{:S(2)}) collective-permute-start(f32[3,36,2,256]{3,2,1,0:T(2,128)S(1)} %pad_maximum_fusion.3), channel_id=1, source_target_pairs={{0,1},{1,2},{2,3},{4,5},{5,6},{6,7},{8,9},{9,10},{10,11},{12,13},{... | collective-permute-start | bytes 663560 | tf_op jit(solution)/shard_map/ppermute | solution.py:195
  104.9 1.6 copy-start.11
  106.5 0.7 copy-start.14
  114.3 19.3 %collective-permute-start.8 = (f32[3,2,32,256]{3,2,1,0:T(8,128)S(1)}, f32[3,2,32,256]{3,2,1,0:T(8,128)S(1)}, u32[]{:S(2)}, u32[]{:S(2)}) collective-permute-start(f32[3,2,32,256]{3,2,1,0:T(8,128)S(1)} %get-tuple-element.264), channel_id=1, source_target_pairs={{0,4},{4,8},{8,12},{12,16},{16,20},{20,24},{24,28},{1,5},{5,9},{9,... | collective-permute-start | bytes 589832 | tf_op jit(solution)/shard_map/ppermute | solution.py:184
  116.2 17.4 %collective-permute-start.9 = (f32[3,2,32,256]{3,2,1,0:T(8,128)S(1)}, f32[3,2,32,256]{3,2,1,0:T(8,128)S(1)}, u32[]{:S(2)}, u32[]{:S(2)}) collective-permute-start(f32[3,2,32,256]{3,2,1,0:T(8,128)S(1)} %get-tuple-element.263), channel_id=1, source_target_pairs={{4,0},{8,4},{12,8},{16,12},{20,16},{24,20},{28,24},{5,1},{9,5},{13... | collective-permute-start | bytes 589832 | tf_op jit(solution)/shard_map/ppermute | solution.py:185
  133.5 9.5 %copy-start.2 = (f32[3,2,32,256]{3,2,1,0:T(8,128)}, f32[3,2,32,256]{3,2,1,0:T(8,128)S(1)}, u32[]{:S(2)}) copy-start(f32[3,2,32,256]{3,2,1,0:T(8,128)S(1)} %collective-permute-done.8.xlo_ref) | copy-start | bytes 589828
  133.6 9.4 %copy-start.4 = (f32[3,2,32,256]{3,2,1,0:T(8,128)}, f32[3,2,32,256]{3,2,1,0:T(8,128)S(1)}, u32[]{:S(2)}) copy-start(f32[3,2,32,256]{3,2,1,0:T(8,128)S(1)} %collective-permute-done.9.xhi_ref) | copy-start | bytes 589828
  133.7 7.7 %collective-permute-start.11 = (f32[3,36,2,256]{3,2,1,0:T(2,128)S(1)}, f32[3,36,2,256]{3,2,1,0:T(2,128)S(1)}, u32[]{:S(2)}, u32[]{:S(2)}) collective-permute-start(f32[3,36,2,256]{3,2,1,0:T(2,128)S(1)} %pad_maximum_fusion.6), channel_id=1, source_target_pairs={{1,0},{2,1},{3,2},{5,4},{6,5},{7,6},{9,8},{10,9},{11,10},{13,12},{... | collective-permute-start | bytes 663560 | tf_op jit(solution)/shard_map/ppermute | solution.py:196
  135.7 7.3 %collective-permute-start.10 = (f32[3,36,2,256]{3,2,1,0:T(2,128)S(1)}, f32[3,36,2,256]{3,2,1,0:T(2,128)S(1)}, u32[]{:S(2)}, u32[]{:S(2)}) collective-permute-start(f32[3,36,2,256]{3,2,1,0:T(2,128)S(1)} %pad_maximum_fusion.5), channel_id=1, source_target_pairs={{0,1},{1,2},{2,3},{4,5},{5,6},{6,7},{8,9},{9,10},{10,11},{12,13},{... | collective-permute-start | bytes 663560 | tf_op jit(solution)/shard_map/ppermute | solution.py:195
  141.4 1.6 copy-start.10
  143.0 0.7 copy-start.13
  150.8 19.2 %collective-permute-start.12 = (f32[3,2,32,256]{3,2,1,0:T(8,128)S(1)}, f32[3,2,32,256]{3,2,1,0:T(8,128)S(1)}, u32[]{:S(2)}, u32[]{:S(2)}) collective-permute-start(f32[3,2,32,256]{3,2,1,0:T(8,128)S(1)} %get-tuple-element.260), channel_id=1, source_target_pairs={{0,4},{4,8},{8,12},{12,16},{16,20},{20,24},{24,28},{1,5},{5,9},{9,... | collective-permute-start | bytes 589832 | tf_op jit(solution)/shard_map/ppermute | solution.py:184
  152.7 17.4 %collective-permute-start.13 = (f32[3,2,32,256]{3,2,1,0:T(8,128)S(1)}, f32[3,2,32,256]{3,2,1,0:T(8,128)S(1)}, u32[]{:S(2)}, u32[]{:S(2)}) collective-permute-start(f32[3,2,32,256]{3,2,1,0:T(8,128)S(1)} %get-tuple-element.259), channel_id=1, source_target_pairs={{4,0},{8,4},{12,8},{16,12},{20,16},{24,20},{28,24},{5,1},{9,5},{13... | collective-permute-start | bytes 589832 | tf_op jit(solution)/shard_map/ppermute | solution.py:185
  170.0 9.5 %copy-start.6 = (f32[3,2,32,256]{3,2,1,0:T(8,128)}, f32[3,2,32,256]{3,2,1,0:T(8,128)S(1)}, u32[]{:S(2)}) copy-start(f32[3,2,32,256]{3,2,1,0:T(8,128)S(1)} %collective-permute-done.12.xlo_ref) | copy-start | bytes 589828
  170.1 9.4 %copy-start.7 = (f32[3,2,32,256]{3,2,1,0:T(8,128)}, f32[3,2,32,256]{3,2,1,0:T(8,128)S(1)}, u32[]{:S(2)}) copy-start(f32[3,2,32,256]{3,2,1,0:T(8,128)S(1)} %collective-permute-done.13.xhi_ref) | copy-start | bytes 589828
  170.2 7.9 %collective-permute-start.15 = (f32[3,36,2,256]{3,2,1,0:T(2,128)S(1)}, f32[3,36,2,256]{3,2,1,0:T(2,128)S(1)}, u32[]{:S(2)}, u32[]{:S(2)}) collective-permute-start(f32[3,36,2,256]{3,2,1,0:T(2,128)S(1)} %pad_maximum_fusion.8), channel_id=1, source_target_pairs={{1,0},{2,1},{3,2},{5,4},{6,5},{7,6},{9,8},{10,9},{11,10},{13,12},{... | collective-permute-start | bytes 663560 | tf_op jit(solution)/shard_map/ppermute | solution.py:196
  172.3 7.3 %collective-permute-start.14 = (f32[3,36,2,256]{3,2,1,0:T(2,128)S(1)}, f32[3,36,2,256]{3,2,1,0:T(2,128)S(1)}, u32[]{:S(2)}, u32[]{:S(2)}) collective-permute-start(f32[3,36,2,256]{3,2,1,0:T(2,128)S(1)} %pad_maximum_fusion.7), channel_id=1, source_target_pairs={{0,1},{1,2},{2,3},{4,5},{5,6},{6,7},{8,9},{9,10},{10,11},{12,13},{... | collective-permute-start | bytes 663560 | tf_op jit(solution)/shard_map/ppermute | solution.py:195
  178.1 1.4 copy-start.12
  179.5 0.7 copy-start.15

commit v13 on v12

--- a/solution.py
+++ b/solution.py
@@ -35,23 +35,28 @@
 YPAD = 8
 
 
-def step_kernel(u_ref, xlo_ref, xhi_ref, ylo_ref, yhi_ref, prev_ref, mod_ref, src_ref, *rest, bx, first, stride):
-    out_ref, up_ref = rest[-2], rest[-1]
+def step_kernel(u_ref, xlo_ref, xhi_ref, ylo_ref, yhi_ref, prev_ref, mod_ref, src_ref, *rest, bx, first, stride, spans):
+    out_ref, up_ref, sems = rest[-3], rest[-2], rest[-1]
     i = first + pl.program_id(0) * stride
     nx, ny = u_ref.shape[1], u_ref.shape[2]
 
     @pl.when(pl.program_id(0) == 0)
     def _():
-        for c in range(3):
-            def fill(x, carry):
-                up_ref[c, x + 2, pl.ds(YPAD, ny), :] = u_ref[c, x]
-                return carry
-
-            lax.fori_loop(0, nx, fill, 0)
+        fills = []
+        for k, (start, size) in enumerate(spans):
+            fill = pltpu.make_async_copy(
+                u_ref.at[:, pl.ds(start, size)],
+                up_ref.at[:, pl.ds(start + 2, size), pl.ds(YPAD, ny), :],
+                sems.at[k],
+            )
+            fill.start()
+            fills.append(fill)
         up_ref[:, 0:2, pl.ds(YPAD, ny), :] = xlo_ref[...]
         up_ref[:, nx + 2:nx + 4, pl.ds(YPAD, ny), :] = xhi_ref[...]
         up_ref[:, :, pl.ds(YPAD - 2, 2), :] = ylo_ref[...]
         up_ref[:, :, pl.ds(YPAD + ny, 2), :] = yhi_ref[...]
+        for fill in fills:
+            fill.wait()
 
     depth = out_ref.shape[3]
     lane = lax.broadcasted_iota(jnp.int32, (8, depth), 1)
@@ -137,11 +142,15 @@
 
 def elastic_part(u, xlo, xhi, ylo, yhi, prev, moduli, sources, bx, first, stride, count, into=None):
     _, nx, ny, depth = u.shape
-    kernel = functools.partial(step_kernel, bx=bx, first=first, stride=stride)
+    if first == 0:
+        spans = ((0, bx + 2), (nx - bx - 2, bx + 2))
+    else:
+        spans = ((bx - 2, nx - 2 * bx + 4),)
+    kernel = functools.partial(step_kernel, bx=bx, first=first, stride=stride, spans=spans)
     block = lambda i: (0, first + i * stride, 0, 0)
     whole = lambda i: (0, 0, 0, 0)
     in_specs = [
-        pl.BlockSpec(u.shape, whole),
+        pl.BlockSpec(memory_space=pl.ANY),
         pl.BlockSpec(xlo.shape, whole),
         pl.BlockSpec(xhi.shape, whole),
         pl.BlockSpec(ylo.shape, whole),
@@ -162,7 +171,10 @@
         in_specs=in_specs,
         out_specs=pl.BlockSpec((3, bx, ny, depth), block),
         out_shape=jax.ShapeDtypeStruct((3, nx, ny, depth), jnp.float32),
-        scratch_shapes=[pltpu.VMEM((3, nx + 4, ny + 2 * YPAD, depth), jnp.float32)],
+        scratch_shapes=[
+            pltpu.VMEM((3, nx + 4, ny + 2 * YPAD, depth), jnp.float32),
+            pltpu.SemaphoreType.DMA((len(spans),)),
+        ],
         compiler_params=pltpu.CompilerParams(dimension_semantics=("arbitrary",)),
         input_output_aliases=aliases,
     )(*operands)

time: 199 us -> 198 us (level)
  no operation moved by 1% of the time
where the time goes in v13:
time: 198 us; the launch traced here: 197 us
  Pallas kernels  67.2 us (34%)
  starting transfers between devices  50.5 us (26%)
  matrix products  29.5 us (15%)
  other arithmetic  20.6 us (10%)
  local copies, waits for them, and re-layouts  15 us (8%)
  waiting for transfers between devices  11 us (6%)
  between operations  2.23 us (1%)
    pallas_call x8, Pallas kernels, elastic_part(): pl.pallas_call(kernel, grid=(count,), in_specs=in_specs, out_specs=pl.Blo...  67.2 us
    ppermute x4, starting transfers between devices, x_halos(): xhi = lax.ppermute(block[:, :width], 'gx', backward_x)  17.5 us
    dot_general x2, matrix products, select_block(): jnp.dot(table_rounded, offset_hot, preferred_element_type=jnp.float32)  13.1 us
    dot_general x4, matrix products, shards(): source = jnp.dot(column_hot, spread, precision=lax.Precision.HIGHEST)  12.8 us
    ppermute x4, starting transfers between devices, y_halos(): ylo = lax.ppermute(rows(slice(ny - width, ny)), 'gy', forward_y)  9.61 us
    ppermute x4, starting transfers between devices, x_halos(): xlo = lax.ppermute(block[:, nx - width:], 'gx', forward_x)  9.46 us
    ppermute x4, starting transfers between devices, y_halos(): yhi = lax.ppermute(rows(slice(0, width)), 'gy', backward_y)  7.95 us
    ppermute x4, waiting for transfers between devices, y_halos(): ylo = lax.ppermute(rows(slice(ny - width, ny)), 'gy', forward_y)  6.2 us
  transfers between devices with their start and end apart: 17, of which 6 were waited for; matrix products, arithmetic and copies ran while one was open for 11% of the time, Pallas kernels for 17%

profile of v13, /device:TPU:12, one launch (start us, length us, event | category | flops | bytes accessed | tf_op | source)
XLA Modules:
  0.0 196.6 jit_solution(14016817349630468496)
XLA Ops:
  2.9 4.9 %sine_multiply_fusion.1 = (f32[32,4,1024]{2,1,0:T(4,128)S(1)}, f32[32,4,1024]{2,1,0:T(4,128)S(1)}, f32[32,4,1024]{2,1,0:T(4,128)S(1)}) fusion(f32[32]{0:T(128)S(1)} %get-tuple-element.307, f32[32,4]{1,0:T(8,128)S(1)} %copy.28, f32[1024]{0:T(1024)S(1)} %multiply_multiply_fusion, f32[1,4,1024]{2,1,0:T(4,128)S(1)} %slice.157, f32[31,4,1024]{2,1,0:T(4,128)S(1)} %slice.156, ...), kind=kLoop, calls=%fused_computation.41 | loop fusion | flops 1441792 | bytes 2102016 | tf_op jit(solution)/shard_map/mul | solution.py:229
  8.1 2.2 %while.32 = (s32[]{:T(128)}, f32[4,1024]{1,0:T(4,128)S(1)}, f32[4,1024]{1,0:T(4,128)S(1)}, f32[32,4,1024]{2,1,0:T(4,128)S(1)}, f32[32,4,1024]{2,1,0:T(4,128)S(1)...) while((s32[]{:T(128)}, f32[4,1024]{1,0:T(4,128)S(1)}, ...), condition=%wide.region_6.7_spmd.clone, body=%wide.region_5.6_spmd.clone.sunk | while | flops 94212 | bytes 147591 | solution.py:245
  11.2 4.3 %fusion.43 = (bf16[1,32,4,1024]{3,2,1,0:T(4,128)(2,1)S(1)}, bf16[1,32,4,1024]{3,2,1,0:T(4,128)(2,1)S(1)}) fusion(f32[32,4,1024]{2,1,0:T(4,128)S(1)} %get-tuple-element.191, f32[32,4,1024]{2,1,0:T(4,128)S(1)} %get-tuple-element.190, f32[32,4,1024]{2,1,0:T(4,128)S(1)} %negate_exponential_fusion, f32[32,4,1024]{2,1,0:T(4,128)S(1)} %fusion.23), kind=kLoop, calls=%fused_computation.74 | loop fusion | flops 1835008 | bytes 2621440 | tf_op jit(solution)/shard_map/stack | solution.py:258
  17.7 3.6 %subtract_convert_fusion = bf16[1024,32,64]{0,2,1:T(8,128)(2,1)} fusion(f32[1024,64]{0,1:T(8,128)S(1)} %get-tuple-element.301, f32[1024,32]{0,1:T(8,128)S(1)} %get-tuple-element.295, f32[1024,64]{0,1:T(8,128)S(1)} %get-tuple-element.300, f32[1024,32]{0,1:T(8,128)S(1)} %get-tuple-element.294), kind=kLoop, calls=%fused_computation.24 | loop fusion | flops 8388608 | bytes 4980736 | tf_op jit(solution)/shard_map/convert_element_type | solution.py:273
  21.4 3.5 %convolution_convert_fusion = bf16[256,2048]{1,0:T(8,128)(2,1)S(1)} fusion(bf16[256,1024]{1,0:T(8,128)(2,1)S(1)} %bitcast.113, bf16[1024,2048]{0,1:T(8,128)(2,1)} %bitcast.111), kind=kOutput, calls=%fused_computation.30 | convolution fusion | flops 1074266112 | bytes 5767168 | tf_op jit(solution)/shard_map/dot_general | solution.py:361
  24.9 13.4 %while.31 = (s32[]{:T(128)}, bf16[2,2,4,4096]{3,2,1,0:T(4,128)(2,1)S(1)}, s32[2,4096]{1,0:T(2,128)S(1)}, bf16[256,2048]{1,0:T(8,128)(2,1)S(1)}, s32[2,4096]{1,0:T(2,128)S(1)}, /*index=5*/s32[]{:T(128)}) while((s32[]{:T(128)}, bf16[2,2,4,4096]{3,2,1,0:T(4,128)(2,1)S(1)}, s32[2,4096]{1,0:T(2,128)S(1)}, bf16[256,2048]{1,0:T(8,128)(2,1)S(1)}, ...), condition=%wide.region_9.10_spmd, body=%wide.region_7.9_spmd.sunk | while | flops 4305682432 | bytes 2392141 | solution.py:384
  25.0 6.5 %multiply_reduce_fusion.2 = bf16[2,4,4096]{2,1,0:T(4,128)(2,1)S(1)} fusion(f32[32,4096]{1,0:T(8,128)S(1)} %fusion.102, bf16[256,2048]{1,0:T(8,128)(2,1)S(1)} %get-tuple-element.448, s32[4096]{0:T(1024)S(1)} %bitcast.115), kind=kOutput, calls=%fused_computation.3.clone.1 | convolution fusion | flops 4305420288 | bytes 1654784 | tf_op jit(solution)/shard_map/while/body/eval_jaxpr/dot_general | solution.py:376
  31.7 6.5 %multiply_reduce_fusion.2 = bf16[2,4,4096]{2,1,0:T(4,128)(2,1)S(1)} fusion(f32[32,4096]{1,0:T(8,128)S(1)} %fusion.102, bf16[256,2048]{1,0:T(8,128)(2,1)S(1)} %get-tuple-element.448, s32[4096]{0:T(1024)S(1)} %bitcast.115), kind=kOutput, calls=%fused_computation.3.clone.1 | convolution fusion | flops 4305420288 | bytes 1654784 | tf_op jit(solution)/shard_map/while/body/eval_jaxpr/dot_general | solution.py:376
  39.3 6.0 %all-to-all-start = ((bf16[2,4,32,256]{3,1,0,2:T(4,128)(2,1)}), bf16[2,4,32,256]{3,1,0,2:T(4,128)(2,1)S(1)}, u32[]{:S(2)}, u32[]{:S(2)}) async-start(bf16[2,4,32,256]{3,1,0,2:T(4,128)(2,1)} %copy.31), calls=%async_computation | async-start | bytes 262144 | tf_op jit(solution)/shard_map/all_to_all | solution.py:391
  45.3 1.1 fusion.85
  46.3 3.4 %collective-permute-start = (f32[3,2,32,256]{3,2,1,0:T(8,128)S(1)}, f32[3,2,32,256]{3,2,1,0:T(8,128)S(1)}, u32[]{:S(2)}, u32[]{:S(2)}) collective-permute-start(f32[3,2,32,256]{3,2,1,0:T(8,128)S(1)} %get-tuple-element.272), channel_id=1, source_target_pairs={{0,4},{4,8},{8,12},{12,16},{16,20},{20,24},{24,28},{1,5},{5,9},{9,... | collective-permute-start | bytes 589832 | tf_op jit(solution)/shard_map/ppermute | solution.py:196
  49.7 3.4 %collective-permute-start.1 = (f32[3,2,32,256]{3,2,1,0:T(8,128)S(1)}, f32[3,2,32,256]{3,2,1,0:T(8,128)S(1)}, u32[]{:S(2)}, u32[]{:S(2)}) collective-permute-start(f32[3,2,32,256]{3,2,1,0:T(8,128)S(1)} %get-tuple-element.271), channel_id=1, source_target_pairs={{4,0},{8,4},{12,8},{16,12},{20,16},{24,20},{28,24},{5,1},{9,5},{13... | collective-permute-start | bytes 589832 | tf_op jit(solution)/shard_map/ppermute | solution.py:197
  53.1 1.5 fusion.84
  56.1 4.2 %collective-permute-done.1.xhi_ref = f32[3,2,32,256]{3,2,1,0:T(8,128)S(1)} collective-permute-done((f32[3,2,32,256]{3,2,1,0:T(8,128)S(1)}, f32[3,2,32,256]{3,2,1,0:T(8,128)S(1)}, u32[]{:S(2)}, u32[]{:S(2)}) %collective-permute-start.1) | collective-permute-done | bytes 196640 | tf_op jit(solution)/shard_map/ppermute | solution.py:197
  60.4 2.2 %collective-permute-start.3 = (f32[3,36,2,256]{3,2,1,0:T(2,128)S(1)}, f32[3,36,2,256]{3,2,1,0:T(2,128)S(1)}, u32[]{:S(2)}, u32[]{:S(2)}) collective-permute-start(f32[3,36,2,256]{3,2,1,0:T(2,128)S(1)} %pad_maximum_fusion.2), channel_id=1, source_target_pairs={{1,0},{2,1},{3,2},{5,4},{6,5},{7,6},{9,8},{10,9},{11,10},{13,12},{... | collective-permute-start | bytes 663560 | tf_op jit(solution)/shard_map/ppermute | solution.py:208
  62.7 2.1 %collective-permute-start.2 = (f32[3,36,2,256]{3,2,1,0:T(2,128)S(1)}, f32[3,36,2,256]{3,2,1,0:T(2,128)S(1)}, u32[]{:S(2)}, u32[]{:S(2)}) collective-permute-start(f32[3,36,2,256]{3,2,1,0:T(2,128)S(1)} %pad_maximum_fusion.1), channel_id=1, source_target_pairs={{0,1},{1,2},{2,3},{4,5},{5,6},{6,7},{8,9},{9,10},{10,11},{12,13},{... | collective-permute-start | bytes 663560 | tf_op jit(solution)/shard_map/ppermute | solution.py:207
  65.1 3.2 %fusion.10 = f32[3072,256]{1,0:T(8,128)} fusion(s32[256]{0:T(256)S(1)} %get-tuple-element.303, f32[256]{0:T(256)S(1)} %bitcast.120, s32[256]{0:T(256)S(1)} %get-tuple-element.302), kind=kOutput, calls=%fused_computation.29 | convolution fusion | flops 2416836608 | bytes 3148800 | tf_op jit(solution)/shard_map/dot_general | solution.py:415
  68.4 1.6 collective-permute-done.2.ylo_ref
  70.6 5.7 %shard_map.122.rest_0_ = f32[3,32,32,256]{3,2,1,0:T(8,128)} custom-call(f32[3,32,32,256]{3,2,1,0:T(8,128)} %prev_ref.7, f32[3,2,32,256]{3,2,1,0:T(8,128)} %copy-done, f32[3,2,32,256]{3,2,1,0:T(8,128)} %copy-done.1, f32[3,36,2,256]{3,2,1,0:T(2,128)} %copy-done.9, f32[3,36,2,256]{3,2,1,0:T(2,128)} %copy-done.8, f32[3,32,32,256]{3,2,1,0:T(8,128)} %prev_ref.5, ...), custom_call_target="tpu_custom_call" | custom-call | tf_op jit(solution)/shard_map/pallas_call | solution.py:168
  76.3 1.1 fusion.83
  77.4 2.2 %collective-permute-start.4 = (f32[3,2,32,256]{3,2,1,0:T(8,128)S(1)}, f32[3,2,32,256]{3,2,1,0:T(8,128)S(1)}, u32[]{:S(2)}, u32[]{:S(2)}) collective-permute-start(f32[3,2,32,256]{3,2,1,0:T(8,128)S(1)} %get-tuple-element.268), channel_id=1, source_target_pairs={{0,4},{4,8},{8,12},{12,16},{16,20},{20,24},{24,28},{1,5},{5,9},{9,... | collective-permute-start | bytes 589832 | tf_op jit(solution)/shard_map/ppermute | solution.py:196
  79.6 4.5 %collective-permute-start.5 = (f32[3,2,32,256]{3,2,1,0:T(8,128)S(1)}, f32[3,2,32,256]{3,2,1,0:T(8,128)S(1)}, u32[]{:S(2)}, u32[]{:S(2)}) collective-permute-start(f32[3,2,32,256]{3,2,1,0:T(8,128)S(1)} %get-tuple-element.267), channel_id=1, source_target_pairs={{4,0},{8,4},{12,8},{16,12},{20,16},{24,20},{28,24},{5,1},{9,5},{13... | collective-permute-start | bytes 589832 | tf_op jit(solution)/shard_map/ppermute | solution.py:197
  84.1 11.1 %shard_map.123.u_ref.prev_ref = f32[3,32,32,256]{3,2,1,0:T(8,128)} custom-call(f32[3,32,32,256]{3,2,1,0:T(8,128)} %prev_ref.7, f32[3,2,32,256]{3,2,1,0:T(8,128)} %copy-done, f32[3,2,32,256]{3,2,1,0:T(8,128)} %copy-done.1, f32[3,36,2,256]{3,2,1,0:T(2,128)} %copy-done.9, f32[3,36,2,256]{3,2,1,0:T(2,128)} %copy-done.8, ...), custom_call_target="tpu_custom_call", output_to_operand_aliasing={{}: (8, {})} | custom-call | tf_op jit(solution)/shard_map/pallas_call | solution.py:168
  95.3 1.5 fusion.82
  97.0 1.9 collective-permute-start.7
  99.0 2.4 %collective-permute-start.6 = (f32[3,36,2,256]{3,2,1,0:T(2,128)S(1)}, f32[3,36,2,256]{3,2,1,0:T(2,128)S(1)}, u32[]{:S(2)}, u32[]{:S(2)}) collective-permute-start(f32[3,36,2,256]{3,2,1,0:T(2,128)S(1)} %pad_maximum_fusion.3), channel_id=1, source_target_pairs={{0,1},{1,2},{2,3},{4,5},{5,6},{6,7},{8,9},{9,10},{10,11},{12,13},{... | collective-permute-start | bytes 663560 | tf_op jit(solution)/shard_map/ppermute | solution.py:207
  101.4 3.2 %fusion.9 = f32[3072,256]{1,0:T(8,128)} fusion(s32[256]{0:T(256)S(1)} %get-tuple-element.303, f32[256]{0:T(256)S(1)} %bitcast.119, s32[256]{0:T(256)S(1)} %get-tuple-element.302), kind=kOutput, calls=%fused_computation.28 | convolution fusion | flops 2416836608 | bytes 3148800 | tf_op jit(solution)/shard_map/dot_general | solution.py:415
  104.7 1.6 collective-permute-done.6.ylo_ref
  107.0 5.7 %shard_map.124.rest_0_ = f32[3,32,32,256]{3,2,1,0:T(8,128)} custom-call(f32[3,32,32,256]{3,2,1,0:T(8,128)} %shard_map.123.u_ref.prev_ref, f32[3,2,32,256]{3,2,1,0:T(8,128)} %copy-done.3, f32[3,2,32,256]{3,2,1,0:T(8,128)} %copy-done.5, f32[3,36,2,256]{3,2,1,0:T(2,128)} %copy-done.14, f32[3,36,2,256]{3,2,1,0:T(2,128)} %copy-done.11, ...), custom_call_target="tpu_custom_call" | custom-call | tf_op jit(solution)/shard_map/pallas_call | solution.py:168
  113.7 1.9 collective-permute-start.8
  115.6 4.8 %collective-permute-start.9 = (f32[3,2,32,256]{3,2,1,0:T(8,128)S(1)}, f32[3,2,32,256]{3,2,1,0:T(8,128)S(1)}, u32[]{:S(2)}, u32[]{:S(2)}) collective-permute-start(f32[3,2,32,256]{3,2,1,0:T(8,128)S(1)} %get-tuple-element.263), channel_id=1, source_target_pairs={{4,0},{8,4},{12,8},{16,12},{20,16},{24,20},{28,24},{5,1},{9,5},{13... | collective-permute-start | bytes 589832 | tf_op jit(solution)/shard_map/ppermute | solution.py:197
  120.5 11.1 %shard_map.125.u_ref.prev_ref = f32[3,32,32,256]{3,2,1,0:T(8,128)} custom-call(f32[3,32,32,256]{3,2,1,0:T(8,128)} %shard_map.123.u_ref.prev_ref, f32[3,2,32,256]{3,2,1,0:T(8,128)} %copy-done.3, f32[3,2,32,256]{3,2,1,0:T(8,128)} %copy-done.5, f32[3,36,2,256]{3,2,1,0:T(2,128)} %copy-done.14, ...), custom_call_target="tpu_custom_call", output_to_operand_aliasing={{}: (8, {})} | custom-call | tf_op jit(solution)/shard_map/pallas_call | solution.py:168
  131.6 1.5 fusion.80
  133.3 1.9 collective-permute-start.11
  135.4 2.4 %collective-permute-start.10 = (f32[3,36,2,256]{3,2,1,0:T(2,128)S(1)}, f32[3,36,2,256]{3,2,1,0:T(2,128)S(1)}, u32[]{:S(2)}, u32[]{:S(2)}) collective-permute-start(f32[3,36,2,256]{3,2,1,0:T(2,128)S(1)} %pad_maximum_fusion.5), channel_id=1, source_target_pairs={{0,1},{1,2},{2,3},{4,5},{5,6},{6,7},{8,9},{9,10},{10,11},{12,13},{... | collective-permute-start | bytes 663560 | tf_op jit(solution)/shard_map/ppermute | solution.py:207
  137.8 3.2 %fusion.8 = f32[3072,256]{1,0:T(8,128)} fusion(s32[256]{0:T(256)S(1)} %get-tuple-element.303, f32[256]{0:T(256)S(1)} %bitcast.118, s32[256]{0:T(256)S(1)} %get-tuple-element.302), kind=kOutput, calls=%fused_computation.27 | convolution fusion | flops 2416836608 | bytes 3148800 | tf_op jit(solution)/shard_map/dot_general | solution.py:415
  141.0 1.6 collective-permute-done.10.ylo_ref
  143.3 5.7 %shard_map.126.rest_0_ = f32[3,32,32,256]{3,2,1,0:T(8,128)} custom-call(f32[3,32,32,256]{3,2,1,0:T(8,128)} %shard_map.125.u_ref.prev_ref, f32[3,2,32,256]{3,2,1,0:T(8,128)} %copy-done.2, f32[3,2,32,256]{3,2,1,0:T(8,128)} %copy-done.4, f32[3,36,2,256]{3,2,1,0:T(2,128)} %copy-done.13, f32[3,36,2,256]{3,2,1,0:T(2,128)} %copy-done.10, ...), custom_call_target="tpu_custom_call" | custom-call | tf_op jit(solution)/shard_map/pallas_call | solution.py:168
  150.1 1.9 collective-permute-start.12
  152.0 4.8 %collective-permute-start.13 = (f32[3,2,32,256]{3,2,1,0:T(8,128)S(1)}, f32[3,2,32,256]{3,2,1,0:T(8,128)S(1)}, u32[]{:S(2)}, u32[]{:S(2)}) collective-permute-start(f32[3,2,32,256]{3,2,1,0:T(8,128)S(1)} %get-tuple-element.259), channel_id=1, source_target_pairs={{4,0},{8,4},{12,8},{16,12},{20,16},{24,20},{28,24},{5,1},{9,5},{13... | collective-permute-start | bytes 589832 | tf_op jit(solution)/shard_map/ppermute | solution.py:197
  156.8 11.1 %shard_map.127.u_ref = f32[3,32,32,256]{3,2,1,0:T(8,128)} custom-call(f32[3,32,32,256]{3,2,1,0:T(8,128)} %shard_map.125.u_ref.prev_ref, f32[3,2,32,256]{3,2,1,0:T(8,128)} %copy-done.2, f32[3,2,32,256]{3,2,1,0:T(8,128)} %copy-done.4, f32[3,36,2,256]{3,2,1,0:T(2,128)} %copy-done.13, f32[3,36,2,256]{3,2,1,0:T(2,128)} %copy-done.10, ...), custom_call_target="tpu_custom_call", output_to_operand_aliasing={{}: (8, {})} | custom-call | tf_op jit(solution)/shard_map/pallas_call | solution.py:168
  167.9 1.5 fusion.78
  169.7 1.9 collective-permute-start.15
  171.7 2.6 %collective-permute-start.14 = (f32[3,36,2,256]{3,2,1,0:T(2,128)S(1)}, f32[3,36,2,256]{3,2,1,0:T(2,128)S(1)}, u32[]{:S(2)}, u32[]{:S(2)}) collective-permute-start(f32[3,36,2,256]{3,2,1,0:T(2,128)S(1)} %pad_maximum_fusion.7), channel_id=1, source_target_pairs={{0,1},{1,2},{2,3},{4,5},{5,6},{6,7},{8,9},{9,10},{10,11},{12,13},{... | collective-permute-start | bytes 663560 | tf_op jit(solution)/shard_map/ppermute | solution.py:207
  174.3 3.2 %fusion.7 = f32[3072,256]{1,0:T(8,128)} fusion(s32[256]{0:T(256)S(1)} %get-tuple-element.303, f32[256]{0:T(256)S(1)} %bitcast.117, s32[256]{0:T(256)S(1)} %get-tuple-element.302), kind=kOutput, calls=%fused_computation.26 | convolution fusion | flops 2416836608 | bytes 3148800 | tf_op jit(solution)/shard_map/dot_general | solution.py:415
  177.5 1.4 collective-permute-done.14.ylo_ref
  179.7 5.7 %shard_map.128.rest_0_ = f32[3,32,32,256]{3,2,1,0:T(8,128)} custom-call(f32[3,32,32,256]{3,2,1,0:T(8,128)} %shard_map.127.u_ref, f32[3,2,32,256]{3,2,1,0:T(8,128)} %copy-done.6, f32[3,2,32,256]{3,2,1,0:T(8,128)} %copy-done.7, f32[3,36,2,256]{3,2,1,0:T(2,128)} %copy-done.15, f32[3,36,2,256]{3,2,1,0:T(2,128)} %copy-done.12, ...), custom_call_target="tpu_custom_call" | custom-call | tf_op jit(solution)/shard_map/pallas_call | solution.py:168
  185.3 11.1 %shard_map.129 = f32[3,32,32,256]{3,2,1,0:T(8,128)} custom-call(f32[3,32,32,256]{3,2,1,0:T(8,128)} %shard_map.127.u_ref, f32[3,2,32,256]{3,2,1,0:T(8,128)} %copy-done.6, f32[3,2,32,256]{3,2,1,0:T(8,128)} %copy-done.7, f32[3,36,2,256]{3,2,1,0:T(2,128)} %copy-done.15, f32[3,36,2,256]{3,2,1,0:T(2,128)} %copy-done.12, ...), custom_call_target="tpu_custom_call", output_to_operand_aliasing={{}: (8, {})} | custom-call | tf_op jit(solution)/shard_map/pallas_call | solution.py:168
  (142 shorter events, 15.3 us)
Async XLA Ops:
  16.0 5.3 %copy-start.16 = (s32[8192]{0:T(1024)S(1)}, s32[8192]{0:T(1024)}, u32[]{:S(2)}) copy-start(s32[8192]{0:T(1024)} %param.19) | copy-start | bytes 98308
  16.0 5.3 %copy-start.17 = (s32[8192]{0:T(1024)S(1)}, s32[8192]{0:T(1024)}, u32[]{:S(2)}) copy-start(s32[8192]{0:T(1024)} %param.20) | copy-start | bytes 98308
  24.8 30.6 %copy-start.18 = (s32[256]{0:T(256)S(1)}, s32[256]{0:T(256)}, u32[]{:S(2)}) copy-start(s32[256]{0:T(256)} %param.21) | copy-start | bytes 3076
  39.3 25.6 %all-to-all-start = ((bf16[2,4,32,256]{3,1,0,2:T(4,128)(2,1)}), bf16[2,4,32,256]{3,1,0,2:T(4,128)(2,1)S(1)}, u32[]{:S(2)}, u32[]{:S(2)}) async-start(bf16[2,4,32,256]{3,1,0,2:T(4,128)(2,1)} %copy.31), calls=%async_computation | async-start | bytes 262144 | tf_op jit(solution)/shard_map/all_to_all | solution.py:391
  46.3 9.7 %collective-permute-start = (f32[3,2,32,256]{3,2,1,0:T(8,128)S(1)}, f32[3,2,32,256]{3,2,1,0:T(8,128)S(1)}, u32[]{:S(2)}, u32[]{:S(2)}) collective-permute-start(f32[3,2,32,256]{3,2,1,0:T(8,128)S(1)} %get-tuple-element.272), channel_id=1, source_target_pairs={{0,4},{4,8},{8,12},{12,16},{16,20},{20,24},{24,28},{1,5},{5,9},{9,... | collective-permute-start | bytes 589832 | tf_op jit(solution)/shard_map/ppermute | solution.py:196
  49.7 10.5 %collective-permute-start.1 = (f32[3,2,32,256]{3,2,1,0:T(8,128)S(1)}, f32[3,2,32,256]{3,2,1,0:T(8,128)S(1)}, u32[]{:S(2)}, u32[]{:S(2)}) collective-permute-start(f32[3,2,32,256]{3,2,1,0:T(8,128)S(1)} %get-tuple-element.271), channel_id=1, source_target_pairs={{4,0},{8,4},{12,8},{16,12},{20,16},{24,20},{28,24},{5,1},{9,5},{13... | collective-permute-start | bytes 589832 | tf_op jit(solution)/shard_map/ppermute | solution.py:197
  56.0 13.9 %copy-start = (f32[3,2,32,256]{3,2,1,0:T(8,128)}, f32[3,2,32,256]{3,2,1,0:T(8,128)S(1)}, u32[]{:S(2)}) copy-start(f32[3,2,32,256]{3,2,1,0:T(8,128)S(1)} %collective-permute-done.xlo_ref) | copy-start | bytes 589828
  60.2 9.7 %copy-start.1 = (f32[3,2,32,256]{3,2,1,0:T(8,128)}, f32[3,2,32,256]{3,2,1,0:T(8,128)S(1)}, u32[]{:S(2)}) copy-start(f32[3,2,32,256]{3,2,1,0:T(8,128)S(1)} %collective-permute-done.1.xhi_ref) | copy-start | bytes 589828
  60.4 8.0 %collective-permute-start.3 = (f32[3,36,2,256]{3,2,1,0:T(2,128)S(1)}, f32[3,36,2,256]{3,2,1,0:T(2,128)S(1)}, u32[]{:S(2)}, u32[]{:S(2)}) collective-permute-start(f32[3,36,2,256]{3,2,1,0:T(2,128)S(1)} %pad_maximum_fusion.2), channel_id=1, source_target_pairs={{1,0},{2,1},{3,2},{5,4},{6,5},{7,6},{9,8},{10,9},{11,10},{13,12},{... | collective-permute-start | bytes 663560 | tf_op jit(solution)/shard_map/ppermute | solution.py:208
  62.7 7.3 %collective-permute-start.2 = (f32[3,36,2,256]{3,2,1,0:T(2,128)S(1)}, f32[3,36,2,256]{3,2,1,0:T(2,128)S(1)}, u32[]{:S(2)}, u32[]{:S(2)}) collective-permute-start(f32[3,36,2,256]{3,2,1,0:T(2,128)S(1)} %pad_maximum_fusion.1), channel_id=1, source_target_pairs={{0,1},{1,2},{2,3},{4,5},{5,6},{6,7},{8,9},{9,10},{10,11},{12,13},{... | collective-permute-start | bytes 663560 | tf_op jit(solution)/shard_map/ppermute | solution.py:207
  68.4 1.6 copy-start.8
  69.9 0.7 copy-start.9
  77.4 19.4 %collective-permute-start.4 = (f32[3,2,32,256]{3,2,1,0:T(8,128)S(1)}, f32[3,2,32,256]{3,2,1,0:T(8,128)S(1)}, u32[]{:S(2)}, u32[]{:S(2)}) collective-permute-start(f32[3,2,32,256]{3,2,1,0:T(8,128)S(1)} %get-tuple-element.268), channel_id=1, source_target_pairs={{0,4},{4,8},{8,12},{12,16},{16,20},{20,24},{24,28},{1,5},{5,9},{9,... | collective-permute-start | bytes 589832 | tf_op jit(solution)/shard_map/ppermute | solution.py:196
  79.6 17.2 %collective-permute-start.5 = (f32[3,2,32,256]{3,2,1,0:T(8,128)S(1)}, f32[3,2,32,256]{3,2,1,0:T(8,128)S(1)}, u32[]{:S(2)}, u32[]{:S(2)}) collective-permute-start(f32[3,2,32,256]{3,2,1,0:T(8,128)S(1)} %get-tuple-element.267), channel_id=1, source_target_pairs={{4,0},{8,4},{12,8},{16,12},{20,16},{24,20},{28,24},{5,1},{9,5},{13... | collective-permute-start | bytes 589832 | tf_op jit(solution)/shard_map/ppermute | solution.py:197
  96.8 9.5 %copy-start.3 = (f32[3,2,32,256]{3,2,1,0:T(8,128)}, f32[3,2,32,256]{3,2,1,0:T(8,128)S(1)}, u32[]{:S(2)}) copy-start(f32[3,2,32,256]{3,2,1,0:T(8,128)S(1)} %collective-permute-done.4.xlo_ref) | copy-start | bytes 589828
  96.8 9.4 %copy-start.5 = (f32[3,2,32,256]{3,2,1,0:T(8,128)}, f32[3,2,32,256]{3,2,1,0:T(8,128)S(1)}, u32[]{:S(2)}) copy-start(f32[3,2,32,256]{3,2,1,0:T(8,128)S(1)} %collective-permute-done.5.xhi_ref) | copy-start | bytes 589828
  97.0 7.7 %collective-permute-start.7 = (f32[3,36,2,256]{3,2,1,0:T(2,128)S(1)}, f32[3,36,2,256]{3,2,1,0:T(2,128)S(1)}, u32[]{:S(2)}, u32[]{:S(2)}) collective-permute-start(f32[3,36,2,256]{3,2,1,0:T(2,128)S(1)} %pad_maximum_fusion.4), channel_id=1, source_target_pairs={{1,0},{2,1},{3,2},{5,4},{6,5},{7,6},{9,8},{10,9},{11,10},{13,12},{... | collective-permute-start | bytes 663560 | tf_op jit(solution)/shard_map/ppermute | solution.py:208
  99.0 7.3 %collective-permute-start.6 = (f32[3,36,2,256]{3,2,1,0:T(2,128)S(1)}, f32[3,36,2,256]{3,2,1,0:T(2,128)S(1)}, u32[]{:S(2)}, u32[]{:S(2)}) collective-permute-start(f32[3,36,2,256]{3,2,1,0:T(2,128)S(1)} %pad_maximum_fusion.3), channel_id=1, source_target_pairs={{0,1},{1,2},{2,3},{4,5},{5,6},{6,7},{8,9},{9,10},{10,11},{12,13},{... | collective-permute-start | bytes 663560 | tf_op jit(solution)/shard_map/ppermute | solution.py:207
  104.7 1.6 copy-start.11
  106.3 0.7 copy-start.14
  113.7 19.4 %collective-permute-start.8 = (f32[3,2,32,256]{3,2,1,0:T(8,128)S(1)}, f32[3,2,32,256]{3,2,1,0:T(8,128)S(1)}, u32[]{:S(2)}, u32[]{:S(2)}) collective-permute-start(f32[3,2,32,256]{3,2,1,0:T(8,128)S(1)} %get-tuple-element.264), channel_id=1, source_target_pairs={{0,4},{4,8},{8,12},{12,16},{16,20},{20,24},{24,28},{1,5},{5,9},{9,... | collective-permute-start | bytes 589832 | tf_op jit(solution)/shard_map/ppermute | solution.py:196
  115.6 17.5 %collective-permute-start.9 = (f32[3,2,32,256]{3,2,1,0:T(8,128)S(1)}, f32[3,2,32,256]{3,2,1,0:T(8,128)S(1)}, u32[]{:S(2)}, u32[]{:S(2)}) collective-permute-start(f32[3,2,32,256]{3,2,1,0:T(8,128)S(1)} %get-tuple-element.263), channel_id=1, source_target_pairs={{4,0},{8,4},{12,8},{16,12},{20,16},{24,20},{28,24},{5,1},{9,5},{13... | collective-permute-start | bytes 589832 | tf_op jit(solution)/shard_map/ppermute | solution.py:197
  133.1 9.5 %copy-start.2 = (f32[3,2,32,256]{3,2,1,0:T(8,128)}, f32[3,2,32,256]{3,2,1,0:T(8,128)S(1)}, u32[]{:S(2)}) copy-start(f32[3,2,32,256]{3,2,1,0:T(8,128)S(1)} %collective-permute-done.8.xlo_ref) | copy-start | bytes 589828
  133.2 9.4 %copy-start.4 = (f32[3,2,32,256]{3,2,1,0:T(8,128)}, f32[3,2,32,256]{3,2,1,0:T(8,128)S(1)}, u32[]{:S(2)}) copy-start(f32[3,2,32,256]{3,2,1,0:T(8,128)S(1)} %collective-permute-done.9.xhi_ref) | copy-start | bytes 589828
  133.3 7.7 %collective-permute-start.11 = (f32[3,36,2,256]{3,2,1,0:T(2,128)S(1)}, f32[3,36,2,256]{3,2,1,0:T(2,128)S(1)}, u32[]{:S(2)}, u32[]{:S(2)}) collective-permute-start(f32[3,36,2,256]{3,2,1,0:T(2,128)S(1)} %pad_maximum_fusion.6), channel_id=1, source_target_pairs={{1,0},{2,1},{3,2},{5,4},{6,5},{7,6},{9,8},{10,9},{11,10},{13,12},{... | collective-permute-start | bytes 663560 | tf_op jit(solution)/shard_map/ppermute | solution.py:208
  135.4 7.3 %collective-permute-start.10 = (f32[3,36,2,256]{3,2,1,0:T(2,128)S(1)}, f32[3,36,2,256]{3,2,1,0:T(2,128)S(1)}, u32[]{:S(2)}, u32[]{:S(2)}) collective-permute-start(f32[3,36,2,256]{3,2,1,0:T(2,128)S(1)} %pad_maximum_fusion.5), channel_id=1, source_target_pairs={{0,1},{1,2},{2,3},{4,5},{5,6},{6,7},{8,9},{9,10},{10,11},{12,13},{... | collective-permute-start | bytes 663560 | tf_op jit(solution)/shard_map/ppermute | solution.py:207
  141.0 1.6 copy-start.10
  142.6 0.7 copy-start.13
  150.1 19.4 %collective-permute-start.12 = (f32[3,2,32,256]{3,2,1,0:T(8,128)S(1)}, f32[3,2,32,256]{3,2,1,0:T(8,128)S(1)}, u32[]{:S(2)}, u32[]{:S(2)}) collective-permute-start(f32[3,2,32,256]{3,2,1,0:T(8,128)S(1)} %get-tuple-element.260), channel_id=1, source_target_pairs={{0,4},{4,8},{8,12},{12,16},{16,20},{20,24},{24,28},{1,5},{5,9},{9,... | collective-permute-start | bytes 589832 | tf_op jit(solution)/shard_map/ppermute | solution.py:196
  152.0 17.5 %collective-permute-start.13 = (f32[3,2,32,256]{3,2,1,0:T(8,128)S(1)}, f32[3,2,32,256]{3,2,1,0:T(8,128)S(1)}, u32[]{:S(2)}, u32[]{:S(2)}) collective-permute-start(f32[3,2,32,256]{3,2,1,0:T(8,128)S(1)} %get-tuple-element.259), channel_id=1, source_target_pairs={{4,0},{8,4},{12,8},{16,12},{20,16},{24,20},{28,24},{5,1},{9,5},{13... | collective-permute-start | bytes 589832 | tf_op jit(solution)/shard_map/ppermute | solution.py:197
  169.5 9.5 %copy-start.6 = (f32[3,2,32,256]{3,2,1,0:T(8,128)}, f32[3,2,32,256]{3,2,1,0:T(8,128)S(1)}, u32[]{:S(2)}) copy-start(f32[3,2,32,256]{3,2,1,0:T(8,128)S(1)} %collective-permute-done.12.xlo_ref) | copy-start | bytes 589828
  169.5 9.4 %copy-start.7 = (f32[3,2,32,256]{3,2,1,0:T(8,128)}, f32[3,2,32,256]{3,2,1,0:T(8,128)S(1)}, u32[]{:S(2)}) copy-start(f32[3,2,32,256]{3,2,1,0:T(8,128)S(1)} %collective-permute-done.13.xhi_ref) | copy-start | bytes 589828
  169.7 7.9 %collective-permute-start.15 = (f32[3,36,2,256]{3,2,1,0:T(2,128)S(1)}, f32[3,36,2,256]{3,2,1,0:T(2,128)S(1)}, u32[]{:S(2)}, u32[]{:S(2)}) collective-permute-start(f32[3,36,2,256]{3,2,1,0:T(2,128)S(1)} %pad_maximum_fusion.8), channel_id=1, source_target_pairs={{1,0},{2,1},{3,2},{5,4},{6,5},{7,6},{9,8},{10,9},{11,10},{13,12},{... | collective-permute-start | bytes 663560 | tf_op jit(solution)/shard_map/ppermute | solution.py:208
  171.7 7.3 %collective-permute-start.14 = (f32[3,36,2,256]{3,2,1,0:T(2,128)S(1)}, f32[3,36,2,256]{3,2,1,0:T(2,128)S(1)}, u32[]{:S(2)}, u32[]{:S(2)}) collective-permute-start(f32[3,36,2,256]{3,2,1,0:T(2,128)S(1)} %pad_maximum_fusion.7), channel_id=1, source_target_pairs={{0,1},{1,2},{2,3},{4,5},{5,6},{6,7},{8,9},{9,10},{10,11},{12,13},{... | collective-permute-start | bytes 663560 | tf_op jit(solution)/shard_map/ppermute | solution.py:207
  177.5 1.4 copy-start.12
  179.0 0.7 copy-start.15

commit v14 on v11

--- a/solution.py
+++ b/solution.py
@@ -134,7 +134,7 @@
     lax.fori_loop(0, bx, plane, 0)
 
 
-def elastic_step(u, xlo, xhi, ylo, yhi, prev, moduli, sources, bx=8):
+def elastic_step(u, xlo, xhi, ylo, yhi, prev, moduli, sources, bx=16):
     _, nx, ny, depth = u.shape
     kernel = functools.partial(step_kernel, bx=bx)
     block = lambda i: (0, i, 0, 0)

time: 196 us -> 199 us (1.015)
  Pallas kernels: 51.3 us -> 54.2 us
    pallas_call x4, Pallas kernels: 51.3 us -> 54.2 us  [elastic_step(): pl.pallas_call(kernel, grid=(nx // bx,), in_specs=[pl.BlockSpec(u.shape,...]
where the time goes in v14:
time: 199 us; the launch traced here: 198 us
  starting transfers between devices  55.9 us (28%)
  Pallas kernels  54.2 us (27%)
  matrix products  29.6 us (15%)
  other arithmetic  20.6 us (10%)
  waiting for transfers between devices  20.6 us (10%)
  local copies, waits for them, and re-layouts  15 us (8%)
    pallas_call x4, Pallas kernels, elastic_step(): pl.pallas_call(kernel, grid=(nx // bx,), in_specs=[pl.BlockSpec(u.shape,...  54.2 us
    ppermute x4, starting transfers between devices, halos(): xhi = lax.ppermute(block[:, :width], 'gx', backward_x)  16.3 us
    ppermute x4, starting transfers between devices, halos(): yhi = lax.ppermute(rows(slice(0, width)), 'gy', backward_y)  15.1 us
    dot_general x2, matrix products, select_block(): jnp.dot(table_rounded, offset_hot, preferred_element_type=jnp.float32)  13.1 us
    dot_general x4, matrix products, shards(): source = jnp.dot(column_hot, spread, precision=lax.Precision.HIGHEST)  12.9 us
    ppermute x4, waiting for transfers between devices, halos(): xhi = lax.ppermute(block[:, :width], 'gx', backward_x)  11.5 us
    ppermute x4, starting transfers between devices, halos(): xlo = lax.ppermute(block[:, nx - width:], 'gx', forward_x)  10.7 us
    ppermute x4, starting transfers between devices, halos(): ylo = lax.ppermute(rows(slice(ny - width, ny)), 'gy', forward_y)  7.91 us
  transfers between devices with their start and end apart: 17, of which 12 were waited for; matrix products, arithmetic and copies ran while one was open for 11% of the time, Pallas kernels for 0%

profile of v14, /device:TPU:12, one launch (start us, length us, event | category | flops | bytes accessed | tf_op | source)
XLA Modules:
  0.0 198.3 jit_solution(5689387568352931129)
XLA Ops:
  2.9 4.9 %sine_multiply_fusion.1 = (f32[32,4,1024]{2,1,0:T(4,128)S(1)}, f32[32,4,1024]{2,1,0:T(4,128)S(1)}, f32[32,4,1024]{2,1,0:T(4,128)S(1)}) fusion(f32[32]{0:T(128)S(1)} %get-tuple-element.307, f32[32,4]{1,0:T(8,128)S(1)} %copy.24, f32[1024]{0:T(1024)S(1)} %multiply_multiply_fusion, f32[1,4,1024]{2,1,0:T(4,128)S(1)} %slice.157, f32[31,4,1024]{2,1,0:T(4,128)S(1)} %slice.156, ...), kind=kLoop, calls=%fused_computation.41 | loop fusion | flops 1441792 | bytes 2102016 | tf_op jit(solution)/shard_map/mul | solution.py:195
  8.1 2.2 %while.32 = (s32[]{:T(128)}, f32[4,1024]{1,0:T(4,128)S(1)}, f32[4,1024]{1,0:T(4,128)S(1)}, f32[32,4,1024]{2,1,0:T(4,128)S(1)}, f32[32,4,1024]{2,1,0:T(4,128)S(1)...) while((s32[]{:T(128)}, f32[4,1024]{1,0:T(4,128)S(1)}, ...), condition=%wide.region_6.7_spmd.clone, body=%wide.region_5.6_spmd.clone.sunk | while | flops 94212 | bytes 147591 | solution.py:211
  11.2 4.3 %fusion.43 = (bf16[1,32,4,1024]{3,2,1,0:T(4,128)(2,1)S(1)}, bf16[1,32,4,1024]{3,2,1,0:T(4,128)(2,1)S(1)}) fusion(f32[32,4,1024]{2,1,0:T(4,128)S(1)} %get-tuple-element.191, f32[32,4,1024]{2,1,0:T(4,128)S(1)} %get-tuple-element.190, f32[32,4,1024]{2,1,0:T(4,128)S(1)} %negate_exponential_fusion, f32[32,4,1024]{2,1,0:T(4,128)S(1)} %fusion.23), kind=kLoop, calls=%fused_computation.74 | loop fusion | flops 1835008 | bytes 2621440 | tf_op jit(solution)/shard_map/stack | solution.py:224
  17.7 3.6 %subtract_convert_fusion = bf16[1024,32,64]{0,2,1:T(8,128)(2,1)} fusion(f32[1024,64]{0,1:T(8,128)S(1)} %get-tuple-element.301, f32[1024,32]{0,1:T(8,128)S(1)} %get-tuple-element.295, f32[1024,64]{0,1:T(8,128)S(1)} %get-tuple-element.300, f32[1024,32]{0,1:T(8,128)S(1)} %get-tuple-element.294), kind=kLoop, calls=%fused_computation.24 | loop fusion | flops 8388608 | bytes 4980736 | tf_op jit(solution)/shard_map/convert_element_type | solution.py:239
  21.4 3.5 %convolution_convert_fusion = bf16[256,2048]{1,0:T(8,128)(2,1)S(1)} fusion(bf16[256,1024]{1,0:T(8,128)(2,1)S(1)} %bitcast.109, bf16[1024,2048]{0,1:T(8,128)(2,1)} %bitcast.107), kind=kOutput, calls=%fused_computation.30 | convolution fusion | flops 1074266112 | bytes 5767168 | tf_op jit(solution)/shard_map/dot_general | solution.py:327
  24.9 13.4 %while.31 = (s32[]{:T(128)}, bf16[2,2,4,4096]{3,2,1,0:T(4,128)(2,1)S(1)}, s32[2,4096]{1,0:T(2,128)S(1)}, bf16[256,2048]{1,0:T(8,128)(2,1)S(1)}, s32[2,4096]{1,0:T(2,128)S(1)}, /*index=5*/s32[]{:T(128)}) while((s32[]{:T(128)}, bf16[2,2,4,4096]{3,2,1,0:T(4,128)(2,1)S(1)}, s32[2,4096]{1,0:T(2,128)S(1)}, bf16[256,2048]{1,0:T(8,128)(2,1)S(1)}, ...), condition=%wide.region_9.10_spmd, body=%wide.region_7.9_spmd.sunk | while | flops 4305682432 | bytes 2392141 | solution.py:350
  25.0 6.5 %multiply_reduce_fusion.2 = bf16[2,4,4096]{2,1,0:T(4,128)(2,1)S(1)} fusion(f32[32,4096]{1,0:T(8,128)S(1)} %fusion.102, bf16[256,2048]{1,0:T(8,128)(2,1)S(1)} %get-tuple-element.448, s32[4096]{0:T(1024)S(1)} %bitcast.111), kind=kOutput, calls=%fused_computation.3.clone.1 | convolution fusion | flops 4305420288 | bytes 1654784 | tf_op jit(solution)/shard_map/while/body/eval_jaxpr/dot_general | solution.py:342
  31.7 6.5 %multiply_reduce_fusion.2 = bf16[2,4,4096]{2,1,0:T(4,128)(2,1)S(1)} fusion(f32[32,4096]{1,0:T(8,128)S(1)} %fusion.102, bf16[256,2048]{1,0:T(8,128)(2,1)S(1)} %get-tuple-element.448, s32[4096]{0:T(1024)S(1)} %bitcast.111), kind=kOutput, calls=%fused_computation.3.clone.1 | convolution fusion | flops 4305420288 | bytes 1654784 | tf_op jit(solution)/shard_map/while/body/eval_jaxpr/dot_general | solution.py:342
  39.3 6.0 %all-to-all-start = ((bf16[2,4,32,256]{3,1,0,2:T(4,128)(2,1)}), bf16[2,4,32,256]{3,1,0,2:T(4,128)(2,1)S(1)}, u32[]{:S(2)}, u32[]{:S(2)}) async-start(bf16[2,4,32,256]{3,1,0,2:T(4,128)(2,1)} %copy.27), calls=%async_computation | async-start | bytes 262144 | tf_op jit(solution)/shard_map/all_to_all | solution.py:357
  45.3 1.1 fusion.85
  46.3 3.4 %collective-permute-start = (f32[3,2,32,256]{3,2,1,0:T(8,128)S(1)}, f32[3,2,32,256]{3,2,1,0:T(8,128)S(1)}, u32[]{:S(2)}, u32[]{:S(2)}) collective-permute-start(f32[3,2,32,256]{3,2,1,0:T(8,128)S(1)} %get-tuple-element.272), channel_id=1, source_target_pairs={{0,4},{4,8},{8,12},{12,16},{16,20},{20,24},{24,28},{1,5},{5,9},{9,... | collective-permute-start | bytes 589832 | tf_op jit(solution)/shard_map/ppermute | solution.py:168
  49.7 3.4 %collective-permute-start.1 = (f32[3,2,32,256]{3,2,1,0:T(8,128)S(1)}, f32[3,2,32,256]{3,2,1,0:T(8,128)S(1)}, u32[]{:S(2)}, u32[]{:S(2)}) collective-permute-start(f32[3,2,32,256]{3,2,1,0:T(8,128)S(1)} %get-tuple-element.271), channel_id=1, source_target_pairs={{4,0},{8,4},{12,8},{16,12},{20,16},{24,20},{28,24},{5,1},{9,5},{13... | collective-permute-start | bytes 589832 | tf_op jit(solution)/shard_map/ppermute | solution.py:169
  53.1 1.5 fusion.84
  56.0 4.2 %collective-permute-done.1.xhi_ref = f32[3,2,32,256]{3,2,1,0:T(8,128)S(1)} collective-permute-done((f32[3,2,32,256]{3,2,1,0:T(8,128)S(1)}, f32[3,2,32,256]{3,2,1,0:T(8,128)S(1)}, u32[]{:S(2)}, u32[]{:S(2)}) %collective-permute-start.1) | collective-permute-done | bytes 196640 | tf_op jit(solution)/shard_map/ppermute | solution.py:169
  60.4 2.2 %collective-permute-start.3 = (f32[3,36,2,256]{3,2,1,0:T(2,128)S(1)}, f32[3,36,2,256]{3,2,1,0:T(2,128)S(1)}, u32[]{:S(2)}, u32[]{:S(2)}) collective-permute-start(f32[3,36,2,256]{3,2,1,0:T(2,128)S(1)} %pad_maximum_fusion.2), channel_id=1, source_target_pairs={{1,0},{2,1},{3,2},{5,4},{6,5},{7,6},{9,8},{10,9},{11,10},{13,12},{... | collective-permute-start | bytes 663560 | tf_op jit(solution)/shard_map/ppermute | solution.py:174
  62.7 2.1 %collective-permute-start.2 = (f32[3,36,2,256]{3,2,1,0:T(2,128)S(1)}, f32[3,36,2,256]{3,2,1,0:T(2,128)S(1)}, u32[]{:S(2)}, u32[]{:S(2)}) collective-permute-start(f32[3,36,2,256]{3,2,1,0:T(2,128)S(1)} %pad_maximum_fusion.1), channel_id=1, source_target_pairs={{0,1},{1,2},{2,3},{4,5},{5,6},{6,7},{8,9},{9,10},{10,11},{12,13},{... | collective-permute-start | bytes 663560 | tf_op jit(solution)/shard_map/ppermute | solution.py:173
  65.1 3.2 %fusion.10 = f32[3072,256]{1,0:T(8,128)} fusion(s32[256]{0:T(256)S(1)} %get-tuple-element.303, f32[256]{0:T(256)S(1)} %bitcast.116, s32[256]{0:T(256)S(1)} %get-tuple-element.302), kind=kOutput, calls=%fused_computation.29 | convolution fusion | flops 2416836608 | bytes 3148800 | tf_op jit(solution)/shard_map/dot_general | solution.py:380
  68.4 1.6 collective-permute-done.2.ylo_ref
  70.6 13.6 %shard_map.122.u_ref.prev_ref = f32[3,32,32,256]{3,2,1,0:T(8,128)} custom-call(f32[3,32,32,256]{3,2,1,0:T(8,128)} %prev_ref.3, f32[3,2,32,256]{3,2,1,0:T(8,128)} %copy-done, f32[3,2,32,256]{3,2,1,0:T(8,128)} %copy-done.1, f32[3,36,2,256]{3,2,1,0:T(2,128)} %copy-done.9, f32[3,36,2,256]{3,2,1,0:T(2,128)} %copy-done.8, f32[3,32,32,256]{3,2,1,0:T(8,128)} %prev_ref.2, ...), custom_call_target="tpu_custom_call" | custom-call | tf_op jit(solution)/shard_map/pallas_call | solution.py:142
  84.2 1.0 fusion.83
  85.2 2.2 %collective-permute-start.4 = (f32[3,2,32,256]{3,2,1,0:T(8,128)S(1)}, f32[3,2,32,256]{3,2,1,0:T(8,128)S(1)}, u32[]{:S(2)}, u32[]{:S(2)}) collective-permute-start(f32[3,2,32,256]{3,2,1,0:T(8,128)S(1)} %get-tuple-element.268), channel_id=1, source_target_pairs={{0,4},{4,8},{8,12},{12,16},{16,20},{20,24},{24,28},{1,5},{5,9},{9,... | collective-permute-start | bytes 589832 | tf_op jit(solution)/shard_map/ppermute | solution.py:168
  87.5 4.5 %collective-permute-start.5 = (f32[3,2,32,256]{3,2,1,0:T(8,128)S(1)}, f32[3,2,32,256]{3,2,1,0:T(8,128)S(1)}, u32[]{:S(2)}, u32[]{:S(2)}) collective-permute-start(f32[3,2,32,256]{3,2,1,0:T(8,128)S(1)} %get-tuple-element.267), channel_id=1, source_target_pairs={{4,0},{8,4},{12,8},{16,12},{20,16},{24,20},{28,24},{5,1},{9,5},{13... | collective-permute-start | bytes 589832 | tf_op jit(solution)/shard_map/ppermute | solution.py:169
  92.0 1.5 fusion.82
  93.8 3.1 %collective-permute-done.5.xhi_ref = f32[3,2,32,256]{3,2,1,0:T(8,128)S(1)} collective-permute-done((f32[3,2,32,256]{3,2,1,0:T(8,128)S(1)}, f32[3,2,32,256]{3,2,1,0:T(8,128)S(1)}, u32[]{:S(2)}, u32[]{:S(2)}) %collective-permute-start.5) | collective-permute-done | bytes 196640 | tf_op jit(solution)/shard_map/ppermute | solution.py:169
  97.0 3.8 %collective-permute-start.7 = (f32[3,36,2,256]{3,2,1,0:T(2,128)S(1)}, f32[3,36,2,256]{3,2,1,0:T(2,128)S(1)}, u32[]{:S(2)}, u32[]{:S(2)}) collective-permute-start(f32[3,36,2,256]{3,2,1,0:T(2,128)S(1)} %pad_maximum_fusion.4), channel_id=1, source_target_pairs={{1,0},{2,1},{3,2},{5,4},{6,5},{7,6},{9,8},{10,9},{11,10},{13,12},{... | collective-permute-start | bytes 663560 | tf_op jit(solution)/shard_map/ppermute | solution.py:174
  100.9 1.9 collective-permute-start.6
  102.9 3.2 %fusion.9 = f32[3072,256]{1,0:T(8,128)} fusion(s32[256]{0:T(256)S(1)} %get-tuple-element.303, f32[256]{0:T(256)S(1)} %bitcast.115, s32[256]{0:T(256)S(1)} %get-tuple-element.302), kind=kOutput, calls=%fused_computation.28 | convolution fusion | flops 2416836608 | bytes 3148800 | tf_op jit(solution)/shard_map/dot_general | solution.py:380
  106.1 2.1 %collective-permute-done.6.ylo_ref = f32[3,36,2,256]{3,2,1,0:T(2,128)S(1)} collective-permute-done((f32[3,36,2,256]{3,2,1,0:T(2,128)S(1)}, f32[3,36,2,256]{3,2,1,0:T(2,128)S(1)}, u32[]{:S(2)}, u32[]{:S(2)}) %collective-permute-start.6) | collective-permute-done | bytes 221216 | tf_op jit(solution)/shard_map/ppermute | solution.py:173
  108.9 13.6 %shard_map.123.u_ref.prev_ref = f32[3,32,32,256]{3,2,1,0:T(8,128)} custom-call(f32[3,32,32,256]{3,2,1,0:T(8,128)} %shard_map.122.u_ref.prev_ref, f32[3,2,32,256]{3,2,1,0:T(8,128)} %copy-done.4, f32[3,2,32,256]{3,2,1,0:T(8,128)} %copy-done.7, f32[3,36,2,256]{3,2,1,0:T(2,128)} %copy-done.15, f32[3,36,2,256]{3,2,1,0:T(2,128)} %copy-done.12, ...), custom_call_target="tpu_custom_call" | custom-call | tf_op jit(solution)/shard_map/pallas_call | solution.py:142
  122.4 1.0 fusion.81
  123.5 2.5 %collective-permute-start.8 = (f32[3,2,32,256]{3,2,1,0:T(8,128)S(1)}, f32[3,2,32,256]{3,2,1,0:T(8,128)S(1)}, u32[]{:S(2)}, u32[]{:S(2)}) collective-permute-start(f32[3,2,32,256]{3,2,1,0:T(8,128)S(1)} %get-tuple-element.264), channel_id=1, source_target_pairs={{0,4},{4,8},{8,12},{12,16},{16,20},{20,24},{24,28},{1,5},{5,9},{9,... | collective-permute-start | bytes 589832 | tf_op jit(solution)/shard_map/ppermute | solution.py:168
  126.0 4.2 %collective-permute-start.9 = (f32[3,2,32,256]{3,2,1,0:T(8,128)S(1)}, f32[3,2,32,256]{3,2,1,0:T(8,128)S(1)}, u32[]{:S(2)}, u32[]{:S(2)}) collective-permute-start(f32[3,2,32,256]{3,2,1,0:T(8,128)S(1)} %get-tuple-element.263), channel_id=1, source_target_pairs={{4,0},{8,4},{12,8},{16,12},{20,16},{24,20},{28,24},{5,1},{9,5},{13... | collective-permute-start | bytes 589832 | tf_op jit(solution)/shard_map/ppermute | solution.py:169
  130.2 1.5 fusion.80
  132.0 2.1 %collective-permute-done.9.xhi_ref = f32[3,2,32,256]{3,2,1,0:T(8,128)S(1)} collective-permute-done((f32[3,2,32,256]{3,2,1,0:T(8,128)S(1)}, f32[3,2,32,256]{3,2,1,0:T(8,128)S(1)}, u32[]{:S(2)}, u32[]{:S(2)}) %collective-permute-start.9) | collective-permute-done | bytes 196640 | tf_op jit(solution)/shard_map/ppermute | solution.py:169
  134.2 4.6 %collective-permute-start.11 = (f32[3,36,2,256]{3,2,1,0:T(2,128)S(1)}, f32[3,36,2,256]{3,2,1,0:T(2,128)S(1)}, u32[]{:S(2)}, u32[]{:S(2)}) collective-permute-start(f32[3,36,2,256]{3,2,1,0:T(2,128)S(1)} %pad_maximum_fusion.6), channel_id=1, source_target_pairs={{1,0},{2,1},{3,2},{5,4},{6,5},{7,6},{9,8},{10,9},{11,10},{13,12},{... | collective-permute-start | bytes 663560 | tf_op jit(solution)/shard_map/ppermute | solution.py:174
  138.9 1.9 collective-permute-start.10
  140.8 3.2 %fusion.8 = f32[3072,256]{1,0:T(8,128)} fusion(s32[256]{0:T(256)S(1)} %get-tuple-element.303, f32[256]{0:T(256)S(1)} %bitcast.114, s32[256]{0:T(256)S(1)} %get-tuple-element.302), kind=kOutput, calls=%fused_computation.27 | convolution fusion | flops 2416836608 | bytes 3148800 | tf_op jit(solution)/shard_map/dot_general | solution.py:380
  144.0 2.1 %collective-permute-done.10.ylo_ref = f32[3,36,2,256]{3,2,1,0:T(2,128)S(1)} collective-permute-done((f32[3,36,2,256]{3,2,1,0:T(2,128)S(1)}, f32[3,36,2,256]{3,2,1,0:T(2,128)S(1)}, u32[]{:S(2)}, u32[]{:S(2)}) %collective-permute-start.10) | collective-permute-done | bytes 221216 | tf_op jit(solution)/shard_map/ppermute | solution.py:173
  146.8 13.5 %shard_map.124.u_ref = f32[3,32,32,256]{3,2,1,0:T(8,128)} custom-call(f32[3,32,32,256]{3,2,1,0:T(8,128)} %shard_map.123.u_ref.prev_ref, f32[3,2,32,256]{3,2,1,0:T(8,128)} %copy-done.3, f32[3,2,32,256]{3,2,1,0:T(8,128)} %copy-done.6, f32[3,36,2,256]{3,2,1,0:T(2,128)} %copy-done.14, f32[3,36,2,256]{3,2,1,0:T(2,128)} %copy-done.11, ...), custom_call_target="tpu_custom_call" | custom-call | tf_op jit(solution)/shard_map/pallas_call | solution.py:142
  161.4 2.5 %collective-permute-start.12 = (f32[3,2,32,256]{3,2,1,0:T(8,128)S(1)}, f32[3,2,32,256]{3,2,1,0:T(8,128)S(1)}, u32[]{:S(2)}, u32[]{:S(2)}) collective-permute-start(f32[3,2,32,256]{3,2,1,0:T(8,128)S(1)} %get-tuple-element.260), channel_id=1, source_target_pairs={{0,4},{4,8},{8,12},{12,16},{16,20},{20,24},{24,28},{1,5},{5,9},{9,... | collective-permute-start | bytes 589832 | tf_op jit(solution)/shard_map/ppermute | solution.py:168
  163.9 4.3 %collective-permute-start.13 = (f32[3,2,32,256]{3,2,1,0:T(8,128)S(1)}, f32[3,2,32,256]{3,2,1,0:T(8,128)S(1)}, u32[]{:S(2)}, u32[]{:S(2)}) collective-permute-start(f32[3,2,32,256]{3,2,1,0:T(8,128)S(1)} %get-tuple-element.259), channel_id=1, source_target_pairs={{4,0},{8,4},{12,8},{16,12},{20,16},{24,20},{28,24},{5,1},{9,5},{13... | collective-permute-start | bytes 589832 | tf_op jit(solution)/shard_map/ppermute | solution.py:169
  168.2 1.5 fusion.78
  169.9 2.1 %collective-permute-done.13.xhi_ref = f32[3,2,32,256]{3,2,1,0:T(8,128)S(1)} collective-permute-done((f32[3,2,32,256]{3,2,1,0:T(8,128)S(1)}, f32[3,2,32,256]{3,2,1,0:T(8,128)S(1)}, u32[]{:S(2)}, u32[]{:S(2)}) %collective-permute-start.13) | collective-permute-done | bytes 196640 | tf_op jit(solution)/shard_map/ppermute | solution.py:169
  172.1 4.6 %collective-permute-start.15 = (f32[3,36,2,256]{3,2,1,0:T(2,128)S(1)}, f32[3,36,2,256]{3,2,1,0:T(2,128)S(1)}, u32[]{:S(2)}, u32[]{:S(2)}) collective-permute-start(f32[3,36,2,256]{3,2,1,0:T(2,128)S(1)} %pad_maximum_fusion.8), channel_id=1, source_target_pairs={{1,0},{2,1},{3,2},{5,4},{6,5},{7,6},{9,8},{10,9},{11,10},{13,12},{... | collective-permute-start | bytes 663560 | tf_op jit(solution)/shard_map/ppermute | solution.py:174
  176.8 1.9 collective-permute-start.14
  178.7 3.2 %fusion.7 = f32[3072,256]{1,0:T(8,128)} fusion(s32[256]{0:T(256)S(1)} %get-tuple-element.303, f32[256]{0:T(256)S(1)} %bitcast.113, s32[256]{0:T(256)S(1)} %get-tuple-element.302), kind=kOutput, calls=%fused_computation.26 | convolution fusion | flops 2416836608 | bytes 3148800 | tf_op jit(solution)/shard_map/dot_general | solution.py:380
  182.0 2.1 %collective-permute-done.14.ylo_ref = f32[3,36,2,256]{3,2,1,0:T(2,128)S(1)} collective-permute-done((f32[3,36,2,256]{3,2,1,0:T(2,128)S(1)}, f32[3,36,2,256]{3,2,1,0:T(2,128)S(1)}, u32[]{:S(2)}, u32[]{:S(2)}) %collective-permute-start.14) | collective-permute-done | bytes 221216 | tf_op jit(solution)/shard_map/ppermute | solution.py:173
  184.8 13.5 %shard_map.125 = f32[3,32,32,256]{3,2,1,0:T(8,128)} custom-call(f32[3,32,32,256]{3,2,1,0:T(8,128)} %shard_map.124.u_ref, f32[3,2,32,256]{3,2,1,0:T(8,128)} %copy-done.2, f32[3,2,32,256]{3,2,1,0:T(8,128)} %copy-done.5, f32[3,36,2,256]{3,2,1,0:T(2,128)} %copy-done.13, f32[3,36,2,256]{3,2,1,0:T(2,128)} %copy-done.10, ...), custom_call_target="tpu_custom_call" | custom-call | tf_op jit(solution)/shard_map/pallas_call | solution.py:142
  (138 shorter events, 14.9 us)
Async XLA Ops:
  16.0 5.3 %copy-start.16 = (s32[8192]{0:T(1024)S(1)}, s32[8192]{0:T(1024)}, u32[]{:S(2)}) copy-start(s32[8192]{0:T(1024)} %param.19) | copy-start | bytes 98308
  16.0 5.3 %copy-start.17 = (s32[8192]{0:T(1024)S(1)}, s32[8192]{0:T(1024)}, u32[]{:S(2)}) copy-start(s32[8192]{0:T(1024)} %param.20) | copy-start | bytes 98308
  24.8 30.6 %copy-start.18 = (s32[256]{0:T(256)S(1)}, s32[256]{0:T(256)}, u32[]{:S(2)}) copy-start(s32[256]{0:T(256)} %param.21) | copy-start | bytes 3076
  39.3 25.6 %all-to-all-start = ((bf16[2,4,32,256]{3,1,0,2:T(4,128)(2,1)}), bf16[2,4,32,256]{3,1,0,2:T(4,128)(2,1)S(1)}, u32[]{:S(2)}, u32[]{:S(2)}) async-start(bf16[2,4,32,256]{3,1,0,2:T(4,128)(2,1)} %copy.27), calls=%async_computation | async-start | bytes 262144 | tf_op jit(solution)/shard_map/all_to_all | solution.py:357
  46.3 9.7 %collective-permute-start = (f32[3,2,32,256]{3,2,1,0:T(8,128)S(1)}, f32[3,2,32,256]{3,2,1,0:T(8,128)S(1)}, u32[]{:S(2)}, u32[]{:S(2)}) collective-permute-start(f32[3,2,32,256]{3,2,1,0:T(8,128)S(1)} %get-tuple-element.272), channel_id=1, source_target_pairs={{0,4},{4,8},{8,12},{12,16},{16,20},{20,24},{24,28},{1,5},{5,9},{9,... | collective-permute-start | bytes 589832 | tf_op jit(solution)/shard_map/ppermute | solution.py:168
  49.7 10.5 %collective-permute-start.1 = (f32[3,2,32,256]{3,2,1,0:T(8,128)S(1)}, f32[3,2,32,256]{3,2,1,0:T(8,128)S(1)}, u32[]{:S(2)}, u32[]{:S(2)}) collective-permute-start(f32[3,2,32,256]{3,2,1,0:T(8,128)S(1)} %get-tuple-element.271), channel_id=1, source_target_pairs={{4,0},{8,4},{12,8},{16,12},{20,16},{24,20},{28,24},{5,1},{9,5},{13... | collective-permute-start | bytes 589832 | tf_op jit(solution)/shard_map/ppermute | solution.py:169
  56.0 13.9 %copy-start = (f32[3,2,32,256]{3,2,1,0:T(8,128)}, f32[3,2,32,256]{3,2,1,0:T(8,128)S(1)}, u32[]{:S(2)}) copy-start(f32[3,2,32,256]{3,2,1,0:T(8,128)S(1)} %collective-permute-done.xlo_ref) | copy-start | bytes 589828
  60.2 9.7 %copy-start.1 = (f32[3,2,32,256]{3,2,1,0:T(8,128)}, f32[3,2,32,256]{3,2,1,0:T(8,128)S(1)}, u32[]{:S(2)}) copy-start(f32[3,2,32,256]{3,2,1,0:T(8,128)S(1)} %collective-permute-done.1.xhi_ref) | copy-start | bytes 589828
  60.4 8.0 %collective-permute-start.3 = (f32[3,36,2,256]{3,2,1,0:T(2,128)S(1)}, f32[3,36,2,256]{3,2,1,0:T(2,128)S(1)}, u32[]{:S(2)}, u32[]{:S(2)}) collective-permute-start(f32[3,36,2,256]{3,2,1,0:T(2,128)S(1)} %pad_maximum_fusion.2), channel_id=1, source_target_pairs={{1,0},{2,1},{3,2},{5,4},{6,5},{7,6},{9,8},{10,9},{11,10},{13,12},{... | collective-permute-start | bytes 663560 | tf_op jit(solution)/shard_map/ppermute | solution.py:174
  62.7 7.3 %collective-permute-start.2 = (f32[3,36,2,256]{3,2,1,0:T(2,128)S(1)}, f32[3,36,2,256]{3,2,1,0:T(2,128)S(1)}, u32[]{:S(2)}, u32[]{:S(2)}) collective-permute-start(f32[3,36,2,256]{3,2,1,0:T(2,128)S(1)} %pad_maximum_fusion.1), channel_id=1, source_target_pairs={{0,1},{1,2},{2,3},{4,5},{5,6},{6,7},{8,9},{9,10},{10,11},{12,13},{... | collective-permute-start | bytes 663560 | tf_op jit(solution)/shard_map/ppermute | solution.py:173
  68.4 1.6 copy-start.8
  69.9 0.7 copy-start.9
  85.2 8.6 %collective-permute-start.4 = (f32[3,2,32,256]{3,2,1,0:T(8,128)S(1)}, f32[3,2,32,256]{3,2,1,0:T(8,128)S(1)}, u32[]{:S(2)}, u32[]{:S(2)}) collective-permute-start(f32[3,2,32,256]{3,2,1,0:T(8,128)S(1)} %get-tuple-element.268), channel_id=1, source_target_pairs={{0,4},{4,8},{8,12},{12,16},{16,20},{20,24},{24,28},{1,5},{5,9},{9,... | collective-permute-start | bytes 589832 | tf_op jit(solution)/shard_map/ppermute | solution.py:168
  87.5 9.4 %collective-permute-start.5 = (f32[3,2,32,256]{3,2,1,0:T(8,128)S(1)}, f32[3,2,32,256]{3,2,1,0:T(8,128)S(1)}, u32[]{:S(2)}, u32[]{:S(2)}) collective-permute-start(f32[3,2,32,256]{3,2,1,0:T(8,128)S(1)} %get-tuple-element.267), channel_id=1, source_target_pairs={{4,0},{8,4},{12,8},{16,12},{20,16},{24,20},{28,24},{5,1},{9,5},{13... | collective-permute-start | bytes 589832 | tf_op jit(solution)/shard_map/ppermute | solution.py:169
  93.8 14.4 %copy-start.4 = (f32[3,2,32,256]{3,2,1,0:T(8,128)}, f32[3,2,32,256]{3,2,1,0:T(8,128)S(1)}, u32[]{:S(2)}) copy-start(f32[3,2,32,256]{3,2,1,0:T(8,128)S(1)} %collective-permute-done.4.xlo_ref) | copy-start | bytes 589828
  96.9 11.3 %copy-start.7 = (f32[3,2,32,256]{3,2,1,0:T(8,128)}, f32[3,2,32,256]{3,2,1,0:T(8,128)S(1)}, u32[]{:S(2)}) copy-start(f32[3,2,32,256]{3,2,1,0:T(8,128)S(1)} %collective-permute-done.5.xhi_ref) | copy-start | bytes 589828
  97.0 9.0 %collective-permute-start.7 = (f32[3,36,2,256]{3,2,1,0:T(2,128)S(1)}, f32[3,36,2,256]{3,2,1,0:T(2,128)S(1)}, u32[]{:S(2)}, u32[]{:S(2)}) collective-permute-start(f32[3,36,2,256]{3,2,1,0:T(2,128)S(1)} %pad_maximum_fusion.4), channel_id=1, source_target_pairs={{1,0},{2,1},{3,2},{5,4},{6,5},{7,6},{9,8},{10,9},{11,10},{13,12},{... | collective-permute-start | bytes 663560 | tf_op jit(solution)/shard_map/ppermute | solution.py:174
  100.9 7.3 %collective-permute-start.6 = (f32[3,36,2,256]{3,2,1,0:T(2,128)S(1)}, f32[3,36,2,256]{3,2,1,0:T(2,128)S(1)}, u32[]{:S(2)}, u32[]{:S(2)}) collective-permute-start(f32[3,36,2,256]{3,2,1,0:T(2,128)S(1)} %pad_maximum_fusion.3), channel_id=1, source_target_pairs={{0,1},{1,2},{2,3},{4,5},{5,6},{6,7},{8,9},{9,10},{10,11},{12,13},{... | collective-permute-start | bytes 663560 | tf_op jit(solution)/shard_map/ppermute | solution.py:173
  106.1 2.1 %copy-start.12 = (f32[3,36,2,256]{3,2,1,0:T(2,128)}, f32[3,36,2,256]{3,2,1,0:T(2,128)S(1)}, u32[]{:S(2)}) copy-start(f32[3,36,2,256]{3,2,1,0:T(2,128)S(1)} %collective-permute-done.7.yhi_ref) | copy-start | bytes 663556
  108.2 0.7 copy-start.15
  123.5 8.5 %collective-permute-start.8 = (f32[3,2,32,256]{3,2,1,0:T(8,128)S(1)}, f32[3,2,32,256]{3,2,1,0:T(8,128)S(1)}, u32[]{:S(2)}, u32[]{:S(2)}) collective-permute-start(f32[3,2,32,256]{3,2,1,0:T(8,128)S(1)} %get-tuple-element.264), channel_id=1, source_target_pairs={{0,4},{4,8},{8,12},{12,16},{16,20},{20,24},{24,28},{1,5},{5,9},{9,... | collective-permute-start | bytes 589832 | tf_op jit(solution)/shard_map/ppermute | solution.py:168
  126.0 8.0 %collective-permute-start.9 = (f32[3,2,32,256]{3,2,1,0:T(8,128)S(1)}, f32[3,2,32,256]{3,2,1,0:T(8,128)S(1)}, u32[]{:S(2)}, u32[]{:S(2)}) collective-permute-start(f32[3,2,32,256]{3,2,1,0:T(8,128)S(1)} %get-tuple-element.263), channel_id=1, source_target_pairs={{4,0},{8,4},{12,8},{16,12},{20,16},{24,20},{28,24},{5,1},{9,5},{13... | collective-permute-start | bytes 589832 | tf_op jit(solution)/shard_map/ppermute | solution.py:169
  132.0 14.2 %copy-start.3 = (f32[3,2,32,256]{3,2,1,0:T(8,128)}, f32[3,2,32,256]{3,2,1,0:T(8,128)S(1)}, u32[]{:S(2)}) copy-start(f32[3,2,32,256]{3,2,1,0:T(8,128)S(1)} %collective-permute-done.8.xlo_ref) | copy-start | bytes 589828
  134.1 12.1 %copy-start.6 = (f32[3,2,32,256]{3,2,1,0:T(8,128)}, f32[3,2,32,256]{3,2,1,0:T(8,128)S(1)}, u32[]{:S(2)}) copy-start(f32[3,2,32,256]{3,2,1,0:T(8,128)S(1)} %collective-permute-done.9.xhi_ref) | copy-start | bytes 589828
  134.2 9.8 %collective-permute-start.11 = (f32[3,36,2,256]{3,2,1,0:T(2,128)S(1)}, f32[3,36,2,256]{3,2,1,0:T(2,128)S(1)}, u32[]{:S(2)}, u32[]{:S(2)}) collective-permute-start(f32[3,36,2,256]{3,2,1,0:T(2,128)S(1)} %pad_maximum_fusion.6), channel_id=1, source_target_pairs={{1,0},{2,1},{3,2},{5,4},{6,5},{7,6},{9,8},{10,9},{11,10},{13,12},{... | collective-permute-start | bytes 663560 | tf_op jit(solution)/shard_map/ppermute | solution.py:174
  138.9 7.3 %collective-permute-start.10 = (f32[3,36,2,256]{3,2,1,0:T(2,128)S(1)}, f32[3,36,2,256]{3,2,1,0:T(2,128)S(1)}, u32[]{:S(2)}, u32[]{:S(2)}) collective-permute-start(f32[3,36,2,256]{3,2,1,0:T(2,128)S(1)} %pad_maximum_fusion.5), channel_id=1, source_target_pairs={{0,1},{1,2},{2,3},{4,5},{5,6},{6,7},{8,9},{9,10},{10,11},{12,13},{... | collective-permute-start | bytes 663560 | tf_op jit(solution)/shard_map/ppermute | solution.py:173
  144.0 2.1 %copy-start.11 = (f32[3,36,2,256]{3,2,1,0:T(2,128)}, f32[3,36,2,256]{3,2,1,0:T(2,128)S(1)}, u32[]{:S(2)}) copy-start(f32[3,36,2,256]{3,2,1,0:T(2,128)S(1)} %collective-permute-done.11.yhi_ref) | copy-start | bytes 663556
  146.1 0.7 copy-start.14
  161.4 8.5 %collective-permute-start.12 = (f32[3,2,32,256]{3,2,1,0:T(8,128)S(1)}, f32[3,2,32,256]{3,2,1,0:T(8,128)S(1)}, u32[]{:S(2)}, u32[]{:S(2)}) collective-permute-start(f32[3,2,32,256]{3,2,1,0:T(8,128)S(1)} %get-tuple-element.260), channel_id=1, source_target_pairs={{0,4},{4,8},{8,12},{12,16},{16,20},{20,24},{24,28},{1,5},{5,9},{9,... | collective-permute-start | bytes 589832 | tf_op jit(solution)/shard_map/ppermute | solution.py:168
  163.9 8.1 %collective-permute-start.13 = (f32[3,2,32,256]{3,2,1,0:T(8,128)S(1)}, f32[3,2,32,256]{3,2,1,0:T(8,128)S(1)}, u32[]{:S(2)}, u32[]{:S(2)}) collective-permute-start(f32[3,2,32,256]{3,2,1,0:T(8,128)S(1)} %get-tuple-element.259), channel_id=1, source_target_pairs={{4,0},{8,4},{12,8},{16,12},{20,16},{24,20},{28,24},{5,1},{9,5},{13... | collective-permute-start | bytes 589832 | tf_op jit(solution)/shard_map/ppermute | solution.py:169
  169.9 14.2 %copy-start.2 = (f32[3,2,32,256]{3,2,1,0:T(8,128)}, f32[3,2,32,256]{3,2,1,0:T(8,128)S(1)}, u32[]{:S(2)}) copy-start(f32[3,2,32,256]{3,2,1,0:T(8,128)S(1)} %collective-permute-done.12.xlo_ref) | copy-start | bytes 589828
  172.0 12.1 %copy-start.5 = (f32[3,2,32,256]{3,2,1,0:T(8,128)}, f32[3,2,32,256]{3,2,1,0:T(8,128)S(1)}, u32[]{:S(2)}) copy-start(f32[3,2,32,256]{3,2,1,0:T(8,128)S(1)} %collective-permute-done.13.xhi_ref) | copy-start | bytes 589828
  172.1 9.8 %collective-permute-start.15 = (f32[3,36,2,256]{3,2,1,0:T(2,128)S(1)}, f32[3,36,2,256]{3,2,1,0:T(2,128)S(1)}, u32[]{:S(2)}, u32[]{:S(2)}) collective-permute-start(f32[3,36,2,256]{3,2,1,0:T(2,128)S(1)} %pad_maximum_fusion.8), channel_id=1, source_target_pairs={{1,0},{2,1},{3,2},{5,4},{6,5},{7,6},{9,8},{10,9},{11,10},{13,12},{... | collective-permute-start | bytes 663560 | tf_op jit(solution)/shard_map/ppermute | solution.py:174
  176.8 7.3 %collective-permute-start.14 = (f32[3,36,2,256]{3,2,1,0:T(2,128)S(1)}, f32[3,36,2,256]{3,2,1,0:T(2,128)S(1)}, u32[]{:S(2)}, u32[]{:S(2)}) collective-permute-start(f32[3,36,2,256]{3,2,1,0:T(2,128)S(1)} %pad_maximum_fusion.7), channel_id=1, source_target_pairs={{0,1},{1,2},{2,3},{4,5},{5,6},{6,7},{8,9},{9,10},{10,11},{12,13},{... | collective-permute-start | bytes 663560 | tf_op jit(solution)/shard_map/ppermute | solution.py:173
  182.0 2.1 %copy-start.10 = (f32[3,36,2,256]{3,2,1,0:T(2,128)}, f32[3,36,2,256]{3,2,1,0:T(2,128)S(1)}, u32[]{:S(2)}) copy-start(f32[3,36,2,256]{3,2,1,0:T(2,128)S(1)} %collective-permute-done.15.yhi_ref) | copy-start | bytes 663556
  184.1 0.7 copy-start.13

commit v15 on v14

--- a/solution.py
+++ b/solution.py
@@ -134,7 +134,7 @@
     lax.fori_loop(0, bx, plane, 0)
 
 
-def elastic_step(u, xlo, xhi, ylo, yhi, prev, moduli, sources, bx=16):
+def elastic_step(u, xlo, xhi, ylo, yhi, prev, moduli, sources, bx=4):
     _, nx, ny, depth = u.shape
     kernel = functools.partial(step_kernel, bx=bx)
     block = lambda i: (0, i, 0, 0)

time: 199 us -> 199 us (level)
  no operation moved by 1% of the time
where the time goes in v15:
time: 199 us; the launch traced here: 198 us
  starting transfers between devices  55.9 us (28%)
  Pallas kernels  53.5 us (27%)
  matrix products  29.6 us (15%)
  other arithmetic  20.6 us (10%)
  waiting for transfers between devices  20.6 us (10%)
  local copies, waits for them, and re-layouts  15 us (8%)
    pallas_call x4, Pallas kernels, elastic_step(): pl.pallas_call(kernel, grid=(nx // bx,), in_specs=[pl.BlockSpec(u.shape,...  53.5 us
    ppermute x4, starting transfers between devices, halos(): xhi = lax.ppermute(block[:, :width], 'gx', backward_x)  16.3 us
    ppermute x4, starting transfers between devices, halos(): yhi = lax.ppermute(rows(slice(0, width)), 'gy', backward_y)  15.1 us
    dot_general x2, matrix products, select_block(): jnp.dot(table_rounded, offset_hot, preferred_element_type=jnp.float32)  13.1 us
    dot_general x4, matrix products, shards(): source = jnp.dot(column_hot, spread, precision=lax.Precision.HIGHEST)  12.9 us
    ppermute x4, waiting for transfers between devices, halos(): xhi = lax.ppermute(block[:, :width], 'gx', backward_x)  11.5 us
    ppermute x4, starting transfers between devices, halos(): xlo = lax.ppermute(block[:, nx - width:], 'gx', forward_x)  10.7 us
    ppermute x4, starting transfers between devices, halos(): ylo = lax.ppermute(rows(slice(ny - width, ny)), 'gy', forward_y)  7.91 us
  transfers between devices with their start and end apart: 17, of which 12 were waited for; matrix products, arithmetic and copies ran while one was open for 11% of the time, Pallas kernels for 0%

profile of v15, /device:TPU:12, one launch (start us, length us, event | category | flops | bytes accessed | tf_op | source)
XLA Modules:
  0.0 197.6 jit_solution(9301343322673296719)
XLA Ops:
  2.9 4.9 %sine_multiply_fusion.1 = (f32[32,4,1024]{2,1,0:T(4,128)S(1)}, f32[32,4,1024]{2,1,0:T(4,128)S(1)}, f32[32,4,1024]{2,1,0:T(4,128)S(1)}) fusion(f32[32]{0:T(128)S(1)} %get-tuple-element.307, f32[32,4]{1,0:T(8,128)S(1)} %copy.24, f32[1024]{0:T(1024)S(1)} %multiply_multiply_fusion, f32[1,4,1024]{2,1,0:T(4,128)S(1)} %slice.157, f32[31,4,1024]{2,1,0:T(4,128)S(1)} %slice.156, ...), kind=kLoop, calls=%fused_computation.41 | loop fusion | flops 1441792 | bytes 2102016 | tf_op jit(solution)/shard_map/mul | solution.py:195
  8.1 2.2 %while.32 = (s32[]{:T(128)}, f32[4,1024]{1,0:T(4,128)S(1)}, f32[4,1024]{1,0:T(4,128)S(1)}, f32[32,4,1024]{2,1,0:T(4,128)S(1)}, f32[32,4,1024]{2,1,0:T(4,128)S(1)...) while((s32[]{:T(128)}, f32[4,1024]{1,0:T(4,128)S(1)}, ...), condition=%wide.region_6.7_spmd.clone, body=%wide.region_5.6_spmd.clone.sunk | while | flops 94212 | bytes 147591 | solution.py:211
  11.2 4.3 %fusion.43 = (bf16[1,32,4,1024]{3,2,1,0:T(4,128)(2,1)S(1)}, bf16[1,32,4,1024]{3,2,1,0:T(4,128)(2,1)S(1)}) fusion(f32[32,4,1024]{2,1,0:T(4,128)S(1)} %get-tuple-element.191, f32[32,4,1024]{2,1,0:T(4,128)S(1)} %get-tuple-element.190, f32[32,4,1024]{2,1,0:T(4,128)S(1)} %negate_exponential_fusion, f32[32,4,1024]{2,1,0:T(4,128)S(1)} %fusion.23), kind=kLoop, calls=%fused_computation.74 | loop fusion | flops 1835008 | bytes 2621440 | tf_op jit(solution)/shard_map/stack | solution.py:224
  17.7 3.6 %subtract_convert_fusion = bf16[1024,32,64]{0,2,1:T(8,128)(2,1)} fusion(f32[1024,64]{0,1:T(8,128)S(1)} %get-tuple-element.301, f32[1024,32]{0,1:T(8,128)S(1)} %get-tuple-element.295, f32[1024,64]{0,1:T(8,128)S(1)} %get-tuple-element.300, f32[1024,32]{0,1:T(8,128)S(1)} %get-tuple-element.294), kind=kLoop, calls=%fused_computation.24 | loop fusion | flops 8388608 | bytes 4980736 | tf_op jit(solution)/shard_map/convert_element_type | solution.py:239
  21.4 3.5 %convolution_convert_fusion = bf16[256,2048]{1,0:T(8,128)(2,1)S(1)} fusion(bf16[256,1024]{1,0:T(8,128)(2,1)S(1)} %bitcast.109, bf16[1024,2048]{0,1:T(8,128)(2,1)} %bitcast.107), kind=kOutput, calls=%fused_computation.30 | convolution fusion | flops 1074266112 | bytes 5767168 | tf_op jit(solution)/shard_map/dot_general | solution.py:327
  24.9 13.4 %while.31 = (s32[]{:T(128)}, bf16[2,2,4,4096]{3,2,1,0:T(4,128)(2,1)S(1)}, s32[2,4096]{1,0:T(2,128)S(1)}, bf16[256,2048]{1,0:T(8,128)(2,1)S(1)}, s32[2,4096]{1,0:T(2,128)S(1)}, /*index=5*/s32[]{:T(128)}) while((s32[]{:T(128)}, bf16[2,2,4,4096]{3,2,1,0:T(4,128)(2,1)S(1)}, s32[2,4096]{1,0:T(2,128)S(1)}, bf16[256,2048]{1,0:T(8,128)(2,1)S(1)}, ...), condition=%wide.region_9.10_spmd, body=%wide.region_7.9_spmd.sunk | while | flops 4305682432 | bytes 2392141 | solution.py:350
  25.0 6.5 %multiply_reduce_fusion.2 = bf16[2,4,4096]{2,1,0:T(4,128)(2,1)S(1)} fusion(f32[32,4096]{1,0:T(8,128)S(1)} %fusion.102, bf16[256,2048]{1,0:T(8,128)(2,1)S(1)} %get-tuple-element.448, s32[4096]{0:T(1024)S(1)} %bitcast.111), kind=kOutput, calls=%fused_computation.3.clone.1 | convolution fusion | flops 4305420288 | bytes 1654784 | tf_op jit(solution)/shard_map/while/body/eval_jaxpr/dot_general | solution.py:342
  31.7 6.5 %multiply_reduce_fusion.2 = bf16[2,4,4096]{2,1,0:T(4,128)(2,1)S(1)} fusion(f32[32,4096]{1,0:T(8,128)S(1)} %fusion.102, bf16[256,2048]{1,0:T(8,128)(2,1)S(1)} %get-tuple-element.448, s32[4096]{0:T(1024)S(1)} %bitcast.111), kind=kOutput, calls=%fused_computation.3.clone.1 | convolution fusion | flops 4305420288 | bytes 1654784 | tf_op jit(solution)/shard_map/while/body/eval_jaxpr/dot_general | solution.py:342
  39.3 6.0 %all-to-all-start = ((bf16[2,4,32,256]{3,1,0,2:T(4,128)(2,1)}), bf16[2,4,32,256]{3,1,0,2:T(4,128)(2,1)S(1)}, u32[]{:S(2)}, u32[]{:S(2)}) async-start(bf16[2,4,32,256]{3,1,0,2:T(4,128)(2,1)} %copy.27), calls=%async_computation | async-start | bytes 262144 | tf_op jit(solution)/shard_map/all_to_all | solution.py:357
  45.3 1.1 fusion.85
  46.3 3.4 %collective-permute-start = (f32[3,2,32,256]{3,2,1,0:T(8,128)S(1)}, f32[3,2,32,256]{3,2,1,0:T(8,128)S(1)}, u32[]{:S(2)}, u32[]{:S(2)}) collective-permute-start(f32[3,2,32,256]{3,2,1,0:T(8,128)S(1)} %get-tuple-element.272), channel_id=1, source_target_pairs={{0,4},{4,8},{8,12},{12,16},{16,20},{20,24},{24,28},{1,5},{5,9},{9,... | collective-permute-start | bytes 589832 | tf_op jit(solution)/shard_map/ppermute | solution.py:168
  49.7 3.4 %collective-permute-start.1 = (f32[3,2,32,256]{3,2,1,0:T(8,128)S(1)}, f32[3,2,32,256]{3,2,1,0:T(8,128)S(1)}, u32[]{:S(2)}, u32[]{:S(2)}) collective-permute-start(f32[3,2,32,256]{3,2,1,0:T(8,128)S(1)} %get-tuple-element.271), channel_id=1, source_target_pairs={{4,0},{8,4},{12,8},{16,12},{20,16},{24,20},{28,24},{5,1},{9,5},{13... | collective-permute-start | bytes 589832 | tf_op jit(solution)/shard_map/ppermute | solution.py:169
  53.1 1.5 fusion.84
  56.0 4.2 %collective-permute-done.1.xhi_ref = f32[3,2,32,256]{3,2,1,0:T(8,128)S(1)} collective-permute-done((f32[3,2,32,256]{3,2,1,0:T(8,128)S(1)}, f32[3,2,32,256]{3,2,1,0:T(8,128)S(1)}, u32[]{:S(2)}, u32[]{:S(2)}) %collective-permute-start.1) | collective-permute-done | bytes 196640 | tf_op jit(solution)/shard_map/ppermute | solution.py:169
  60.4 2.2 %collective-permute-start.3 = (f32[3,36,2,256]{3,2,1,0:T(2,128)S(1)}, f32[3,36,2,256]{3,2,1,0:T(2,128)S(1)}, u32[]{:S(2)}, u32[]{:S(2)}) collective-permute-start(f32[3,36,2,256]{3,2,1,0:T(2,128)S(1)} %pad_maximum_fusion.2), channel_id=1, source_target_pairs={{1,0},{2,1},{3,2},{5,4},{6,5},{7,6},{9,8},{10,9},{11,10},{13,12},{... | collective-permute-start | bytes 663560 | tf_op jit(solution)/shard_map/ppermute | solution.py:174
  62.7 2.1 %collective-permute-start.2 = (f32[3,36,2,256]{3,2,1,0:T(2,128)S(1)}, f32[3,36,2,256]{3,2,1,0:T(2,128)S(1)}, u32[]{:S(2)}, u32[]{:S(2)}) collective-permute-start(f32[3,36,2,256]{3,2,1,0:T(2,128)S(1)} %pad_maximum_fusion.1), channel_id=1, source_target_pairs={{0,1},{1,2},{2,3},{4,5},{5,6},{6,7},{8,9},{9,10},{10,11},{12,13},{... | collective-permute-start | bytes 663560 | tf_op jit(solution)/shard_map/ppermute | solution.py:173
  65.1 3.2 %fusion.10 = f32[3072,256]{1,0:T(8,128)} fusion(s32[256]{0:T(256)S(1)} %get-tuple-element.303, f32[256]{0:T(256)S(1)} %bitcast.116, s32[256]{0:T(256)S(1)} %get-tuple-element.302), kind=kOutput, calls=%fused_computation.29 | convolution fusion | flops 2416836608 | bytes 3148800 | tf_op jit(solution)/shard_map/dot_general | solution.py:380
  68.4 1.6 collective-permute-done.2.ylo_ref
  70.6 13.4 %shard_map.122.u_ref.prev_ref = f32[3,32,32,256]{3,2,1,0:T(8,128)} custom-call(f32[3,32,32,256]{3,2,1,0:T(8,128)} %prev_ref.3, f32[3,2,32,256]{3,2,1,0:T(8,128)} %copy-done, f32[3,2,32,256]{3,2,1,0:T(8,128)} %copy-done.1, f32[3,36,2,256]{3,2,1,0:T(2,128)} %copy-done.9, f32[3,36,2,256]{3,2,1,0:T(2,128)} %copy-done.8, f32[3,32,32,256]{3,2,1,0:T(8,128)} %prev_ref.2, ...), custom_call_target="tpu_custom_call" | custom-call | tf_op jit(solution)/shard_map/pallas_call | solution.py:142
  84.0 1.0 fusion.83
  85.0 2.2 %collective-permute-start.4 = (f32[3,2,32,256]{3,2,1,0:T(8,128)S(1)}, f32[3,2,32,256]{3,2,1,0:T(8,128)S(1)}, u32[]{:S(2)}, u32[]{:S(2)}) collective-permute-start(f32[3,2,32,256]{3,2,1,0:T(8,128)S(1)} %get-tuple-element.268), channel_id=1, source_target_pairs={{0,4},{4,8},{8,12},{12,16},{16,20},{20,24},{24,28},{1,5},{5,9},{9,... | collective-permute-start | bytes 589832 | tf_op jit(solution)/shard_map/ppermute | solution.py:168
  87.3 4.5 %collective-permute-start.5 = (f32[3,2,32,256]{3,2,1,0:T(8,128)S(1)}, f32[3,2,32,256]{3,2,1,0:T(8,128)S(1)}, u32[]{:S(2)}, u32[]{:S(2)}) collective-permute-start(f32[3,2,32,256]{3,2,1,0:T(8,128)S(1)} %get-tuple-element.267), channel_id=1, source_target_pairs={{4,0},{8,4},{12,8},{16,12},{20,16},{24,20},{28,24},{5,1},{9,5},{13... | collective-permute-start | bytes 589832 | tf_op jit(solution)/shard_map/ppermute | solution.py:169
  91.8 1.5 fusion.82
  93.6 3.1 %collective-permute-done.5.xhi_ref = f32[3,2,32,256]{3,2,1,0:T(8,128)S(1)} collective-permute-done((f32[3,2,32,256]{3,2,1,0:T(8,128)S(1)}, f32[3,2,32,256]{3,2,1,0:T(8,128)S(1)}, u32[]{:S(2)}, u32[]{:S(2)}) %collective-permute-start.5) | collective-permute-done | bytes 196640 | tf_op jit(solution)/shard_map/ppermute | solution.py:169
  96.9 3.8 %collective-permute-start.7 = (f32[3,36,2,256]{3,2,1,0:T(2,128)S(1)}, f32[3,36,2,256]{3,2,1,0:T(2,128)S(1)}, u32[]{:S(2)}, u32[]{:S(2)}) collective-permute-start(f32[3,36,2,256]{3,2,1,0:T(2,128)S(1)} %pad_maximum_fusion.4), channel_id=1, source_target_pairs={{1,0},{2,1},{3,2},{5,4},{6,5},{7,6},{9,8},{10,9},{11,10},{13,12},{... | collective-permute-start | bytes 663560 | tf_op jit(solution)/shard_map/ppermute | solution.py:174
  100.7 1.9 collective-permute-start.6
  102.7 3.2 %fusion.9 = f32[3072,256]{1,0:T(8,128)} fusion(s32[256]{0:T(256)S(1)} %get-tuple-element.303, f32[256]{0:T(256)S(1)} %bitcast.115, s32[256]{0:T(256)S(1)} %get-tuple-element.302), kind=kOutput, calls=%fused_computation.28 | convolution fusion | flops 2416836608 | bytes 3148800 | tf_op jit(solution)/shard_map/dot_general | solution.py:380
  105.9 2.1 %collective-permute-done.6.ylo_ref = f32[3,36,2,256]{3,2,1,0:T(2,128)S(1)} collective-permute-done((f32[3,36,2,256]{3,2,1,0:T(2,128)S(1)}, f32[3,36,2,256]{3,2,1,0:T(2,128)S(1)}, u32[]{:S(2)}, u32[]{:S(2)}) %collective-permute-start.6) | collective-permute-done | bytes 221216 | tf_op jit(solution)/shard_map/ppermute | solution.py:173
  108.7 13.4 %shard_map.123.u_ref.prev_ref = f32[3,32,32,256]{3,2,1,0:T(8,128)} custom-call(f32[3,32,32,256]{3,2,1,0:T(8,128)} %shard_map.122.u_ref.prev_ref, f32[3,2,32,256]{3,2,1,0:T(8,128)} %copy-done.4, f32[3,2,32,256]{3,2,1,0:T(8,128)} %copy-done.7, f32[3,36,2,256]{3,2,1,0:T(2,128)} %copy-done.15, f32[3,36,2,256]{3,2,1,0:T(2,128)} %copy-done.12, ...), custom_call_target="tpu_custom_call" | custom-call | tf_op jit(solution)/shard_map/pallas_call | solution.py:142
  123.1 2.5 %collective-permute-start.8 = (f32[3,2,32,256]{3,2,1,0:T(8,128)S(1)}, f32[3,2,32,256]{3,2,1,0:T(8,128)S(1)}, u32[]{:S(2)}, u32[]{:S(2)}) collective-permute-start(f32[3,2,32,256]{3,2,1,0:T(8,128)S(1)} %get-tuple-element.264), channel_id=1, source_target_pairs={{0,4},{4,8},{8,12},{12,16},{16,20},{20,24},{24,28},{1,5},{5,9},{9,... | collective-permute-start | bytes 589832 | tf_op jit(solution)/shard_map/ppermute | solution.py:168
  125.7 4.2 %collective-permute-start.9 = (f32[3,2,32,256]{3,2,1,0:T(8,128)S(1)}, f32[3,2,32,256]{3,2,1,0:T(8,128)S(1)}, u32[]{:S(2)}, u32[]{:S(2)}) collective-permute-start(f32[3,2,32,256]{3,2,1,0:T(8,128)S(1)} %get-tuple-element.263), channel_id=1, source_target_pairs={{4,0},{8,4},{12,8},{16,12},{20,16},{24,20},{28,24},{5,1},{9,5},{13... | collective-permute-start | bytes 589832 | tf_op jit(solution)/shard_map/ppermute | solution.py:169
  129.9 1.5 fusion.80
  131.6 2.1 %collective-permute-done.9.xhi_ref = f32[3,2,32,256]{3,2,1,0:T(8,128)S(1)} collective-permute-done((f32[3,2,32,256]{3,2,1,0:T(8,128)S(1)}, f32[3,2,32,256]{3,2,1,0:T(8,128)S(1)}, u32[]{:S(2)}, u32[]{:S(2)}) %collective-permute-start.9) | collective-permute-done | bytes 196640 | tf_op jit(solution)/shard_map/ppermute | solution.py:169
  133.8 4.6 %collective-permute-start.11 = (f32[3,36,2,256]{3,2,1,0:T(2,128)S(1)}, f32[3,36,2,256]{3,2,1,0:T(2,128)S(1)}, u32[]{:S(2)}, u32[]{:S(2)}) collective-permute-start(f32[3,36,2,256]{3,2,1,0:T(2,128)S(1)} %pad_maximum_fusion.6), channel_id=1, source_target_pairs={{1,0},{2,1},{3,2},{5,4},{6,5},{7,6},{9,8},{10,9},{11,10},{13,12},{... | collective-permute-start | bytes 663560 | tf_op jit(solution)/shard_map/ppermute | solution.py:174
  138.5 1.9 collective-permute-start.10
  140.4 3.2 %fusion.8 = f32[3072,256]{1,0:T(8,128)} fusion(s32[256]{0:T(256)S(1)} %get-tuple-element.303, f32[256]{0:T(256)S(1)} %bitcast.114, s32[256]{0:T(256)S(1)} %get-tuple-element.302), kind=kOutput, calls=%fused_computation.27 | convolution fusion | flops 2416836608 | bytes 3148800 | tf_op jit(solution)/shard_map/dot_general | solution.py:380
  143.6 2.1 %collective-permute-done.10.ylo_ref = f32[3,36,2,256]{3,2,1,0:T(2,128)S(1)} collective-permute-done((f32[3,36,2,256]{3,2,1,0:T(2,128)S(1)}, f32[3,36,2,256]{3,2,1,0:T(2,128)S(1)}, u32[]{:S(2)}, u32[]{:S(2)}) %collective-permute-start.10) | collective-permute-done | bytes 221216 | tf_op jit(solution)/shard_map/ppermute | solution.py:173
  146.5 13.4 %shard_map.124.u_ref = f32[3,32,32,256]{3,2,1,0:T(8,128)} custom-call(f32[3,32,32,256]{3,2,1,0:T(8,128)} %shard_map.123.u_ref.prev_ref, f32[3,2,32,256]{3,2,1,0:T(8,128)} %copy-done.3, f32[3,2,32,256]{3,2,1,0:T(8,128)} %copy-done.6, f32[3,36,2,256]{3,2,1,0:T(2,128)} %copy-done.14, f32[3,36,2,256]{3,2,1,0:T(2,128)} %copy-done.11, ...), custom_call_target="tpu_custom_call" | custom-call | tf_op jit(solution)/shard_map/pallas_call | solution.py:142
  159.8 1.0 fusion.79
  160.9 2.5 %collective-permute-start.12 = (f32[3,2,32,256]{3,2,1,0:T(8,128)S(1)}, f32[3,2,32,256]{3,2,1,0:T(8,128)S(1)}, u32[]{:S(2)}, u32[]{:S(2)}) collective-permute-start(f32[3,2,32,256]{3,2,1,0:T(8,128)S(1)} %get-tuple-element.260), channel_id=1, source_target_pairs={{0,4},{4,8},{8,12},{12,16},{16,20},{20,24},{24,28},{1,5},{5,9},{9,... | collective-permute-start | bytes 589832 | tf_op jit(solution)/shard_map/ppermute | solution.py:168
  163.4 4.3 %collective-permute-start.13 = (f32[3,2,32,256]{3,2,1,0:T(8,128)S(1)}, f32[3,2,32,256]{3,2,1,0:T(8,128)S(1)}, u32[]{:S(2)}, u32[]{:S(2)}) collective-permute-start(f32[3,2,32,256]{3,2,1,0:T(8,128)S(1)} %get-tuple-element.259), channel_id=1, source_target_pairs={{4,0},{8,4},{12,8},{16,12},{20,16},{24,20},{28,24},{5,1},{9,5},{13... | collective-permute-start | bytes 589832 | tf_op jit(solution)/shard_map/ppermute | solution.py:169
  167.6 1.5 fusion.78
  169.4 2.1 %collective-permute-done.13.xhi_ref = f32[3,2,32,256]{3,2,1,0:T(8,128)S(1)} collective-permute-done((f32[3,2,32,256]{3,2,1,0:T(8,128)S(1)}, f32[3,2,32,256]{3,2,1,0:T(8,128)S(1)}, u32[]{:S(2)}, u32[]{:S(2)}) %collective-permute-start.13) | collective-permute-done | bytes 196640 | tf_op jit(solution)/shard_map/ppermute | solution.py:169
  171.6 4.6 %collective-permute-start.15 = (f32[3,36,2,256]{3,2,1,0:T(2,128)S(1)}, f32[3,36,2,256]{3,2,1,0:T(2,128)S(1)}, u32[]{:S(2)}, u32[]{:S(2)}) collective-permute-start(f32[3,36,2,256]{3,2,1,0:T(2,128)S(1)} %pad_maximum_fusion.8), channel_id=1, source_target_pairs={{1,0},{2,1},{3,2},{5,4},{6,5},{7,6},{9,8},{10,9},{11,10},{13,12},{... | collective-permute-start | bytes 663560 | tf_op jit(solution)/shard_map/ppermute | solution.py:174
  176.3 1.9 collective-permute-start.14
  178.2 3.2 %fusion.7 = f32[3072,256]{1,0:T(8,128)} fusion(s32[256]{0:T(256)S(1)} %get-tuple-element.303, f32[256]{0:T(256)S(1)} %bitcast.113, s32[256]{0:T(256)S(1)} %get-tuple-element.302), kind=kOutput, calls=%fused_computation.26 | convolution fusion | flops 2416836608 | bytes 3148800 | tf_op jit(solution)/shard_map/dot_general | solution.py:380
  181.4 2.1 %collective-permute-done.14.ylo_ref = f32[3,36,2,256]{3,2,1,0:T(2,128)S(1)} collective-permute-done((f32[3,36,2,256]{3,2,1,0:T(2,128)S(1)}, f32[3,36,2,256]{3,2,1,0:T(2,128)S(1)}, u32[]{:S(2)}, u32[]{:S(2)}) %collective-permute-start.14) | collective-permute-done | bytes 221216 | tf_op jit(solution)/shard_map/ppermute | solution.py:173
  184.2 13.4 %shard_map.125 = f32[3,32,32,256]{3,2,1,0:T(8,128)} custom-call(f32[3,32,32,256]{3,2,1,0:T(8,128)} %shard_map.124.u_ref, f32[3,2,32,256]{3,2,1,0:T(8,128)} %copy-done.2, f32[3,2,32,256]{3,2,1,0:T(8,128)} %copy-done.5, f32[3,36,2,256]{3,2,1,0:T(2,128)} %copy-done.13, f32[3,36,2,256]{3,2,1,0:T(2,128)} %copy-done.10, ...), custom_call_target="tpu_custom_call" | custom-call | tf_op jit(solution)/shard_map/pallas_call | solution.py:142
  (138 shorter events, 14.9 us)
Async XLA Ops:
  16.0 5.3 %copy-start.16 = (s32[8192]{0:T(1024)S(1)}, s32[8192]{0:T(1024)}, u32[]{:S(2)}) copy-start(s32[8192]{0:T(1024)} %param.19) | copy-start | bytes 98308
  16.0 5.3 %copy-start.17 = (s32[8192]{0:T(1024)S(1)}, s32[8192]{0:T(1024)}, u32[]{:S(2)}) copy-start(s32[8192]{0:T(1024)} %param.20) | copy-start | bytes 98308
  24.8 30.6 %copy-start.18 = (s32[256]{0:T(256)S(1)}, s32[256]{0:T(256)}, u32[]{:S(2)}) copy-start(s32[256]{0:T(256)} %param.21) | copy-start | bytes 3076
  39.3 25.6 %all-to-all-start = ((bf16[2,4,32,256]{3,1,0,2:T(4,128)(2,1)}), bf16[2,4,32,256]{3,1,0,2:T(4,128)(2,1)S(1)}, u32[]{:S(2)}, u32[]{:S(2)}) async-start(bf16[2,4,32,256]{3,1,0,2:T(4,128)(2,1)} %copy.27), calls=%async_computation | async-start | bytes 262144 | tf_op jit(solution)/shard_map/all_to_all | solution.py:357
  46.3 9.7 %collective-permute-start = (f32[3,2,32,256]{3,2,1,0:T(8,128)S(1)}, f32[3,2,32,256]{3,2,1,0:T(8,128)S(1)}, u32[]{:S(2)}, u32[]{:S(2)}) collective-permute-start(f32[3,2,32,256]{3,2,1,0:T(8,128)S(1)} %get-tuple-element.272), channel_id=1, source_target_pairs={{0,4},{4,8},{8,12},{12,16},{16,20},{20,24},{24,28},{1,5},{5,9},{9,... | collective-permute-start | bytes 589832 | tf_op jit(solution)/shard_map/ppermute | solution.py:168
  49.7 10.5 %collective-permute-start.1 = (f32[3,2,32,256]{3,2,1,0:T(8,128)S(1)}, f32[3,2,32,256]{3,2,1,0:T(8,128)S(1)}, u32[]{:S(2)}, u32[]{:S(2)}) collective-permute-start(f32[3,2,32,256]{3,2,1,0:T(8,128)S(1)} %get-tuple-element.271), channel_id=1, source_target_pairs={{4,0},{8,4},{12,8},{16,12},{20,16},{24,20},{28,24},{5,1},{9,5},{13... | collective-permute-start | bytes 589832 | tf_op jit(solution)/shard_map/ppermute | solution.py:169
  56.0 13.9 %copy-start = (f32[3,2,32,256]{3,2,1,0:T(8,128)}, f32[3,2,32,256]{3,2,1,0:T(8,128)S(1)}, u32[]{:S(2)}) copy-start(f32[3,2,32,256]{3,2,1,0:T(8,128)S(1)} %collective-permute-done.xlo_ref) | copy-start | bytes 589828
  60.2 9.7 %copy-start.1 = (f32[3,2,32,256]{3,2,1,0:T(8,128)}, f32[3,2,32,256]{3,2,1,0:T(8,128)S(1)}, u32[]{:S(2)}) copy-start(f32[3,2,32,256]{3,2,1,0:T(8,128)S(1)} %collective-permute-done.1.xhi_ref) | copy-start | bytes 589828
  60.4 8.0 %collective-permute-start.3 = (f32[3,36,2,256]{3,2,1,0:T(2,128)S(1)}, f32[3,36,2,256]{3,2,1,0:T(2,128)S(1)}, u32[]{:S(2)}, u32[]{:S(2)}) collective-permute-start(f32[3,36,2,256]{3,2,1,0:T(2,128)S(1)} %pad_maximum_fusion.2), channel_id=1, source_target_pairs={{1,0},{2,1},{3,2},{5,4},{6,5},{7,6},{9,8},{10,9},{11,10},{13,12},{... | collective-permute-start | bytes 663560 | tf_op jit(solution)/shard_map/ppermute | solution.py:174
  62.7 7.3 %collective-permute-start.2 = (f32[3,36,2,256]{3,2,1,0:T(2,128)S(1)}, f32[3,36,2,256]{3,2,1,0:T(2,128)S(1)}, u32[]{:S(2)}, u32[]{:S(2)}) collective-permute-start(f32[3,36,2,256]{3,2,1,0:T(2,128)S(1)} %pad_maximum_fusion.1), channel_id=1, source_target_pairs={{0,1},{1,2},{2,3},{4,5},{5,6},{6,7},{8,9},{9,10},{10,11},{12,13},{... | collective-permute-start | bytes 663560 | tf_op jit(solution)/shard_map/ppermute | solution.py:173
  68.4 1.6 copy-start.8
  69.9 0.7 copy-start.9
  85.0 8.6 %collective-permute-start.4 = (f32[3,2,32,256]{3,2,1,0:T(8,128)S(1)}, f32[3,2,32,256]{3,2,1,0:T(8,128)S(1)}, u32[]{:S(2)}, u32[]{:S(2)}) collective-permute-start(f32[3,2,32,256]{3,2,1,0:T(8,128)S(1)} %get-tuple-element.268), channel_id=1, source_target_pairs={{0,4},{4,8},{8,12},{12,16},{16,20},{20,24},{24,28},{1,5},{5,9},{9,... | collective-permute-start | bytes 589832 | tf_op jit(solution)/shard_map/ppermute | solution.py:168
  87.3 9.4 %collective-permute-start.5 = (f32[3,2,32,256]{3,2,1,0:T(8,128)S(1)}, f32[3,2,32,256]{3,2,1,0:T(8,128)S(1)}, u32[]{:S(2)}, u32[]{:S(2)}) collective-permute-start(f32[3,2,32,256]{3,2,1,0:T(8,128)S(1)} %get-tuple-element.267), channel_id=1, source_target_pairs={{4,0},{8,4},{12,8},{16,12},{20,16},{24,20},{28,24},{5,1},{9,5},{13... | collective-permute-start | bytes 589832 | tf_op jit(solution)/shard_map/ppermute | solution.py:169
  93.6 14.4 %copy-start.4 = (f32[3,2,32,256]{3,2,1,0:T(8,128)}, f32[3,2,32,256]{3,2,1,0:T(8,128)S(1)}, u32[]{:S(2)}) copy-start(f32[3,2,32,256]{3,2,1,0:T(8,128)S(1)} %collective-permute-done.4.xlo_ref) | copy-start | bytes 589828
  96.7 11.3 %copy-start.7 = (f32[3,2,32,256]{3,2,1,0:T(8,128)}, f32[3,2,32,256]{3,2,1,0:T(8,128)S(1)}, u32[]{:S(2)}) copy-start(f32[3,2,32,256]{3,2,1,0:T(8,128)S(1)} %collective-permute-done.5.xhi_ref) | copy-start | bytes 589828
  96.9 9.0 %collective-permute-start.7 = (f32[3,36,2,256]{3,2,1,0:T(2,128)S(1)}, f32[3,36,2,256]{3,2,1,0:T(2,128)S(1)}, u32[]{:S(2)}, u32[]{:S(2)}) collective-permute-start(f32[3,36,2,256]{3,2,1,0:T(2,128)S(1)} %pad_maximum_fusion.4), channel_id=1, source_target_pairs={{1,0},{2,1},{3,2},{5,4},{6,5},{7,6},{9,8},{10,9},{11,10},{13,12},{... | collective-permute-start | bytes 663560 | tf_op jit(solution)/shard_map/ppermute | solution.py:174
  100.7 7.3 %collective-permute-start.6 = (f32[3,36,2,256]{3,2,1,0:T(2,128)S(1)}, f32[3,36,2,256]{3,2,1,0:T(2,128)S(1)}, u32[]{:S(2)}, u32[]{:S(2)}) collective-permute-start(f32[3,36,2,256]{3,2,1,0:T(2,128)S(1)} %pad_maximum_fusion.3), channel_id=1, source_target_pairs={{0,1},{1,2},{2,3},{4,5},{5,6},{6,7},{8,9},{9,10},{10,11},{12,13},{... | collective-permute-start | bytes 663560 | tf_op jit(solution)/shard_map/ppermute | solution.py:173
  105.9 2.1 %copy-start.12 = (f32[3,36,2,256]{3,2,1,0:T(2,128)}, f32[3,36,2,256]{3,2,1,0:T(2,128)S(1)}, u32[]{:S(2)}) copy-start(f32[3,36,2,256]{3,2,1,0:T(2,128)S(1)} %collective-permute-done.7.yhi_ref) | copy-start | bytes 663556
  108.0 0.7 copy-start.15
  123.1 8.5 %collective-permute-start.8 = (f32[3,2,32,256]{3,2,1,0:T(8,128)S(1)}, f32[3,2,32,256]{3,2,1,0:T(8,128)S(1)}, u32[]{:S(2)}, u32[]{:S(2)}) collective-permute-start(f32[3,2,32,256]{3,2,1,0:T(8,128)S(1)} %get-tuple-element.264), channel_id=1, source_target_pairs={{0,4},{4,8},{8,12},{12,16},{16,20},{20,24},{24,28},{1,5},{5,9},{9,... | collective-permute-start | bytes 589832 | tf_op jit(solution)/shard_map/ppermute | solution.py:168
  125.7 8.0 %collective-permute-start.9 = (f32[3,2,32,256]{3,2,1,0:T(8,128)S(1)}, f32[3,2,32,256]{3,2,1,0:T(8,128)S(1)}, u32[]{:S(2)}, u32[]{:S(2)}) collective-permute-start(f32[3,2,32,256]{3,2,1,0:T(8,128)S(1)} %get-tuple-element.263), channel_id=1, source_target_pairs={{4,0},{8,4},{12,8},{16,12},{20,16},{24,20},{28,24},{5,1},{9,5},{13... | collective-permute-start | bytes 589832 | tf_op jit(solution)/shard_map/ppermute | solution.py:169
  131.6 14.2 %copy-start.3 = (f32[3,2,32,256]{3,2,1,0:T(8,128)}, f32[3,2,32,256]{3,2,1,0:T(8,128)S(1)}, u32[]{:S(2)}) copy-start(f32[3,2,32,256]{3,2,1,0:T(8,128)S(1)} %collective-permute-done.8.xlo_ref) | copy-start | bytes 589828
  133.7 12.1 %copy-start.6 = (f32[3,2,32,256]{3,2,1,0:T(8,128)}, f32[3,2,32,256]{3,2,1,0:T(8,128)S(1)}, u32[]{:S(2)}) copy-start(f32[3,2,32,256]{3,2,1,0:T(8,128)S(1)} %collective-permute-done.9.xhi_ref) | copy-start | bytes 589828
  133.8 9.8 %collective-permute-start.11 = (f32[3,36,2,256]{3,2,1,0:T(2,128)S(1)}, f32[3,36,2,256]{3,2,1,0:T(2,128)S(1)}, u32[]{:S(2)}, u32[]{:S(2)}) collective-permute-start(f32[3,36,2,256]{3,2,1,0:T(2,128)S(1)} %pad_maximum_fusion.6), channel_id=1, source_target_pairs={{1,0},{2,1},{3,2},{5,4},{6,5},{7,6},{9,8},{10,9},{11,10},{13,12},{... | collective-permute-start | bytes 663560 | tf_op jit(solution)/shard_map/ppermute | solution.py:174
  138.5 7.3 %collective-permute-start.10 = (f32[3,36,2,256]{3,2,1,0:T(2,128)S(1)}, f32[3,36,2,256]{3,2,1,0:T(2,128)S(1)}, u32[]{:S(2)}, u32[]{:S(2)}) collective-permute-start(f32[3,36,2,256]{3,2,1,0:T(2,128)S(1)} %pad_maximum_fusion.5), channel_id=1, source_target_pairs={{0,1},{1,2},{2,3},{4,5},{5,6},{6,7},{8,9},{9,10},{10,11},{12,13},{... | collective-permute-start | bytes 663560 | tf_op jit(solution)/shard_map/ppermute | solution.py:173
  143.6 2.1 %copy-start.11 = (f32[3,36,2,256]{3,2,1,0:T(2,128)}, f32[3,36,2,256]{3,2,1,0:T(2,128)S(1)}, u32[]{:S(2)}) copy-start(f32[3,36,2,256]{3,2,1,0:T(2,128)S(1)} %collective-permute-done.11.yhi_ref) | copy-start | bytes 663556
  145.8 0.7 copy-start.14
  160.9 8.5 %collective-permute-start.12 = (f32[3,2,32,256]{3,2,1,0:T(8,128)S(1)}, f32[3,2,32,256]{3,2,1,0:T(8,128)S(1)}, u32[]{:S(2)}, u32[]{:S(2)}) collective-permute-start(f32[3,2,32,256]{3,2,1,0:T(8,128)S(1)} %get-tuple-element.260), channel_id=1, source_target_pairs={{0,4},{4,8},{8,12},{12,16},{16,20},{20,24},{24,28},{1,5},{5,9},{9,... | collective-permute-start | bytes 589832 | tf_op jit(solution)/shard_map/ppermute | solution.py:168
  163.4 8.1 %collective-permute-start.13 = (f32[3,2,32,256]{3,2,1,0:T(8,128)S(1)}, f32[3,2,32,256]{3,2,1,0:T(8,128)S(1)}, u32[]{:S(2)}, u32[]{:S(2)}) collective-permute-start(f32[3,2,32,256]{3,2,1,0:T(8,128)S(1)} %get-tuple-element.259), channel_id=1, source_target_pairs={{4,0},{8,4},{12,8},{16,12},{20,16},{24,20},{28,24},{5,1},{9,5},{13... | collective-permute-start | bytes 589832 | tf_op jit(solution)/shard_map/ppermute | solution.py:169
  169.4 14.2 %copy-start.2 = (f32[3,2,32,256]{3,2,1,0:T(8,128)}, f32[3,2,32,256]{3,2,1,0:T(8,128)S(1)}, u32[]{:S(2)}) copy-start(f32[3,2,32,256]{3,2,1,0:T(8,128)S(1)} %collective-permute-done.12.xlo_ref) | copy-start | bytes 589828
  171.4 12.1 %copy-start.5 = (f32[3,2,32,256]{3,2,1,0:T(8,128)}, f32[3,2,32,256]{3,2,1,0:T(8,128)S(1)}, u32[]{:S(2)}) copy-start(f32[3,2,32,256]{3,2,1,0:T(8,128)S(1)} %collective-permute-done.13.xhi_ref) | copy-start | bytes 589828
  171.6 9.8 %collective-permute-start.15 = (f32[3,36,2,256]{3,2,1,0:T(2,128)S(1)}, f32[3,36,2,256]{3,2,1,0:T(2,128)S(1)}, u32[]{:S(2)}, u32[]{:S(2)}) collective-permute-start(f32[3,36,2,256]{3,2,1,0:T(2,128)S(1)} %pad_maximum_fusion.8), channel_id=1, source_target_pairs={{1,0},{2,1},{3,2},{5,4},{6,5},{7,6},{9,8},{10,9},{11,10},{13,12},{... | collective-permute-start | bytes 663560 | tf_op jit(solution)/shard_map/ppermute | solution.py:174
  176.3 7.3 %collective-permute-start.14 = (f32[3,36,2,256]{3,2,1,0:T(2,128)S(1)}, f32[3,36,2,256]{3,2,1,0:T(2,128)S(1)}, u32[]{:S(2)}, u32[]{:S(2)}) collective-permute-start(f32[3,36,2,256]{3,2,1,0:T(2,128)S(1)} %pad_maximum_fusion.7), channel_id=1, source_target_pairs={{0,1},{1,2},{2,3},{4,5},{5,6},{6,7},{8,9},{9,10},{10,11},{12,13},{... | collective-permute-start | bytes 663560 | tf_op jit(solution)/shard_map/ppermute | solution.py:173
  181.4 2.1 %copy-start.10 = (f32[3,36,2,256]{3,2,1,0:T(2,128)}, f32[3,36,2,256]{3,2,1,0:T(2,128)S(1)}, u32[]{:S(2)}) copy-start(f32[3,36,2,256]{3,2,1,0:T(2,128)S(1)} %collective-permute-done.15.yhi_ref) | copy-start | bytes 663556
  183.5 0.7 copy-start.13

commit v16 on v11

--- a/solution.py
+++ b/solution.py
@@ -159,19 +159,30 @@
     )(u, xlo, xhi, ylo, yhi, prev, moduli, sources)
 
 
-def halos(block, width):
+def x_halos(block, width):
     size_x = lax.axis_size("gx")
-    size_y = lax.axis_size("gy")
-    nx, ny = block.shape[1], block.shape[2]
+    nx = block.shape[1]
     forward_x = [(i, i + 1) for i in range(size_x - 1)]
     backward_x = [(t, s) for s, t in forward_x]
     xlo = lax.ppermute(block[:, nx - width:], "gx", forward_x)
     xhi = lax.ppermute(block[:, :width], "gx", backward_x)
+    return xlo, xhi
+
+
+def y_halos(block, xlo, xhi, width):
+    size_y = lax.axis_size("gy")
+    ny = block.shape[2]
     forward_y = [(i, i + 1) for i in range(size_y - 1)]
     backward_y = [(t, s) for s, t in forward_y]
     rows = lambda sl: jnp.concatenate([xlo[:, :, sl], block[:, :, sl], xhi[:, :, sl]], axis=1)
     ylo = lax.ppermute(rows(slice(ny - width, ny)), "gy", forward_y)
     yhi = lax.ppermute(rows(slice(0, width)), "gy", backward_y)
+    return ylo, yhi
+
+
+def halos(block, width):
+    xlo, xhi = x_halos(block, width)
+    ylo, yhi = y_halos(block, xlo, xhi, width)
     return xlo, xhi, ylo, yhi
 
 
@@ -328,6 +339,8 @@
         kernel.reshape(2 * per_device * ND, NK), cosines, preferred_element_type=jnp.float32
     )
     table_rounded = spectrum_table.astype(jnp.bfloat16)
+    later_now, table_rounded = lax.optimization_barrier((field_now, table_rounded))
+    first_x = x_halos(later_now, 2)
     all_slots = slot_offset.shape[0]
     width = math.gcd(all_slots, 4096)
     count_blocks = all_slots // width
@@ -353,6 +366,7 @@
     )
     slots_dev = slot_target.shape[0]
     occupied = (jnp.arange(slots_dev, dtype=jnp.int32) < live_count[0]).astype(jnp.float32)
+    first_x, spectra = lax.optimization_barrier((first_x, spectra))
     parcel = spectra.reshape(2, per_device, groups, slots_dev)
     arrived = lax.all_to_all(parcel, ("gx", "gy"), split_axis=2, concat_axis=1, tiled=True)
     freq_order = jnp.arange(F, dtype=jnp.int32)
@@ -379,7 +393,11 @@
         spread = weighted[instant][:, None] * depth_hot
         source = jnp.dot(column_hot, spread, precision=lax.Precision.HIGHEST)
         source = source.reshape(3, block_x, block_y, depth)
-        xlo, xhi, ylo, yhi = halos(current, 2)
+        if instant == 0:
+            xlo, xhi = first_x
+            ylo, yhi = y_halos(current, xlo, xhi, 2)
+        else:
+            xlo, xhi, ylo, yhi = halos(current, 2)
         advanced = elastic_step(current, xlo, xhi, ylo, yhi, previous, moduli, source)
         previous, current = (current, advanced)
     return (current, previous)

time: 196 us -> 187 us (0.954)
  starting transfers between devices: 55.9 us -> 53.6 us
  matrix products: 29.6 us -> 27.4 us
  waiting for transfers between devices: 20.6 us -> 18.4 us
  other arithmetic: 20.6 us -> 18.6 us
    ppermute x16, waiting for transfers between devices: 20.6 us -> 17.1 us  [the longest x4 7.37 us: x_halos(): xhi = lax.ppermute(block[:, :width], 'gx', backward_x)]
    dot_general x1, matrix products: 3.47 us -> 1.29 us  [shards(): jnp.dot(kernel.reshape(2 * per_device * ND, NK), cosines, preferred_eleme...]
    slice x16 -> x15, local copies, waits for them, and re-layouts: 10.3 us -> 10.3 us  [the longest x4 6.06 us: y_halos(): block[:, :, sl]]
  transfers between devices with their start and end apart: 17 -> 17, of which waited for: 12 -> 11; matrix products, arithmetic and copies ran while one was open for 11% -> 18% of each run, Pallas kernels for 0% -> 0%
where the time goes in v16:
time: 187 us
  starting transfers between devices  53.6 us (29%)
  Pallas kernels  51.3 us (27%)
  matrix products  27.4 us (15%)
  other arithmetic  18.6 us (10%)
  waiting for transfers between devices  18.4 us (10%)
  local copies, waits for them, and re-layouts  14.8 us (8%)
  between operations  1.89 us (1%)
    pallas_call x4, Pallas kernels, elastic_step(): pl.pallas_call(kernel, grid=(nx // bx,), in_specs=[pl.BlockSpec(u.shape,...  51.3 us
    ppermute x4, starting transfers between devices, x_halos(): xhi = lax.ppermute(block[:, :width], 'gx', backward_x)  16.2 us
    ppermute x4, starting transfers between devices, y_halos(): yhi = lax.ppermute(rows(slice(0, width)), 'gy', backward_y)  13.1 us
    dot_general x2, matrix products, select_block(): jnp.dot(table_rounded, offset_hot, preferred_element_type=jnp.float32)  13.1 us
    dot_general x4, matrix products, shards(): source = jnp.dot(column_hot, spread, precision=lax.Precision.HIGHEST)  12.9 us
    ppermute x4, starting transfers between devices, x_halos(): xlo = lax.ppermute(block[:, nx - width:], 'gx', forward_x)  10.9 us
    ppermute x4, starting transfers between devices, y_halos(): ylo = lax.ppermute(rows(slice(ny - width, ny)), 'gy', forward_y)  8.31 us
    ppermute x4, waiting for transfers between devices, x_halos(): xhi = lax.ppermute(block[:, :width], 'gx', backward_x)  7.37 us
  transfers between devices with their start and end apart: 17, of which 11 were waited for; matrix products, arithmetic and copies ran while one was open for 18% of the time, Pallas kernels for 0%

profile of v16, /device:TPU:12, one launch (start us, length us, event | category | flops | bytes accessed | tf_op | source)
XLA Modules:
  0.0 186.6 jit_solution(7324782560248778178)
XLA Ops:
  2.9 4.9 %sine_multiply_fusion.1 = (f32[32,4,1024]{2,1,0:T(4,128)S(1)}, f32[32,4,1024]{2,1,0:T(4,128)S(1)}, f32[32,4,1024]{2,1,0:T(4,128)S(1)}) fusion(f32[32]{0:T(128)S(1)} %get-tuple-element.317, f32[32,4]{1,0:T(8,128)S(1)} %copy.24, f32[1024]{0:T(1024)S(1)} %multiply_multiply_fusion, f32[1,4,1024]{2,1,0:T(4,128)S(1)} %slice.153, f32[31,4,1024]{2,1,0:T(4,128)S(1)} %slice.152, ...), kind=kLoop, calls=%fused_computation.41 | loop fusion | flops 1441792 | bytes 2102016 | tf_op jit(solution)/shard_map/mul | solution.py:206
  8.1 2.2 %while.32 = (s32[]{:T(128)}, f32[4,1024]{1,0:T(4,128)S(1)}, f32[4,1024]{1,0:T(4,128)S(1)}, f32[32,4,1024]{2,1,0:T(4,128)S(1)}, f32[32,4,1024]{2,1,0:T(4,128)S(1)...) while((s32[]{:T(128)}, f32[4,1024]{1,0:T(4,128)S(1)}, ...), condition=%wide.region_6.7_spmd.clone, body=%wide.region_5.6_spmd.clone.sunk | while | flops 94212 | bytes 147591 | solution.py:222
  11.2 4.3 %fusion.43 = (bf16[1,32,4,1024]{3,2,1,0:T(4,128)(2,1)S(1)}, bf16[1,32,4,1024]{3,2,1,0:T(4,128)(2,1)S(1)}) fusion(f32[32,4,1024]{2,1,0:T(4,128)S(1)} %get-tuple-element.196, f32[32,4,1024]{2,1,0:T(4,128)S(1)} %get-tuple-element.195, f32[32,4,1024]{2,1,0:T(4,128)S(1)} %negate_exponential_fusion, f32[32,4,1024]{2,1,0:T(4,128)S(1)} %fusion.23), kind=kLoop, calls=%fused_computation.74 | loop fusion | flops 1835008 | bytes 2621440 | tf_op jit(solution)/shard_map/stack | solution.py:235
  17.6 1.7 subtract_convert_fusion
  19.4 1.3 convolution_convert_fusion
  20.7 1.1 fusion.85
  21.7 3.4 %collective-permute-start = (f32[3,2,32,256]{3,2,1,0:T(8,128)S(1)}, f32[3,2,32,256]{3,2,1,0:T(8,128)S(1)}, u32[]{:S(2)}, u32[]{:S(2)}) collective-permute-start(f32[3,2,32,256]{3,2,1,0:T(8,128)S(1)} %get-tuple-element.282), channel_id=1, source_target_pairs={{0,4},{4,8},{8,12},{12,16},{16,20},{20,24},{24,28},{1,5},{5,9},{9,... | collective-permute-start | bytes 589832 | tf_op jit(solution)/shard_map/ppermute | solution.py:167
  25.1 3.5 %collective-permute-start.1 = (f32[3,2,32,256]{3,2,1,0:T(8,128)S(1)}, f32[3,2,32,256]{3,2,1,0:T(8,128)S(1)}, u32[]{:S(2)}, u32[]{:S(2)}) collective-permute-start(f32[3,2,32,256]{3,2,1,0:T(8,128)S(1)} %get-tuple-element.281), channel_id=1, source_target_pairs={{4,0},{8,4},{12,8},{16,12},{20,16},{24,20},{28,24},{5,1},{9,5},{13... | collective-permute-start | bytes 589832 | tf_op jit(solution)/shard_map/ppermute | solution.py:168
  28.7 1.5 fusion.84
  30.3 13.4 %while.31 = (s32[]{:T(128)}, bf16[2,2,4,4096]{3,2,1,0:T(4,128)(2,1)S(1)}, s32[2,4096]{1,0:T(2,128)S(1)}, bf16[256,2048]{1,0:T(8,128)(2,1)S(1)}, s32[2,4096]{1,0:T(2,128)S(1)}, /*index=5*/s32[]{:T(128)}) while((s32[]{:T(128)}, bf16[2,2,4,4096]{3,2,1,0:T(4,128)(2,1)S(1)}, s32[2,4096]{1,0:T(2,128)S(1)}, bf16[256,2048]{1,0:T(8,128)(2,1)S(1)}, ...), condition=%wide.region_9.10_spmd, body=%wide.region_7.9_spmd.sunk | while | flops 4305682432 | bytes 2392141 | solution.py:363
  30.4 6.5 %multiply_reduce_fusion.2 = bf16[2,4,4096]{2,1,0:T(4,128)(2,1)S(1)} fusion(f32[32,4096]{1,0:T(8,128)S(1)} %fusion.102, bf16[256,2048]{1,0:T(8,128)(2,1)S(1)} %get-tuple-element.460, s32[4096]{0:T(1024)S(1)} %bitcast.118), kind=kOutput, calls=%fused_computation.3.clone.1 | convolution fusion | flops 4305420288 | bytes 1654784 | tf_op jit(solution)/shard_map/while/body/eval_jaxpr/dot_general | solution.py:355
  37.1 6.5 %multiply_reduce_fusion.2 = bf16[2,4,4096]{2,1,0:T(4,128)(2,1)S(1)} fusion(f32[32,4096]{1,0:T(8,128)S(1)} %fusion.102, bf16[256,2048]{1,0:T(8,128)(2,1)S(1)} %get-tuple-element.460, s32[4096]{0:T(1024)S(1)} %bitcast.118), kind=kOutput, calls=%fused_computation.3.clone.1 | convolution fusion | flops 4305420288 | bytes 1654784 | tf_op jit(solution)/shard_map/while/body/eval_jaxpr/dot_general | solution.py:355
  45.3 5.1 %all-to-all-start = ((bf16[2,4,32,256]{3,1,0,2:T(4,128)(2,1)}), bf16[2,4,32,256]{3,1,0,2:T(4,128)(2,1)S(1)}, u32[]{:S(2)}, u32[]{:S(2)}) async-start(bf16[2,4,32,256]{3,1,0,2:T(4,128)(2,1)} %bitcast.95), calls=%async_computation | async-start | bytes 262144 | tf_op jit(solution)/shard_map/all_to_all | solution.py:371
  50.6 2.2 %collective-permute-start.3 = (f32[3,36,2,256]{3,2,1,0:T(2,128)S(1)}, f32[3,36,2,256]{3,2,1,0:T(2,128)S(1)}, u32[]{:S(2)}, u32[]{:S(2)}) collective-permute-start(f32[3,36,2,256]{3,2,1,0:T(2,128)S(1)} %pad_maximum_fusion.2), channel_id=1, source_target_pairs={{1,0},{2,1},{3,2},{5,4},{6,5},{7,6},{9,8},{10,9},{11,10},{13,12},{... | collective-permute-start | bytes 663560 | tf_op jit(solution)/shard_map/ppermute | solution.py:179
  52.9 2.1 %collective-permute-start.2 = (f32[3,36,2,256]{3,2,1,0:T(2,128)S(1)}, f32[3,36,2,256]{3,2,1,0:T(2,128)S(1)}, u32[]{:S(2)}, u32[]{:S(2)}) collective-permute-start(f32[3,36,2,256]{3,2,1,0:T(2,128)S(1)} %pad_maximum_fusion.1), channel_id=1, source_target_pairs={{0,1},{1,2},{2,3},{4,5},{5,6},{6,7},{8,9},{9,10},{10,11},{12,13},{... | collective-permute-start | bytes 663560 | tf_op jit(solution)/shard_map/ppermute | solution.py:178
  55.0 1.3 all-to-all-done
  56.6 3.2 %fusion.10 = f32[3072,256]{1,0:T(8,128)} fusion(s32[256]{0:T(256)S(1)} %get-tuple-element.313, f32[256]{0:T(256)S(1)} %bitcast.123, s32[256]{0:T(256)S(1)} %get-tuple-element.312), kind=kOutput, calls=%fused_computation.29 | convolution fusion | flops 2416836608 | bytes 3148800 | tf_op jit(solution)/shard_map/dot_general | solution.py:394
  60.8 12.8 %shard_map.122.u_ref.prev_ref = f32[3,32,32,256]{3,2,1,0:T(8,128)} custom-call(f32[3,32,32,256]{3,2,1,0:T(8,128)} %prev_ref.3, f32[3,2,32,256]{3,2,1,0:T(8,128)} %copy-done, f32[3,2,32,256]{3,2,1,0:T(8,128)} %copy-done.1, f32[3,36,2,256]{3,2,1,0:T(2,128)} %copy-done.9, f32[3,36,2,256]{3,2,1,0:T(2,128)} %copy-done.8, f32[3,32,32,256]{3,2,1,0:T(8,128)} %prev_ref.2, ...), custom_call_target="tpu_custom_call" | custom-call | tf_op jit(solution)/shard_map/pallas_call | solution.py:142
  74.7 3.4 %collective-permute-start.4 = (f32[3,2,32,256]{3,2,1,0:T(8,128)S(1)}, f32[3,2,32,256]{3,2,1,0:T(8,128)S(1)}, u32[]{:S(2)}, u32[]{:S(2)}) collective-permute-start(f32[3,2,32,256]{3,2,1,0:T(8,128)S(1)} %get-tuple-element.278), channel_id=1, source_target_pairs={{0,4},{4,8},{8,12},{12,16},{16,20},{20,24},{24,28},{1,5},{5,9},{9,... | collective-permute-start | bytes 589832 | tf_op jit(solution)/shard_map/ppermute | solution.py:167
  78.1 3.4 %collective-permute-start.5 = (f32[3,2,32,256]{3,2,1,0:T(8,128)S(1)}, f32[3,2,32,256]{3,2,1,0:T(8,128)S(1)}, u32[]{:S(2)}, u32[]{:S(2)}) collective-permute-start(f32[3,2,32,256]{3,2,1,0:T(8,128)S(1)} %get-tuple-element.277), channel_id=1, source_target_pairs={{4,0},{8,4},{12,8},{16,12},{20,16},{24,20},{28,24},{5,1},{9,5},{13... | collective-permute-start | bytes 589832 | tf_op jit(solution)/shard_map/ppermute | solution.py:168
  81.5 1.5 fusion.82
  83.0 3.0 %collective-permute-done.4.xlo_ref = f32[3,2,32,256]{3,2,1,0:T(8,128)S(1)} collective-permute-done((f32[3,2,32,256]{3,2,1,0:T(8,128)S(1)}, f32[3,2,32,256]{3,2,1,0:T(8,128)S(1)}, u32[]{:S(2)}, u32[]{:S(2)}) %collective-permute-start.4) | collective-permute-done | bytes 196640 | tf_op jit(solution)/shard_map/ppermute | solution.py:167
  86.0 2.6 %collective-permute-done.5.xhi_ref = f32[3,2,32,256]{3,2,1,0:T(8,128)S(1)} collective-permute-done((f32[3,2,32,256]{3,2,1,0:T(8,128)S(1)}, f32[3,2,32,256]{3,2,1,0:T(8,128)S(1)}, u32[]{:S(2)}, u32[]{:S(2)}) %collective-permute-start.5) | collective-permute-done | bytes 196640 | tf_op jit(solution)/shard_map/ppermute | solution.py:168
  88.7 2.2 %collective-permute-start.7 = (f32[3,36,2,256]{3,2,1,0:T(2,128)S(1)}, f32[3,36,2,256]{3,2,1,0:T(2,128)S(1)}, u32[]{:S(2)}, u32[]{:S(2)}) collective-permute-start(f32[3,36,2,256]{3,2,1,0:T(2,128)S(1)} %pad_maximum_fusion.4), channel_id=1, source_target_pairs={{1,0},{2,1},{3,2},{5,4},{6,5},{7,6},{9,8},{10,9},{11,10},{13,12},{... | collective-permute-start | bytes 663560 | tf_op jit(solution)/shard_map/ppermute | solution.py:179
  91.1 2.1 %collective-permute-start.6 = (f32[3,36,2,256]{3,2,1,0:T(2,128)S(1)}, f32[3,36,2,256]{3,2,1,0:T(2,128)S(1)}, u32[]{:S(2)}, u32[]{:S(2)}) collective-permute-start(f32[3,36,2,256]{3,2,1,0:T(2,128)S(1)} %pad_maximum_fusion.3), channel_id=1, source_target_pairs={{0,1},{1,2},{2,3},{4,5},{5,6},{6,7},{8,9},{9,10},{10,11},{12,13},{... | collective-permute-start | bytes 663560 | tf_op jit(solution)/shard_map/ppermute | solution.py:178
  93.2 3.2 %fusion.9 = f32[3072,256]{1,0:T(8,128)} fusion(s32[256]{0:T(256)S(1)} %get-tuple-element.313, f32[256]{0:T(256)S(1)} %bitcast.122, s32[256]{0:T(256)S(1)} %get-tuple-element.312), kind=kOutput, calls=%fused_computation.28 | convolution fusion | flops 2416836608 | bytes 3148800 | tf_op jit(solution)/shard_map/dot_general | solution.py:394
  96.4 1.9 %collective-permute-done.6.ylo_ref = f32[3,36,2,256]{3,2,1,0:T(2,128)S(1)} collective-permute-done((f32[3,36,2,256]{3,2,1,0:T(2,128)S(1)}, f32[3,36,2,256]{3,2,1,0:T(2,128)S(1)}, u32[]{:S(2)}, u32[]{:S(2)}) %collective-permute-start.6) | collective-permute-done | bytes 221216 | tf_op jit(solution)/shard_map/ppermute | solution.py:178
  99.0 12.8 %shard_map.123.u_ref.prev_ref = f32[3,32,32,256]{3,2,1,0:T(8,128)} custom-call(f32[3,32,32,256]{3,2,1,0:T(8,128)} %shard_map.122.u_ref.prev_ref, f32[3,2,32,256]{3,2,1,0:T(8,128)} %copy-done.4, f32[3,2,32,256]{3,2,1,0:T(8,128)} %copy-done.7, f32[3,36,2,256]{3,2,1,0:T(2,128)} %copy-done.15, f32[3,36,2,256]{3,2,1,0:T(2,128)} %copy-done.12, ...), custom_call_target="tpu_custom_call" | custom-call | tf_op jit(solution)/shard_map/pallas_call | solution.py:142
  111.8 1.0 fusion.81
  112.9 1.9 %collective-permute-start.8 = (f32[3,2,32,256]{3,2,1,0:T(8,128)S(1)}, f32[3,2,32,256]{3,2,1,0:T(8,128)S(1)}, u32[]{:S(2)}, u32[]{:S(2)}) collective-permute-start(f32[3,2,32,256]{3,2,1,0:T(8,128)S(1)} %get-tuple-element.274), channel_id=1, source_target_pairs={{0,4},{4,8},{8,12},{12,16},{16,20},{20,24},{24,28},{1,5},{5,9},{9,... | collective-permute-start | bytes 589832 | tf_op jit(solution)/shard_map/ppermute | solution.py:167
  114.8 4.8 %collective-permute-start.9 = (f32[3,2,32,256]{3,2,1,0:T(8,128)S(1)}, f32[3,2,32,256]{3,2,1,0:T(8,128)S(1)}, u32[]{:S(2)}, u32[]{:S(2)}) collective-permute-start(f32[3,2,32,256]{3,2,1,0:T(8,128)S(1)} %get-tuple-element.273), channel_id=1, source_target_pairs={{4,0},{8,4},{12,8},{16,12},{20,16},{24,20},{28,24},{5,1},{9,5},{13... | collective-permute-start | bytes 589832 | tf_op jit(solution)/shard_map/ppermute | solution.py:168
  119.6 1.5 fusion.80
  121.5 2.8 %collective-permute-done.9.xhi_ref = f32[3,2,32,256]{3,2,1,0:T(8,128)S(1)} collective-permute-done((f32[3,2,32,256]{3,2,1,0:T(8,128)S(1)}, f32[3,2,32,256]{3,2,1,0:T(8,128)S(1)}, u32[]{:S(2)}, u32[]{:S(2)}) %collective-permute-start.9) | collective-permute-done | bytes 196640 | tf_op jit(solution)/shard_map/ppermute | solution.py:168
  124.4 3.9 %collective-permute-start.11 = (f32[3,36,2,256]{3,2,1,0:T(2,128)S(1)}, f32[3,36,2,256]{3,2,1,0:T(2,128)S(1)}, u32[]{:S(2)}, u32[]{:S(2)}) collective-permute-start(f32[3,36,2,256]{3,2,1,0:T(2,128)S(1)} %pad_maximum_fusion.6), channel_id=1, source_target_pairs={{1,0},{2,1},{3,2},{5,4},{6,5},{7,6},{9,8},{10,9},{11,10},{13,12},{... | collective-permute-start | bytes 663560 | tf_op jit(solution)/shard_map/ppermute | solution.py:179
  128.4 2.1 %collective-permute-start.10 = (f32[3,36,2,256]{3,2,1,0:T(2,128)S(1)}, f32[3,36,2,256]{3,2,1,0:T(2,128)S(1)}, u32[]{:S(2)}, u32[]{:S(2)}) collective-permute-start(f32[3,36,2,256]{3,2,1,0:T(2,128)S(1)} %pad_maximum_fusion.5), channel_id=1, source_target_pairs={{0,1},{1,2},{2,3},{4,5},{5,6},{6,7},{8,9},{9,10},{10,11},{12,13},{... | collective-permute-start | bytes 663560 | tf_op jit(solution)/shard_map/ppermute | solution.py:178
  130.5 3.2 %fusion.8 = f32[3072,256]{1,0:T(8,128)} fusion(s32[256]{0:T(256)S(1)} %get-tuple-element.313, f32[256]{0:T(256)S(1)} %bitcast.121, s32[256]{0:T(256)S(1)} %get-tuple-element.312), kind=kOutput, calls=%fused_computation.27 | convolution fusion | flops 2416836608 | bytes 3148800 | tf_op jit(solution)/shard_map/dot_general | solution.py:394
  133.7 1.9 %collective-permute-done.10.ylo_ref = f32[3,36,2,256]{3,2,1,0:T(2,128)S(1)} collective-permute-done((f32[3,36,2,256]{3,2,1,0:T(2,128)S(1)}, f32[3,36,2,256]{3,2,1,0:T(2,128)S(1)}, u32[]{:S(2)}, u32[]{:S(2)}) %collective-permute-start.10) | collective-permute-done | bytes 221216 | tf_op jit(solution)/shard_map/ppermute | solution.py:178
  136.3 12.8 %shard_map.124.u_ref = f32[3,32,32,256]{3,2,1,0:T(8,128)} custom-call(f32[3,32,32,256]{3,2,1,0:T(8,128)} %shard_map.123.u_ref.prev_ref, f32[3,2,32,256]{3,2,1,0:T(8,128)} %copy-done.3, f32[3,2,32,256]{3,2,1,0:T(8,128)} %copy-done.6, f32[3,36,2,256]{3,2,1,0:T(2,128)} %copy-done.14, f32[3,36,2,256]{3,2,1,0:T(2,128)} %copy-done.11, ...), custom_call_target="tpu_custom_call" | custom-call | tf_op jit(solution)/shard_map/pallas_call | solution.py:142
  149.1 1.0 fusion.79
  150.2 2.2 %collective-permute-start.12 = (f32[3,2,32,256]{3,2,1,0:T(8,128)S(1)}, f32[3,2,32,256]{3,2,1,0:T(8,128)S(1)}, u32[]{:S(2)}, u32[]{:S(2)}) collective-permute-start(f32[3,2,32,256]{3,2,1,0:T(8,128)S(1)} %get-tuple-element.270), channel_id=1, source_target_pairs={{0,4},{4,8},{8,12},{12,16},{16,20},{20,24},{24,28},{1,5},{5,9},{9,... | collective-permute-start | bytes 589832 | tf_op jit(solution)/shard_map/ppermute | solution.py:167
  152.4 4.5 %collective-permute-start.13 = (f32[3,2,32,256]{3,2,1,0:T(8,128)S(1)}, f32[3,2,32,256]{3,2,1,0:T(8,128)S(1)}, u32[]{:S(2)}, u32[]{:S(2)}) collective-permute-start(f32[3,2,32,256]{3,2,1,0:T(8,128)S(1)} %get-tuple-element.269), channel_id=1, source_target_pairs={{4,0},{8,4},{12,8},{16,12},{20,16},{24,20},{28,24},{5,1},{9,5},{13... | collective-permute-start | bytes 589832 | tf_op jit(solution)/shard_map/ppermute | solution.py:168
  157.0 1.5 fusion.78
  158.7 2.0 %collective-permute-done.13.xhi_ref = f32[3,2,32,256]{3,2,1,0:T(8,128)S(1)} collective-permute-done((f32[3,2,32,256]{3,2,1,0:T(8,128)S(1)}, f32[3,2,32,256]{3,2,1,0:T(8,128)S(1)}, u32[]{:S(2)}, u32[]{:S(2)}) %collective-permute-start.13) | collective-permute-done | bytes 196640 | tf_op jit(solution)/shard_map/ppermute | solution.py:168
  160.9 4.8 %collective-permute-start.15 = (f32[3,36,2,256]{3,2,1,0:T(2,128)S(1)}, f32[3,36,2,256]{3,2,1,0:T(2,128)S(1)}, u32[]{:S(2)}, u32[]{:S(2)}) collective-permute-start(f32[3,36,2,256]{3,2,1,0:T(2,128)S(1)} %pad_maximum_fusion.8), channel_id=1, source_target_pairs={{1,0},{2,1},{3,2},{5,4},{6,5},{7,6},{9,8},{10,9},{11,10},{13,12},{... | collective-permute-start | bytes 663560 | tf_op jit(solution)/shard_map/ppermute | solution.py:179
  165.8 1.9 %collective-permute-start.14 = (f32[3,36,2,256]{3,2,1,0:T(2,128)S(1)}, f32[3,36,2,256]{3,2,1,0:T(2,128)S(1)}, u32[]{:S(2)}, u32[]{:S(2)}) collective-permute-start(f32[3,36,2,256]{3,2,1,0:T(2,128)S(1)} %pad_maximum_fusion.7), channel_id=1, source_target_pairs={{0,1},{1,2},{2,3},{4,5},{5,6},{6,7},{8,9},{9,10},{10,11},{12,13},{... | collective-permute-start | bytes 663560 | tf_op jit(solution)/shard_map/ppermute | solution.py:178
  167.7 3.2 %fusion.7 = f32[3072,256]{1,0:T(8,128)} fusion(s32[256]{0:T(256)S(1)} %get-tuple-element.313, f32[256]{0:T(256)S(1)} %bitcast.120, s32[256]{0:T(256)S(1)} %get-tuple-element.312), kind=kOutput, calls=%fused_computation.26 | convolution fusion | flops 2416836608 | bytes 3148800 | tf_op jit(solution)/shard_map/dot_general | solution.py:394
  171.0 2.1 %collective-permute-done.14.ylo_ref = f32[3,36,2,256]{3,2,1,0:T(2,128)S(1)} collective-permute-done((f32[3,36,2,256]{3,2,1,0:T(2,128)S(1)}, f32[3,36,2,256]{3,2,1,0:T(2,128)S(1)}, u32[]{:S(2)}, u32[]{:S(2)}) %collective-permute-start.14) | collective-permute-done | bytes 221216 | tf_op jit(solution)/shard_map/ppermute | solution.py:178
  173.7 12.8 %shard_map.125 = f32[3,32,32,256]{3,2,1,0:T(8,128)} custom-call(f32[3,32,32,256]{3,2,1,0:T(8,128)} %shard_map.124.u_ref, f32[3,2,32,256]{3,2,1,0:T(8,128)} %copy-done.2, f32[3,2,32,256]{3,2,1,0:T(8,128)} %copy-done.5, f32[3,36,2,256]{3,2,1,0:T(2,128)} %copy-done.13, f32[3,36,2,256]{3,2,1,0:T(2,128)} %copy-done.10, ...), custom_call_target="tpu_custom_call" | custom-call | tf_op jit(solution)/shard_map/pallas_call | solution.py:142
  (136 shorter events, 14.3 us)
Async XLA Ops:
  19.3 10.9 %copy-start.16 = (s32[8192]{0:T(1024)S(1)}, s32[8192]{0:T(1024)}, u32[]{:S(2)}) copy-start(s32[8192]{0:T(1024)} %param.19) | copy-start | bytes 98308
  19.3 10.9 %copy-start.17 = (s32[8192]{0:T(1024)S(1)}, s32[8192]{0:T(1024)}, u32[]{:S(2)}) copy-start(s32[8192]{0:T(1024)} %param.20) | copy-start | bytes 98308
  21.7 22.8 %collective-permute-start = (f32[3,2,32,256]{3,2,1,0:T(8,128)S(1)}, f32[3,2,32,256]{3,2,1,0:T(8,128)S(1)}, u32[]{:S(2)}, u32[]{:S(2)}) collective-permute-start(f32[3,2,32,256]{3,2,1,0:T(8,128)S(1)} %get-tuple-element.282), channel_id=1, source_target_pairs={{0,4},{4,8},{8,12},{12,16},{16,20},{20,24},{24,28},{1,5},{5,9},{9,... | collective-permute-start | bytes 589832 | tf_op jit(solution)/shard_map/ppermute | solution.py:167
  25.1 19.5 %collective-permute-start.1 = (f32[3,2,32,256]{3,2,1,0:T(8,128)S(1)}, f32[3,2,32,256]{3,2,1,0:T(8,128)S(1)}, u32[]{:S(2)}, u32[]{:S(2)}) collective-permute-start(f32[3,2,32,256]{3,2,1,0:T(8,128)S(1)} %get-tuple-element.281), channel_id=1, source_target_pairs={{4,0},{8,4},{12,8},{16,12},{20,16},{24,20},{28,24},{5,1},{9,5},{13... | collective-permute-start | bytes 589832 | tf_op jit(solution)/shard_map/ppermute | solution.py:168
  30.3 14.2 %copy-start.18 = (s32[256]{0:T(256)S(1)}, s32[256]{0:T(256)}, u32[]{:S(2)}) copy-start(s32[256]{0:T(256)} %param.21) | copy-start | bytes 3076
  44.6 15.6 %copy-start = (f32[3,2,32,256]{3,2,1,0:T(8,128)}, f32[3,2,32,256]{3,2,1,0:T(8,128)S(1)}, u32[]{:S(2)}) copy-start(f32[3,2,32,256]{3,2,1,0:T(8,128)S(1)} %collective-permute-done.xlo_ref) | copy-start | bytes 589828
  44.6 15.6 %copy-start.1 = (f32[3,2,32,256]{3,2,1,0:T(8,128)}, f32[3,2,32,256]{3,2,1,0:T(8,128)S(1)}, u32[]{:S(2)}) copy-start(f32[3,2,32,256]{3,2,1,0:T(8,128)S(1)} %collective-permute-done.1.xhi_ref) | copy-start | bytes 589828
  45.3 11.0 %all-to-all-start = ((bf16[2,4,32,256]{3,1,0,2:T(4,128)(2,1)}), bf16[2,4,32,256]{3,1,0,2:T(4,128)(2,1)S(1)}, u32[]{:S(2)}, u32[]{:S(2)}) async-start(bf16[2,4,32,256]{3,1,0,2:T(4,128)(2,1)} %bitcast.95), calls=%async_computation | async-start | bytes 262144 | tf_op jit(solution)/shard_map/all_to_all | solution.py:371
  50.6 9.2 %collective-permute-start.3 = (f32[3,36,2,256]{3,2,1,0:T(2,128)S(1)}, f32[3,36,2,256]{3,2,1,0:T(2,128)S(1)}, u32[]{:S(2)}, u32[]{:S(2)}) collective-permute-start(f32[3,36,2,256]{3,2,1,0:T(2,128)S(1)} %pad_maximum_fusion.2), channel_id=1, source_target_pairs={{1,0},{2,1},{3,2},{5,4},{6,5},{7,6},{9,8},{10,9},{11,10},{13,12},{... | collective-permute-start | bytes 663560 | tf_op jit(solution)/shard_map/ppermute | solution.py:179
  52.9 7.3 %collective-permute-start.2 = (f32[3,36,2,256]{3,2,1,0:T(2,128)S(1)}, f32[3,36,2,256]{3,2,1,0:T(2,128)S(1)}, u32[]{:S(2)}, u32[]{:S(2)}) collective-permute-start(f32[3,36,2,256]{3,2,1,0:T(2,128)S(1)} %pad_maximum_fusion.1), channel_id=1, source_target_pairs={{0,1},{1,2},{2,3},{4,5},{5,6},{6,7},{8,9},{9,10},{10,11},{12,13},{... | collective-permute-start | bytes 663560 | tf_op jit(solution)/shard_map/ppermute | solution.py:178
  59.8 0.7 copy-start.8
  60.1 0.7 copy-start.9
  74.7 11.3 %collective-permute-start.4 = (f32[3,2,32,256]{3,2,1,0:T(8,128)S(1)}, f32[3,2,32,256]{3,2,1,0:T(8,128)S(1)}, u32[]{:S(2)}, u32[]{:S(2)}) collective-permute-start(f32[3,2,32,256]{3,2,1,0:T(8,128)S(1)} %get-tuple-element.278), channel_id=1, source_target_pairs={{0,4},{4,8},{8,12},{12,16},{16,20},{20,24},{24,28},{1,5},{5,9},{9,... | collective-permute-start | bytes 589832 | tf_op jit(solution)/shard_map/ppermute | solution.py:167
  78.1 10.5 %collective-permute-start.5 = (f32[3,2,32,256]{3,2,1,0:T(8,128)S(1)}, f32[3,2,32,256]{3,2,1,0:T(8,128)S(1)}, u32[]{:S(2)}, u32[]{:S(2)}) collective-permute-start(f32[3,2,32,256]{3,2,1,0:T(8,128)S(1)} %get-tuple-element.277), channel_id=1, source_target_pairs={{4,0},{8,4},{12,8},{16,12},{20,16},{24,20},{28,24},{5,1},{9,5},{13... | collective-permute-start | bytes 589832 | tf_op jit(solution)/shard_map/ppermute | solution.py:168
  86.0 12.3 %copy-start.4 = (f32[3,2,32,256]{3,2,1,0:T(8,128)}, f32[3,2,32,256]{3,2,1,0:T(8,128)S(1)}, u32[]{:S(2)}) copy-start(f32[3,2,32,256]{3,2,1,0:T(8,128)S(1)} %collective-permute-done.4.xlo_ref) | copy-start | bytes 589828
  88.6 9.7 %copy-start.7 = (f32[3,2,32,256]{3,2,1,0:T(8,128)}, f32[3,2,32,256]{3,2,1,0:T(8,128)S(1)}, u32[]{:S(2)}) copy-start(f32[3,2,32,256]{3,2,1,0:T(8,128)S(1)} %collective-permute-done.5.xhi_ref) | copy-start | bytes 589828
  88.7 7.7 %collective-permute-start.7 = (f32[3,36,2,256]{3,2,1,0:T(2,128)S(1)}, f32[3,36,2,256]{3,2,1,0:T(2,128)S(1)}, u32[]{:S(2)}, u32[]{:S(2)}) collective-permute-start(f32[3,36,2,256]{3,2,1,0:T(2,128)S(1)} %pad_maximum_fusion.4), channel_id=1, source_target_pairs={{1,0},{2,1},{3,2},{5,4},{6,5},{7,6},{9,8},{10,9},{11,10},{13,12},{... | collective-permute-start | bytes 663560 | tf_op jit(solution)/shard_map/ppermute | solution.py:179
  91.1 7.3 %collective-permute-start.6 = (f32[3,36,2,256]{3,2,1,0:T(2,128)S(1)}, f32[3,36,2,256]{3,2,1,0:T(2,128)S(1)}, u32[]{:S(2)}, u32[]{:S(2)}) collective-permute-start(f32[3,36,2,256]{3,2,1,0:T(2,128)S(1)} %pad_maximum_fusion.3), channel_id=1, source_target_pairs={{0,1},{1,2},{2,3},{4,5},{5,6},{6,7},{8,9},{9,10},{10,11},{12,13},{... | collective-permute-start | bytes 663560 | tf_op jit(solution)/shard_map/ppermute | solution.py:178
  96.4 1.9 %copy-start.12 = (f32[3,36,2,256]{3,2,1,0:T(2,128)}, f32[3,36,2,256]{3,2,1,0:T(2,128)S(1)}, u32[]{:S(2)}) copy-start(f32[3,36,2,256]{3,2,1,0:T(2,128)S(1)} %collective-permute-done.7.yhi_ref) | copy-start | bytes 663556
  98.3 0.7 copy-start.15
  112.9 8.6 %collective-permute-start.8 = (f32[3,2,32,256]{3,2,1,0:T(8,128)S(1)}, f32[3,2,32,256]{3,2,1,0:T(8,128)S(1)}, u32[]{:S(2)}, u32[]{:S(2)}) collective-permute-start(f32[3,2,32,256]{3,2,1,0:T(8,128)S(1)} %get-tuple-element.274), channel_id=1, source_target_pairs={{0,4},{4,8},{8,12},{12,16},{16,20},{20,24},{24,28},{1,5},{5,9},{9,... | collective-permute-start | bytes 589832 | tf_op jit(solution)/shard_map/ppermute | solution.py:167
  114.8 9.4 %collective-permute-start.9 = (f32[3,2,32,256]{3,2,1,0:T(8,128)S(1)}, f32[3,2,32,256]{3,2,1,0:T(8,128)S(1)}, u32[]{:S(2)}, u32[]{:S(2)}) collective-permute-start(f32[3,2,32,256]{3,2,1,0:T(8,128)S(1)} %get-tuple-element.273), channel_id=1, source_target_pairs={{4,0},{8,4},{12,8},{16,12},{20,16},{24,20},{28,24},{5,1},{9,5},{13... | collective-permute-start | bytes 589832 | tf_op jit(solution)/shard_map/ppermute | solution.py:168
  121.4 14.2 %copy-start.3 = (f32[3,2,32,256]{3,2,1,0:T(8,128)}, f32[3,2,32,256]{3,2,1,0:T(8,128)S(1)}, u32[]{:S(2)}) copy-start(f32[3,2,32,256]{3,2,1,0:T(8,128)S(1)} %collective-permute-done.8.xlo_ref) | copy-start | bytes 589828
  124.2 11.4 %copy-start.6 = (f32[3,2,32,256]{3,2,1,0:T(8,128)}, f32[3,2,32,256]{3,2,1,0:T(8,128)S(1)}, u32[]{:S(2)}) copy-start(f32[3,2,32,256]{3,2,1,0:T(8,128)S(1)} %collective-permute-done.9.xhi_ref) | copy-start | bytes 589828
  124.4 9.4 %collective-permute-start.11 = (f32[3,36,2,256]{3,2,1,0:T(2,128)S(1)}, f32[3,36,2,256]{3,2,1,0:T(2,128)S(1)}, u32[]{:S(2)}, u32[]{:S(2)}) collective-permute-start(f32[3,36,2,256]{3,2,1,0:T(2,128)S(1)} %pad_maximum_fusion.6), channel_id=1, source_target_pairs={{1,0},{2,1},{3,2},{5,4},{6,5},{7,6},{9,8},{10,9},{11,10},{13,12},{... | collective-permute-start | bytes 663560 | tf_op jit(solution)/shard_map/ppermute | solution.py:179
  128.4 7.3 %collective-permute-start.10 = (f32[3,36,2,256]{3,2,1,0:T(2,128)S(1)}, f32[3,36,2,256]{3,2,1,0:T(2,128)S(1)}, u32[]{:S(2)}, u32[]{:S(2)}) collective-permute-start(f32[3,36,2,256]{3,2,1,0:T(2,128)S(1)} %pad_maximum_fusion.5), channel_id=1, source_target_pairs={{0,1},{1,2},{2,3},{4,5},{5,6},{6,7},{8,9},{9,10},{10,11},{12,13},{... | collective-permute-start | bytes 663560 | tf_op jit(solution)/shard_map/ppermute | solution.py:178
  133.7 1.9 %copy-start.11 = (f32[3,36,2,256]{3,2,1,0:T(2,128)}, f32[3,36,2,256]{3,2,1,0:T(2,128)S(1)}, u32[]{:S(2)}) copy-start(f32[3,36,2,256]{3,2,1,0:T(2,128)S(1)} %collective-permute-done.11.yhi_ref) | copy-start | bytes 663556
  135.6 0.7 copy-start.14
  150.2 8.5 %collective-permute-start.12 = (f32[3,2,32,256]{3,2,1,0:T(8,128)S(1)}, f32[3,2,32,256]{3,2,1,0:T(8,128)S(1)}, u32[]{:S(2)}, u32[]{:S(2)}) collective-permute-start(f32[3,2,32,256]{3,2,1,0:T(8,128)S(1)} %get-tuple-element.270), channel_id=1, source_target_pairs={{0,4},{4,8},{8,12},{12,16},{16,20},{20,24},{24,28},{1,5},{5,9},{9,... | collective-permute-start | bytes 589832 | tf_op jit(solution)/shard_map/ppermute | solution.py:167
  152.4 8.3 %collective-permute-start.13 = (f32[3,2,32,256]{3,2,1,0:T(8,128)S(1)}, f32[3,2,32,256]{3,2,1,0:T(8,128)S(1)}, u32[]{:S(2)}, u32[]{:S(2)}) collective-permute-start(f32[3,2,32,256]{3,2,1,0:T(8,128)S(1)} %get-tuple-element.269), channel_id=1, source_target_pairs={{4,0},{8,4},{12,8},{16,12},{20,16},{24,20},{28,24},{5,1},{9,5},{13... | collective-permute-start | bytes 589832 | tf_op jit(solution)/shard_map/ppermute | solution.py:168
  158.7 14.3 %copy-start.2 = (f32[3,2,32,256]{3,2,1,0:T(8,128)}, f32[3,2,32,256]{3,2,1,0:T(8,128)S(1)}, u32[]{:S(2)}) copy-start(f32[3,2,32,256]{3,2,1,0:T(8,128)S(1)} %collective-permute-done.12.xlo_ref) | copy-start | bytes 589828
  160.8 12.3 %copy-start.5 = (f32[3,2,32,256]{3,2,1,0:T(8,128)}, f32[3,2,32,256]{3,2,1,0:T(8,128)S(1)}, u32[]{:S(2)}) copy-start(f32[3,2,32,256]{3,2,1,0:T(8,128)S(1)} %collective-permute-done.13.xhi_ref) | copy-start | bytes 589828
  160.9 10.1 %collective-permute-start.15 = (f32[3,36,2,256]{3,2,1,0:T(2,128)S(1)}, f32[3,36,2,256]{3,2,1,0:T(2,128)S(1)}, u32[]{:S(2)}, u32[]{:S(2)}) collective-permute-start(f32[3,36,2,256]{3,2,1,0:T(2,128)S(1)} %pad_maximum_fusion.8), channel_id=1, source_target_pairs={{1,0},{2,1},{3,2},{5,4},{6,5},{7,6},{9,8},{10,9},{11,10},{13,12},{... | collective-permute-start | bytes 663560 | tf_op jit(solution)/shard_map/ppermute | solution.py:179
  165.8 7.3 %collective-permute-start.14 = (f32[3,36,2,256]{3,2,1,0:T(2,128)S(1)}, f32[3,36,2,256]{3,2,1,0:T(2,128)S(1)}, u32[]{:S(2)}, u32[]{:S(2)}) collective-permute-start(f32[3,36,2,256]{3,2,1,0:T(2,128)S(1)} %pad_maximum_fusion.7), channel_id=1, source_target_pairs={{0,1},{1,2},{2,3},{4,5},{5,6},{6,7},{8,9},{9,10},{10,11},{12,13},{... | collective-permute-start | bytes 663560 | tf_op jit(solution)/shard_map/ppermute | solution.py:178
  171.0 2.1 %copy-start.10 = (f32[3,36,2,256]{3,2,1,0:T(2,128)}, f32[3,36,2,256]{3,2,1,0:T(2,128)S(1)}, u32[]{:S(2)}) copy-start(f32[3,36,2,256]{3,2,1,0:T(2,128)S(1)} %collective-permute-done.15.yhi_ref) | copy-start | bytes 663556
  173.0 0.7 copy-start.13

commit v17 on v16

--- a/solution.py
+++ b/solution.py
@@ -334,13 +334,15 @@
     rigidity = level_table(layer_rigidity, layer_of_level)
     damping = level_table(layer_damping, layer_of_level)
     kernel = wave_kernel(angular, slowness, rigidity, damping, NK).astype(jnp.bfloat16)
+    later_now, kernel = lax.optimization_barrier((field_now, kernel))
+    first_x = x_halos(later_now, 2)
     cosines = offset_basis(NK, NR)
     spectrum_table = jnp.dot(
         kernel.reshape(2 * per_device * ND, NK), cosines, preferred_element_type=jnp.float32
     )
     table_rounded = spectrum_table.astype(jnp.bfloat16)
-    later_now, table_rounded = lax.optimization_barrier((field_now, table_rounded))
-    first_x = x_halos(later_now, 2)
+    first_x, table_rounded = lax.optimization_barrier((first_x, table_rounded))
+    first_y = y_halos(field_now, first_x[0], first_x[1], 2)
     all_slots = slot_offset.shape[0]
     width = math.gcd(all_slots, 4096)
     count_blocks = all_slots // width
@@ -366,7 +368,7 @@
     )
     slots_dev = slot_target.shape[0]
     occupied = (jnp.arange(slots_dev, dtype=jnp.int32) < live_count[0]).astype(jnp.float32)
-    first_x, spectra = lax.optimization_barrier((first_x, spectra))
+    first_y, spectra = lax.optimization_barrier((first_y, spectra))
     parcel = spectra.reshape(2, per_device, groups, slots_dev)
     arrived = lax.all_to_all(parcel, ("gx", "gy"), split_axis=2, concat_axis=1, tiled=True)
     freq_order = jnp.arange(F, dtype=jnp.int32)
@@ -395,7 +397,7 @@
         source = source.reshape(3, block_x, block_y, depth)
         if instant == 0:
             xlo, xhi = first_x
-            ylo, yhi = y_halos(current, xlo, xhi, 2)
+            ylo, yhi = first_y
         else:
             xlo, xhi, ylo, yhi = halos(current, 2)
         advanced = elastic_step(current, xlo, xhi, ylo, yhi, previous, moduli, source)

time: 187 us -> 195 us (1.043)
  waiting for transfers between devices: 18.4 us -> 22.8 us
  matrix products: 27.4 us -> 29.6 us
  other arithmetic: 18.6 us -> 20.6 us
    all_to_all x1, waiting for transfers between devices: 1.27 us -> 5.74 us  [shards(): lax.all_to_all(parcel, ('gx', 'gy'), split_axis=2, concat_axis=1, tiled=T...]
    dot_general x1, matrix products: 1.29 us -> 3.48 us  [shards(): jnp.dot(kernel.reshape(2 * per_device * ND, NK), cosines, preferred_eleme...]
  transfers between devices with their start and end apart: 17 -> 17, of which waited for: 11 -> 10; matrix products, arithmetic and copies ran while one was open for 18% -> 20% of each run, Pallas kernels for 0% -> 0%
where the time goes in v17:
time: 195 us
  starting transfers between devices  53.7 us (28%)
  Pallas kernels  51.3 us (26%)
  matrix products  29.6 us (15%)
  waiting for transfers between devices  22.8 us (12%)
  other arithmetic  20.6 us (11%)
  local copies, waits for them, and re-layouts  14.1 us (7%)
    pallas_call x4, Pallas kernels, elastic_step(): pl.pallas_call(kernel, grid=(nx // bx,), in_specs=[pl.BlockSpec(u.shape,...  51.3 us
    ppermute x4, starting transfers between devices, x_halos(): xhi = lax.ppermute(block[:, :width], 'gx', backward_x)  16.3 us
    dot_general x2, matrix products, select_block(): jnp.dot(table_rounded, offset_hot, preferred_element_type=jnp.float32)  13.1 us
    dot_general x4, matrix products, shards(): source = jnp.dot(column_hot, spread, precision=lax.Precision.HIGHEST)  12.9 us
    ppermute x4, starting transfers between devices, y_halos(): yhi = lax.ppermute(rows(slice(0, width)), 'gy', backward_y)  12.8 us
    ppermute x4, starting transfers between devices, x_halos(): xlo = lax.ppermute(block[:, nx - width:], 'gx', forward_x)  10.7 us
    ppermute x4, starting transfers between devices, y_halos(): ylo = lax.ppermute(rows(slice(ny - width, ny)), 'gy', forward_y)  8.76 us
    ppermute x4, waiting for transfers between devices, x_halos(): xhi = lax.ppermute(block[:, :width], 'gx', backward_x)  7.37 us
  transfers between devices with their start and end apart: 17, of which 10 were waited for; matrix products, arithmetic and copies ran while one was open for 20% of the time, Pallas kernels for 0%

profile of v17, /device:TPU:12, one launch (start us, length us, event | category | flops | bytes accessed | tf_op | source)
XLA Modules:
  0.0 194.5 jit_solution(13326564706208940474)
XLA Ops:
  2.9 4.9 %sine_multiply_fusion.1 = (f32[32,4,1024]{2,1,0:T(4,128)S(1)}, f32[32,4,1024]{2,1,0:T(4,128)S(1)}, f32[32,4,1024]{2,1,0:T(4,128)S(1)}) fusion(f32[32]{0:T(128)S(1)} %get-tuple-element.323, f32[32,4]{1,0:T(8,128)S(1)} %copy.24, f32[1024]{0:T(1024)S(1)} %multiply_multiply_fusion, f32[1,4,1024]{2,1,0:T(4,128)S(1)} %slice.153, f32[31,4,1024]{2,1,0:T(4,128)S(1)} %slice.152, ...), kind=kLoop, calls=%fused_computation.41 | loop fusion | flops 1441792 | bytes 2102016 | tf_op jit(solution)/shard_map/mul | solution.py:206
  8.1 2.2 %while.32 = (s32[]{:T(128)}, f32[4,1024]{1,0:T(4,128)S(1)}, f32[4,1024]{1,0:T(4,128)S(1)}, f32[32,4,1024]{2,1,0:T(4,128)S(1)}, f32[32,4,1024]{2,1,0:T(4,128)S(1)...) while((s32[]{:T(128)}, f32[4,1024]{1,0:T(4,128)S(1)}, ...), condition=%wide.region_6.7_spmd.clone, body=%wide.region_5.6_spmd.clone.sunk | while | flops 94212 | bytes 147591 | solution.py:222
  11.2 4.3 %fusion.43 = (bf16[1,32,4,1024]{3,2,1,0:T(4,128)(2,1)S(1)}, bf16[1,32,4,1024]{3,2,1,0:T(4,128)(2,1)S(1)}) fusion(f32[32,4,1024]{2,1,0:T(4,128)S(1)} %get-tuple-element.199, f32[32,4,1024]{2,1,0:T(4,128)S(1)} %get-tuple-element.198, f32[32,4,1024]{2,1,0:T(4,128)S(1)} %negate_exponential_fusion, f32[32,4,1024]{2,1,0:T(4,128)S(1)} %fusion.23), kind=kLoop, calls=%fused_computation.74 | loop fusion | flops 1835008 | bytes 2621440 | tf_op jit(solution)/shard_map/stack | solution.py:235
  15.8 1.1 fusion.85
  16.9 3.4 %collective-permute-start = (f32[3,2,32,256]{3,2,1,0:T(8,128)S(1)}, f32[3,2,32,256]{3,2,1,0:T(8,128)S(1)}, u32[]{:S(2)}, u32[]{:S(2)}) collective-permute-start(f32[3,2,32,256]{3,2,1,0:T(8,128)S(1)} %get-tuple-element.288), channel_id=1, source_target_pairs={{0,4},{4,8},{8,12},{12,16},{16,20},{20,24},{24,28},{1,5},{5,9},{9,... | collective-permute-start | bytes 589832 | tf_op jit(solution)/shard_map/ppermute | solution.py:167
  20.3 3.3 %collective-permute-start.1 = (f32[3,2,32,256]{3,2,1,0:T(8,128)S(1)}, f32[3,2,32,256]{3,2,1,0:T(8,128)S(1)}, u32[]{:S(2)}, u32[]{:S(2)}) collective-permute-start(f32[3,2,32,256]{3,2,1,0:T(8,128)S(1)} %get-tuple-element.287), channel_id=1, source_target_pairs={{4,0},{8,4},{12,8},{16,12},{20,16},{24,20},{28,24},{5,1},{9,5},{13... | collective-permute-start | bytes 589832 | tf_op jit(solution)/shard_map/ppermute | solution.py:168
  23.7 1.5 fusion.84
  27.0 3.6 %subtract_convert_fusion = bf16[1024,32,64]{0,2,1:T(8,128)(2,1)} fusion(f32[1024,64]{0,1:T(8,128)S(1)} %get-tuple-element.317, f32[1024,32]{0,1:T(8,128)S(1)} %get-tuple-element.311, f32[1024,64]{0,1:T(8,128)S(1)} %get-tuple-element.316, f32[1024,32]{0,1:T(8,128)S(1)} %get-tuple-element.310), kind=kLoop, calls=%fused_computation.24 | loop fusion | flops 8388608 | bytes 4980736 | tf_op jit(solution)/shard_map/convert_element_type | solution.py:250
  31.4 3.5 %convolution_convert_fusion = bf16[256,2048]{1,0:T(8,128)(2,1)S(1)} fusion(bf16[256,1024]{1,0:T(8,128)(2,1)S(1)} %bitcast.115, bf16[1024,2048]{0,1:T(8,128)(2,1)} %bitcast.113), kind=kOutput, calls=%fused_computation.30 | convolution fusion | flops 1074266112 | bytes 5767168 | tf_op jit(solution)/shard_map/dot_general | solution.py:340
  35.1 1.9 collective-permute-start.3
  37.1 2.6 %collective-permute-start.2 = (f32[3,36,2,256]{3,2,1,0:T(2,128)S(1)}, f32[3,36,2,256]{3,2,1,0:T(2,128)S(1)}, u32[]{:S(2)}, u32[]{:S(2)}) collective-permute-start(f32[3,36,2,256]{3,2,1,0:T(2,128)S(1)} %pad_maximum_fusion.1), channel_id=1, source_target_pairs={{0,1},{1,2},{2,3},{4,5},{5,6},{6,7},{8,9},{9,10},{10,11},{12,13},{... | collective-permute-start | bytes 663560 | tf_op jit(solution)/shard_map/ppermute | solution.py:178
  39.7 13.4 %while.31 = (s32[]{:T(128)}, bf16[2,2,4,4096]{3,2,1,0:T(4,128)(2,1)S(1)}, s32[2,4096]{1,0:T(2,128)S(1)}, bf16[256,2048]{1,0:T(8,128)(2,1)S(1)}, s32[2,4096]{1,0:T(2,128)S(1)}, /*index=5*/s32[]{:T(128)}) while((s32[]{:T(128)}, bf16[2,2,4,4096]{3,2,1,0:T(4,128)(2,1)S(1)}, s32[2,4096]{1,0:T(2,128)S(1)}, bf16[256,2048]{1,0:T(8,128)(2,1)S(1)}, ...), condition=%wide.region_9.10_spmd, body=%wide.region_7.9_spmd.sunk | while | flops 4305682432 | bytes 2392141 | solution.py:365
  39.8 6.5 %multiply_reduce_fusion.2 = bf16[2,4,4096]{2,1,0:T(4,128)(2,1)S(1)} fusion(f32[32,4096]{1,0:T(8,128)S(1)} %fusion.102, bf16[256,2048]{1,0:T(8,128)(2,1)S(1)} %get-tuple-element.466, s32[4096]{0:T(1024)S(1)} %bitcast.118), kind=kOutput, calls=%fused_computation.3.clone.1 | convolution fusion | flops 4305420288 | bytes 1654784 | tf_op jit(solution)/shard_map/while/body/eval_jaxpr/dot_general | solution.py:357
  46.5 6.5 %multiply_reduce_fusion.2 = bf16[2,4,4096]{2,1,0:T(4,128)(2,1)S(1)} fusion(f32[32,4096]{1,0:T(8,128)S(1)} %fusion.102, bf16[256,2048]{1,0:T(8,128)(2,1)S(1)} %get-tuple-element.466, s32[4096]{0:T(1024)S(1)} %bitcast.118), kind=kOutput, calls=%fused_computation.3.clone.1 | convolution fusion | flops 4305420288 | bytes 1654784 | tf_op jit(solution)/shard_map/while/body/eval_jaxpr/dot_general | solution.py:357
  54.0 5.1 %all-to-all-start = ((bf16[2,4,32,256]{3,1,0,2:T(4,128)(2,1)}), bf16[2,4,32,256]{3,1,0,2:T(4,128)(2,1)S(1)}, u32[]{:S(2)}, u32[]{:S(2)}) async-start(bf16[2,4,32,256]{3,1,0,2:T(4,128)(2,1)} %bitcast.95), calls=%async_computation | async-start | bytes 262144 | tf_op jit(solution)/shard_map/all_to_all | solution.py:373
  59.2 5.7 %all-to-all-done = bf16[2,4,32,256]{3,1,0,2:T(4,128)(2,1)S(1)} async-done(((bf16[2,4,32,256]{3,1,0,2:T(4,128)(2,1)}), bf16[2,4,32,256]{3,1,0,2:T(4,128)(2,1)S(1)}, u32[]{:S(2)}, u32[]{:S(2)}) %all-to-all-start) | async-done | bytes 131104 | tf_op jit(solution)/shard_map/all_to_all | solution.py:373
  65.3 3.2 %fusion.10 = f32[3072,256]{1,0:T(8,128)} fusion(s32[256]{0:T(256)S(1)} %get-tuple-element.319, f32[256]{0:T(256)S(1)} %bitcast.123, s32[256]{0:T(256)S(1)} %get-tuple-element.318), kind=kOutput, calls=%fused_computation.29 | convolution fusion | flops 2416836608 | bytes 3148800 | tf_op jit(solution)/shard_map/dot_general | solution.py:396
  68.5 12.9 %shard_map.122.u_ref.prev_ref = f32[3,32,32,256]{3,2,1,0:T(8,128)} custom-call(f32[3,32,32,256]{3,2,1,0:T(8,128)} %prev_ref.3, f32[3,2,32,256]{3,2,1,0:T(8,128)} %copy-done, f32[3,2,32,256]{3,2,1,0:T(8,128)} %copy-done.1, f32[3,36,2,256]{3,2,1,0:T(2,128)} %copy-done.9, f32[3,36,2,256]{3,2,1,0:T(2,128)} %copy-done.8, f32[3,32,32,256]{3,2,1,0:T(8,128)} %prev_ref.2, ...), custom_call_target="tpu_custom_call" | custom-call | tf_op jit(solution)/shard_map/pallas_call | solution.py:142
  81.3 1.0 fusion.83
  82.4 3.1 %collective-permute-start.4 = (f32[3,2,32,256]{3,2,1,0:T(8,128)S(1)}, f32[3,2,32,256]{3,2,1,0:T(8,128)S(1)}, u32[]{:S(2)}, u32[]{:S(2)}) collective-permute-start(f32[3,2,32,256]{3,2,1,0:T(8,128)S(1)} %get-tuple-element.284), channel_id=1, source_target_pairs={{0,4},{4,8},{8,12},{12,16},{16,20},{20,24},{24,28},{1,5},{5,9},{9,... | collective-permute-start | bytes 589832 | tf_op jit(solution)/shard_map/ppermute | solution.py:167
  85.5 3.6 %collective-permute-start.5 = (f32[3,2,32,256]{3,2,1,0:T(8,128)S(1)}, f32[3,2,32,256]{3,2,1,0:T(8,128)S(1)}, u32[]{:S(2)}, u32[]{:S(2)}) collective-permute-start(f32[3,2,32,256]{3,2,1,0:T(8,128)S(1)} %get-tuple-element.283), channel_id=1, source_target_pairs={{4,0},{8,4},{12,8},{16,12},{20,16},{24,20},{28,24},{5,1},{9,5},{13... | collective-permute-start | bytes 589832 | tf_op jit(solution)/shard_map/ppermute | solution.py:168
  89.1 1.5 fusion.82
  90.7 3.3 %collective-permute-done.4.xlo_ref = f32[3,2,32,256]{3,2,1,0:T(8,128)S(1)} collective-permute-done((f32[3,2,32,256]{3,2,1,0:T(8,128)S(1)}, f32[3,2,32,256]{3,2,1,0:T(8,128)S(1)}, u32[]{:S(2)}, u32[]{:S(2)}) %collective-permute-start.4) | collective-permute-done | bytes 196640 | tf_op jit(solution)/shard_map/ppermute | solution.py:167
  94.0 2.6 %collective-permute-done.5.xhi_ref = f32[3,2,32,256]{3,2,1,0:T(8,128)S(1)} collective-permute-done((f32[3,2,32,256]{3,2,1,0:T(8,128)S(1)}, f32[3,2,32,256]{3,2,1,0:T(8,128)S(1)}, u32[]{:S(2)}, u32[]{:S(2)}) %collective-permute-start.5) | collective-permute-done | bytes 196640 | tf_op jit(solution)/shard_map/ppermute | solution.py:168
  96.6 2.2 %collective-permute-start.7 = (f32[3,36,2,256]{3,2,1,0:T(2,128)S(1)}, f32[3,36,2,256]{3,2,1,0:T(2,128)S(1)}, u32[]{:S(2)}, u32[]{:S(2)}) collective-permute-start(f32[3,36,2,256]{3,2,1,0:T(2,128)S(1)} %pad_maximum_fusion.4), channel_id=1, source_target_pairs={{1,0},{2,1},{3,2},{5,4},{6,5},{7,6},{9,8},{10,9},{11,10},{13,12},{... | collective-permute-start | bytes 663560 | tf_op jit(solution)/shard_map/ppermute | solution.py:179
  99.0 2.1 %collective-permute-start.6 = (f32[3,36,2,256]{3,2,1,0:T(2,128)S(1)}, f32[3,36,2,256]{3,2,1,0:T(2,128)S(1)}, u32[]{:S(2)}, u32[]{:S(2)}) collective-permute-start(f32[3,36,2,256]{3,2,1,0:T(2,128)S(1)} %pad_maximum_fusion.3), channel_id=1, source_target_pairs={{0,1},{1,2},{2,3},{4,5},{5,6},{6,7},{8,9},{9,10},{10,11},{12,13},{... | collective-permute-start | bytes 663560 | tf_op jit(solution)/shard_map/ppermute | solution.py:178
  101.1 3.2 %fusion.9 = f32[3072,256]{1,0:T(8,128)} fusion(s32[256]{0:T(256)S(1)} %get-tuple-element.319, f32[256]{0:T(256)S(1)} %bitcast.122, s32[256]{0:T(256)S(1)} %get-tuple-element.318), kind=kOutput, calls=%fused_computation.28 | convolution fusion | flops 2416836608 | bytes 3148800 | tf_op jit(solution)/shard_map/dot_general | solution.py:396
  104.3 1.9 collective-permute-done.6.ylo_ref
  106.9 12.8 %shard_map.123.u_ref.prev_ref = f32[3,32,32,256]{3,2,1,0:T(8,128)} custom-call(f32[3,32,32,256]{3,2,1,0:T(8,128)} %shard_map.122.u_ref.prev_ref, f32[3,2,32,256]{3,2,1,0:T(8,128)} %copy-done.4, f32[3,2,32,256]{3,2,1,0:T(8,128)} %copy-done.7, f32[3,36,2,256]{3,2,1,0:T(2,128)} %copy-done.15, f32[3,36,2,256]{3,2,1,0:T(2,128)} %copy-done.12, ...), custom_call_target="tpu_custom_call" | custom-call | tf_op jit(solution)/shard_map/pallas_call | solution.py:142
  119.8 1.0 fusion.81
  120.8 1.9 collective-permute-start.8
  122.7 4.8 %collective-permute-start.9 = (f32[3,2,32,256]{3,2,1,0:T(8,128)S(1)}, f32[3,2,32,256]{3,2,1,0:T(8,128)S(1)}, u32[]{:S(2)}, u32[]{:S(2)}) collective-permute-start(f32[3,2,32,256]{3,2,1,0:T(8,128)S(1)} %get-tuple-element.279), channel_id=1, source_target_pairs={{4,0},{8,4},{12,8},{16,12},{20,16},{24,20},{28,24},{5,1},{9,5},{13... | collective-permute-start | bytes 589832 | tf_op jit(solution)/shard_map/ppermute | solution.py:168
  127.6 1.5 fusion.80
  129.4 2.8 %collective-permute-done.9.xhi_ref = f32[3,2,32,256]{3,2,1,0:T(8,128)S(1)} collective-permute-done((f32[3,2,32,256]{3,2,1,0:T(8,128)S(1)}, f32[3,2,32,256]{3,2,1,0:T(8,128)S(1)}, u32[]{:S(2)}, u32[]{:S(2)}) %collective-permute-start.9) | collective-permute-done | bytes 196640 | tf_op jit(solution)/shard_map/ppermute | solution.py:168
  132.3 3.9 %collective-permute-start.11 = (f32[3,36,2,256]{3,2,1,0:T(2,128)S(1)}, f32[3,36,2,256]{3,2,1,0:T(2,128)S(1)}, u32[]{:S(2)}, u32[]{:S(2)}) collective-permute-start(f32[3,36,2,256]{3,2,1,0:T(2,128)S(1)} %pad_maximum_fusion.6), channel_id=1, source_target_pairs={{1,0},{2,1},{3,2},{5,4},{6,5},{7,6},{9,8},{10,9},{11,10},{13,12},{... | collective-permute-start | bytes 663560 | tf_op jit(solution)/shard_map/ppermute | solution.py:179
  136.3 2.1 %collective-permute-start.10 = (f32[3,36,2,256]{3,2,1,0:T(2,128)S(1)}, f32[3,36,2,256]{3,2,1,0:T(2,128)S(1)}, u32[]{:S(2)}, u32[]{:S(2)}) collective-permute-start(f32[3,36,2,256]{3,2,1,0:T(2,128)S(1)} %pad_maximum_fusion.5), channel_id=1, source_target_pairs={{0,1},{1,2},{2,3},{4,5},{5,6},{6,7},{8,9},{9,10},{10,11},{12,13},{... | collective-permute-start | bytes 663560 | tf_op jit(solution)/shard_map/ppermute | solution.py:178
  138.4 3.2 %fusion.8 = f32[3072,256]{1,0:T(8,128)} fusion(s32[256]{0:T(256)S(1)} %get-tuple-element.319, f32[256]{0:T(256)S(1)} %bitcast.121, s32[256]{0:T(256)S(1)} %get-tuple-element.318), kind=kOutput, calls=%fused_computation.27 | convolution fusion | flops 2416836608 | bytes 3148800 | tf_op jit(solution)/shard_map/dot_general | solution.py:396
  141.7 1.9 collective-permute-done.10.ylo_ref
  144.3 12.8 %shard_map.124.u_ref = f32[3,32,32,256]{3,2,1,0:T(8,128)} custom-call(f32[3,32,32,256]{3,2,1,0:T(8,128)} %shard_map.123.u_ref.prev_ref, f32[3,2,32,256]{3,2,1,0:T(8,128)} %copy-done.3, f32[3,2,32,256]{3,2,1,0:T(8,128)} %copy-done.6, f32[3,36,2,256]{3,2,1,0:T(2,128)} %copy-done.14, f32[3,36,2,256]{3,2,1,0:T(2,128)} %copy-done.11, ...), custom_call_target="tpu_custom_call" | custom-call | tf_op jit(solution)/shard_map/pallas_call | solution.py:142
  158.1 2.2 %collective-permute-start.12 = (f32[3,2,32,256]{3,2,1,0:T(8,128)S(1)}, f32[3,2,32,256]{3,2,1,0:T(8,128)S(1)}, u32[]{:S(2)}, u32[]{:S(2)}) collective-permute-start(f32[3,2,32,256]{3,2,1,0:T(8,128)S(1)} %get-tuple-element.276), channel_id=1, source_target_pairs={{0,4},{4,8},{8,12},{12,16},{16,20},{20,24},{24,28},{1,5},{5,9},{9,... | collective-permute-start | bytes 589832 | tf_op jit(solution)/shard_map/ppermute | solution.py:167
  160.4 4.5 %collective-permute-start.13 = (f32[3,2,32,256]{3,2,1,0:T(8,128)S(1)}, f32[3,2,32,256]{3,2,1,0:T(8,128)S(1)}, u32[]{:S(2)}, u32[]{:S(2)}) collective-permute-start(f32[3,2,32,256]{3,2,1,0:T(8,128)S(1)} %get-tuple-element.275), channel_id=1, source_target_pairs={{4,0},{8,4},{12,8},{16,12},{20,16},{24,20},{28,24},{5,1},{9,5},{13... | collective-permute-start | bytes 589832 | tf_op jit(solution)/shard_map/ppermute | solution.py:168
  164.9 1.5 fusion.78
  166.7 2.0 %collective-permute-done.13.xhi_ref = f32[3,2,32,256]{3,2,1,0:T(8,128)S(1)} collective-permute-done((f32[3,2,32,256]{3,2,1,0:T(8,128)S(1)}, f32[3,2,32,256]{3,2,1,0:T(8,128)S(1)}, u32[]{:S(2)}, u32[]{:S(2)}) %collective-permute-start.13) | collective-permute-done | bytes 196640 | tf_op jit(solution)/shard_map/ppermute | solution.py:168
  168.8 4.8 %collective-permute-start.15 = (f32[3,36,2,256]{3,2,1,0:T(2,128)S(1)}, f32[3,36,2,256]{3,2,1,0:T(2,128)S(1)}, u32[]{:S(2)}, u32[]{:S(2)}) collective-permute-start(f32[3,36,2,256]{3,2,1,0:T(2,128)S(1)} %pad_maximum_fusion.8), channel_id=1, source_target_pairs={{1,0},{2,1},{3,2},{5,4},{6,5},{7,6},{9,8},{10,9},{11,10},{13,12},{... | collective-permute-start | bytes 663560 | tf_op jit(solution)/shard_map/ppermute | solution.py:179
  173.7 1.9 collective-permute-start.14
  175.7 3.2 %fusion.7 = f32[3072,256]{1,0:T(8,128)} fusion(s32[256]{0:T(256)S(1)} %get-tuple-element.319, f32[256]{0:T(256)S(1)} %bitcast.120, s32[256]{0:T(256)S(1)} %get-tuple-element.318), kind=kOutput, calls=%fused_computation.26 | convolution fusion | flops 2416836608 | bytes 3148800 | tf_op jit(solution)/shard_map/dot_general | solution.py:396
  178.9 2.1 %collective-permute-done.14.ylo_ref = f32[3,36,2,256]{3,2,1,0:T(2,128)S(1)} collective-permute-done((f32[3,36,2,256]{3,2,1,0:T(2,128)S(1)}, f32[3,36,2,256]{3,2,1,0:T(2,128)S(1)}, u32[]{:S(2)}, u32[]{:S(2)}) %collective-permute-start.14) | collective-permute-done | bytes 221216 | tf_op jit(solution)/shard_map/ppermute | solution.py:178
  181.7 12.8 %shard_map.125 = f32[3,32,32,256]{3,2,1,0:T(8,128)} custom-call(f32[3,32,32,256]{3,2,1,0:T(8,128)} %shard_map.124.u_ref, f32[3,2,32,256]{3,2,1,0:T(8,128)} %copy-done.2, f32[3,2,32,256]{3,2,1,0:T(8,128)} %copy-done.5, f32[3,36,2,256]{3,2,1,0:T(2,128)} %copy-done.13, f32[3,36,2,256]{3,2,1,0:T(2,128)} %copy-done.10, ...), custom_call_target="tpu_custom_call" | custom-call | tf_op jit(solution)/shard_map/pallas_call | solution.py:142
  (136 shorter events, 13.3 us)
Async XLA Ops:
  16.9 18.0 %collective-permute-start = (f32[3,2,32,256]{3,2,1,0:T(8,128)S(1)}, f32[3,2,32,256]{3,2,1,0:T(8,128)S(1)}, u32[]{:S(2)}, u32[]{:S(2)}) collective-permute-start(f32[3,2,32,256]{3,2,1,0:T(8,128)S(1)} %get-tuple-element.288), channel_id=1, source_target_pairs={{0,4},{4,8},{8,12},{12,16},{16,20},{20,24},{24,28},{1,5},{5,9},{9,... | collective-permute-start | bytes 589832 | tf_op jit(solution)/shard_map/ppermute | solution.py:167
  20.3 14.6 %collective-permute-start.1 = (f32[3,2,32,256]{3,2,1,0:T(8,128)S(1)}, f32[3,2,32,256]{3,2,1,0:T(8,128)S(1)}, u32[]{:S(2)}, u32[]{:S(2)}) collective-permute-start(f32[3,2,32,256]{3,2,1,0:T(8,128)S(1)} %get-tuple-element.287), channel_id=1, source_target_pairs={{4,0},{8,4},{12,8},{16,12},{20,16},{24,20},{28,24},{5,1},{9,5},{13... | collective-permute-start | bytes 589832 | tf_op jit(solution)/shard_map/ppermute | solution.py:168
  25.4 5.3 %copy-start.16 = (s32[8192]{0:T(1024)S(1)}, s32[8192]{0:T(1024)}, u32[]{:S(2)}) copy-start(s32[8192]{0:T(1024)} %param.19) | copy-start | bytes 98308
  25.4 5.3 %copy-start.17 = (s32[8192]{0:T(1024)S(1)}, s32[8192]{0:T(1024)}, u32[]{:S(2)}) copy-start(s32[8192]{0:T(1024)} %param.20) | copy-start | bytes 98308
  31.4 3.5 %copy-start.18 = (s32[256]{0:T(256)S(1)}, s32[256]{0:T(256)}, u32[]{:S(2)}) copy-start(s32[256]{0:T(256)} %param.21) | copy-start | bytes 3076
  34.9 4.8 %copy-start = (f32[3,2,32,256]{3,2,1,0:T(8,128)}, f32[3,2,32,256]{3,2,1,0:T(8,128)S(1)}, u32[]{:S(2)}) copy-start(f32[3,2,32,256]{3,2,1,0:T(8,128)S(1)} %collective-permute-done.xlo_ref) | copy-start | bytes 589828
  34.9 4.8 %copy-start.1 = (f32[3,2,32,256]{3,2,1,0:T(8,128)}, f32[3,2,32,256]{3,2,1,0:T(8,128)S(1)}, u32[]{:S(2)}) copy-start(f32[3,2,32,256]{3,2,1,0:T(8,128)S(1)} %collective-permute-done.1.xhi_ref) | copy-start | bytes 589828
  35.1 18.1 %collective-permute-start.3 = (f32[3,36,2,256]{3,2,1,0:T(2,128)S(1)}, f32[3,36,2,256]{3,2,1,0:T(2,128)S(1)}, u32[]{:S(2)}, u32[]{:S(2)}) collective-permute-start(f32[3,36,2,256]{3,2,1,0:T(2,128)S(1)} %pad_maximum_fusion.2), channel_id=1, source_target_pairs={{1,0},{2,1},{3,2},{5,4},{6,5},{7,6},{9,8},{10,9},{11,10},{13,12},{... | collective-permute-start | bytes 663560 | tf_op jit(solution)/shard_map/ppermute | solution.py:179
  37.1 16.1 %collective-permute-start.2 = (f32[3,36,2,256]{3,2,1,0:T(2,128)S(1)}, f32[3,36,2,256]{3,2,1,0:T(2,128)S(1)}, u32[]{:S(2)}, u32[]{:S(2)}) collective-permute-start(f32[3,36,2,256]{3,2,1,0:T(2,128)S(1)} %pad_maximum_fusion.1), channel_id=1, source_target_pairs={{0,1},{1,2},{2,3},{4,5},{5,6},{6,7},{8,9},{9,10},{10,11},{12,13},{... | collective-permute-start | bytes 663560 | tf_op jit(solution)/shard_map/ppermute | solution.py:178
  53.2 15.3 %copy-start.8 = (f32[3,36,2,256]{3,2,1,0:T(2,128)}, f32[3,36,2,256]{3,2,1,0:T(2,128)S(1)}, u32[]{:S(2)}) copy-start(f32[3,36,2,256]{3,2,1,0:T(2,128)S(1)} %collective-permute-done.3.yhi_ref) | copy-start | bytes 663556
  53.2 15.3 %copy-start.9 = (f32[3,36,2,256]{3,2,1,0:T(2,128)}, f32[3,36,2,256]{3,2,1,0:T(2,128)S(1)}, u32[]{:S(2)}) copy-start(f32[3,36,2,256]{3,2,1,0:T(2,128)S(1)} %collective-permute-done.2.ylo_ref) | copy-start | bytes 663556
  54.0 11.0 %all-to-all-start = ((bf16[2,4,32,256]{3,1,0,2:T(4,128)(2,1)}), bf16[2,4,32,256]{3,1,0,2:T(4,128)(2,1)S(1)}, u32[]{:S(2)}, u32[]{:S(2)}) async-start(bf16[2,4,32,256]{3,1,0,2:T(4,128)(2,1)} %bitcast.95), calls=%async_computation | async-start | bytes 262144 | tf_op jit(solution)/shard_map/all_to_all | solution.py:373
  82.4 11.6 %collective-permute-start.4 = (f32[3,2,32,256]{3,2,1,0:T(8,128)S(1)}, f32[3,2,32,256]{3,2,1,0:T(8,128)S(1)}, u32[]{:S(2)}, u32[]{:S(2)}) collective-permute-start(f32[3,2,32,256]{3,2,1,0:T(8,128)S(1)} %get-tuple-element.284), channel_id=1, source_target_pairs={{0,4},{4,8},{8,12},{12,16},{16,20},{20,24},{24,28},{1,5},{5,9},{9,... | collective-permute-start | bytes 589832 | tf_op jit(solution)/shard_map/ppermute | solution.py:167
  85.5 11.0 %collective-permute-start.5 = (f32[3,2,32,256]{3,2,1,0:T(8,128)S(1)}, f32[3,2,32,256]{3,2,1,0:T(8,128)S(1)}, u32[]{:S(2)}, u32[]{:S(2)}) collective-permute-start(f32[3,2,32,256]{3,2,1,0:T(8,128)S(1)} %get-tuple-element.283), channel_id=1, source_target_pairs={{4,0},{8,4},{12,8},{16,12},{20,16},{24,20},{28,24},{5,1},{9,5},{13... | collective-permute-start | bytes 589832 | tf_op jit(solution)/shard_map/ppermute | solution.py:168
  93.9 12.3 %copy-start.4 = (f32[3,2,32,256]{3,2,1,0:T(8,128)}, f32[3,2,32,256]{3,2,1,0:T(8,128)S(1)}, u32[]{:S(2)}) copy-start(f32[3,2,32,256]{3,2,1,0:T(8,128)S(1)} %collective-permute-done.4.xlo_ref) | copy-start | bytes 589828
  96.5 9.7 %copy-start.7 = (f32[3,2,32,256]{3,2,1,0:T(8,128)}, f32[3,2,32,256]{3,2,1,0:T(8,128)S(1)}, u32[]{:S(2)}) copy-start(f32[3,2,32,256]{3,2,1,0:T(8,128)S(1)} %collective-permute-done.5.xhi_ref) | copy-start | bytes 589828
  96.6 7.7 %collective-permute-start.7 = (f32[3,36,2,256]{3,2,1,0:T(2,128)S(1)}, f32[3,36,2,256]{3,2,1,0:T(2,128)S(1)}, u32[]{:S(2)}, u32[]{:S(2)}) collective-permute-start(f32[3,36,2,256]{3,2,1,0:T(2,128)S(1)} %pad_maximum_fusion.4), channel_id=1, source_target_pairs={{1,0},{2,1},{3,2},{5,4},{6,5},{7,6},{9,8},{10,9},{11,10},{13,12},{... | collective-permute-start | bytes 663560 | tf_op jit(solution)/shard_map/ppermute | solution.py:179
  99.0 7.3 %collective-permute-start.6 = (f32[3,36,2,256]{3,2,1,0:T(2,128)S(1)}, f32[3,36,2,256]{3,2,1,0:T(2,128)S(1)}, u32[]{:S(2)}, u32[]{:S(2)}) collective-permute-start(f32[3,36,2,256]{3,2,1,0:T(2,128)S(1)} %pad_maximum_fusion.3), channel_id=1, source_target_pairs={{0,1},{1,2},{2,3},{4,5},{5,6},{6,7},{8,9},{9,10},{10,11},{12,13},{... | collective-permute-start | bytes 663560 | tf_op jit(solution)/shard_map/ppermute | solution.py:178
  104.3 1.9 copy-start.12
  106.2 0.7 copy-start.15
  120.8 8.6 %collective-permute-start.8 = (f32[3,2,32,256]{3,2,1,0:T(8,128)S(1)}, f32[3,2,32,256]{3,2,1,0:T(8,128)S(1)}, u32[]{:S(2)}, u32[]{:S(2)}) collective-permute-start(f32[3,2,32,256]{3,2,1,0:T(8,128)S(1)} %get-tuple-element.280), channel_id=1, source_target_pairs={{0,4},{4,8},{8,12},{12,16},{16,20},{20,24},{24,28},{1,5},{5,9},{9,... | collective-permute-start | bytes 589832 | tf_op jit(solution)/shard_map/ppermute | solution.py:167
  122.7 9.4 %collective-permute-start.9 = (f32[3,2,32,256]{3,2,1,0:T(8,128)S(1)}, f32[3,2,32,256]{3,2,1,0:T(8,128)S(1)}, u32[]{:S(2)}, u32[]{:S(2)}) collective-permute-start(f32[3,2,32,256]{3,2,1,0:T(8,128)S(1)} %get-tuple-element.279), channel_id=1, source_target_pairs={{4,0},{8,4},{12,8},{16,12},{20,16},{24,20},{28,24},{5,1},{9,5},{13... | collective-permute-start | bytes 589832 | tf_op jit(solution)/shard_map/ppermute | solution.py:168
  129.4 14.2 %copy-start.3 = (f32[3,2,32,256]{3,2,1,0:T(8,128)}, f32[3,2,32,256]{3,2,1,0:T(8,128)S(1)}, u32[]{:S(2)}) copy-start(f32[3,2,32,256]{3,2,1,0:T(8,128)S(1)} %collective-permute-done.8.xlo_ref) | copy-start | bytes 589828
  132.2 11.4 %copy-start.6 = (f32[3,2,32,256]{3,2,1,0:T(8,128)}, f32[3,2,32,256]{3,2,1,0:T(8,128)S(1)}, u32[]{:S(2)}) copy-start(f32[3,2,32,256]{3,2,1,0:T(8,128)S(1)} %collective-permute-done.9.xhi_ref) | copy-start | bytes 589828
  132.3 9.4 %collective-permute-start.11 = (f32[3,36,2,256]{3,2,1,0:T(2,128)S(1)}, f32[3,36,2,256]{3,2,1,0:T(2,128)S(1)}, u32[]{:S(2)}, u32[]{:S(2)}) collective-permute-start(f32[3,36,2,256]{3,2,1,0:T(2,128)S(1)} %pad_maximum_fusion.6), channel_id=1, source_target_pairs={{1,0},{2,1},{3,2},{5,4},{6,5},{7,6},{9,8},{10,9},{11,10},{13,12},{... | collective-permute-start | bytes 663560 | tf_op jit(solution)/shard_map/ppermute | solution.py:179
  136.3 7.3 %collective-permute-start.10 = (f32[3,36,2,256]{3,2,1,0:T(2,128)S(1)}, f32[3,36,2,256]{3,2,1,0:T(2,128)S(1)}, u32[]{:S(2)}, u32[]{:S(2)}) collective-permute-start(f32[3,36,2,256]{3,2,1,0:T(2,128)S(1)} %pad_maximum_fusion.5), channel_id=1, source_target_pairs={{0,1},{1,2},{2,3},{4,5},{5,6},{6,7},{8,9},{9,10},{10,11},{12,13},{... | collective-permute-start | bytes 663560 | tf_op jit(solution)/shard_map/ppermute | solution.py:178
  141.7 1.9 copy-start.11
  143.6 0.7 copy-start.14
  158.1 8.5 %collective-permute-start.12 = (f32[3,2,32,256]{3,2,1,0:T(8,128)S(1)}, f32[3,2,32,256]{3,2,1,0:T(8,128)S(1)}, u32[]{:S(2)}, u32[]{:S(2)}) collective-permute-start(f32[3,2,32,256]{3,2,1,0:T(8,128)S(1)} %get-tuple-element.276), channel_id=1, source_target_pairs={{0,4},{4,8},{8,12},{12,16},{16,20},{20,24},{24,28},{1,5},{5,9},{9,... | collective-permute-start | bytes 589832 | tf_op jit(solution)/shard_map/ppermute | solution.py:167
  160.4 8.3 %collective-permute-start.13 = (f32[3,2,32,256]{3,2,1,0:T(8,128)S(1)}, f32[3,2,32,256]{3,2,1,0:T(8,128)S(1)}, u32[]{:S(2)}, u32[]{:S(2)}) collective-permute-start(f32[3,2,32,256]{3,2,1,0:T(8,128)S(1)} %get-tuple-element.275), channel_id=1, source_target_pairs={{4,0},{8,4},{12,8},{16,12},{20,16},{24,20},{28,24},{5,1},{9,5},{13... | collective-permute-start | bytes 589832 | tf_op jit(solution)/shard_map/ppermute | solution.py:168
  166.6 14.3 %copy-start.2 = (f32[3,2,32,256]{3,2,1,0:T(8,128)}, f32[3,2,32,256]{3,2,1,0:T(8,128)S(1)}, u32[]{:S(2)}) copy-start(f32[3,2,32,256]{3,2,1,0:T(8,128)S(1)} %collective-permute-done.12.xlo_ref) | copy-start | bytes 589828
  168.7 12.3 %copy-start.5 = (f32[3,2,32,256]{3,2,1,0:T(8,128)}, f32[3,2,32,256]{3,2,1,0:T(8,128)S(1)}, u32[]{:S(2)}) copy-start(f32[3,2,32,256]{3,2,1,0:T(8,128)S(1)} %collective-permute-done.13.xhi_ref) | copy-start | bytes 589828
  168.8 10.1 %collective-permute-start.15 = (f32[3,36,2,256]{3,2,1,0:T(2,128)S(1)}, f32[3,36,2,256]{3,2,1,0:T(2,128)S(1)}, u32[]{:S(2)}, u32[]{:S(2)}) collective-permute-start(f32[3,36,2,256]{3,2,1,0:T(2,128)S(1)} %pad_maximum_fusion.8), channel_id=1, source_target_pairs={{1,0},{2,1},{3,2},{5,4},{6,5},{7,6},{9,8},{10,9},{11,10},{13,12},{... | collective-permute-start | bytes 663560 | tf_op jit(solution)/shard_map/ppermute | solution.py:179
  173.7 7.3 %collective-permute-start.14 = (f32[3,36,2,256]{3,2,1,0:T(2,128)S(1)}, f32[3,36,2,256]{3,2,1,0:T(2,128)S(1)}, u32[]{:S(2)}, u32[]{:S(2)}) collective-permute-start(f32[3,36,2,256]{3,2,1,0:T(2,128)S(1)} %pad_maximum_fusion.7), channel_id=1, source_target_pairs={{0,1},{1,2},{2,3},{4,5},{5,6},{6,7},{8,9},{9,10},{10,11},{12,13},{... | collective-permute-start | bytes 663560 | tf_op jit(solution)/shard_map/ppermute | solution.py:178
  178.9 2.1 %copy-start.10 = (f32[3,36,2,256]{3,2,1,0:T(2,128)}, f32[3,36,2,256]{3,2,1,0:T(2,128)S(1)}, u32[]{:S(2)}) copy-start(f32[3,36,2,256]{3,2,1,0:T(2,128)S(1)} %collective-permute-done.15.yhi_ref) | copy-start | bytes 663556
  181.0 0.7 copy-start.13
